TPU v7x, 256 devices: a whole 4x4x8 slice. The times are simulated.
256 devices in a mesh: section: 8 (over z), ctx: 32 (over x, y, core).
Axes of the slice: x: 4, y: 4, z: 8, core: 2. Of those that a mesh axis runs over, the one named last changes fastest.
Arguments:
- query_rows: bfloat16 [8, 8192, 2048], P('section', 'ctx'), may hold values from -40 to 40
- key_rows: bfloat16 [8, 8192, 1024], P('section', 'ctx'), may hold values from -6 to 6
- value_rows: bfloat16 [8, 8192, 1024], P('section', 'ctx'), may hold values from -6 to 6
- finished_grad: bfloat16 [8, 8192, 2048], P('section', 'ctx'), may hold values from -96 to 96
- doc_lengths: int32 [4], replicated, may hold values from 1 to 4096, as said below
Outputs:
- query_grad: bfloat16 [8, 8192, 2048], P('section', 'ctx')
- key_grad: bfloat16 [8, 8192, 1024], P('section', 'ctx')
- value_grad: bfloat16 [8, 8192, 1024], P('section', 'ctx')
Inputs may be any that keep to these rules, and one draw needn't show every extreme that they name: `doc_lengths`: document lengths add up to 8192; the longest is exactly 4096.
All inputs are finite; a program needn't handle non-finite values.
Results may differ from a plain program's by a relative error of at most 0.04.
Values may be sent and summed in bfloat16 or wider, within the bound.
No kernel may reach another device: no remote copies, remote signals or barrier semaphores. Data moves between devices by JAX's collectives and lax.ppermute only.
A program may use at most 128 MiB of HBM per device.

v0:
```python
import jax
import jax.numpy as jnp
from jax import lax
from jax.sharding import PartitionSpec as P

WINDOW = 1024
KV_HEADS = 8


SCORE_SCALE = 168.0 ** (-0.5)


def passed_along(shard, axis, by):
    count = lax.axis_size(axis)
    return lax.ppermute(shard, axis, [(i, (i + by) % count) for i in range(count)])


def shifted(value, axis, steps):
    count = lax.axis_size(axis)
    initial, last = (max(0, -steps), min(count, count - steps))
    return lax.ppermute(value, axis, [(source, source + steps) for source in range(initial, last)])


def doc_number(positions, doc_lengths):
    ends = jnp.cumsum(doc_lengths)
    return jnp.sum((positions[:, None] >= ends[None, :]).astype(jnp.int32), axis=1)


def window_mask(query_pos, key_pos, doc_lengths):
    same_doc = (
        doc_number(query_pos, doc_lengths)[:, None] == doc_number(key_pos, doc_lengths)[None, :]
    )
    spacing = query_pos[:, None] - key_pos[None, :]
    return same_doc & (spacing >= 0) & (spacing < WINDOW) & (key_pos[None, :] >= 0)


def group_pass(query_part, key_part, value_part, grad_part, allowed):
    count_rows = query_part.shape[0]
    head_size = key_part.shape[1]
    query_head = query_part.reshape(count_rows, -1, head_size)
    grad_head = grad_part.reshape(count_rows, -1, head_size)
    scores = SCORE_SCALE * jnp.einsum(
        "rjd,kd->jrk", query_head, key_part, preferred_element_type=jnp.float32
    )
    scores = jnp.where(allowed[None], scores, -jnp.inf)
    highest = jnp.max(scores, axis=-1, keepdims=True)
    log_total = highest + jnp.log(jnp.sum(jnp.exp(scores - highest), axis=-1, keepdims=True))
    weights = jnp.exp(scores - log_total)
    weight_half = weights.astype(jnp.bfloat16)
    attended = jnp.einsum(
        "jrk,kd->rjd", weight_half, value_part, preferred_element_type=jnp.float32
    ).astype(jnp.bfloat16)
    row_dot = jnp.transpose(
        jnp.sum(attended.astype(jnp.float32) * grad_head.astype(jnp.float32), axis=-1)
    )
    weight_grad = jnp.einsum(
        "rjd,kd->jrk", grad_head, value_part, preferred_element_type=jnp.float32
    )
    score_grad = (weights * (weight_grad - row_dot[:, :, None])).astype(jnp.bfloat16)
    query_back = SCORE_SCALE * jnp.einsum(
        "jrk,kd->rjd", score_grad, key_part, preferred_element_type=jnp.float32
    )
    key_back = SCORE_SCALE * jnp.einsum(
        "jrk,rjd->kd", score_grad, query_head, preferred_element_type=jnp.float32
    )
    value_back = jnp.einsum(
        "jrk,rjd->kd", weight_half, grad_head, preferred_element_type=jnp.float32
    )
    return (query_back.reshape(count_rows, -1), key_back, value_back, log_total[:, :, 0], row_dot)


def local(query_rows, key_rows, value_rows, finished_grad, doc_lengths):
    queries = query_rows[0]
    keys_here = key_rows[0]
    values_here = value_rows[0]
    count_rows = queries.shape[0]
    reach_blocks = WINDOW // count_rows
    pair_width = keys_here.shape[1]
    head_size = pair_width // KV_HEADS
    group_width = queries.shape[1] // KV_HEADS
    heads_group = group_width // head_size
    rank_here = lax.axis_index("ctx")
    first_pos = rank_here * count_rows
    arriving = passed_along(finished_grad, "section", -1)[0]
    own_pair = jnp.stack([keys_here, values_here])
    pieces = [shifted(own_pair, "ctx", distance) for distance in range(reach_blocks, 0, -1)] + [
        own_pair
    ]
    window_pair = jnp.concatenate(pieces, axis=1)
    span = window_pair.shape[1]
    query_pos = first_pos + jnp.arange(count_rows, dtype=jnp.int32)
    key_pos = first_pos - WINDOW + jnp.arange(span, dtype=jnp.int32)
    allowed = window_mask(query_pos, key_pos, doc_lengths)

    def per_group(group, carry):
        query_acc, keys_acc, values_acc, log_totals, row_dots = carry
        query_part = lax.dynamic_slice_in_dim(queries, group * group_width, group_width, 1)
        grad_part = lax.dynamic_slice_in_dim(arriving, group * group_width, group_width, 1)
        key_part = lax.dynamic_slice_in_dim(window_pair[0], group * head_size, head_size, 1)
        value_part = lax.dynamic_slice_in_dim(window_pair[1], group * head_size, head_size, 1)
        query_back, key_back, value_back, log_total, row_dot = group_pass(
            query_part, key_part, value_part, grad_part, allowed
        )
        query_acc = lax.dynamic_update_slice_in_dim(
            query_acc, query_back.astype(jnp.bfloat16), group * group_width, 1
        )
        keys_acc = lax.dynamic_update_slice_in_dim(keys_acc, key_back, group * head_size, 1)
        values_acc = lax.dynamic_update_slice_in_dim(values_acc, value_back, group * head_size, 1)
        log_totals = lax.dynamic_update_slice_in_dim(log_totals, log_total, group * heads_group, 0)
        row_dots = lax.dynamic_update_slice_in_dim(row_dots, row_dot, group * heads_group, 0)
        return (query_acc, keys_acc, values_acc, log_totals, row_dots)

    start_carry = (
        jnp.zeros(queries.shape, jnp.bfloat16),
        jnp.zeros((span, pair_width), jnp.float32),
        jnp.zeros((span, pair_width), jnp.float32),
        jnp.zeros((KV_HEADS * heads_group, count_rows), jnp.float32),
        jnp.zeros((KV_HEADS * heads_group, count_rows), jnp.float32),
    )
    grad_query, grad_keys, grad_values, log_totals, row_dots = lax.fori_loop(
        0, KV_HEADS, per_group, start_carry
    )
    own_start = reach_blocks * count_rows
    grad_pair = jnp.stack([grad_keys, grad_values])
    key_total = grad_pair[:, own_start:]
    for distance in range(1, reach_blocks + 1):
        lower = (reach_blocks - distance) * count_rows
        sent_terms = grad_pair[:, lower : lower + count_rows].astype(jnp.bfloat16)
        key_total = key_total + shifted(sent_terms, "ctx", -distance).astype(jnp.float32)
    return (
        grad_query[None],
        key_total[0].astype(jnp.bfloat16)[None],
        key_total[1].astype(jnp.bfloat16)[None],
    )


def solution(mesh):
    return jax.shard_map(
        local,
        mesh=mesh,
        in_specs=(
            P("section", "ctx", None),
            P("section", "ctx", None),
            P("section", "ctx", None),
            P("section", "ctx", None),
            P(),
        ),
        out_specs=(P("section", "ctx", None), P("section", "ctx", None), P("section", "ctx", None)),
        check_vma=False,
    )
```

profile of v0, /device:TPU:120, one launch (start us, length us, event | category | flops | bytes accessed | tf_op | source)
XLA Modules:
  0.0 303.9 jit_solution(7399210223299168528)
XLA Ops:
  0.7 2.0 constant_dynamic-update-slice_fusion.2
  2.7 1.9 constant_dynamic-update-slice_fusion.1
  4.5 4.1 %collective-permute-start = (bf16[2,256,1024]{2,1,0:T(8,128)(2,1)}, bf16[2,256,1024]{2,1,0:T(8,128)(2,1)}, u32[]{:S(2)}, u32[]{:S(2)}) collective-permute-start(bf16[2,256,1024]{2,1,0:T(8,128)(2,1)} %constant_dynamic-update-slice_fusion.1), channel_id=1, source_target_pairs={{0,4},{1,5},{2,6},{3,7},{4,8},{5,9},{6,10},{7,11},{8,12},{9,13},{1... | collective-permute-start | bytes 3145736 | tf_op jit(solution)/shard_map/ppermute | solution.py:21
  8.6 3.3 %collective-permute-start.1 = (bf16[2,256,1024]{2,1,0:T(8,128)(2,1)}, bf16[2,256,1024]{2,1,0:T(8,128)(2,1)}, u32[]{:S(2)}, u32[]{:S(2)}) collective-permute-start(bf16[2,256,1024]{2,1,0:T(8,128)(2,1)} %constant_dynamic-update-slice_fusion.1), channel_id=1, source_target_pairs={{0,3},{1,4},{2,5},{3,6},{4,7},{5,8},{6,9},{7,10},{8,11},{9,12},{10... | collective-permute-start | bytes 3145736 | tf_op jit(solution)/shard_map/ppermute | solution.py:21
  11.9 2.8 collective-permute-start.2
  14.6 3.0 collective-permute-start.3
  18.6 1.3 copy.33
  20.1 14.2 %collective-permute-done = bf16[2,256,1024]{2,1,0:T(8,128)(2,1)} collective-permute-done((bf16[2,256,1024]{2,1,0:T(8,128)(2,1)}, bf16[2,256,1024]{2,1,0:T(8,128)(2,1)}, u32[]{:S(2)}, u32[]{:S(2)}) %collective-permute-start) | collective-permute-done | bytes 1048608 | tf_op jit(solution)/shard_map/ppermute | solution.py:21
  34.3 2.3 constant_dynamic-update-slice_fusion.8
  36.6 19.7 %collective-permute-done.1 = bf16[2,256,1024]{2,1,0:T(8,128)(2,1)} collective-permute-done((bf16[2,256,1024]{2,1,0:T(8,128)(2,1)}, bf16[2,256,1024]{2,1,0:T(8,128)(2,1)}, u32[]{:S(2)}, u32[]{:S(2)}) %collective-permute-start.1) | collective-permute-done | bytes 1048608 | tf_op jit(solution)/shard_map/ppermute | solution.py:21
  56.3 2.3 constant_dynamic-update-slice_fusion.7
  58.5 20.2 %collective-permute-done.2 = bf16[2,256,1024]{2,1,0:T(8,128)(2,1)} collective-permute-done((bf16[2,256,1024]{2,1,0:T(8,128)(2,1)}, bf16[2,256,1024]{2,1,0:T(8,128)(2,1)}, u32[]{:S(2)}, u32[]{:S(2)}) %collective-permute-start.2) | collective-permute-done | bytes 1048608 | tf_op jit(solution)/shard_map/ppermute | solution.py:21
  78.7 2.3 constant_dynamic-update-slice_fusion.6
  81.0 2.3 constant_dynamic-update-slice_fusion.5
  85.0 1.1 broadcast_in_dim.53.clone
  86.1 3.0 broadcast.53.clone
  89.1 3.0 broadcast.53
  92.0 99.1 %while.18 = (s32[]{:T(128)}, bf16[256,2048]{1,0:T(8,128)(2,1)}, f32[1280,1024]{1,0:T(8,128)}, f32[1280,1024]{1,0:T(8,128)}, bf16[2,1280,1024]{2,1,0:T(8,128)(2,1...) while((s32[]{:T(128)}, bf16[256,2048]{1,0:T(8,128)(2,1)}, ...), condition=%wide.region_7.8_spmd.clone, body=%wide.region_3.7_spmd.clone.sunk | while | flops 1018067968 | bytes 43159136 | solution.py:120
  93.0 1.1 fusion.81
  94.1 3.1 %fusion.80 = (bf16[1,1280,1024]{2,1,0:T(8,128)(2,1)S(1)}, bf16[1,1280,1024]{2,1,0:T(8,128)(2,1)S(1)}) fusion(bf16[2,1280,1024]{2,1,0:T(8,128)(2,1)} %get-tuple-element.339), kind=kLoop, calls=%fused_computation.67.clone.1 | loop fusion | bytes 10485760 | tf_op jit(solution)/shard_map/while/body/eval_jaxpr/slice | solution.py:100
  99.4 1.1 copy-done
  101.6 1.4 fusion.87
  103.0 1.4 fusion.86
  105.4 1.1 fusion.81
  106.5 3.1 %fusion.80 = (bf16[1,1280,1024]{2,1,0:T(8,128)(2,1)S(1)}, bf16[1,1280,1024]{2,1,0:T(8,128)(2,1)S(1)}) fusion(bf16[2,1280,1024]{2,1,0:T(8,128)(2,1)} %get-tuple-element.339), kind=kLoop, calls=%fused_computation.67.clone.1 | loop fusion | bytes 10485760 | tf_op jit(solution)/shard_map/while/body/eval_jaxpr/slice | solution.py:100
  111.8 1.1 copy-done
  114.0 1.4 fusion.87
  115.4 1.4 fusion.86
  117.8 1.1 fusion.81
  118.9 3.1 %fusion.80 = (bf16[1,1280,1024]{2,1,0:T(8,128)(2,1)S(1)}, bf16[1,1280,1024]{2,1,0:T(8,128)(2,1)S(1)}) fusion(bf16[2,1280,1024]{2,1,0:T(8,128)(2,1)} %get-tuple-element.339), kind=kLoop, calls=%fused_computation.67.clone.1 | loop fusion | bytes 10485760 | tf_op jit(solution)/shard_map/while/body/eval_jaxpr/slice | solution.py:100
  124.1 1.1 copy-done
  126.4 1.4 fusion.87
  127.8 1.4 fusion.86
  130.2 1.1 fusion.81
  131.3 3.1 %fusion.80 = (bf16[1,1280,1024]{2,1,0:T(8,128)(2,1)S(1)}, bf16[1,1280,1024]{2,1,0:T(8,128)(2,1)S(1)}) fusion(bf16[2,1280,1024]{2,1,0:T(8,128)(2,1)} %get-tuple-element.339), kind=kLoop, calls=%fused_computation.67.clone.1 | loop fusion | bytes 10485760 | tf_op jit(solution)/shard_map/while/body/eval_jaxpr/slice | solution.py:100
  136.5 1.1 copy-done
  138.8 1.4 fusion.87
  140.2 1.4 fusion.86
  142.5 1.1 fusion.81
  143.6 3.1 %fusion.80 = (bf16[1,1280,1024]{2,1,0:T(8,128)(2,1)S(1)}, bf16[1,1280,1024]{2,1,0:T(8,128)(2,1)S(1)}) fusion(bf16[2,1280,1024]{2,1,0:T(8,128)(2,1)} %get-tuple-element.339), kind=kLoop, calls=%fused_computation.67.clone.1 | loop fusion | bytes 10485760 | tf_op jit(solution)/shard_map/while/body/eval_jaxpr/slice | solution.py:100
  148.9 1.1 copy-done
  151.1 1.4 fusion.87
  152.6 1.4 fusion.86
  154.9 1.1 fusion.81
  156.0 3.1 %fusion.80 = (bf16[1,1280,1024]{2,1,0:T(8,128)(2,1)S(1)}, bf16[1,1280,1024]{2,1,0:T(8,128)(2,1)S(1)}) fusion(bf16[2,1280,1024]{2,1,0:T(8,128)(2,1)} %get-tuple-element.339), kind=kLoop, calls=%fused_computation.67.clone.1 | loop fusion | bytes 10485760 | tf_op jit(solution)/shard_map/while/body/eval_jaxpr/slice | solution.py:100
  163.5 1.4 fusion.87
  165.0 1.4 fusion.86
  167.4 1.1 fusion.81
  168.5 3.1 %fusion.80 = (bf16[1,1280,1024]{2,1,0:T(8,128)(2,1)S(1)}, bf16[1,1280,1024]{2,1,0:T(8,128)(2,1)S(1)}) fusion(bf16[2,1280,1024]{2,1,0:T(8,128)(2,1)} %get-tuple-element.339), kind=kLoop, calls=%fused_computation.67.clone.1 | loop fusion | bytes 10485760 | tf_op jit(solution)/shard_map/while/body/eval_jaxpr/slice | solution.py:100
  175.9 1.4 fusion.87
  177.3 1.4 fusion.86
  179.7 1.1 fusion.81
  180.8 3.1 %fusion.80 = (bf16[1,1280,1024]{2,1,0:T(8,128)(2,1)S(1)}, bf16[1,1280,1024]{2,1,0:T(8,128)(2,1)S(1)}) fusion(bf16[2,1280,1024]{2,1,0:T(8,128)(2,1)} %get-tuple-element.339), kind=kLoop, calls=%fused_computation.67.clone.1 | loop fusion | bytes 10485760 | tf_op jit(solution)/shard_map/while/body/eval_jaxpr/slice | solution.py:100
  188.3 1.4 fusion.87
  189.7 1.4 fusion.86
  191.1 7.7 %fusion.33 = bf16[2,1280,1024]{2,1,0:T(8,128)(2,1)} fusion(f32[1,1280,1024]{2,1,0:T(8,128)} %bitcast.104, f32[1,1280,1024]{2,1,0:T(8,128)} %bitcast.108), kind=kLoop, calls=%fused_computation.47 | loop fusion | flops 2621440 | bytes 15728640 | tf_op jit(solution)/shard_map/convert.6
  198.8 2.9 fusion.42
  201.7 1.9 collective-permute-start.5
  203.6 12.7 %collective-permute-start.8 = (bf16[2,256,1024]{2,1,0:T(8,128)(2,1)S(1)}, bf16[2,256,1024]{2,1,0:T(8,128)(2,1)S(1)}, u32[]{:S(2)}, u32[]{:S(2)}) collective-permute-start(bf16[2,256,1024]{2,1,0:T(8,128)(2,1)S(1)} %get-tuple-element.209), channel_id=1, source_target_pairs={{4,0},{5,1},{6,2},{7,3},{8,4},{9,5},{10,6},{11,7},{12,8},{13,9},{1... | collective-permute-start | bytes 3145736 | tf_op jit(solution)/shard_map/ppermute | solution.py:21
  216.4 1.9 collective-permute-start.7
  218.3 2.3 collective-permute-start.6
  220.6 34.5 %collective-permute-done.8 = bf16[2,256,1024]{2,1,0:T(8,128)(2,1)S(1)} collective-permute-done((bf16[2,256,1024]{2,1,0:T(8,128)(2,1)S(1)}, bf16[2,256,1024]{2,1,0:T(8,128)(2,1)S(1)}, u32[]{:S(2)}, u32[]{:S(2)}) %collective-permute-start.8) | collective-permute-done | bytes 1048608 | tf_op jit(solution)/shard_map/ppermute | solution.py:21
  255.2 16.5 %collective-permute-done.7 = bf16[2,256,1024]{2,1,0:T(8,128)(2,1)S(1)} collective-permute-done((bf16[2,256,1024]{2,1,0:T(8,128)(2,1)S(1)}, bf16[2,256,1024]{2,1,0:T(8,128)(2,1)S(1)}, u32[]{:S(2)}, u32[]{:S(2)}) %collective-permute-start.7) | collective-permute-done | bytes 1048608 | tf_op jit(solution)/shard_map/ppermute | solution.py:21
  271.7 30.2 %collective-permute-done.6 = bf16[2,256,1024]{2,1,0:T(8,128)(2,1)S(1)} collective-permute-done((bf16[2,256,1024]{2,1,0:T(8,128)(2,1)S(1)}, bf16[2,256,1024]{2,1,0:T(8,128)(2,1)S(1)}, u32[]{:S(2)}, u32[]{:S(2)}) %collective-permute-start.6) | collective-permute-done | bytes 1048608 | tf_op jit(solution)/shard_map/ppermute | solution.py:21
  (134 shorter events, 42.0 us)
Async XLA Ops:
  0.6 17.0 %copy-start.4 = (bf16[1,256,2048]{2,1,0:T(8,128)(2,1)S(1)}, bf16[1,256,2048]{2,1,0:T(8,128)(2,1)}, u32[]{:S(2)}) copy-start(bf16[1,256,2048]{2,1,0:T(8,128)(2,1)} %param.10) | copy-start | bytes 3145732
  0.6 17.8 %copy-start.6 = (s32[4]{0:T(128)S(1)}, s32[4]{0:T(128)}, u32[]{:S(2)}) copy-start(s32[4]{0:T(128)} %param.11) | copy-start | bytes 52
  0.7 17.9 %copy-start.5 = (bf16[1,256,2048]{2,1,0:T(8,128)(2,1)S(1)}, bf16[1,256,2048]{2,1,0:T(8,128)(2,1)}, u32[]{:S(2)}) copy-start(bf16[1,256,2048]{2,1,0:T(8,128)(2,1)} %param.7) | copy-start | bytes 3145732
  4.5 29.7 %collective-permute-start = (bf16[2,256,1024]{2,1,0:T(8,128)(2,1)}, bf16[2,256,1024]{2,1,0:T(8,128)(2,1)}, u32[]{:S(2)}, u32[]{:S(2)}) collective-permute-start(bf16[2,256,1024]{2,1,0:T(8,128)(2,1)} %constant_dynamic-update-slice_fusion.1), channel_id=1, source_target_pairs={{0,4},{1,5},{2,6},{3,7},{4,8},{5,9},{6,10},{7,11},{8,12},{9,13},{1... | collective-permute-start | bytes 3145736 | tf_op jit(solution)/shard_map/ppermute | solution.py:21
  8.6 47.7 %collective-permute-start.1 = (bf16[2,256,1024]{2,1,0:T(8,128)(2,1)}, bf16[2,256,1024]{2,1,0:T(8,128)(2,1)}, u32[]{:S(2)}, u32[]{:S(2)}) collective-permute-start(bf16[2,256,1024]{2,1,0:T(8,128)(2,1)} %constant_dynamic-update-slice_fusion.1), channel_id=1, source_target_pairs={{0,3},{1,4},{2,5},{3,6},{4,7},{5,8},{6,9},{7,10},{8,11},{9,12},{10... | collective-permute-start | bytes 3145736 | tf_op jit(solution)/shard_map/ppermute | solution.py:21
  11.9 66.9 %collective-permute-start.2 = (bf16[2,256,1024]{2,1,0:T(8,128)(2,1)}, bf16[2,256,1024]{2,1,0:T(8,128)(2,1)}, u32[]{:S(2)}, u32[]{:S(2)}) collective-permute-start(bf16[2,256,1024]{2,1,0:T(8,128)(2,1)} %constant_dynamic-update-slice_fusion.1), channel_id=1, source_target_pairs={{0,2},{1,3},{2,4},{3,5},{4,6},{5,7},{6,8},{7,9},{8,10},{9,11},{10,... | collective-permute-start | bytes 3145736 | tf_op jit(solution)/shard_map/ppermute | solution.py:21
  14.6 66.4 %collective-permute-start.3 = (bf16[2,256,1024]{2,1,0:T(8,128)(2,1)}, bf16[2,256,1024]{2,1,0:T(8,128)(2,1)}, u32[]{:S(2)}, u32[]{:S(2)}) collective-permute-start(bf16[2,256,1024]{2,1,0:T(8,128)(2,1)} %constant_dynamic-update-slice_fusion.1), channel_id=1, source_target_pairs={{0,1},{1,2},{2,3},{3,4},{4,5},{5,6},{6,7},{7,8},{8,9},{9,10},{10,1... | collective-permute-start | bytes 3145736 | tf_op jit(solution)/shard_map/ppermute | solution.py:21
  18.2 66.8 %collective-permute-start.4 = (bf16[1,256,2048]{1,2,0:T(8,128)(2,1)S(1)}, bf16[1,256,2048]{1,2,0:T(8,128)(2,1)}, u32[]{:S(2)}, u32[]{:S(2)}) collective-permute-start(bf16[1,256,2048]{1,2,0:T(8,128)(2,1)S(1)} %copy.34), channel_id=1, source_target_pairs={{0,224},{32,0},{64,32},{96,64},{128,96},{160,128},{192,160},{224,1... | collective-permute-start | bytes 3145736 | tf_op jit(solution)/shard_map/ppermute | solution.py:15
  36.6 46.7 %copy-start.2 = (bf16[1,256,1024]{2,1,0:T(8,128)(2,1)S(1)}, bf16[1,256,1024]{2,1,0:T(8,128)(2,1)}, u32[]{:S(2)}) copy-start(bf16[1,256,1024]{2,1,0:T(8,128)(2,1)} %param.8) | copy-start | bytes 1572868
  58.5 25.6 %copy-start.3 = (bf16[1,256,1024]{2,1,0:T(8,128)(2,1)S(1)}, bf16[1,256,1024]{2,1,0:T(8,128)(2,1)}, u32[]{:S(2)}) copy-start(bf16[1,256,1024]{2,1,0:T(8,128)(2,1)} %param.9) | copy-start | bytes 1572868
  99.4 1.1 copy-start
  100.9 2.1 copy-start.1
  111.8 1.1 copy-start
  113.3 2.1 copy-start.1
  124.1 1.1 copy-start
  125.7 2.1 copy-start.1
  136.5 1.1 copy-start
  138.1 2.1 copy-start.1
  148.9 1.1 copy-start
  150.4 2.1 copy-start.1
  161.3 1.1 copy-start
  162.9 2.1 copy-start.1
  173.7 1.1 copy-start
  175.2 2.1 copy-start.1
  186.0 1.1 copy-start
  187.6 2.1 copy-start.1
  191.1 110.7 %slice-start = ((s8[5242880]{0:T(1024)(128)(4,1)}), s8[4194304]{0:T(1024)(128)(4,1)S(1)}, s32[]{:S(2)}) async-start(s8[5242880]{0:T(1024)(128)(4,1)} %bitcast.105), calls=%async_computation | async-start | bytes 8388608
  191.1 110.7 %slice-start.2 = ((s8[5242880]{0:T(1024)(128)(4,1)}), s8[4194304]{0:T(1024)(128)(4,1)S(1)}, s32[]{:S(2)}) async-start(s8[5242880]{0:T(1024)(128)(4,1)} %bitcast.109), calls=%async_computation.2 | async-start | bytes 8388608
  191.1 110.7 %slice-start.1 = ((s8[5242880]{0:T(1024)(128)(4,1)}), s8[1048576]{0:T(1024)(128)(4,1)S(1)}, s32[]{:S(2)}) async-start(s8[5242880]{0:T(1024)(128)(4,1)} %bitcast.105), calls=%async_computation.1 | async-start | bytes 2097152
  191.1 110.7 %slice-start.3 = ((s8[5242880]{0:T(1024)(128)(4,1)}), s8[1048576]{0:T(1024)(128)(4,1)S(1)}, s32[]{:S(2)}) async-start(s8[5242880]{0:T(1024)(128)(4,1)} %bitcast.109), calls=%async_computation.3 | async-start | bytes 2097152
  201.7 18.9 %collective-permute-start.5 = (bf16[2,256,1024]{2,1,0:T(8,128)(2,1)S(1)}, bf16[2,256,1024]{2,1,0:T(8,128)(2,1)S(1)}, u32[]{:S(2)}, u32[]{:S(2)}) collective-permute-start(bf16[2,256,1024]{2,1,0:T(8,128)(2,1)S(1)} %get-tuple-element.208), channel_id=1, source_target_pairs={{1,0},{2,1},{3,2},{4,3},{5,4},{6,5},{7,6},{8,7},{9,8},{10,9},{11,1... | collective-permute-start | bytes 3145736 | tf_op jit(solution)/shard_map/ppermute | solution.py:21
  203.6 51.5 %collective-permute-start.8 = (bf16[2,256,1024]{2,1,0:T(8,128)(2,1)S(1)}, bf16[2,256,1024]{2,1,0:T(8,128)(2,1)S(1)}, u32[]{:S(2)}, u32[]{:S(2)}) collective-permute-start(bf16[2,256,1024]{2,1,0:T(8,128)(2,1)S(1)} %get-tuple-element.209), channel_id=1, source_target_pairs={{4,0},{5,1},{6,2},{7,3},{8,4},{9,5},{10,6},{11,7},{12,8},{13,9},{1... | collective-permute-start | bytes 3145736 | tf_op jit(solution)/shard_map/ppermute | solution.py:21
  216.4 55.3 %collective-permute-start.7 = (bf16[2,256,1024]{2,1,0:T(8,128)(2,1)S(1)}, bf16[2,256,1024]{2,1,0:T(8,128)(2,1)S(1)}, u32[]{:S(2)}, u32[]{:S(2)}) collective-permute-start(bf16[2,256,1024]{2,1,0:T(8,128)(2,1)S(1)} %get-tuple-element.210), channel_id=1, source_target_pairs={{3,0},{4,1},{5,2},{6,3},{7,4},{8,5},{9,6},{10,7},{11,8},{12,9},{13... | collective-permute-start | bytes 3145736 | tf_op jit(solution)/shard_map/ppermute | solution.py:21
  218.3 83.5 %collective-permute-start.6 = (bf16[2,256,1024]{2,1,0:T(8,128)(2,1)S(1)}, bf16[2,256,1024]{2,1,0:T(8,128)(2,1)S(1)}, u32[]{:S(2)}, u32[]{:S(2)}) collective-permute-start(bf16[2,256,1024]{2,1,0:T(8,128)(2,1)S(1)} %get-tuple-element.211), channel_id=1, source_target_pairs={{2,0},{3,1},{4,2},{5,3},{6,4},{7,5},{8,6},{9,7},{10,8},{11,9},{12,... | collective-permute-start | bytes 3145736 | tf_op jit(solution)/shard_map/ppermute | solution.py:21
where the time goes:
time: 305 us; the launch traced here: 304 us
  waiting for transfers between devices  135 us (44%)
  local copies, waits for them, and re-layouts  75 us (25%)
  matrix products  39.3 us (13%)
  starting transfers between devices  32.2 us (11%)
  other arithmetic  20.8 us (7%)
    ppermute x8, waiting for transfers between devices, shifted(): lax.ppermute(value, axis, [(source, source + steps) for source in range(i...  135 us
    ppermute x8, starting transfers between devices, shifted(): lax.ppermute(value, axis, [(source, source + steps) for source in range(i...  32 us
    slice x8, local copies, waits for them, and re-layouts, per_group(): window_pair[1]  24.9 us
    unnamed x26, local copies, waits for them, and re-layouts  13.8 us
    dot_general x8, matrix products, group_pass(): jnp.einsum('jrk,rjd->kd', weight_half, grad_head, preferred_element_type=...  11.4 us
    dot_general x8, matrix products, group_pass(): jnp.einsum('jrk,rjd->kd', score_grad, query_head, preferred_element_type=...  11.1 us
    another operation x3, other arithmetic  8.87 us
    and x8, other arithmetic, window_mask(): same_doc & (spacing >= 0) & (spacing < WINDOW) & (key_pos[None, :] >= 0)  8.76 us
  transfers between devices with their start and end apart: 9, of which 6 were waited for; matrix products, arithmetic and copies ran while one was open for 4% of the time, Pallas kernels for 0%

commit v1 on v0

--- a/solution.py
+++ b/solution.py
@@ -83,9 +83,11 @@
     first_pos = rank_here * count_rows
     arriving = passed_along(finished_grad, "section", -1)[0]
     own_pair = jnp.stack([keys_here, values_here])
-    pieces = [shifted(own_pair, "ctx", distance) for distance in range(reach_blocks, 0, -1)] + [
-        own_pair
-    ]
+    pieces = [own_pair]
+    relayed = own_pair
+    for _ in range(reach_blocks):
+        relayed = shifted(relayed, "ctx", 1)
+        pieces.insert(0, relayed)
     window_pair = jnp.concatenate(pieces, axis=1)
     span = window_pair.shape[1]
     query_pos = first_pos + jnp.arange(count_rows, dtype=jnp.int32)
@@ -122,11 +124,12 @@
     )
     own_start = reach_blocks * count_rows
     grad_pair = jnp.stack([grad_keys, grad_values])
-    key_total = grad_pair[:, own_start:]
-    for distance in range(1, reach_blocks + 1):
-        lower = (reach_blocks - distance) * count_rows
-        sent_terms = grad_pair[:, lower : lower + count_rows].astype(jnp.bfloat16)
-        key_total = key_total + shifted(sent_terms, "ctx", -distance).astype(jnp.float32)
+    partial = grad_pair[:, :count_rows].astype(jnp.bfloat16)
+    for block in range(1, reach_blocks):
+        term = grad_pair[:, block * count_rows : (block + 1) * count_rows]
+        arrived = shifted(partial, "ctx", -1).astype(jnp.float32)
+        partial = (arrived + term.astype(jnp.bfloat16).astype(jnp.float32)).astype(jnp.bfloat16)
+    key_total = grad_pair[:, own_start:] + shifted(partial, "ctx", -1).astype(jnp.float32)
     return (
         grad_query[None],
         key_total[0].astype(jnp.bfloat16)[None],

time: 305 us -> 283 us (0.928)
  the two profiles are of different devices: /device:TPU:120 before, /device:TPU:25 now
where the time goes in v1:
time: 283 us; the launch traced here: 282 us
  waiting for transfers between devices  110 us (39%)
  local copies, waits for them, and re-layouts  69.1 us (24%)
  matrix products  39.4 us (14%)
  starting transfers between devices  36.2 us (13%)
  other arithmetic  26.5 us (9%)
    ppermute x8, waiting for transfers between devices, shifted(): lax.ppermute(value, axis, [(source, source + steps) for source in range(i...  104 us
    ppermute x8, starting transfers between devices, shifted(): lax.ppermute(value, axis, [(source, source + steps) for source in range(i...  30.6 us
    slice x8, local copies, waits for them, and re-layouts, per_group(): window_pair[1]  24.9 us
    dot_general x8, matrix products, group_pass(): jnp.einsum('jrk,rjd->kd', weight_half, grad_head, preferred_element_type=...  11.3 us
    unnamed x29, local copies, waits for them, and re-layouts  11.2 us
    dot_general x8, matrix products, group_pass(): jnp.einsum('jrk,rjd->kd', score_grad, query_head, preferred_element_type=...  11.1 us
    and x8, other arithmetic, window_mask(): same_doc & (spacing >= 0) & (spacing < WINDOW) & (key_pos[None, :] >= 0)  8.76 us
    while x32, local copies, waits for them, and re-layouts  8.48 us
  transfers between devices with their start and end apart: 9, of which 9 were waited for; matrix products, arithmetic and copies ran while one was open for 4% of the time, Pallas kernels for 0%

profile of v1, /device:TPU:25, one launch (start us, length us, event | category | flops | bytes accessed | tf_op | source)
XLA Modules:
  0.0 282.3 jit_solution(18294278342920480126)
XLA Ops:
  0.7 1.4 pad_maximum_fusion.1
  2.1 3.3 %collective-permute-start = (bf16[2,256,1024]{2,1,0:T(8,128)(2,1)S(1)}, bf16[2,256,1024]{2,1,0:T(8,128)(2,1)S(1)}, u32[]{:S(2)}, u32[]{:S(2)}) collective-permute-start(bf16[2,256,1024]{2,1,0:T(8,128)(2,1)S(1)} %pad_maximum_fusion.1), channel_id=1, source_target_pairs={{0,1},{1,2},{2,3},{3,4},{4,5},{5,6},{6,7},{7,8},{8,9},{9,10},{10,1... | collective-permute-start | bytes 3145736 | tf_op jit(solution)/shard_map/ppermute | solution.py:21
  5.5 11.7 %collective-permute-done = bf16[2,256,1024]{2,1,0:T(8,128)(2,1)S(1)} collective-permute-done((bf16[2,256,1024]{2,1,0:T(8,128)(2,1)S(1)}, bf16[2,256,1024]{2,1,0:T(8,128)(2,1)S(1)}, u32[]{:S(2)}, u32[]{:S(2)}) %collective-permute-start) | collective-permute-done | bytes 1048608 | tf_op jit(solution)/shard_map/ppermute | solution.py:21
  17.2 6.5 %collective-permute-start.1 = (bf16[2,256,1024]{2,1,0:T(8,128)(2,1)S(1)}, bf16[2,256,1024]{2,1,0:T(8,128)(2,1)S(1)}, u32[]{:S(2)}, u32[]{:S(2)}) collective-permute-start(bf16[2,256,1024]{2,1,0:T(8,128)(2,1)S(1)} %collective-permute-done), channel_id=1, source_target_pairs={{0,1},{1,2},{2,3},{3,4},{4,5},{5,6},{6,7},{7,8},{8,9},{9,10},{10,1... | collective-permute-start | bytes 3145736 | tf_op jit(solution)/shard_map/ppermute | solution.py:21
  23.7 11.7 %collective-permute-done.1 = bf16[2,256,1024]{2,1,0:T(8,128)(2,1)S(1)} collective-permute-done((bf16[2,256,1024]{2,1,0:T(8,128)(2,1)S(1)}, bf16[2,256,1024]{2,1,0:T(8,128)(2,1)S(1)}, u32[]{:S(2)}, u32[]{:S(2)}) %collective-permute-start.1) | collective-permute-done | bytes 1048608 | tf_op jit(solution)/shard_map/ppermute | solution.py:21
  36.4 6.5 %collective-permute-start.2 = (bf16[2,256,1024]{2,1,0:T(8,128)(2,1)S(1)}, bf16[2,256,1024]{2,1,0:T(8,128)(2,1)}, u32[]{:S(2)}, u32[]{:S(2)}) collective-permute-start(bf16[2,256,1024]{2,1,0:T(8,128)(2,1)S(1)} %collective-permute-done.1), channel_id=1, source_target_pairs={{0,1},{1,2},{2,3},{3,4},{4,5},{5,6},{6,7},{7,8},{8,9},{9,10},{10,1... | collective-permute-start | bytes 3145736 | tf_op jit(solution)/shard_map/ppermute | solution.py:21
  42.9 11.7 %collective-permute-done.2 = bf16[2,256,1024]{2,1,0:T(8,128)(2,1)} collective-permute-done((bf16[2,256,1024]{2,1,0:T(8,128)(2,1)S(1)}, bf16[2,256,1024]{2,1,0:T(8,128)(2,1)}, u32[]{:S(2)}, u32[]{:S(2)}) %collective-permute-start.2) | collective-permute-done | bytes 1048608 | tf_op jit(solution)/shard_map/ppermute | solution.py:21
  54.6 6.6 %collective-permute-start.3 = (bf16[2,256,1024]{2,1,0:T(8,128)(2,1)}, bf16[2,256,1024]{2,1,0:T(8,128)(2,1)}, u32[]{:S(2)}, u32[]{:S(2)}) collective-permute-start(bf16[2,256,1024]{2,1,0:T(8,128)(2,1)} %collective-permute-done.2), channel_id=1, source_target_pairs={{0,1},{1,2},{2,3},{3,4},{4,5},{5,6},{6,7},{7,8},{8,9},{9,10},{10,1... | collective-permute-start | bytes 3145736 | tf_op jit(solution)/shard_map/ppermute | solution.py:21
  61.2 1.3 copy.34
  62.5 5.6 %collective-permute-start.4 = (bf16[1,256,2048]{1,2,0:T(8,128)(2,1)}, bf16[1,256,2048]{1,2,0:T(8,128)(2,1)}, u32[]{:S(2)}, u32[]{:S(2)}) collective-permute-start(bf16[1,256,2048]{1,2,0:T(8,128)(2,1)} %copy.34), channel_id=1, source_target_pairs={{0,224},{32,0},{64,32},{96,64},{128,96},{160,128},{192,160},{224,1... | collective-permute-start | bytes 3145736 | tf_op jit(solution)/shard_map/ppermute | solution.py:15
  68.3 1.3 copy.33
  69.8 3.4 %collective-permute-done.3 = bf16[2,256,1024]{2,1,0:T(8,128)(2,1)} collective-permute-done((bf16[2,256,1024]{2,1,0:T(8,128)(2,1)}, bf16[2,256,1024]{2,1,0:T(8,128)(2,1)}, u32[]{:S(2)}, u32[]{:S(2)}) %collective-permute-start.3) | collective-permute-done | bytes 1048608 | tf_op jit(solution)/shard_map/ppermute | solution.py:21
  73.2 2.3 constant_dynamic-update-slice_fusion.6
  75.5 2.3 constant_dynamic-update-slice_fusion.5
  81.7 6.0 %collective-permute-done.4 = bf16[1,256,2048]{1,2,0:T(8,128)(2,1)} collective-permute-done((bf16[1,256,2048]{1,2,0:T(8,128)(2,1)}, bf16[1,256,2048]{1,2,0:T(8,128)(2,1)}, u32[]{:S(2)}, u32[]{:S(2)}) %collective-permute-start.4) | collective-permute-done | bytes 1048608 | tf_op jit(solution)/shard_map/ppermute | solution.py:15
  87.7 1.1 broadcast_in_dim.53.clone
  88.7 3.0 %broadcast.53.clone = f32[1280,1024]{1,0:T(8,128)} broadcast(f32[]{:T(128)} %constant.84.clone.1), dimensions={} | broadcast | bytes 5242884 | tf_op jit(solution)/shard_map/broadcast.7
  91.7 3.0 %broadcast.53 = f32[1280,1024]{1,0:T(8,128)} broadcast(f32[]{:T(128)} %constant.84.clone.1), dimensions={} | broadcast | bytes 5242884 | tf_op jit(solution)/shard_map/broadcast.7
  94.7 99.1 %while.18 = (s32[]{:T(128)}, bf16[256,2048]{1,0:T(8,128)(2,1)}, f32[1280,1024]{1,0:T(8,128)}, f32[1280,1024]{1,0:T(8,128)}, bf16[2,1280,1024]{2,1,0:T(8,128)(2,1...) while((s32[]{:T(128)}, bf16[256,2048]{1,0:T(8,128)(2,1)}, ...), condition=%wide.region_7.8_spmd.clone, body=%wide.region_3.7_spmd.clone.sunk | while | flops 1018067968 | bytes 43159136 | solution.py:122
  95.7 1.1 fusion.77
  96.8 3.1 %fusion.76 = (bf16[1,1280,1024]{2,1,0:T(8,128)(2,1)S(1)}, bf16[1,1280,1024]{2,1,0:T(8,128)(2,1)S(1)}) fusion(bf16[2,1280,1024]{2,1,0:T(8,128)(2,1)} %get-tuple-element.335), kind=kLoop, calls=%fused_computation.66.clone.1 | loop fusion | bytes 10485760 | tf_op jit(solution)/shard_map/while/body/eval_jaxpr/slice | solution.py:102
  104.3 1.4 fusion.83
  105.7 1.4 fusion.82
  108.1 1.1 fusion.77
  109.2 3.1 %fusion.76 = (bf16[1,1280,1024]{2,1,0:T(8,128)(2,1)S(1)}, bf16[1,1280,1024]{2,1,0:T(8,128)(2,1)S(1)}) fusion(bf16[2,1280,1024]{2,1,0:T(8,128)(2,1)} %get-tuple-element.335), kind=kLoop, calls=%fused_computation.66.clone.1 | loop fusion | bytes 10485760 | tf_op jit(solution)/shard_map/while/body/eval_jaxpr/slice | solution.py:102
  116.7 1.4 fusion.83
  118.2 1.4 fusion.82
  120.5 1.1 fusion.77
  121.6 3.1 %fusion.76 = (bf16[1,1280,1024]{2,1,0:T(8,128)(2,1)S(1)}, bf16[1,1280,1024]{2,1,0:T(8,128)(2,1)S(1)}) fusion(bf16[2,1280,1024]{2,1,0:T(8,128)(2,1)} %get-tuple-element.335), kind=kLoop, calls=%fused_computation.66.clone.1 | loop fusion | bytes 10485760 | tf_op jit(solution)/shard_map/while/body/eval_jaxpr/slice | solution.py:102
  129.1 1.4 fusion.83
  130.5 1.4 fusion.82
  132.9 1.1 fusion.77
  134.0 3.1 %fusion.76 = (bf16[1,1280,1024]{2,1,0:T(8,128)(2,1)S(1)}, bf16[1,1280,1024]{2,1,0:T(8,128)(2,1)S(1)}) fusion(bf16[2,1280,1024]{2,1,0:T(8,128)(2,1)} %get-tuple-element.335), kind=kLoop, calls=%fused_computation.66.clone.1 | loop fusion | bytes 10485760 | tf_op jit(solution)/shard_map/while/body/eval_jaxpr/slice | solution.py:102
  141.5 1.4 fusion.83
  142.9 1.4 fusion.82
  145.3 1.1 fusion.77
  146.4 3.1 %fusion.76 = (bf16[1,1280,1024]{2,1,0:T(8,128)(2,1)S(1)}, bf16[1,1280,1024]{2,1,0:T(8,128)(2,1)S(1)}) fusion(bf16[2,1280,1024]{2,1,0:T(8,128)(2,1)} %get-tuple-element.335), kind=kLoop, calls=%fused_computation.66.clone.1 | loop fusion | bytes 10485760 | tf_op jit(solution)/shard_map/while/body/eval_jaxpr/slice | solution.py:102
  153.9 1.4 fusion.83
  155.3 1.4 fusion.82
  157.7 1.1 fusion.77
  158.8 3.1 %fusion.76 = (bf16[1,1280,1024]{2,1,0:T(8,128)(2,1)S(1)}, bf16[1,1280,1024]{2,1,0:T(8,128)(2,1)S(1)}) fusion(bf16[2,1280,1024]{2,1,0:T(8,128)(2,1)} %get-tuple-element.335), kind=kLoop, calls=%fused_computation.66.clone.1 | loop fusion | bytes 10485760 | tf_op jit(solution)/shard_map/while/body/eval_jaxpr/slice | solution.py:102
  166.3 1.4 fusion.83
  167.7 1.4 fusion.82
  170.1 1.1 fusion.77
  171.2 3.1 %fusion.76 = (bf16[1,1280,1024]{2,1,0:T(8,128)(2,1)S(1)}, bf16[1,1280,1024]{2,1,0:T(8,128)(2,1)S(1)}) fusion(bf16[2,1280,1024]{2,1,0:T(8,128)(2,1)} %get-tuple-element.335), kind=kLoop, calls=%fused_computation.66.clone.1 | loop fusion | bytes 10485760 | tf_op jit(solution)/shard_map/while/body/eval_jaxpr/slice | solution.py:102
  178.6 1.4 fusion.83
  180.1 1.4 fusion.82
  182.5 1.1 fusion.77
  183.6 3.1 %fusion.76 = (bf16[1,1280,1024]{2,1,0:T(8,128)(2,1)S(1)}, bf16[1,1280,1024]{2,1,0:T(8,128)(2,1)S(1)}) fusion(bf16[2,1280,1024]{2,1,0:T(8,128)(2,1)} %get-tuple-element.335), kind=kLoop, calls=%fused_computation.66.clone.1 | loop fusion | bytes 10485760 | tf_op jit(solution)/shard_map/while/body/eval_jaxpr/slice | solution.py:102
  191.0 1.4 fusion.83
  192.4 1.4 fusion.82
  193.8 7.7 %fusion.33 = bf16[2,1280,1024]{2,1,0:T(8,128)(2,1)} fusion(f32[1,1280,1024]{2,1,0:T(8,128)} %bitcast.104, f32[1,1280,1024]{2,1,0:T(8,128)} %bitcast.108), kind=kLoop, calls=%fused_computation.47 | loop fusion | flops 2621440 | bytes 15728640 | tf_op jit(solution)/shard_map/convert.6
  201.5 1.6 slice.52
  203.1 1.9 collective-permute-start.5
  205.0 16.3 %collective-permute-done.5 = bf16[2,256,1024]{2,1,0:T(8,128)(2,1)S(1)} collective-permute-done((bf16[2,256,1024]{2,1,0:T(8,128)(2,1)S(1)}, bf16[2,256,1024]{2,1,0:T(8,128)(2,1)S(1)}, u32[]{:S(2)}, u32[]{:S(2)}) %collective-permute-start.5) | collective-permute-done | bytes 1048608 | tf_op jit(solution)/shard_map/ppermute | solution.py:21
  221.3 1.6 add_convert_fusion.2
  222.9 1.9 collective-permute-start.6
  224.8 16.3 %collective-permute-done.6 = bf16[2,256,1024]{2,1,0:T(8,128)(2,1)S(1)} collective-permute-done((bf16[2,256,1024]{2,1,0:T(8,128)(2,1)S(1)}, bf16[2,256,1024]{2,1,0:T(8,128)(2,1)S(1)}, u32[]{:S(2)}, u32[]{:S(2)}) %collective-permute-start.6) | collective-permute-done | bytes 1048608 | tf_op jit(solution)/shard_map/ppermute | solution.py:21
  241.1 1.6 add_convert_fusion.1
  242.8 1.9 collective-permute-start.7
  244.7 16.3 %collective-permute-done.7 = bf16[2,256,1024]{2,1,0:T(8,128)(2,1)S(1)} collective-permute-done((bf16[2,256,1024]{2,1,0:T(8,128)(2,1)S(1)}, bf16[2,256,1024]{2,1,0:T(8,128)(2,1)S(1)}, u32[]{:S(2)}, u32[]{:S(2)}) %collective-permute-start.7) | collective-permute-done | bytes 1048608 | tf_op jit(solution)/shard_map/ppermute | solution.py:21
  261.0 1.6 add_convert_fusion
  262.6 1.9 collective-permute-start.8
  264.6 16.3 %collective-permute-done.8 = bf16[2,256,1024]{2,1,0:T(8,128)(2,1)S(1)} collective-permute-done((bf16[2,256,1024]{2,1,0:T(8,128)(2,1)S(1)}, bf16[2,256,1024]{2,1,0:T(8,128)(2,1)S(1)}, u32[]{:S(2)}, u32[]{:S(2)}) %collective-permute-start.8) | collective-permute-done | bytes 1048608 | tf_op jit(solution)/shard_map/ppermute | solution.py:21
  (140 shorter events, 49.0 us)
Async XLA Ops:
  0.6 60.6 %copy-start.4 = (bf16[1,256,2048]{2,1,0:T(8,128)(2,1)S(1)}, bf16[1,256,2048]{2,1,0:T(8,128)(2,1)}, u32[]{:S(2)}) copy-start(bf16[1,256,2048]{2,1,0:T(8,128)(2,1)} %param.10) | copy-start | bytes 3145732
  0.6 67.5 %copy-start.8 = (s32[4]{0:T(128)S(1)}, s32[4]{0:T(128)}, u32[]{:S(2)}) copy-start(s32[4]{0:T(128)} %param.11) | copy-start | bytes 52
  0.7 67.7 %copy-start.5 = (bf16[1,256,2048]{2,1,0:T(8,128)(2,1)S(1)}, bf16[1,256,2048]{2,1,0:T(8,128)(2,1)}, u32[]{:S(2)}) copy-start(bf16[1,256,2048]{2,1,0:T(8,128)(2,1)} %param.7) | copy-start | bytes 3145732
  2.1 15.1 %collective-permute-start = (bf16[2,256,1024]{2,1,0:T(8,128)(2,1)S(1)}, bf16[2,256,1024]{2,1,0:T(8,128)(2,1)S(1)}, u32[]{:S(2)}, u32[]{:S(2)}) collective-permute-start(bf16[2,256,1024]{2,1,0:T(8,128)(2,1)S(1)} %pad_maximum_fusion.1), channel_id=1, source_target_pairs={{0,1},{1,2},{2,3},{3,4},{4,5},{5,6},{6,7},{7,8},{8,9},{9,10},{10,1... | collective-permute-start | bytes 3145736 | tf_op jit(solution)/shard_map/ppermute | solution.py:21
  17.2 18.2 %collective-permute-start.1 = (bf16[2,256,1024]{2,1,0:T(8,128)(2,1)S(1)}, bf16[2,256,1024]{2,1,0:T(8,128)(2,1)S(1)}, u32[]{:S(2)}, u32[]{:S(2)}) collective-permute-start(bf16[2,256,1024]{2,1,0:T(8,128)(2,1)S(1)} %collective-permute-done), channel_id=1, source_target_pairs={{0,1},{1,2},{2,3},{3,4},{4,5},{5,6},{6,7},{7,8},{8,9},{9,10},{10,1... | collective-permute-start | bytes 3145736 | tf_op jit(solution)/shard_map/ppermute | solution.py:21
  35.4 1.0 copy-start.6
  36.4 18.2 %collective-permute-start.2 = (bf16[2,256,1024]{2,1,0:T(8,128)(2,1)S(1)}, bf16[2,256,1024]{2,1,0:T(8,128)(2,1)}, u32[]{:S(2)}, u32[]{:S(2)}) collective-permute-start(bf16[2,256,1024]{2,1,0:T(8,128)(2,1)S(1)} %collective-permute-done.1), channel_id=1, source_target_pairs={{0,1},{1,2},{2,3},{3,4},{4,5},{5,6},{6,7},{7,8},{8,9},{9,10},{10,1... | collective-permute-start | bytes 3145736 | tf_op jit(solution)/shard_map/ppermute | solution.py:21
  54.6 18.6 %collective-permute-start.3 = (bf16[2,256,1024]{2,1,0:T(8,128)(2,1)}, bf16[2,256,1024]{2,1,0:T(8,128)(2,1)}, u32[]{:S(2)}, u32[]{:S(2)}) collective-permute-start(bf16[2,256,1024]{2,1,0:T(8,128)(2,1)} %collective-permute-done.2), channel_id=1, source_target_pairs={{0,1},{1,2},{2,3},{3,4},{4,5},{5,6},{6,7},{7,8},{8,9},{9,10},{10,1... | collective-permute-start | bytes 3145736 | tf_op jit(solution)/shard_map/ppermute | solution.py:21
  62.5 25.1 %collective-permute-start.4 = (bf16[1,256,2048]{1,2,0:T(8,128)(2,1)}, bf16[1,256,2048]{1,2,0:T(8,128)(2,1)}, u32[]{:S(2)}, u32[]{:S(2)}) collective-permute-start(bf16[1,256,2048]{1,2,0:T(8,128)(2,1)} %copy.34), channel_id=1, source_target_pairs={{0,224},{32,0},{64,32},{96,64},{128,96},{160,128},{192,160},{224,1... | collective-permute-start | bytes 3145736 | tf_op jit(solution)/shard_map/ppermute | solution.py:15
  69.6 8.2 %copy-start.7 = (bf16[2,256,1024]{2,1,0:T(8,128)(2,1)S(1)}, bf16[2,256,1024]{2,1,0:T(8,128)(2,1)}, u32[]{:S(2)}) copy-start(bf16[2,256,1024]{2,1,0:T(8,128)(2,1)} %copy-done.6) | copy-start | bytes 3145732
  75.5 4.4 %copy-start.2 = (bf16[1,256,1024]{2,1,0:T(8,128)(2,1)S(1)}, bf16[1,256,1024]{2,1,0:T(8,128)(2,1)}, u32[]{:S(2)}) copy-start(bf16[1,256,1024]{2,1,0:T(8,128)(2,1)} %param.8) | copy-start | bytes 1572868
  77.9 3.0 %copy-start.3 = (bf16[1,256,1024]{2,1,0:T(8,128)(2,1)S(1)}, bf16[1,256,1024]{2,1,0:T(8,128)(2,1)}, u32[]{:S(2)}) copy-start(bf16[1,256,1024]{2,1,0:T(8,128)(2,1)} %param.9) | copy-start | bytes 1572868
  102.0 1.1 copy-start
  103.6 2.1 copy-start.1
  114.5 1.1 copy-start
  116.0 2.1 copy-start.1
  126.9 1.1 copy-start
  128.4 2.1 copy-start.1
  139.2 1.1 copy-start
  140.8 2.1 copy-start.1
  151.7 1.1 copy-start
  153.2 2.1 copy-start.1
  164.0 1.1 copy-start
  165.6 2.1 copy-start.1
  176.4 1.1 copy-start
  177.9 2.1 copy-start.1
  188.8 1.1 copy-start
  190.3 2.1 copy-start.1
  193.8 87.1 %slice-start = ((s8[5242880]{0:T(1024)(128)(4,1)}), s8[4194304]{0:T(1024)(128)(4,1)S(1)}, s32[]{:S(2)}) async-start(s8[5242880]{0:T(1024)(128)(4,1)} %bitcast.105), calls=%async_computation | async-start | bytes 8388608
  193.8 87.1 %slice-start.2 = ((s8[5242880]{0:T(1024)(128)(4,1)}), s8[4194304]{0:T(1024)(128)(4,1)S(1)}, s32[]{:S(2)}) async-start(s8[5242880]{0:T(1024)(128)(4,1)} %bitcast.109), calls=%async_computation.2 | async-start | bytes 8388608
  193.8 87.1 %slice-start.1 = ((s8[5242880]{0:T(1024)(128)(4,1)}), s8[1048576]{0:T(1024)(128)(4,1)S(1)}, s32[]{:S(2)}) async-start(s8[5242880]{0:T(1024)(128)(4,1)} %bitcast.105), calls=%async_computation.1 | async-start | bytes 2097152
  193.8 87.1 %slice-start.3 = ((s8[5242880]{0:T(1024)(128)(4,1)}), s8[1048576]{0:T(1024)(128)(4,1)S(1)}, s32[]{:S(2)}) async-start(s8[5242880]{0:T(1024)(128)(4,1)} %bitcast.109), calls=%async_computation.3 | async-start | bytes 2097152
  203.1 18.2 %collective-permute-start.5 = (bf16[2,256,1024]{2,1,0:T(8,128)(2,1)S(1)}, bf16[2,256,1024]{2,1,0:T(8,128)(2,1)S(1)}, u32[]{:S(2)}, u32[]{:S(2)}) collective-permute-start(bf16[2,256,1024]{2,1,0:T(8,128)(2,1)S(1)} %slice.52), channel_id=1, source_target_pairs={{1,0},{2,1},{3,2},{4,3},{5,4},{6,5},{7,6},{8,7},{9,8},{10,9},{11,1... | collective-permute-start | bytes 3145736 | tf_op jit(solution)/shard_map/ppermute | solution.py:21
  222.9 18.2 %collective-permute-start.6 = (bf16[2,256,1024]{2,1,0:T(8,128)(2,1)S(1)}, bf16[2,256,1024]{2,1,0:T(8,128)(2,1)S(1)}, u32[]{:S(2)}, u32[]{:S(2)}) collective-permute-start(bf16[2,256,1024]{2,1,0:T(8,128)(2,1)S(1)} %add_convert_fusion.2), channel_id=1, source_target_pairs={{1,0},{2,1},{3,2},{4,3},{5,4},{6,5},{7,6},{8,7},{9,8},{10,9},{11,1... | collective-permute-start | bytes 3145736 | tf_op jit(solution)/shard_map/ppermute | solution.py:21
  242.8 18.2 %collective-permute-start.7 = (bf16[2,256,1024]{2,1,0:T(8,128)(2,1)S(1)}, bf16[2,256,1024]{2,1,0:T(8,128)(2,1)S(1)}, u32[]{:S(2)}, u32[]{:S(2)}) collective-permute-start(bf16[2,256,1024]{2,1,0:T(8,128)(2,1)S(1)} %add_convert_fusion.1), channel_id=1, source_target_pairs={{1,0},{2,1},{3,2},{4,3},{5,4},{6,5},{7,6},{8,7},{9,8},{10,9},{11,1... | collective-permute-start | bytes 3145736 | tf_op jit(solution)/shard_map/ppermute | solution.py:21
  262.6 18.2 %collective-permute-start.8 = (bf16[2,256,1024]{2,1,0:T(8,128)(2,1)S(1)}, bf16[2,256,1024]{2,1,0:T(8,128)(2,1)S(1)}, u32[]{:S(2)}, u32[]{:S(2)}) collective-permute-start(bf16[2,256,1024]{2,1,0:T(8,128)(2,1)S(1)} %add_convert_fusion), channel_id=1, source_target_pairs={{1,0},{2,1},{3,2},{4,3},{5,4},{6,5},{7,6},{8,7},{9,8},{10,9},{11,1... | collective-permute-start | bytes 3145736 | tf_op jit(solution)/shard_map/ppermute | solution.py:21

commit v2 on v1

--- a/solution.py
+++ b/solution.py
@@ -1,6 +1,8 @@
 import jax
 import jax.numpy as jnp
 from jax import lax
+from jax.experimental import pallas as pl
+from jax.experimental.pallas import tpu as pltpu
 from jax.sharding import PartitionSpec as P
 
 WINDOW = 1024
@@ -8,6 +10,62 @@
 
 
 SCORE_SCALE = 168.0 ** (-0.5)
+
+
+def product(a, b, dims):
+    return lax.dot_general(a, b, dims, preferred_element_type=jnp.float32)
+
+
+def attention_back_kernel(q_ref, do_ref, k_ref, v_ref, mask_ref, dq_ref, dk_ref, dv_ref):
+    head_size = k_ref.shape[1]
+    heads = q_ref.shape[1] // head_size
+    allowed = mask_ref[...] > 0
+    keys = k_ref[...]
+    values = v_ref[...]
+    queries = jnp.concatenate([q_ref[:, h * head_size:(h + 1) * head_size] for h in range(heads)], axis=0)
+    grads = jnp.concatenate([do_ref[:, h * head_size:(h + 1) * head_size] for h in range(heads)], axis=0)
+    allowed = jnp.concatenate([allowed] * heads, axis=0)
+    nt = (((1,), (1,)), ((), ()))
+    tn = (((0,), (0,)), ((), ()))
+    nn = (((1,), (0,)), ((), ()))
+    scores = SCORE_SCALE * product(queries, keys, nt)
+    scores = jnp.where(allowed, scores, -jnp.inf)
+    highest = jnp.max(scores, axis=-1, keepdims=True)
+    log_total = highest + jnp.log(jnp.sum(jnp.exp(scores - highest), axis=-1, keepdims=True))
+    weights = jnp.exp(scores - log_total)
+    weight_half = weights.astype(jnp.bfloat16)
+    attended = product(weight_half, values, nn).astype(jnp.bfloat16)
+    row_dot = jnp.sum(attended.astype(jnp.float32) * grads.astype(jnp.float32), axis=-1, keepdims=True)
+    weight_grad = product(grads, values, nt)
+    score_grad = (weights * (weight_grad - row_dot)).astype(jnp.bfloat16)
+    query_back = SCORE_SCALE * product(score_grad, keys, nn)
+    rows = q_ref.shape[0]
+    for h in range(heads):
+        dq_ref[:, h * head_size:(h + 1) * head_size] = query_back[h * rows:(h + 1) * rows].astype(dq_ref.dtype)
+    dk_ref[...] = SCORE_SCALE * product(score_grad, queries, tn)
+    dv_ref[...] = product(weight_half, grads, tn)
+
+
+def attention_back(queries, grads, window_keys, window_values, allowed, groups):
+    rows, width = queries.shape
+    span, pair_width = window_keys.shape
+    head_size = pair_width // groups
+    group_width = width // groups
+    q_spec = pl.BlockSpec((rows, group_width), lambda g: (0, g))
+    kv_spec = pl.BlockSpec((span, head_size), lambda g: (0, g))
+    mask_spec = pl.BlockSpec((rows, span), lambda g: (0, 0))
+    return pl.pallas_call(
+        attention_back_kernel,
+        grid=(groups,),
+        in_specs=[q_spec, q_spec, kv_spec, kv_spec, mask_spec],
+        out_specs=[q_spec, kv_spec, kv_spec],
+        out_shape=[
+            jax.ShapeDtypeStruct((rows, width), jnp.bfloat16),
+            jax.ShapeDtypeStruct((span, pair_width), jnp.float32),
+            jax.ShapeDtypeStruct((span, pair_width), jnp.float32),
+        ],
+        compiler_params=pltpu.CompilerParams(vmem_limit_bytes=60 * 1024 * 1024),
+    )(queries, grads, window_keys, window_values, allowed)
 
 
 def passed_along(shard, axis, by):
@@ -94,33 +152,8 @@
     key_pos = first_pos - WINDOW + jnp.arange(span, dtype=jnp.int32)
     allowed = window_mask(query_pos, key_pos, doc_lengths)
 
-    def per_group(group, carry):
-        query_acc, keys_acc, values_acc, log_totals, row_dots = carry
-        query_part = lax.dynamic_slice_in_dim(queries, group * group_width, group_width, 1)
-        grad_part = lax.dynamic_slice_in_dim(arriving, group * group_width, group_width, 1)
-        key_part = lax.dynamic_slice_in_dim(window_pair[0], group * head_size, head_size, 1)
-        value_part = lax.dynamic_slice_in_dim(window_pair[1], group * head_size, head_size, 1)
-        query_back, key_back, value_back, log_total, row_dot = group_pass(
-            query_part, key_part, value_part, grad_part, allowed
-        )
-        query_acc = lax.dynamic_update_slice_in_dim(
-            query_acc, query_back.astype(jnp.bfloat16), group * group_width, 1
-        )
-        keys_acc = lax.dynamic_update_slice_in_dim(keys_acc, key_back, group * head_size, 1)
-        values_acc = lax.dynamic_update_slice_in_dim(values_acc, value_back, group * head_size, 1)
-        log_totals = lax.dynamic_update_slice_in_dim(log_totals, log_total, group * heads_group, 0)
-        row_dots = lax.dynamic_update_slice_in_dim(row_dots, row_dot, group * heads_group, 0)
-        return (query_acc, keys_acc, values_acc, log_totals, row_dots)
-
-    start_carry = (
-        jnp.zeros(queries.shape, jnp.bfloat16),
-        jnp.zeros((span, pair_width), jnp.float32),
-        jnp.zeros((span, pair_width), jnp.float32),
-        jnp.zeros((KV_HEADS * heads_group, count_rows), jnp.float32),
-        jnp.zeros((KV_HEADS * heads_group, count_rows), jnp.float32),
-    )
-    grad_query, grad_keys, grad_values, log_totals, row_dots = lax.fori_loop(
-        0, KV_HEADS, per_group, start_carry
+    grad_query, grad_keys, grad_values = attention_back(
+        queries, arriving, window_pair[0], window_pair[1], allowed.astype(jnp.float32), KV_HEADS
     )
     own_start = reach_blocks * count_rows
     grad_pair = jnp.stack([grad_keys, grad_values])

time: 283 us -> 197 us (0.70)
  local copies, waits for them, and re-layouts: 69.1 us -> 9.36 us
  matrix products: 39.4 us -> 0 us
  Pallas kernels: 0 us -> 27.9 us
  other arithmetic: 26.5 us -> 16.9 us
  waiting for transfers between devices: 110 us -> 105 us
    dot_general x48 -> x0, matrix products: 39.4 us -> none  [the longest x8 11.3 us: group_pass(): jnp.einsum('jrk,rjd->kd', weight_half, grad_head, preferred_element_type=...]
    pallas_call x0 -> x1, Pallas kernels: none -> 27.9 us  [attention_back(): pl.pallas_call(attention_back_kernel, grid=(groups,), in_specs=[q_spec, q...]
    slice x8 -> x0, local copies, waits for them, and re-layouts: 24.9 us -> none  [per_group(): window_pair[1]]
    and x8 -> x0, other arithmetic: 8.76 us -> none  [window_mask(): same_doc & (spacing >= 0) & (spacing < WINDOW) & (key_pos[None, :] >= 0)]
    while x32 -> x0, local copies, waits for them, and re-layouts: 8.48 us -> none
    dynamic_slice x8 -> x0, local copies, waits for them, and re-layouts: 7.88 us -> none  [per_group(): lax.dynamic_slice_in_dim(arriving, group * group_width, group_width, 1)]
    unnamed x29 -> x19, local copies, waits for them, and re-layouts: 11.2 us -> 3.79 us
    dynamic_update_slice x16 -> x0, local copies, waits for them, and re-layouts: 6.16 us -> none  [per_group(): lax.dynamic_update_slice_in_dim(query_acc, query_back.astype(jnp.bfloat16...]
  transfers between devices with their start and end apart: 9 -> 9, of which waited for: 9 -> 8; matrix products, arithmetic and copies ran while one was open for 4% -> 4% of each run, Pallas kernels for 0% -> 0%
where the time goes in v2:
time: 197 us; the launch traced here: 196 us
  waiting for transfers between devices  105 us (53%)
  starting transfers between devices  36.4 us (18%)
  Pallas kernels  27.9 us (14%)
  other arithmetic  16.9 us (9%)
  local copies, waits for them, and re-layouts  9.36 us (5%)
    ppermute x8, waiting for transfers between devices, shifted(): lax.ppermute(value, axis, [(source, source + steps) for source in range(i...  105 us
    ppermute x8, starting transfers between devices, shifted(): lax.ppermute(value, axis, [(source, source + steps) for source in range(i...  30.7 us
    pallas_call x1, Pallas kernels, attention_back(): pl.pallas_call(attention_back_kernel, grid=(groups,), in_specs=[q_spec, q...  27.9 us
    another operation x3, other arithmetic  8.91 us
    ppermute x1, starting transfers between devices, passed_along(): lax.ppermute(shard, axis, [(i, (i + by) % count) for i in range(count)])  5.65 us
    convert_element_type x3, other arithmetic, local(): (arrived + term.astype(jnp.bfloat16).astype(jnp.float32)).astype(jnp.bflo...  4.87 us
  transfers between devices with their start and end apart: 9, of which 8 were waited for; matrix products, arithmetic and copies ran while one was open for 4% of the time, Pallas kernels for 0%

profile of v2, /device:TPU:25, one launch (start us, length us, event | category | flops | bytes accessed | tf_op | source)
XLA Modules:
  0.0 196.5 jit_solution(15448041685536775007)
XLA Ops:
  0.6 1.3 pad_maximum_fusion.1
  1.9 0.0 copy-start
  1.9 3.5 %collective-permute-start.1 = (bf16[2,256,1024]{2,1,0:T(8,128)(2,1)S(1)}, bf16[2,256,1024]{2,1,0:T(8,128)(2,1)S(1)}, u32[]{:S(2)}, u32[]{:S(2)}) collective-permute-start(bf16[2,256,1024]{2,1,0:T(8,128)(2,1)S(1)} %pad_maximum_fusion.1), channel_id=1, source_target_pairs={{0,1},{1,2},{2,3},{3,4},{4,5},{5,6},{6,7},{7,8},{8,9},{9,10},{10,1... | collective-permute-start | bytes 3145736 | tf_op jit(solution)/shard_map/ppermute | solution.py:79
  5.4 11.7 %collective-permute-done.1 = bf16[2,256,1024]{2,1,0:T(8,128)(2,1)S(1)} collective-permute-done((bf16[2,256,1024]{2,1,0:T(8,128)(2,1)S(1)}, bf16[2,256,1024]{2,1,0:T(8,128)(2,1)S(1)}, u32[]{:S(2)}, u32[]{:S(2)}) %collective-permute-start.1) | collective-permute-done | bytes 1048608 | tf_op jit(solution)/shard_map/ppermute | solution.py:79
  17.1 6.5 %collective-permute-start.2 = (bf16[2,256,1024]{2,1,0:T(8,128)(2,1)S(1)}, bf16[2,256,1024]{2,1,0:T(8,128)(2,1)}, u32[]{:S(2)}, u32[]{:S(2)}) collective-permute-start(bf16[2,256,1024]{2,1,0:T(8,128)(2,1)S(1)} %collective-permute-done.1), channel_id=1, source_target_pairs={{0,1},{1,2},{2,3},{3,4},{4,5},{5,6},{6,7},{7,8},{8,9},{9,10},{10,1... | collective-permute-start | bytes 3145736 | tf_op jit(solution)/shard_map/ppermute | solution.py:79
  23.6 11.7 %collective-permute-done.2 = bf16[2,256,1024]{2,1,0:T(8,128)(2,1)} collective-permute-done((bf16[2,256,1024]{2,1,0:T(8,128)(2,1)S(1)}, bf16[2,256,1024]{2,1,0:T(8,128)(2,1)}, u32[]{:S(2)}, u32[]{:S(2)}) %collective-permute-start.2) | collective-permute-done | bytes 1048608 | tf_op jit(solution)/shard_map/ppermute | solution.py:79
  35.4 6.6 %collective-permute-start.3 = (bf16[2,256,1024]{2,1,0:T(8,128)(2,1)}, bf16[2,256,1024]{2,1,0:T(8,128)(2,1)}, u32[]{:S(2)}, u32[]{:S(2)}) collective-permute-start(bf16[2,256,1024]{2,1,0:T(8,128)(2,1)} %collective-permute-done.2), channel_id=1, source_target_pairs={{0,1},{1,2},{2,3},{3,4},{4,5},{5,6},{6,7},{7,8},{8,9},{9,10},{10,1... | collective-permute-start | bytes 3145736 | tf_op jit(solution)/shard_map/ppermute | solution.py:79
  42.0 5.7 %collective-permute-start = (bf16[1,256,2048]{2,1,0:T(8,128)(2,1)}, bf16[1,256,2048]{2,1,0:T(8,128)(2,1)S(1)}, u32[]{:S(2)}, u32[]{:S(2)}) collective-permute-start(bf16[1,256,2048]{2,1,0:T(8,128)(2,1)} %param.8), channel_id=1, source_target_pairs={{0,224},{32,0},{64,32},{96,64},{128,96},{160,128},{192,160},{224,1... | collective-permute-start | bytes 3145736 | tf_op jit(solution)/shard_map/ppermute | solution.py:73
  47.6 0.8 reduce-window.8
  48.4 5.6 %collective-permute-done.3 = bf16[2,256,1024]{2,1,0:T(8,128)(2,1)} collective-permute-done((bf16[2,256,1024]{2,1,0:T(8,128)(2,1)}, bf16[2,256,1024]{2,1,0:T(8,128)(2,1)}, u32[]{:S(2)}, u32[]{:S(2)}) %collective-permute-start.3) | collective-permute-done | bytes 1048608 | tf_op jit(solution)/shard_map/ppermute | solution.py:79
  54.0 6.5 %collective-permute-start.4 = (bf16[2,256,1024]{2,1,0:T(8,128)(2,1)}, bf16[2,256,1024]{2,1,0:T(8,128)(2,1)S(1)}, u32[]{:S(2)}, u32[]{:S(2)}) collective-permute-start(bf16[2,256,1024]{2,1,0:T(8,128)(2,1)} %collective-permute-done.3), channel_id=1, source_target_pairs={{0,1},{1,2},{2,3},{3,4},{4,5},{5,6},{6,7},{7,8},{8,9},{9,10},{10,1... | collective-permute-start | bytes 3145736 | tf_op jit(solution)/shard_map/ppermute | solution.py:79
  60.5 0.1 convert_reduce_fusion.1
  60.6 0.1 convert_reduce_fusion
  60.7 0.0 copy-start.1
  60.7 1.6 fusion.7.mask_ref
  62.3 10.2 %collective-permute-done.4 = bf16[2,256,1024]{2,1,0:T(8,128)(2,1)S(1)} collective-permute-done((bf16[2,256,1024]{2,1,0:T(8,128)(2,1)}, bf16[2,256,1024]{2,1,0:T(8,128)(2,1)S(1)}, u32[]{:S(2)}, u32[]{:S(2)}) %collective-permute-start.4) | collective-permute-done | bytes 1048608 | tf_op jit(solution)/shard_map/ppermute | solution.py:79
  72.5 0.1 constant_dynamic-update-slice_fusion.5
  72.6 1.3 constant_dynamic-update-slice_fusion.4
  73.9 1.3 constant_dynamic-update-slice_fusion.3
  75.2 0.1 constant_dynamic-update-slice_fusion.2
  75.3 0.0 copy-done
  75.3 0.0 copy-done.1
  75.4 2.9 %slice_bitcast_fusion = (bf16[1280,1024]{1,0:T(8,128)(2,1)}, bf16[1280,1024]{1,0:T(8,128)(2,1)}) fusion(bf16[2,1280,1024]{2,1,0:T(8,128)(2,1)S(1)} %constant_dynamic-update-slice_fusion), kind=kLoop, calls=%fused_computation.4 | loop fusion | bytes 10485760 | tf_op jit(solution)/shard_map/squeeze | solution.py:156
  78.3 0.0 collective-permute-done
  78.3 0.0 copy-start.2
  78.3 1.0 copy-done.2
  79.3 27.9 %shard_map.76 = (bf16[256,2048]{1,0:T(8,128)(2,1)}, f32[1280,1024]{1,0:T(8,128)}, f32[1280,1024]{1,0:T(8,128)}) custom-call(bf16[256,2048]{1,0:T(8,128)(2,1)} %bitcast.19, bf16[256,2048]{1,0:T(8,128)(2,1)} %bitcast.20, bf16[1280,1024]{1,0:T(8,128)(2,1)} %get-tuple-element.10.k_ref, bf16[1280,1024]{1,0:T(8,128)(2,1)} %get-tuple-element.9.v_ref, ...), custom_call_target="tpu_custom_call" | custom-call | tf_op jit(solution)/shard_map/pallas_call | solution.py:57
  107.3 0.0 slice-start
  107.3 0.0 slice-start.2
  107.3 0.0 slice-start.1
  107.3 0.0 slice-start.3
  107.3 7.7 %fusion = bf16[2,1280,1024]{2,1,0:T(8,128)(2,1)} fusion(f32[1,1280,1024]{2,1,0:T(8,128)} %bitcast.15, f32[1,1280,1024]{2,1,0:T(8,128)} %bitcast.11), kind=kLoop, calls=%fused_computation.3 | loop fusion | flops 2621440 | bytes 15728640 | tf_op jit(solution)/shard_map/convert.5
  115.0 1.6 slice.46
  116.5 1.9 collective-permute-start.5
  118.5 16.9 %collective-permute-done.5 = bf16[2,256,1024]{2,1,0:T(8,128)(2,1)S(1)} collective-permute-done((bf16[2,256,1024]{2,1,0:T(8,128)(2,1)S(1)}, bf16[2,256,1024]{2,1,0:T(8,128)(2,1)S(1)}, u32[]{:S(2)}, u32[]{:S(2)}) %collective-permute-start.5) | collective-permute-done | bytes 1048608 | tf_op jit(solution)/shard_map/ppermute | solution.py:79
  135.4 1.6 add_convert_fusion.2
  137.0 1.9 collective-permute-start.6
  139.0 16.3 %collective-permute-done.6 = bf16[2,256,1024]{2,1,0:T(8,128)(2,1)S(1)} collective-permute-done((bf16[2,256,1024]{2,1,0:T(8,128)(2,1)S(1)}, bf16[2,256,1024]{2,1,0:T(8,128)(2,1)S(1)}, u32[]{:S(2)}, u32[]{:S(2)}) %collective-permute-start.6) | collective-permute-done | bytes 1048608 | tf_op jit(solution)/shard_map/ppermute | solution.py:79
  155.3 1.6 add_convert_fusion.1
  156.9 1.9 collective-permute-start.7
  158.8 16.3 %collective-permute-done.7 = bf16[2,256,1024]{2,1,0:T(8,128)(2,1)S(1)} collective-permute-done((bf16[2,256,1024]{2,1,0:T(8,128)(2,1)S(1)}, bf16[2,256,1024]{2,1,0:T(8,128)(2,1)S(1)}, u32[]{:S(2)}, u32[]{:S(2)}) %collective-permute-start.7) | collective-permute-done | bytes 1048608 | tf_op jit(solution)/shard_map/ppermute | solution.py:79
  175.1 1.6 add_convert_fusion
  176.8 1.9 collective-permute-start.8
  178.7 16.3 %collective-permute-done.8 = bf16[2,256,1024]{2,1,0:T(8,128)(2,1)S(1)} collective-permute-done((bf16[2,256,1024]{2,1,0:T(8,128)(2,1)S(1)}, bf16[2,256,1024]{2,1,0:T(8,128)(2,1)S(1)}, u32[]{:S(2)}, u32[]{:S(2)}) %collective-permute-start.8) | collective-permute-done | bytes 1048608 | tf_op jit(solution)/shard_map/ppermute | solution.py:79
  195.0 0.0 slice-done
  195.0 0.0 slice-done.2
  195.0 0.0 slice-done.1
  195.0 0.0 slice-done.3
  195.0 0.4 fusion.3
  195.4 1.0 fusion.8
  (7 shorter events, 0.1 us)
Async XLA Ops:
  1.9 73.3 %copy-start = (bf16[1,256,1024]{2,1,0:T(8,128)(2,1)S(1)}, bf16[1,256,1024]{2,1,0:T(8,128)(2,1)}, u32[]{:S(2)}) copy-start(bf16[1,256,1024]{2,1,0:T(8,128)(2,1)} %param.6) | copy-start | bytes 1572868
  1.9 15.2 %collective-permute-start.1 = (bf16[2,256,1024]{2,1,0:T(8,128)(2,1)S(1)}, bf16[2,256,1024]{2,1,0:T(8,128)(2,1)S(1)}, u32[]{:S(2)}, u32[]{:S(2)}) collective-permute-start(bf16[2,256,1024]{2,1,0:T(8,128)(2,1)S(1)} %pad_maximum_fusion.1), channel_id=1, source_target_pairs={{0,1},{1,2},{2,3},{3,4},{4,5},{5,6},{6,7},{7,8},{8,9},{9,10},{10,1... | collective-permute-start | bytes 3145736 | tf_op jit(solution)/shard_map/ppermute | solution.py:79
  17.1 18.2 %collective-permute-start.2 = (bf16[2,256,1024]{2,1,0:T(8,128)(2,1)S(1)}, bf16[2,256,1024]{2,1,0:T(8,128)(2,1)}, u32[]{:S(2)}, u32[]{:S(2)}) collective-permute-start(bf16[2,256,1024]{2,1,0:T(8,128)(2,1)S(1)} %collective-permute-done.1), channel_id=1, source_target_pairs={{0,1},{1,2},{2,3},{3,4},{4,5},{5,6},{6,7},{7,8},{8,9},{9,10},{10,1... | collective-permute-start | bytes 3145736 | tf_op jit(solution)/shard_map/ppermute | solution.py:79
  35.4 18.6 %collective-permute-start.3 = (bf16[2,256,1024]{2,1,0:T(8,128)(2,1)}, bf16[2,256,1024]{2,1,0:T(8,128)(2,1)}, u32[]{:S(2)}, u32[]{:S(2)}) collective-permute-start(bf16[2,256,1024]{2,1,0:T(8,128)(2,1)} %collective-permute-done.2), channel_id=1, source_target_pairs={{0,1},{1,2},{2,3},{3,4},{4,5},{5,6},{6,7},{7,8},{8,9},{9,10},{10,1... | collective-permute-start | bytes 3145736 | tf_op jit(solution)/shard_map/ppermute | solution.py:79
  42.0 36.4 %collective-permute-start = (bf16[1,256,2048]{2,1,0:T(8,128)(2,1)}, bf16[1,256,2048]{2,1,0:T(8,128)(2,1)S(1)}, u32[]{:S(2)}, u32[]{:S(2)}) collective-permute-start(bf16[1,256,2048]{2,1,0:T(8,128)(2,1)} %param.8), channel_id=1, source_target_pairs={{0,224},{32,0},{64,32},{96,64},{128,96},{160,128},{192,160},{224,1... | collective-permute-start | bytes 3145736 | tf_op jit(solution)/shard_map/ppermute | solution.py:73
  54.0 18.5 %collective-permute-start.4 = (bf16[2,256,1024]{2,1,0:T(8,128)(2,1)}, bf16[2,256,1024]{2,1,0:T(8,128)(2,1)S(1)}, u32[]{:S(2)}, u32[]{:S(2)}) collective-permute-start(bf16[2,256,1024]{2,1,0:T(8,128)(2,1)} %collective-permute-done.3), channel_id=1, source_target_pairs={{0,1},{1,2},{2,3},{3,4},{4,5},{5,6},{6,7},{7,8},{8,9},{9,10},{10,1... | collective-permute-start | bytes 3145736 | tf_op jit(solution)/shard_map/ppermute | solution.py:79
  60.7 14.6 %copy-start.1 = (bf16[1,256,1024]{2,1,0:T(8,128)(2,1)S(1)}, bf16[1,256,1024]{2,1,0:T(8,128)(2,1)}, u32[]{:S(2)}) copy-start(bf16[1,256,1024]{2,1,0:T(8,128)(2,1)} %param.7) | copy-start | bytes 1572868
  78.3 1.0 copy-start.2
  107.3 87.7 %slice-start = ((s8[5242880]{0:T(1024)(128)(4,1)}), s8[4194304]{0:T(1024)(128)(4,1)S(1)}, s32[]{:S(2)}) async-start(s8[5242880]{0:T(1024)(128)(4,1)} %bitcast.12), calls=%async_computation | async-start | bytes 8388608
  107.3 87.7 %slice-start.2 = ((s8[5242880]{0:T(1024)(128)(4,1)}), s8[4194304]{0:T(1024)(128)(4,1)S(1)}, s32[]{:S(2)}) async-start(s8[5242880]{0:T(1024)(128)(4,1)} %bitcast.16), calls=%async_computation.2 | async-start | bytes 8388608
  107.3 87.7 %slice-start.1 = ((s8[5242880]{0:T(1024)(128)(4,1)}), s8[1048576]{0:T(1024)(128)(4,1)S(1)}, s32[]{:S(2)}) async-start(s8[5242880]{0:T(1024)(128)(4,1)} %bitcast.12), calls=%async_computation.1 | async-start | bytes 2097152
  107.3 87.7 %slice-start.3 = ((s8[5242880]{0:T(1024)(128)(4,1)}), s8[1048576]{0:T(1024)(128)(4,1)S(1)}, s32[]{:S(2)}) async-start(s8[5242880]{0:T(1024)(128)(4,1)} %bitcast.16), calls=%async_computation.3 | async-start | bytes 2097152
  116.5 18.9 %collective-permute-start.5 = (bf16[2,256,1024]{2,1,0:T(8,128)(2,1)S(1)}, bf16[2,256,1024]{2,1,0:T(8,128)(2,1)S(1)}, u32[]{:S(2)}, u32[]{:S(2)}) collective-permute-start(bf16[2,256,1024]{2,1,0:T(8,128)(2,1)S(1)} %slice.46), channel_id=1, source_target_pairs={{1,0},{2,1},{3,2},{4,3},{5,4},{6,5},{7,6},{8,7},{9,8},{10,9},{11,1... | collective-permute-start | bytes 3145736 | tf_op jit(solution)/shard_map/ppermute | solution.py:79
  137.0 18.2 %collective-permute-start.6 = (bf16[2,256,1024]{2,1,0:T(8,128)(2,1)S(1)}, bf16[2,256,1024]{2,1,0:T(8,128)(2,1)S(1)}, u32[]{:S(2)}, u32[]{:S(2)}) collective-permute-start(bf16[2,256,1024]{2,1,0:T(8,128)(2,1)S(1)} %add_convert_fusion.2), channel_id=1, source_target_pairs={{1,0},{2,1},{3,2},{4,3},{5,4},{6,5},{7,6},{8,7},{9,8},{10,9},{11,1... | collective-permute-start | bytes 3145736 | tf_op jit(solution)/shard_map/ppermute | solution.py:79
  156.9 18.2 %collective-permute-start.7 = (bf16[2,256,1024]{2,1,0:T(8,128)(2,1)S(1)}, bf16[2,256,1024]{2,1,0:T(8,128)(2,1)S(1)}, u32[]{:S(2)}, u32[]{:S(2)}) collective-permute-start(bf16[2,256,1024]{2,1,0:T(8,128)(2,1)S(1)} %add_convert_fusion.1), channel_id=1, source_target_pairs={{1,0},{2,1},{3,2},{4,3},{5,4},{6,5},{7,6},{8,7},{9,8},{10,9},{11,1... | collective-permute-start | bytes 3145736 | tf_op jit(solution)/shard_map/ppermute | solution.py:79
  176.8 18.2 %collective-permute-start.8 = (bf16[2,256,1024]{2,1,0:T(8,128)(2,1)S(1)}, bf16[2,256,1024]{2,1,0:T(8,128)(2,1)S(1)}, u32[]{:S(2)}, u32[]{:S(2)}) collective-permute-start(bf16[2,256,1024]{2,1,0:T(8,128)(2,1)S(1)} %add_convert_fusion), channel_id=1, source_target_pairs={{1,0},{2,1},{3,2},{4,3},{5,4},{6,5},{7,6},{8,7},{9,8},{10,9},{11,1... | collective-permute-start | bytes 3145736 | tf_op jit(solution)/shard_map/ppermute | solution.py:79

commit v3 on v2

--- a/solution.py
+++ b/solution.py
@@ -7,6 +7,7 @@
 
 WINDOW = 1024
 KV_HEADS = 8
+CHUNKS = 2
 
 
 SCORE_SCALE = 168.0 ** (-0.5)
@@ -16,9 +17,13 @@
     return lax.dot_general(a, b, dims, preferred_element_type=jnp.float32)
 
 
-def attention_back_kernel(q_ref, do_ref, k_ref, v_ref, mask_ref, dq_ref, dk_ref, dv_ref):
+def attention_back_kernel(
+    q_ref, do_ref, k_ref, v_ref, mask_ref, dq_ref, dk_far_ref, dv_far_ref, dk_own_ref, dv_own_ref
+):
     head_size = k_ref.shape[1]
     heads = q_ref.shape[1] // head_size
+    rows = q_ref.shape[0]
+    far = dk_far_ref.shape[0]
     allowed = mask_ref[...] > 0
     keys = k_ref[...]
     values = v_ref[...]
@@ -39,30 +44,39 @@
     weight_grad = product(grads, values, nt)
     score_grad = (weights * (weight_grad - row_dot)).astype(jnp.bfloat16)
     query_back = SCORE_SCALE * product(score_grad, keys, nn)
-    rows = q_ref.shape[0]
     for h in range(heads):
         dq_ref[:, h * head_size:(h + 1) * head_size] = query_back[h * rows:(h + 1) * rows].astype(dq_ref.dtype)
-    dk_ref[...] = SCORE_SCALE * product(score_grad, queries, tn)
-    dv_ref[...] = product(weight_half, grads, tn)
-
-
-def attention_back(queries, grads, window_keys, window_values, allowed, groups):
+    key_back = SCORE_SCALE * product(score_grad, queries, tn)
+    value_back = product(weight_half, grads, tn)
+    dk_far_ref[...] = key_back[:far].astype(dk_far_ref.dtype)
+    dv_far_ref[...] = value_back[:far].astype(dv_far_ref.dtype)
+    dk_own_ref[...] = key_back[far:]
+    dv_own_ref[...] = value_back[far:]
+
+
+def attention_back(queries, grads, window_keys, window_values, allowed, first_group, groups):
     rows, width = queries.shape
     span, pair_width = window_keys.shape
     head_size = pair_width // groups
-    group_width = width // groups
-    q_spec = pl.BlockSpec((rows, group_width), lambda g: (0, g))
+    group_width = 2 * head_size
+    far = span - rows
+    q_spec = pl.BlockSpec((rows, group_width), lambda g: (0, g + first_group))
+    dq_spec = pl.BlockSpec((rows, group_width), lambda g: (0, g))
     kv_spec = pl.BlockSpec((span, head_size), lambda g: (0, g))
+    far_spec = pl.BlockSpec((far, head_size), lambda g: (0, g))
+    own_spec = pl.BlockSpec((rows, head_size), lambda g: (0, g))
     mask_spec = pl.BlockSpec((rows, span), lambda g: (0, 0))
     return pl.pallas_call(
         attention_back_kernel,
         grid=(groups,),
         in_specs=[q_spec, q_spec, kv_spec, kv_spec, mask_spec],
-        out_specs=[q_spec, kv_spec, kv_spec],
+        out_specs=[dq_spec, far_spec, far_spec, own_spec, own_spec],
         out_shape=[
-            jax.ShapeDtypeStruct((rows, width), jnp.bfloat16),
-            jax.ShapeDtypeStruct((span, pair_width), jnp.float32),
-            jax.ShapeDtypeStruct((span, pair_width), jnp.float32),
+            jax.ShapeDtypeStruct((rows, groups * group_width), jnp.bfloat16),
+            jax.ShapeDtypeStruct((far, pair_width), jnp.bfloat16),
+            jax.ShapeDtypeStruct((far, pair_width), jnp.bfloat16),
+            jax.ShapeDtypeStruct((rows, pair_width), jnp.float32),
+            jax.ShapeDtypeStruct((rows, pair_width), jnp.float32),
         ],
         compiler_params=pltpu.CompilerParams(vmem_limit_bytes=60 * 1024 * 1024),
     )(queries, grads, window_keys, window_values, allowed)
@@ -140,33 +154,38 @@
     rank_here = lax.axis_index("ctx")
     first_pos = rank_here * count_rows
     arriving = passed_along(finished_grad, "section", -1)[0]
-    own_pair = jnp.stack([keys_here, values_here])
-    pieces = [own_pair]
-    relayed = own_pair
-    for _ in range(reach_blocks):
-        relayed = shifted(relayed, "ctx", 1)
-        pieces.insert(0, relayed)
-    window_pair = jnp.concatenate(pieces, axis=1)
-    span = window_pair.shape[1]
     query_pos = first_pos + jnp.arange(count_rows, dtype=jnp.int32)
-    key_pos = first_pos - WINDOW + jnp.arange(span, dtype=jnp.int32)
-    allowed = window_mask(query_pos, key_pos, doc_lengths)
-
-    grad_query, grad_keys, grad_values = attention_back(
-        queries, arriving, window_pair[0], window_pair[1], allowed.astype(jnp.float32), KV_HEADS
-    )
-    own_start = reach_blocks * count_rows
-    grad_pair = jnp.stack([grad_keys, grad_values])
-    partial = grad_pair[:, :count_rows].astype(jnp.bfloat16)
-    for block in range(1, reach_blocks):
-        term = grad_pair[:, block * count_rows : (block + 1) * count_rows]
+    key_pos = first_pos - WINDOW + jnp.arange(WINDOW + count_rows, dtype=jnp.int32)
+    allowed = window_mask(query_pos, key_pos, doc_lengths).astype(jnp.float32)
+    chunk_groups = KV_HEADS // CHUNKS
+    chunk_width = chunk_groups * head_size
+    query_grads, key_grads, value_grads = [], [], []
+    for chunk in range(CHUNKS):
+        cols = slice(chunk * chunk_width, (chunk + 1) * chunk_width)
+        own_pair = jnp.stack([keys_here[:, cols], values_here[:, cols]])
+        pieces = [own_pair]
+        relayed = own_pair
+        for _ in range(reach_blocks):
+            relayed = shifted(relayed, "ctx", 1)
+            pieces.insert(0, relayed)
+        window_pair = jnp.concatenate(pieces, axis=1)
+        grad_query, keys_far, values_far, keys_own, values_own = attention_back(
+            queries, arriving, window_pair[0], window_pair[1], allowed, chunk * chunk_groups, chunk_groups
+        )
+        far_pair = jnp.stack([keys_far, values_far])
+        partial = far_pair[:, :count_rows]
+        for block in range(1, reach_blocks):
+            term = far_pair[:, block * count_rows : (block + 1) * count_rows].astype(jnp.float32)
+            arrived = shifted(partial, "ctx", -1).astype(jnp.float32)
+            partial = (arrived + term).astype(jnp.bfloat16)
         arrived = shifted(partial, "ctx", -1).astype(jnp.float32)
-        partial = (arrived + term.astype(jnp.bfloat16).astype(jnp.float32)).astype(jnp.bfloat16)
-    key_total = grad_pair[:, own_start:] + shifted(partial, "ctx", -1).astype(jnp.float32)
+        query_grads.append(grad_query)
+        key_grads.append((keys_own + arrived[0]).astype(jnp.bfloat16))
+        value_grads.append((values_own + arrived[1]).astype(jnp.bfloat16))
     return (
-        grad_query[None],
-        key_total[0].astype(jnp.bfloat16)[None],
-        key_total[1].astype(jnp.bfloat16)[None],
+        jnp.concatenate(query_grads, axis=1)[None],
+        jnp.concatenate(key_grads, axis=1)[None],
+        jnp.concatenate(value_grads, axis=1)[None],
     )
 
 

time: 197 us -> 150 us (0.76)
  waiting for transfers between devices: 105 us -> 39.1 us
  starting transfers between devices: 36.4 us -> 59.4 us
  other arithmetic: 16.9 us -> 8.8 us
  Pallas kernels: 27.9 us -> 30.3 us
    ppermute x8 -> x16, waiting for transfers between devices: 105 us -> 38.8 us  [shifted(): lax.ppermute(value, axis, [(source, source + steps) for source in range(i...]
    ppermute x8 -> x16, starting transfers between devices: 30.7 us -> 53.8 us  [shifted(): lax.ppermute(value, axis, [(source, source + steps) for source in range(i...]
    another operation x4 -> x5, other arithmetic: 10.2 us -> 2.59 us  [the longest x2 2.31 us: local(): far_pair = jnp.stack([keys_far, values_far])]
    convert_element_type x4 -> x11, other arithmetic: 6.47 us -> 3.17 us  [the longest x1 1.6 us: local(): allowed = window_mask(query_pos, key_pos, doc_lengths).astype(jnp.float32)]
    broadcast_in_dim x0 -> x3, other arithmetic: none -> 2.78 us  [the longest x1 1.06 us: local(): jnp.concatenate(query_grads, axis=1)[None]]
    slice x2 -> x0, local copies, waits for them, and re-layouts: 2.59 us -> none  [the longest x1 1.56 us: local(): partial = grad_pair[:, :count_rows].astype(jnp.bfloat16)]
    pallas_call x1 -> x2, Pallas kernels: 27.9 us -> 30.3 us  [attention_back(): pl.pallas_call(attention_back_kernel, grid=(groups,), in_specs=[q_spec, q...]
    unnamed x19 -> x36, local copies, waits for them, and re-layouts: 3.79 us -> 5.48 us
  transfers between devices with their start and end apart: 9 -> 17, of which waited for: 8 -> 10; matrix products, arithmetic and copies ran while one was open for 4% -> 10% of each run, Pallas kernels for 0% -> 20%
where the time goes in v3:
time: 150 us; the launch traced here: 149 us
  starting transfers between devices  59.4 us (40%)
  waiting for transfers between devices  39.1 us (26%)
  Pallas kernels  30.3 us (20%)
  local copies, waits for them, and re-layouts  10 us (7%)
  other arithmetic  8.8 us (6%)
    ppermute x16, starting transfers between devices, shifted(): lax.ppermute(value, axis, [(source, source + steps) for source in range(i...  53.8 us
    ppermute x16, waiting for transfers between devices, shifted(): lax.ppermute(value, axis, [(source, source + steps) for source in range(i...  38.8 us
    pallas_call x2, Pallas kernels, attention_back(): pl.pallas_call(attention_back_kernel, grid=(groups,), in_specs=[q_spec, q...  30.3 us
    ppermute x1, starting transfers between devices, passed_along(): lax.ppermute(shard, axis, [(i, (i + by) % count) for i in range(count)])  5.65 us
    unnamed x36, local copies, waits for them, and re-layouts  5.48 us
    squeeze x2, local copies, waits for them, and re-layouts, local(): window_pair[1]  3.29 us
  transfers between devices with their start and end apart: 17, of which 10 were waited for; matrix products, arithmetic and copies ran while one was open for 10% of the time, Pallas kernels for 20%

profile of v3, /device:TPU:25, one launch (start us, length us, event | category | flops | bytes accessed | tf_op | source)
XLA Modules:
  0.0 148.8 jit_solution(7756388093451626930)
XLA Ops:
  0.6 1.3 slice_bitcast_fusion.10
  1.9 0.1 pad_maximum_fusion.2
  2.0 3.3 %collective-permute-start.1 = (bf16[2,256,512]{2,1,0:T(8,128)(2,1)S(1)}, bf16[2,256,512]{2,1,0:T(8,128)(2,1)S(1)}, u32[]{:S(2)}, u32[]{:S(2)}) collective-permute-start(bf16[2,256,512]{2,1,0:T(8,128)(2,1)S(1)} %pad_maximum_fusion.2), channel_id=1, source_target_pairs={{0,1},{1,2},{2,3},{3,4},{4,5},{5,6},{6,7},{7,8},{8,9},{9,10},{10,1... | collective-permute-start | bytes 1572872 | tf_op jit(solution)/shard_map/ppermute | solution.py:93
  5.3 0.1 pad_maximum_fusion.3
  5.4 1.9 %collective-permute-start.5 = (bf16[2,256,512]{2,1,0:T(8,128)(2,1)S(1)}, bf16[2,256,512]{2,1,0:T(8,128)(2,1)S(1)}, u32[]{:S(2)}, u32[]{:S(2)}) collective-permute-start(bf16[2,256,512]{2,1,0:T(8,128)(2,1)S(1)} %pad_maximum_fusion.3), channel_id=1, source_target_pairs={{0,1},{1,2},{2,3},{3,4},{4,5},{5,6},{6,7},{7,8},{8,9},{9,10},{10,1... | collective-permute-start | bytes 1572872 | tf_op jit(solution)/shard_map/ppermute | solution.py:93
  7.3 4.1 %collective-permute-done.1 = bf16[2,256,512]{2,1,0:T(8,128)(2,1)S(1)} collective-permute-done((bf16[2,256,512]{2,1,0:T(8,128)(2,1)S(1)}, bf16[2,256,512]{2,1,0:T(8,128)(2,1)S(1)}, u32[]{:S(2)}, u32[]{:S(2)}) %collective-permute-start.1) | collective-permute-done | bytes 524320 | tf_op jit(solution)/shard_map/ppermute | solution.py:93
  11.4 6.5 %collective-permute-start.2 = (bf16[2,256,512]{2,1,0:T(8,128)(2,1)S(1)}, bf16[2,256,512]{2,1,0:T(8,128)(2,1)}, u32[]{:S(2)}, u32[]{:S(2)}) collective-permute-start(bf16[2,256,512]{2,1,0:T(8,128)(2,1)S(1)} %collective-permute-done.1), channel_id=1, source_target_pairs={{0,1},{1,2},{2,3},{3,4},{4,5},{5,6},{6,7},{7,8},{8,9},{9,10},{10,1... | collective-permute-start | bytes 1572872 | tf_op jit(solution)/shard_map/ppermute | solution.py:93
  17.9 0.0 collective-permute-done.5
  17.9 5.6 %collective-permute-start.6 = (bf16[2,256,512]{2,1,0:T(8,128)(2,1)S(1)}, bf16[2,256,512]{2,1,0:T(8,128)(2,1)S(1)}, u32[]{:S(2)}, u32[]{:S(2)}) collective-permute-start(bf16[2,256,512]{2,1,0:T(8,128)(2,1)S(1)} %collective-permute-done.5), channel_id=1, source_target_pairs={{0,1},{1,2},{2,3},{3,4},{4,5},{5,6},{6,7},{7,8},{8,9},{9,10},{10,1... | collective-permute-start | bytes 1572872 | tf_op jit(solution)/shard_map/ppermute | solution.py:93
  23.5 0.5 collective-permute-done.2
  24.0 6.6 %collective-permute-start.3 = (bf16[2,256,512]{2,1,0:T(8,128)(2,1)}, bf16[2,256,512]{2,1,0:T(8,128)(2,1)}, u32[]{:S(2)}, u32[]{:S(2)}) collective-permute-start(bf16[2,256,512]{2,1,0:T(8,128)(2,1)} %collective-permute-done.2), channel_id=1, source_target_pairs={{0,1},{1,2},{2,3},{3,4},{4,5},{5,6},{6,7},{7,8},{8,9},{9,10},{10,1... | collective-permute-start | bytes 1572872 | tf_op jit(solution)/shard_map/ppermute | solution.py:93
  30.6 5.7 %collective-permute-start = (bf16[1,256,2048]{2,1,0:T(8,128)(2,1)}, bf16[1,256,2048]{2,1,0:T(8,128)(2,1)S(1)}, u32[]{:S(2)}, u32[]{:S(2)}) collective-permute-start(bf16[1,256,2048]{2,1,0:T(8,128)(2,1)} %param.8), channel_id=1, source_target_pairs={{0,224},{32,0},{64,32},{96,64},{128,96},{160,128},{192,160},{224,1... | collective-permute-start | bytes 3145736 | tf_op jit(solution)/shard_map/ppermute | solution.py:87
  36.3 0.2 reduce-window.8
  36.5 0.1 convert_reduce_fusion.1
  36.5 0.1 convert_reduce_fusion
  36.6 0.0 collective-permute-done.6
  36.6 2.2 %collective-permute-start.7 = (bf16[2,256,512]{2,1,0:T(8,128)(2,1)S(1)}, bf16[2,256,512]{2,1,0:T(8,128)(2,1)}, u32[]{:S(2)}, u32[]{:S(2)}) collective-permute-start(bf16[2,256,512]{2,1,0:T(8,128)(2,1)S(1)} %collective-permute-done.6), channel_id=1, source_target_pairs={{0,1},{1,2},{2,3},{3,4},{4,5},{5,6},{6,7},{7,8},{8,9},{9,10},{10,1... | collective-permute-start | bytes 1572872 | tf_op jit(solution)/shard_map/ppermute | solution.py:93
  38.9 0.0 collective-permute-done.3
  38.9 4.7 %collective-permute-start.4 = (bf16[2,256,512]{2,1,0:T(8,128)(2,1)}, bf16[2,256,512]{2,1,0:T(8,128)(2,1)S(1)}, u32[]{:S(2)}, u32[]{:S(2)}) collective-permute-start(bf16[2,256,512]{2,1,0:T(8,128)(2,1)} %collective-permute-done.3), channel_id=1, source_target_pairs={{0,1},{1,2},{2,3},{3,4},{4,5},{5,6},{6,7},{7,8},{8,9},{9,10},{10,1... | collective-permute-start | bytes 1572872 | tf_op jit(solution)/shard_map/ppermute | solution.py:93
  43.5 1.6 %fusion.3.mask_ref = f32[256,1280]{1,0:T(8,128)} fusion(s32[1280]{0:T(1024)S(1)} %iota_add_fusion, s32[256]{0:T(256)S(1)} %iota_add_fusion.1, s32[1280]{0:T(1024)S(1)} %convert_reduce_fusion, s32[256]{0:T(256)S(1)} %convert_reduce_fusion.1, pred[1280]{0:T(1024)(128)(4,1)S(1)} %broadcast_compare_fusion), kind=kLoop, calls=%fused_computation.21 | loop fusion | flops 2621440 | bytes 1324288 | tf_op jit(solution)/shard_map/convert_element_type | solution.py:159
  45.2 6.4 %collective-permute-start.8 = (bf16[2,256,512]{2,1,0:T(8,128)(2,1)}, bf16[2,256,512]{2,1,0:T(8,128)(2,1)}, u32[]{:S(2)}, u32[]{:S(2)}) collective-permute-start(bf16[2,256,512]{2,1,0:T(8,128)(2,1)} %collective-permute-done.7), channel_id=1, source_target_pairs={{0,1},{1,2},{2,3},{3,4},{4,5},{5,6},{6,7},{7,8},{8,9},{9,10},{10,1... | collective-permute-start | bytes 1572872 | tf_op jit(solution)/shard_map/ppermute | solution.py:93
  51.6 0.0 collective-permute-done.4
  51.6 1.1 constant_dynamic-update-slice_fusion.3
  52.7 1.1 constant_dynamic-update-slice_fusion.2
  53.9 1.6 %slice_bitcast_fusion.2 = (bf16[1280,512]{1,0:T(8,128)(2,1)}, bf16[1280,512]{1,0:T(8,128)(2,1)}) fusion(bf16[2,1280,512]{2,1,0:T(8,128)(2,1)S(1)} %constant_dynamic-update-slice_fusion), kind=kLoop, calls=%fused_computation.16 | loop fusion | bytes 5242880 | tf_op jit(solution)/shard_map/squeeze | solution.py:173
  55.5 0.3 collective-permute-done
  55.8 1.0 copy-done.4
  56.8 15.2 %shard_map.76 = (bf16[256,1024]{1,0:T(8,128)(2,1)}, bf16[1024,512]{1,0:T(8,128)(2,1)}, bf16[1024,512]{1,0:T(8,128)(2,1)}, f32[256,512]{1,0:T(8,128)}, f32[256,512]{1,0:T(8,128)}) custom-call(bf16[256,2048]{1,0:T(8,128)(2,1)} %bitcast.72, bf16[256,2048]{1,0:T(8,128)(2,1)} %bitcast.74, bf16[1280,512]{1,0:T(8,128)(2,1)} %get-tuple-element.24.k_ref, ...), custom_call_target="tpu_custom_call" | custom-call | tf_op jit(solution)/shard_map/pallas_call | solution.py:69
  72.0 1.1 fusion.8
  73.1 1.9 %collective-permute-start.9 = (bf16[2,256,512]{2,1,0:T(8,128)(2,1)S(1)}, bf16[2,256,512]{2,1,0:T(8,128)(2,1)S(1)}, u32[]{:S(2)}, u32[]{:S(2)}) collective-permute-start(bf16[2,256,512]{2,1,0:T(8,128)(2,1)S(1)} %fusion.8), channel_id=1, source_target_pairs={{1,0},{2,1},{3,2},{4,3},{5,4},{6,5},{7,6},{8,7},{9,8},{10,9},{11,1... | collective-permute-start | bytes 1572872 | tf_op jit(solution)/shard_map/ppermute | solution.py:93
  75.0 0.0 collective-permute-done.8
  75.0 1.1 constant_dynamic-update-slice_fusion.9
  76.1 1.1 constant_dynamic-update-slice_fusion.8
  77.3 1.6 %slice_bitcast_fusion = (bf16[1280,512]{1,0:T(8,128)(2,1)}, bf16[1280,512]{1,0:T(8,128)(2,1)}) fusion(bf16[2,1280,512]{2,1,0:T(8,128)(2,1)S(1)} %constant_dynamic-update-slice_fusion.5), kind=kLoop, calls=%fused_computation.14 | loop fusion | bytes 5242880 | tf_op jit(solution)/shard_map/squeeze | solution.py:173
  79.0 15.1 %shard_map.77 = (bf16[256,1024]{1,0:T(8,128)(2,1)}, bf16[1024,512]{1,0:T(8,128)(2,1)}, bf16[1024,512]{1,0:T(8,128)(2,1)}, f32[256,512]{1,0:T(8,128)}, f32[256,512]{1,0:T(8,128)}) custom-call(bf16[256,2048]{1,0:T(8,128)(2,1)} %bitcast.73, bf16[256,2048]{1,0:T(8,128)(2,1)} %bitcast.75, bf16[1280,512]{1,0:T(8,128)(2,1)} %get-tuple-element.26.k_ref, ...), custom_call_target="tpu_custom_call" | custom-call | tf_op jit(solution)/shard_map/pallas_call | solution.py:69
  94.1 1.2 fusion.5
  95.4 2.9 %collective-permute-start.13 = (bf16[2,256,512]{2,1,0:T(8,128)(2,1)S(1)}, bf16[2,256,512]{2,1,0:T(8,128)(2,1)S(1)}, u32[]{:S(2)}, u32[]{:S(2)}) collective-permute-start(bf16[2,256,512]{2,1,0:T(8,128)(2,1)S(1)} %fusion.5), channel_id=1, source_target_pairs={{1,0},{2,1},{3,2},{4,3},{5,4},{6,5},{7,6},{8,7},{9,8},{10,9},{11,1... | collective-permute-start | bytes 1572872 | tf_op jit(solution)/shard_map/ppermute | solution.py:93
  98.3 0.1 add_convert_fusion.5
  98.4 1.9 %collective-permute-start.10 = (bf16[2,256,512]{2,1,0:T(8,128)(2,1)S(1)}, bf16[2,256,512]{2,1,0:T(8,128)(2,1)S(1)}, u32[]{:S(2)}, u32[]{:S(2)}) collective-permute-start(bf16[2,256,512]{2,1,0:T(8,128)(2,1)S(1)} %add_convert_fusion.5), channel_id=1, source_target_pairs={{1,0},{2,1},{3,2},{4,3},{5,4},{6,5},{7,6},{8,7},{9,8},{10,9},{11,1... | collective-permute-start | bytes 1572872 | tf_op jit(solution)/shard_map/ppermute | solution.py:93
  100.3 7.8 %collective-permute-done.13 = bf16[2,256,512]{2,1,0:T(8,128)(2,1)S(1)} collective-permute-done((bf16[2,256,512]{2,1,0:T(8,128)(2,1)S(1)}, bf16[2,256,512]{2,1,0:T(8,128)(2,1)S(1)}, u32[]{:S(2)}, u32[]{:S(2)}) %collective-permute-start.13) | collective-permute-done | bytes 524320 | tf_op jit(solution)/shard_map/ppermute | solution.py:93
  108.1 0.1 add_convert_fusion.2
  108.3 1.9 %collective-permute-start.14 = (bf16[2,256,512]{2,1,0:T(8,128)(2,1)S(1)}, bf16[2,256,512]{2,1,0:T(8,128)(2,1)S(1)}, u32[]{:S(2)}, u32[]{:S(2)}) collective-permute-start(bf16[2,256,512]{2,1,0:T(8,128)(2,1)S(1)} %add_convert_fusion.2), channel_id=1, source_target_pairs={{1,0},{2,1},{3,2},{4,3},{5,4},{6,5},{7,6},{8,7},{9,8},{10,9},{11,1... | collective-permute-start | bytes 1572872 | tf_op jit(solution)/shard_map/ppermute | solution.py:93
  110.2 3.5 %collective-permute-done.10 = bf16[2,256,512]{2,1,0:T(8,128)(2,1)S(1)} collective-permute-done((bf16[2,256,512]{2,1,0:T(8,128)(2,1)S(1)}, bf16[2,256,512]{2,1,0:T(8,128)(2,1)S(1)}, u32[]{:S(2)}, u32[]{:S(2)}) %collective-permute-start.10) | collective-permute-done | bytes 524320 | tf_op jit(solution)/shard_map/ppermute | solution.py:93
  113.7 0.1 add_convert_fusion.4
  113.9 1.9 %collective-permute-start.11 = (bf16[2,256,512]{2,1,0:T(8,128)(2,1)S(1)}, bf16[2,256,512]{2,1,0:T(8,128)(2,1)S(1)}, u32[]{:S(2)}, u32[]{:S(2)}) collective-permute-start(bf16[2,256,512]{2,1,0:T(8,128)(2,1)S(1)} %add_convert_fusion.4), channel_id=1, source_target_pairs={{1,0},{2,1},{3,2},{4,3},{5,4},{6,5},{7,6},{8,7},{9,8},{10,9},{11,1... | collective-permute-start | bytes 1572872 | tf_op jit(solution)/shard_map/ppermute | solution.py:93
  115.8 5.1 %collective-permute-done.14 = bf16[2,256,512]{2,1,0:T(8,128)(2,1)S(1)} collective-permute-done((bf16[2,256,512]{2,1,0:T(8,128)(2,1)S(1)}, bf16[2,256,512]{2,1,0:T(8,128)(2,1)S(1)}, u32[]{:S(2)}, u32[]{:S(2)}) %collective-permute-start.14) | collective-permute-done | bytes 524320 | tf_op jit(solution)/shard_map/ppermute | solution.py:93
  120.9 0.1 add_convert_fusion.1
  121.0 0.0 copy-start.12
  121.0 2.1 %collective-permute-start.15 = (bf16[2,256,512]{2,1,0:T(8,128)(2,1)S(1)}, bf16[2,256,512]{2,1,0:T(8,128)(2,1)S(1)}, u32[]{:S(2)}, u32[]{:S(2)}) collective-permute-start(bf16[2,256,512]{2,1,0:T(8,128)(2,1)S(1)} %add_convert_fusion.1), channel_id=1, source_target_pairs={{1,0},{2,1},{3,2},{4,3},{5,4},{6,5},{7,6},{8,7},{9,8},{10,9},{11,1... | collective-permute-start | bytes 1572872 | tf_op jit(solution)/shard_map/ppermute | solution.py:93
  123.1 3.4 %collective-permute-done.11 = bf16[2,256,512]{2,1,0:T(8,128)(2,1)S(1)} collective-permute-done((bf16[2,256,512]{2,1,0:T(8,128)(2,1)S(1)}, bf16[2,256,512]{2,1,0:T(8,128)(2,1)S(1)}, u32[]{:S(2)}, u32[]{:S(2)}) %collective-permute-start.11) | collective-permute-done | bytes 524320 | tf_op jit(solution)/shard_map/ppermute | solution.py:93
  126.5 0.1 add_convert_fusion.3
  126.6 1.9 %collective-permute-start.12 = (bf16[2,256,512]{2,1,0:T(8,128)(2,1)S(1)}, bf16[2,256,512]{2,1,0:T(8,128)(2,1)S(1)}, u32[]{:S(2)}, u32[]{:S(2)}) collective-permute-start(bf16[2,256,512]{2,1,0:T(8,128)(2,1)S(1)} %add_convert_fusion.3), channel_id=1, source_target_pairs={{1,0},{2,1},{3,2},{4,3},{5,4},{6,5},{7,6},{8,7},{9,8},{10,9},{11,1... | collective-permute-start | bytes 1572872 | tf_op jit(solution)/shard_map/ppermute | solution.py:93
  128.5 5.2 %collective-permute-done.15 = bf16[2,256,512]{2,1,0:T(8,128)(2,1)S(1)} collective-permute-done((bf16[2,256,512]{2,1,0:T(8,128)(2,1)S(1)}, bf16[2,256,512]{2,1,0:T(8,128)(2,1)S(1)}, u32[]{:S(2)}, u32[]{:S(2)}) %collective-permute-start.15) | collective-permute-done | bytes 524320 | tf_op jit(solution)/shard_map/ppermute | solution.py:93
  133.8 0.1 add_convert_fusion
  133.9 2.1 %collective-permute-start.16 = (bf16[2,256,512]{2,1,0:T(8,128)(2,1)S(1)}, bf16[2,256,512]{2,1,0:T(8,128)(2,1)S(1)}, u32[]{:S(2)}, u32[]{:S(2)}) collective-permute-start(bf16[2,256,512]{2,1,0:T(8,128)(2,1)S(1)} %add_convert_fusion), channel_id=1, source_target_pairs={{1,0},{2,1},{3,2},{4,3},{5,4},{6,5},{7,6},{8,7},{9,8},{10,9},{11,1... | collective-permute-start | bytes 1572872 | tf_op jit(solution)/shard_map/ppermute | solution.py:93
  136.0 1.1 maximum_bitcast_fusion
  137.1 2.3 %collective-permute-done.12 = bf16[2,256,512]{2,1,0:T(8,128)(2,1)S(1)} collective-permute-done((bf16[2,256,512]{2,1,0:T(8,128)(2,1)S(1)}, bf16[2,256,512]{2,1,0:T(8,128)(2,1)S(1)}, u32[]{:S(2)}, u32[]{:S(2)}) %collective-permute-start.12) | collective-permute-done | bytes 524320 | tf_op jit(solution)/shard_map/ppermute | solution.py:93
  139.4 0.1 convert_element_type.93
  139.5 0.3 fusion.13
  139.8 6.9 %collective-permute-done.16 = bf16[2,256,512]{2,1,0:T(8,128)(2,1)S(1)} collective-permute-done((bf16[2,256,512]{2,1,0:T(8,128)(2,1)S(1)}, bf16[2,256,512]{2,1,0:T(8,128)(2,1)S(1)}, u32[]{:S(2)}, u32[]{:S(2)}) %collective-permute-start.16) | collective-permute-done | bytes 524320 | tf_op jit(solution)/shard_map/ppermute | solution.py:93
  146.7 0.1 convert_element_type.104
  146.8 0.3 fusion.11
  147.1 0.9 maximum_bitcast_fusion.2
  147.9 0.9 maximum_bitcast_fusion.1
  (37 shorter events, 0.3 us)
Async XLA Ops:
  0.6 35.6 %copy-start.13 = (s32[4]{0:T(128)S(1)}, s32[4]{0:T(128)}, u32[]{:S(2)}) copy-start(s32[4]{0:T(128)} %param.9) | copy-start | bytes 52
  2.0 9.4 %collective-permute-start.1 = (bf16[2,256,512]{2,1,0:T(8,128)(2,1)S(1)}, bf16[2,256,512]{2,1,0:T(8,128)(2,1)S(1)}, u32[]{:S(2)}, u32[]{:S(2)}) collective-permute-start(bf16[2,256,512]{2,1,0:T(8,128)(2,1)S(1)} %pad_maximum_fusion.2), channel_id=1, source_target_pairs={{0,1},{1,2},{2,3},{3,4},{4,5},{5,6},{6,7},{7,8},{8,9},{9,10},{10,1... | collective-permute-start | bytes 1572872 | tf_op jit(solution)/shard_map/ppermute | solution.py:93
  5.4 12.5 %collective-permute-start.5 = (bf16[2,256,512]{2,1,0:T(8,128)(2,1)S(1)}, bf16[2,256,512]{2,1,0:T(8,128)(2,1)S(1)}, u32[]{:S(2)}, u32[]{:S(2)}) collective-permute-start(bf16[2,256,512]{2,1,0:T(8,128)(2,1)S(1)} %pad_maximum_fusion.3), channel_id=1, source_target_pairs={{0,1},{1,2},{2,3},{3,4},{4,5},{5,6},{6,7},{7,8},{8,9},{9,10},{10,1... | collective-permute-start | bytes 1572872 | tf_op jit(solution)/shard_map/ppermute | solution.py:93
  11.4 12.6 %copy-start.9 = (bf16[2,256,512]{2,1,0:T(8,128)(2,1)}, bf16[2,256,512]{2,1,0:T(8,128)(2,1)S(1)}, u32[]{:S(2)}) copy-start(bf16[2,256,512]{2,1,0:T(8,128)(2,1)S(1)} %collective-permute-done.1) | copy-start | bytes 1572868
  11.4 12.6 %collective-permute-start.2 = (bf16[2,256,512]{2,1,0:T(8,128)(2,1)S(1)}, bf16[2,256,512]{2,1,0:T(8,128)(2,1)}, u32[]{:S(2)}, u32[]{:S(2)}) collective-permute-start(bf16[2,256,512]{2,1,0:T(8,128)(2,1)S(1)} %collective-permute-done.1), channel_id=1, source_target_pairs={{0,1},{1,2},{2,3},{3,4},{4,5},{5,6},{6,7},{7,8},{8,9},{9,10},{10,1... | collective-permute-start | bytes 1572872 | tf_op jit(solution)/shard_map/ppermute | solution.py:93
  17.9 18.7 %collective-permute-start.6 = (bf16[2,256,512]{2,1,0:T(8,128)(2,1)S(1)}, bf16[2,256,512]{2,1,0:T(8,128)(2,1)S(1)}, u32[]{:S(2)}, u32[]{:S(2)}) collective-permute-start(bf16[2,256,512]{2,1,0:T(8,128)(2,1)S(1)} %collective-permute-done.5), channel_id=1, source_target_pairs={{0,1},{1,2},{2,3},{3,4},{4,5},{5,6},{6,7},{7,8},{8,9},{9,10},{10,1... | collective-permute-start | bytes 1572872 | tf_op jit(solution)/shard_map/ppermute | solution.py:93
  24.0 14.8 %collective-permute-start.3 = (bf16[2,256,512]{2,1,0:T(8,128)(2,1)}, bf16[2,256,512]{2,1,0:T(8,128)(2,1)}, u32[]{:S(2)}, u32[]{:S(2)}) collective-permute-start(bf16[2,256,512]{2,1,0:T(8,128)(2,1)} %collective-permute-done.2), channel_id=1, source_target_pairs={{0,1},{1,2},{2,3},{3,4},{4,5},{5,6},{6,7},{7,8},{8,9},{9,10},{10,1... | collective-permute-start | bytes 1572872 | tf_op jit(solution)/shard_map/ppermute | solution.py:93
  30.6 25.2 %collective-permute-start = (bf16[1,256,2048]{2,1,0:T(8,128)(2,1)}, bf16[1,256,2048]{2,1,0:T(8,128)(2,1)S(1)}, u32[]{:S(2)}, u32[]{:S(2)}) collective-permute-start(bf16[1,256,2048]{2,1,0:T(8,128)(2,1)} %param.8), channel_id=1, source_target_pairs={{0,224},{32,0},{64,32},{96,64},{128,96},{160,128},{192,160},{224,1... | collective-permute-start | bytes 3145736 | tf_op jit(solution)/shard_map/ppermute | solution.py:87
  36.5 17.3 %copy-start.10 = (bf16[2,256,512]{2,1,0:T(8,128)(2,1)S(1)}, bf16[2,256,512]{2,1,0:T(8,128)(2,1)}, u32[]{:S(2)}) copy-start(bf16[2,256,512]{2,1,0:T(8,128)(2,1)} %copy-done.9) | copy-start | bytes 1572868
  36.6 8.5 %collective-permute-start.7 = (bf16[2,256,512]{2,1,0:T(8,128)(2,1)S(1)}, bf16[2,256,512]{2,1,0:T(8,128)(2,1)}, u32[]{:S(2)}, u32[]{:S(2)}) collective-permute-start(bf16[2,256,512]{2,1,0:T(8,128)(2,1)S(1)} %collective-permute-done.6), channel_id=1, source_target_pairs={{0,1},{1,2},{2,3},{3,4},{4,5},{5,6},{6,7},{7,8},{8,9},{9,10},{10,1... | collective-permute-start | bytes 1572872 | tf_op jit(solution)/shard_map/ppermute | solution.py:93
  38.9 12.7 %collective-permute-start.4 = (bf16[2,256,512]{2,1,0:T(8,128)(2,1)}, bf16[2,256,512]{2,1,0:T(8,128)(2,1)S(1)}, u32[]{:S(2)}, u32[]{:S(2)}) collective-permute-start(bf16[2,256,512]{2,1,0:T(8,128)(2,1)} %collective-permute-done.3), channel_id=1, source_target_pairs={{0,1},{1,2},{2,3},{3,4},{4,5},{5,6},{6,7},{7,8},{8,9},{9,10},{10,1... | collective-permute-start | bytes 1572872 | tf_op jit(solution)/shard_map/ppermute | solution.py:93
  45.2 29.9 %collective-permute-start.8 = (bf16[2,256,512]{2,1,0:T(8,128)(2,1)}, bf16[2,256,512]{2,1,0:T(8,128)(2,1)}, u32[]{:S(2)}, u32[]{:S(2)}) collective-permute-start(bf16[2,256,512]{2,1,0:T(8,128)(2,1)} %collective-permute-done.7), channel_id=1, source_target_pairs={{0,1},{1,2},{2,3},{3,4},{4,5},{5,6},{6,7},{7,8},{8,9},{9,10},{10,1... | collective-permute-start | bytes 1572872 | tf_op jit(solution)/shard_map/ppermute | solution.py:93
  55.8 1.0 copy-start.4
  73.1 25.2 %collective-permute-start.9 = (bf16[2,256,512]{2,1,0:T(8,128)(2,1)S(1)}, bf16[2,256,512]{2,1,0:T(8,128)(2,1)S(1)}, u32[]{:S(2)}, u32[]{:S(2)}) collective-permute-start(bf16[2,256,512]{2,1,0:T(8,128)(2,1)S(1)} %fusion.8), channel_id=1, source_target_pairs={{1,0},{2,1},{3,2},{4,3},{5,4},{6,5},{7,6},{8,7},{9,8},{10,9},{11,1... | collective-permute-start | bytes 1572872 | tf_op jit(solution)/shard_map/ppermute | solution.py:93
  94.1 4.1 %copy-start = (bf16[1024,512]{1,0:T(8,128)(2,1)S(1)}, bf16[1024,512]{1,0:T(8,128)(2,1)}, u32[]{:S(2)}) copy-start(bf16[1024,512]{1,0:T(8,128)(2,1)} %get-tuple-element.16) | copy-start | bytes 3145732
  94.1 4.2 %copy-start.1 = (bf16[1024,512]{1,0:T(8,128)(2,1)S(1)}, bf16[1024,512]{1,0:T(8,128)(2,1)}, u32[]{:S(2)}) copy-start(bf16[1024,512]{1,0:T(8,128)(2,1)} %get-tuple-element.17) | copy-start | bytes 3145732
  94.1 14.0 %copy-start.2 = (bf16[1024,512]{1,0:T(8,128)(2,1)S(1)}, bf16[1024,512]{1,0:T(8,128)(2,1)}, u32[]{:S(2)}) copy-start(bf16[1024,512]{1,0:T(8,128)(2,1)} %get-tuple-element.19) | copy-start | bytes 3145732
  94.1 14.0 %copy-start.3 = (bf16[1024,512]{1,0:T(8,128)(2,1)S(1)}, bf16[1024,512]{1,0:T(8,128)(2,1)}, u32[]{:S(2)}) copy-start(bf16[1024,512]{1,0:T(8,128)(2,1)} %get-tuple-element.20) | copy-start | bytes 3145732
  95.4 12.7 %collective-permute-start.13 = (bf16[2,256,512]{2,1,0:T(8,128)(2,1)S(1)}, bf16[2,256,512]{2,1,0:T(8,128)(2,1)S(1)}, u32[]{:S(2)}, u32[]{:S(2)}) collective-permute-start(bf16[2,256,512]{2,1,0:T(8,128)(2,1)S(1)} %fusion.5), channel_id=1, source_target_pairs={{1,0},{2,1},{3,2},{4,3},{5,4},{6,5},{7,6},{8,7},{9,8},{10,9},{11,1... | collective-permute-start | bytes 1572872 | tf_op jit(solution)/shard_map/ppermute | solution.py:93
  98.4 15.3 %collective-permute-start.10 = (bf16[2,256,512]{2,1,0:T(8,128)(2,1)S(1)}, bf16[2,256,512]{2,1,0:T(8,128)(2,1)S(1)}, u32[]{:S(2)}, u32[]{:S(2)}) collective-permute-start(bf16[2,256,512]{2,1,0:T(8,128)(2,1)S(1)} %add_convert_fusion.5), channel_id=1, source_target_pairs={{1,0},{2,1},{3,2},{4,3},{5,4},{6,5},{7,6},{8,7},{9,8},{10,9},{11,1... | collective-permute-start | bytes 1572872 | tf_op jit(solution)/shard_map/ppermute | solution.py:93
  108.3 12.6 %collective-permute-start.14 = (bf16[2,256,512]{2,1,0:T(8,128)(2,1)S(1)}, bf16[2,256,512]{2,1,0:T(8,128)(2,1)S(1)}, u32[]{:S(2)}, u32[]{:S(2)}) collective-permute-start(bf16[2,256,512]{2,1,0:T(8,128)(2,1)S(1)} %add_convert_fusion.2), channel_id=1, source_target_pairs={{1,0},{2,1},{3,2},{4,3},{5,4},{6,5},{7,6},{8,7},{9,8},{10,9},{11,1... | collective-permute-start | bytes 1572872 | tf_op jit(solution)/shard_map/ppermute | solution.py:93
  113.9 12.6 %collective-permute-start.11 = (bf16[2,256,512]{2,1,0:T(8,128)(2,1)S(1)}, bf16[2,256,512]{2,1,0:T(8,128)(2,1)S(1)}, u32[]{:S(2)}, u32[]{:S(2)}) collective-permute-start(bf16[2,256,512]{2,1,0:T(8,128)(2,1)S(1)} %add_convert_fusion.4), channel_id=1, source_target_pairs={{1,0},{2,1},{3,2},{4,3},{5,4},{6,5},{7,6},{8,7},{9,8},{10,9},{11,1... | collective-permute-start | bytes 1572872 | tf_op jit(solution)/shard_map/ppermute | solution.py:93
  121.0 15.0 %copy-start.11 = (bf16[256,1024]{1,0:T(8,128)(2,1)S(1)}, bf16[256,1024]{1,0:T(8,128)(2,1)}, u32[]{:S(2)}) copy-start(bf16[256,1024]{1,0:T(8,128)(2,1)} %get-tuple-element.13) | copy-start | bytes 1572868
  121.0 15.0 %copy-start.12 = (bf16[256,1024]{1,0:T(8,128)(2,1)S(1)}, bf16[256,1024]{1,0:T(8,128)(2,1)}, u32[]{:S(2)}) copy-start(bf16[256,1024]{1,0:T(8,128)(2,1)} %get-tuple-element.14) | copy-start | bytes 1572868
  121.0 12.7 %collective-permute-start.15 = (bf16[2,256,512]{2,1,0:T(8,128)(2,1)S(1)}, bf16[2,256,512]{2,1,0:T(8,128)(2,1)S(1)}, u32[]{:S(2)}, u32[]{:S(2)}) collective-permute-start(bf16[2,256,512]{2,1,0:T(8,128)(2,1)S(1)} %add_convert_fusion.1), channel_id=1, source_target_pairs={{1,0},{2,1},{3,2},{4,3},{5,4},{6,5},{7,6},{8,7},{9,8},{10,9},{11,1... | collective-permute-start | bytes 1572872 | tf_op jit(solution)/shard_map/ppermute | solution.py:93
  126.6 12.8 %collective-permute-start.12 = (bf16[2,256,512]{2,1,0:T(8,128)(2,1)S(1)}, bf16[2,256,512]{2,1,0:T(8,128)(2,1)S(1)}, u32[]{:S(2)}, u32[]{:S(2)}) collective-permute-start(bf16[2,256,512]{2,1,0:T(8,128)(2,1)S(1)} %add_convert_fusion.3), channel_id=1, source_target_pairs={{1,0},{2,1},{3,2},{4,3},{5,4},{6,5},{7,6},{8,7},{9,8},{10,9},{11,1... | collective-permute-start | bytes 1572872 | tf_op jit(solution)/shard_map/ppermute | solution.py:93
  133.9 5.6 %copy-start.5 = (f32[256,512]{1,0:T(8,128)S(1)}, f32[256,512]{1,0:T(8,128)}, u32[]{:S(2)}) copy-start(f32[256,512]{1,0:T(8,128)} %get-tuple-element.15) | copy-start | bytes 1572868
  133.9 5.6 %copy-start.6 = (f32[256,512]{1,0:T(8,128)S(1)}, f32[256,512]{1,0:T(8,128)}, u32[]{:S(2)}) copy-start(f32[256,512]{1,0:T(8,128)} %get-tuple-element.21) | copy-start | bytes 1572868
  133.9 12.7 %collective-permute-start.16 = (bf16[2,256,512]{2,1,0:T(8,128)(2,1)S(1)}, bf16[2,256,512]{2,1,0:T(8,128)(2,1)S(1)}, u32[]{:S(2)}, u32[]{:S(2)}) collective-permute-start(bf16[2,256,512]{2,1,0:T(8,128)(2,1)S(1)} %add_convert_fusion), channel_id=1, source_target_pairs={{1,0},{2,1},{3,2},{4,3},{5,4},{6,5},{7,6},{8,7},{9,8},{10,9},{11,1... | collective-permute-start | bytes 1572872 | tf_op jit(solution)/shard_map/ppermute | solution.py:93
  137.1 9.7 %copy-start.7 = (f32[256,512]{1,0:T(8,128)S(1)}, f32[256,512]{1,0:T(8,128)}, u32[]{:S(2)}) copy-start(f32[256,512]{1,0:T(8,128)} %get-tuple-element.18) | copy-start | bytes 1572868
  137.1 9.7 %copy-start.8 = (f32[256,512]{1,0:T(8,128)S(1)}, f32[256,512]{1,0:T(8,128)}, u32[]{:S(2)}) copy-start(f32[256,512]{1,0:T(8,128)} %get-tuple-element.22) | copy-start | bytes 1572868

commit v4 on v3

v4 whole, which is shorter than its diff:
```python
import jax
import jax.numpy as jnp
from jax import lax
from jax.experimental import pallas as pl
from jax.experimental.pallas import tpu as pltpu
from jax.sharding import PartitionSpec as P


WINDOW = 1024
KV_HEADS = 8
CHUNKS = 2
GROUP = 2


SCORE_SCALE = 168.0 ** (-0.5)


def product(a, b, dims):
    return lax.dot_general(a, b, dims, preferred_element_type=jnp.float32)


def attention_back_kernel(
    at_ref, q_ref, do_ref, k_ref, v_ref, mask_ref, dq_ref, dk_far_ref, dv_far_ref, dk_own_ref, dv_own_ref
):
    head_size = k_ref.shape[1]
    heads = q_ref.shape[1] // head_size
    rows = q_ref.shape[0]
    far = dk_far_ref.shape[0]
    allowed = mask_ref[...] > 0
    keys = k_ref[...]
    values = v_ref[...]
    queries = jnp.concatenate([q_ref[:, h * head_size:(h + 1) * head_size] for h in range(heads)], axis=0)
    grads = jnp.concatenate([do_ref[:, h * head_size:(h + 1) * head_size] for h in range(heads)], axis=0)
    allowed = jnp.concatenate([allowed] * heads, axis=0)
    nt = (((1,), (1,)), ((), ()))
    tn = (((0,), (0,)), ((), ()))
    nn = (((1,), (0,)), ((), ()))
    scores = SCORE_SCALE * product(queries, keys, nt)
    scores = jnp.where(allowed, scores, -jnp.inf)
    highest = jnp.max(scores, axis=-1, keepdims=True)
    log_total = highest + jnp.log(jnp.sum(jnp.exp(scores - highest), axis=-1, keepdims=True))
    weights = jnp.exp(scores - log_total)
    weight_half = weights.astype(jnp.bfloat16)
    attended = product(weight_half, values, nn).astype(jnp.bfloat16)
    row_dot = jnp.sum(attended.astype(jnp.float32) * grads.astype(jnp.float32), axis=-1, keepdims=True)
    weight_grad = product(grads, values, nt)
    score_grad = (weights * (weight_grad - row_dot)).astype(jnp.bfloat16)
    query_back = SCORE_SCALE * product(score_grad, keys, nn)
    for h in range(heads):
        dq_ref[:, h * head_size:(h + 1) * head_size] = query_back[h * rows:(h + 1) * rows].astype(dq_ref.dtype)
    key_back = SCORE_SCALE * product(score_grad, queries, tn)
    value_back = product(weight_half, grads, tn)
    dk_far_ref[...] = key_back[:far].astype(dk_far_ref.dtype)
    dv_far_ref[...] = value_back[:far].astype(dv_far_ref.dtype)
    dk_own_ref[...] = key_back[far:]
    dv_own_ref[...] = value_back[far:]


def attention_back(queries, grads, window_keys, window_values, allowed, first_group, kv_group, groups):
    rows, width = queries.shape
    span = window_keys.shape[0]
    head_size = width // (GROUP * KV_HEADS)
    pair_width = groups * head_size
    group_width = GROUP * head_size
    far = span - rows
    q_spec = pl.BlockSpec((rows, group_width), lambda g, at: (0, g + at[0]))
    dq_spec = pl.BlockSpec((rows, group_width), lambda g, at: (0, g))
    kv_spec = pl.BlockSpec((span, head_size), lambda g, at: (0, g + at[1]))
    far_spec = pl.BlockSpec((far, head_size), lambda g, at: (0, g))
    own_spec = pl.BlockSpec((rows, head_size), lambda g, at: (0, g))
    mask_spec = pl.BlockSpec((rows, span), lambda g, at: (0, 0))
    grid_spec = pltpu.PrefetchScalarGridSpec(
        num_scalar_prefetch=1,
        grid=(groups,),
        in_specs=[q_spec, q_spec, kv_spec, kv_spec, mask_spec],
        out_specs=[dq_spec, far_spec, far_spec, own_spec, own_spec],
    )
    return pl.pallas_call(
        attention_back_kernel,
        grid_spec=grid_spec,
        out_shape=[
            jax.ShapeDtypeStruct((rows, groups * group_width), jnp.bfloat16),
            jax.ShapeDtypeStruct((far, pair_width), jnp.bfloat16),
            jax.ShapeDtypeStruct((far, pair_width), jnp.bfloat16),
            jax.ShapeDtypeStruct((rows, pair_width), jnp.float32),
            jax.ShapeDtypeStruct((rows, pair_width), jnp.float32),
        ],
        compiler_params=pltpu.CompilerParams(vmem_limit_bytes=60 * 1024 * 1024),
    )(jnp.array([first_group, kv_group], jnp.int32), queries, grads, window_keys, window_values, allowed)


def passed_along(shard, axis, by):
    count = lax.axis_size(axis)
    return lax.ppermute(shard, axis, [(i, (i + by) % count) for i in range(count)])


def shifted(value, axis, steps):
    count = lax.axis_size(axis)
    initial, last = (max(0, -steps), min(count, count - steps))
    return lax.ppermute(value, axis, [(source, source + steps) for source in range(initial, last)])


def doc_number(positions, doc_lengths):
    ends = jnp.cumsum(doc_lengths)
    return jnp.sum((positions[:, None] >= ends[None, :]).astype(jnp.int32), axis=1)


def window_mask(query_pos, key_pos, doc_lengths):
    same_doc = (
        doc_number(query_pos, doc_lengths)[:, None] == doc_number(key_pos, doc_lengths)[None, :]
    )
    spacing = query_pos[:, None] - key_pos[None, :]
    return same_doc & (spacing >= 0) & (spacing < WINDOW) & (key_pos[None, :] >= 0)


def local_body(query_rows, key_rows, value_rows, finished_grad, doc_lengths):
    queries = query_rows[0]
    keys_here = key_rows[0]
    values_here = value_rows[0]
    count_rows = queries.shape[0]
    reach_blocks = WINDOW // count_rows
    pair_width = keys_here.shape[1]
    head_size = pair_width // KV_HEADS
    rank_here = lax.axis_index("ctx")
    first_pos = rank_here * count_rows
    arriving = passed_along(finished_grad, "section", -1)[0]
    query_pos = first_pos + jnp.arange(count_rows, dtype=jnp.int32)
    key_pos = first_pos - WINDOW + jnp.arange(WINDOW + count_rows, dtype=jnp.int32)
    allowed = window_mask(query_pos, key_pos, doc_lengths).astype(jnp.float32)
    chunk_groups = KV_HEADS // CHUNKS
    chunk_width = chunk_groups * head_size

    def own_pair_of(chunk):
        cols = slice(chunk * chunk_width, (chunk + 1) * chunk_width)
        return jnp.stack([keys_here[:, cols], values_here[:, cols]])

    def joined(*values):
        return lax.optimization_barrier(values)

    def far_payload(pieces, block):
        rows = slice(block * count_rows, (block + 1) * count_rows)
        return jnp.stack(
            [
                jnp.concatenate([piece[1][rows] for piece in pieces], axis=1),
                jnp.concatenate([piece[2][rows] for piece in pieces], axis=1),
            ]
        )

    def return_hop(partial, pieces, block):
        arrived = shifted(partial, "ctx", -1).astype(jnp.float32)
        return (arrived + far_payload(pieces, block).astype(jnp.float32)).astype(jnp.bfloat16)

    def run_chunk(chunk, window_pair, side_step, side_value):
        pieces = []
        tied = (queries, arriving, window_pair)
        for group in range(chunk_groups):
            side_value = side_step(group, side_value)
            piece = attention_back(
                tied[0], tied[1], tied[2][0], tied[2][1], allowed,
                chunk * chunk_groups + group, group, 1,
            )
            pieces.append(piece)
            side_value, tied, _ = joined(side_value, tied, piece)
        return pieces, side_value

    relayed = own_pair_of(0)
    window_a = [relayed]
    for _ in range(reach_blocks):
        relayed = shifted(relayed, "ctx", 1)
        window_a.insert(0, relayed)
    window_a = jnp.concatenate(window_a, axis=1)

    window_b = []

    def forward_step(group, relayed_b):
        window_b.insert(0, relayed_b)
        return shifted(relayed_b, "ctx", 1)

    pieces_a, relayed_b = run_chunk(0, window_a, forward_step, own_pair_of(1))
    window_b = jnp.concatenate([relayed_b] + window_b, axis=1)

    def return_step(group, partial):
        if group + 1 < reach_blocks:
            return return_hop(partial, pieces_a, group + 1)
        return shifted(partial, "ctx", -1).astype(jnp.float32)

    pieces_b, arrived_a = run_chunk(1, window_b, return_step, far_payload(pieces_a, 0))

    partial_b = far_payload(pieces_b, 0)
    for block in range(1, reach_blocks):
        partial_b = return_hop(partial_b, pieces_b, block)
    arrived_b = shifted(partial_b, "ctx", -1).astype(jnp.float32)

    query_grad = jnp.concatenate([piece[0] for piece in pieces_a + pieces_b], axis=1)
    key_grads, value_grads = [], []
    for pieces, arrived in ((pieces_a, arrived_a), (pieces_b, arrived_b)):
        key_own = jnp.concatenate([piece[3] for piece in pieces], axis=1)
        value_own = jnp.concatenate([piece[4] for piece in pieces], axis=1)
        key_grads.append((key_own + arrived[0]).astype(jnp.bfloat16))
        value_grads.append((value_own + arrived[1]).astype(jnp.bfloat16))
    return (
        query_grad[None],
        jnp.concatenate(key_grads, axis=1)[None],
        jnp.concatenate(value_grads, axis=1)[None],
    )


def solution(mesh):
    return jax.shard_map(
        local_body,
        mesh=mesh,
        in_specs=(
            P("section", "ctx", None),
            P("section", "ctx", None),
            P("section", "ctx", None),
            P("section", "ctx", None),
            P(),
        ),
        out_specs=(P("section", "ctx", None), P("section", "ctx", None), P("section", "ctx", None)),
        check_vma=False,
    )
```

time: 150 us -> 234 us (1.56)
  local copies, waits for them, and re-layouts: 10 us -> 46.3 us
  Pallas kernels: 30.3 us -> 50.3 us
  waiting for transfers between devices: 39.1 us -> 58.8 us
  other arithmetic: 8.8 us -> 14.4 us
    slice x0 -> x16, local copies, waits for them, and re-layouts: none -> 20.9 us  [the longest x8 11.1 us: far_payload(): piece[1][rows]]
    ppermute x16, waiting for transfers between devices: 38.8 us -> 58.8 us  [shifted(): lax.ppermute(value, axis, [(source, source + steps) for source in range(i...]
    pallas_call x2 -> x8, Pallas kernels: 30.3 us -> 50.3 us  [attention_back(): pl.pallas_call(attention_back_kernel, grid_spec=grid_spec, out_shape=[jax...]
    squeeze x2 -> x8, local copies, waits for them, and re-layouts: 3.29 us -> 15.3 us  [run_chunk(): tied[2][1]]
    convert_element_type x11, other arithmetic: 3.17 us -> 7.71 us  [the longest x6 5.51 us: return_hop(): (arrived + far_payload(pieces, block).astype(jnp.float32)).astype(jnp.bfl...]
    unnamed x36 -> x157, local copies, waits for them, and re-layouts: 5.48 us -> 6.48 us
  transfers between devices with their start and end apart: 17 -> 17, of which waited for: 10 -> 11; matrix products, arithmetic and copies ran while one was open for 10% -> 16% of each run, Pallas kernels for 20% -> 16%
where the time goes in v4:
time: 234 us; the launch traced here: 232 us
  starting transfers between devices  60.6 us (26%)
  waiting for transfers between devices  58.8 us (25%)
  Pallas kernels  50.3 us (21%)
  local copies, waits for them, and re-layouts  46.3 us (20%)
  other arithmetic  14.4 us (6%)
    ppermute x16, waiting for transfers between devices, shifted(): lax.ppermute(value, axis, [(source, source + steps) for source in range(i...  58.8 us
    ppermute x16, starting transfers between devices, shifted(): lax.ppermute(value, axis, [(source, source + steps) for source in range(i...  55 us
    pallas_call x8, Pallas kernels, attention_back(): pl.pallas_call(attention_back_kernel, grid_spec=grid_spec, out_shape=[jax...  50.3 us
    squeeze x8, local copies, waits for them, and re-layouts, run_chunk(): tied[2][1]  15.3 us
    slice x8, local copies, waits for them, and re-layouts, far_payload(): piece[1][rows]  11.1 us
    slice x8, local copies, waits for them, and re-layouts, far_payload(): piece[2][rows]  9.84 us
    unnamed x157, local copies, waits for them, and re-layouts  6.48 us
    ppermute x1, starting transfers between devices, passed_along(): lax.ppermute(shard, axis, [(i, (i + by) % count) for i in range(count)])  5.65 us
  transfers between devices with their start and end apart: 17, of which 11 were waited for; matrix products, arithmetic and copies ran while one was open for 16% of the time, Pallas kernels for 16%

profile of v4, /device:TPU:25, one launch (start us, length us, event | category | flops | bytes accessed | tf_op | source)
XLA Modules:
  0.0 232.3 jit_solution(5335945840613823543)
XLA Ops:
  0.6 1.3 slice_bitcast_fusion.18
  2.0 3.3 %collective-permute-start.1 = (bf16[2,256,512]{2,1,0:T(8,128)(2,1)S(1)}, bf16[2,256,512]{2,1,0:T(8,128)(2,1)S(1)}, u32[]{:S(2)}, u32[]{:S(2)}) collective-permute-start(bf16[2,256,512]{2,1,0:T(8,128)(2,1)S(1)} %pad_maximum_fusion), channel_id=1, source_target_pairs={{0,1},{1,2},{2,3},{3,4},{4,5},{5,6},{6,7},{7,8},{8,9},{9,10},{10,1... | collective-permute-start | bytes 1572872 | tf_op jit(solution)/shard_map/ppermute | solution.py:100
  5.3 6.1 %collective-permute-done.1 = bf16[2,256,512]{2,1,0:T(8,128)(2,1)S(1)} collective-permute-done((bf16[2,256,512]{2,1,0:T(8,128)(2,1)S(1)}, bf16[2,256,512]{2,1,0:T(8,128)(2,1)S(1)}, u32[]{:S(2)}, u32[]{:S(2)}) %collective-permute-start.1) | collective-permute-done | bytes 524320 | tf_op jit(solution)/shard_map/ppermute | solution.py:100
  12.2 6.5 %collective-permute-start.2 = (bf16[2,256,512]{2,1,0:T(8,128)(2,1)S(1)}, bf16[2,256,512]{2,1,0:T(8,128)(2,1)}, u32[]{:S(2)}, u32[]{:S(2)}) collective-permute-start(bf16[2,256,512]{2,1,0:T(8,128)(2,1)S(1)} %collective-permute-done.1), channel_id=1, source_target_pairs={{0,1},{1,2},{2,3},{3,4},{4,5},{5,6},{6,7},{7,8},{8,9},{9,10},{10,1... | collective-permute-start | bytes 1572872 | tf_op jit(solution)/shard_map/ppermute | solution.py:100
  18.7 5.7 %collective-permute-start = (bf16[1,256,2048]{2,1,0:T(8,128)(2,1)}, bf16[1,256,2048]{2,1,0:T(8,128)(2,1)S(1)}, u32[]{:S(2)}, u32[]{:S(2)}) collective-permute-start(bf16[1,256,2048]{2,1,0:T(8,128)(2,1)} %param.16), channel_id=1, source_target_pairs={{0,224},{32,0},{64,32},{96,64},{128,96},{160,128},{192,160},{224,1... | collective-permute-start | bytes 3145736 | tf_op jit(solution)/shard_map/ppermute | solution.py:94
  24.8 6.6 %collective-permute-start.3 = (bf16[2,256,512]{2,1,0:T(8,128)(2,1)}, bf16[2,256,512]{2,1,0:T(8,128)(2,1)}, u32[]{:S(2)}, u32[]{:S(2)}) collective-permute-start(bf16[2,256,512]{2,1,0:T(8,128)(2,1)} %collective-permute-done.2), channel_id=1, source_target_pairs={{0,1},{1,2},{2,3},{3,4},{4,5},{5,6},{6,7},{7,8},{8,9},{9,10},{10,1... | collective-permute-start | bytes 1572872 | tf_op jit(solution)/shard_map/ppermute | solution.py:100
  32.3 1.9 collective-permute-start.5
  34.6 3.3 %collective-permute-done.3 = bf16[2,256,512]{2,1,0:T(8,128)(2,1)} collective-permute-done((bf16[2,256,512]{2,1,0:T(8,128)(2,1)}, bf16[2,256,512]{2,1,0:T(8,128)(2,1)}, u32[]{:S(2)}, u32[]{:S(2)}) %collective-permute-start.3) | collective-permute-done | bytes 524320 | tf_op jit(solution)/shard_map/ppermute | solution.py:100
  37.9 6.5 %collective-permute-start.4 = (bf16[2,256,512]{2,1,0:T(8,128)(2,1)}, bf16[2,256,512]{2,1,0:T(8,128)(2,1)S(1)}, u32[]{:S(2)}, u32[]{:S(2)}) collective-permute-start(bf16[2,256,512]{2,1,0:T(8,128)(2,1)} %collective-permute-done.3), channel_id=1, source_target_pairs={{0,1},{1,2},{2,3},{3,4},{4,5},{5,6},{6,7},{7,8},{8,9},{9,10},{10,1... | collective-permute-start | bytes 1572872 | tf_op jit(solution)/shard_map/ppermute | solution.py:100
  44.4 1.6 fusion.3.mask_ref
  46.0 4.8 %collective-permute-done.4 = bf16[2,256,512]{2,1,0:T(8,128)(2,1)S(1)} collective-permute-done((bf16[2,256,512]{2,1,0:T(8,128)(2,1)}, bf16[2,256,512]{2,1,0:T(8,128)(2,1)S(1)}, u32[]{:S(2)}, u32[]{:S(2)}) %collective-permute-start.4) | collective-permute-done | bytes 524320 | tf_op jit(solution)/shard_map/ppermute | solution.py:100
  50.8 1.1 constant_dynamic-update-slice_fusion.3
  51.9 1.1 constant_dynamic-update-slice_fusion.2
  53.1 1.8 slice_bitcast_fusion.2
  56.3 6.2 %shard_map.148 = (bf16[256,256]{1,0:T(8,128)(2,1)}, bf16[1024,128]{1,0:T(8,128)(2,1)}, bf16[1024,128]{1,0:T(8,128)(2,1)}, f32[256,128]{1,0:T(8,128)}, f32[256,128]{1,0:T(8,128)}) custom-call(s32[2]{0:T(128)} %call_exported.0.at_ref, bf16[256,2048]{1,0:T(8,128)(2,1)} %bitcast.99, bf16[256,2048]{1,0:T(8,128)(2,1)} %bitcast.107, ...), custom_call_target="tpu_custom_call" | custom-call | tf_op jit(solution)/shard_map/pallas_call | solution.py:78
  63.5 3.6 %slice_bitcast_fusion.14 = (bf16[1280,512]{1,0:T(8,128)(2,1)}, bf16[1280,512]{1,0:T(8,128)(2,1)}) fusion(bf16[2,1280,512]{2,1,0:T(8,128)(2,1)} %copy-done.1), kind=kLoop, calls=%fused_computation.16 | loop fusion | bytes 5242880 | tf_op jit(solution)/shard_map/squeeze | solution.py:159
  67.1 6.4 %collective-permute-start.6 = (bf16[2,256,512]{2,1,0:T(8,128)(2,1)S(1)}, bf16[2,256,512]{2,1,0:T(8,128)(2,1)}, u32[]{:S(2)}, u32[]{:S(2)}) collective-permute-start(bf16[2,256,512]{2,1,0:T(8,128)(2,1)S(1)} %collective-permute-done.5), channel_id=1, source_target_pairs={{0,1},{1,2},{2,3},{3,4},{4,5},{5,6},{6,7},{7,8},{8,9},{9,10},{10,1... | collective-permute-start | bytes 1572872 | tf_op jit(solution)/shard_map/ppermute | solution.py:100
  74.7 6.3 %shard_map.149 = (bf16[256,256]{1,0:T(8,128)(2,1)}, bf16[1024,128]{1,0:T(8,128)(2,1)}, bf16[1024,128]{1,0:T(8,128)(2,1)}, f32[256,128]{1,0:T(8,128)}, f32[256,128]{1,0:T(8,128)}) custom-call(s32[2]{0:T(128)} %call_exported.1.at_ref, bf16[256,2048]{1,0:T(8,128)(2,1)} %bitcast.100, bf16[256,2048]{1,0:T(8,128)(2,1)} %bitcast.108, ...), custom_call_target="tpu_custom_call" | custom-call | tf_op jit(solution)/shard_map/pallas_call | solution.py:78
  81.0 1.6 fusion.19
  82.6 1.7 fusion.23
  84.3 2.1 collective-permute-start.7
  86.4 1.7 slice_bitcast_fusion.12
  88.6 6.2 %shard_map.150 = (bf16[256,256]{1,0:T(8,128)(2,1)}, bf16[1024,128]{1,0:T(8,128)(2,1)}, bf16[1024,128]{1,0:T(8,128)(2,1)}, f32[256,128]{1,0:T(8,128)}, f32[256,128]{1,0:T(8,128)}) custom-call(s32[2]{0:T(128)} %call_exported.2.at_ref, bf16[256,2048]{1,0:T(8,128)(2,1)} %bitcast.101, bf16[256,2048]{1,0:T(8,128)(2,1)} %bitcast.109, ...), custom_call_target="tpu_custom_call" | custom-call | tf_op jit(solution)/shard_map/pallas_call | solution.py:78
  94.8 1.6 fusion.20
  96.4 1.6 fusion.24
  98.0 1.7 slice_bitcast_fusion.10
  100.3 6.3 %shard_map.151 = (bf16[256,256]{1,0:T(8,128)(2,1)}, bf16[1024,128]{1,0:T(8,128)(2,1)}, bf16[1024,128]{1,0:T(8,128)(2,1)}, f32[256,128]{1,0:T(8,128)}, f32[256,128]{1,0:T(8,128)}) custom-call(s32[2]{0:T(128)} %call_exported.3.at_ref, bf16[256,2048]{1,0:T(8,128)(2,1)} %bitcast.102, bf16[256,2048]{1,0:T(8,128)(2,1)} %bitcast.110, ...), custom_call_target="tpu_custom_call" | custom-call | tf_op jit(solution)/shard_map/pallas_call | solution.py:78
  106.6 1.0 fusion.21
  107.6 1.0 fusion.25
  109.6 2.5 %collective-permute-start.9 = (bf16[2,256,512]{2,1,0:T(8,128)(2,1)}, bf16[2,256,512]{2,1,0:T(8,128)(2,1)}, u32[]{:S(2)}, u32[]{:S(2)}) collective-permute-start(bf16[2,256,512]{2,1,0:T(8,128)(2,1)} %pad_maximum_fusion.2), channel_id=1, source_target_pairs={{1,0},{2,1},{3,2},{4,3},{5,4},{6,5},{7,6},{8,7},{9,8},{10,9},{11,1... | collective-permute-start | bytes 1572872 | tf_op jit(solution)/shard_map/ppermute | solution.py:100
  112.2 5.3 %collective-permute-start.8 = (bf16[2,256,512]{2,1,0:T(8,128)(2,1)}, bf16[2,256,512]{2,1,0:T(8,128)(2,1)S(1)}, u32[]{:S(2)}, u32[]{:S(2)}) collective-permute-start(bf16[2,256,512]{2,1,0:T(8,128)(2,1)} %collective-permute-done.7), channel_id=1, source_target_pairs={{0,1},{1,2},{2,3},{3,4},{4,5},{5,6},{6,7},{7,8},{8,9},{9,10},{10,1... | collective-permute-start | bytes 1572872 | tf_op jit(solution)/shard_map/ppermute | solution.py:100
  119.9 3.9 %collective-permute-done.8 = bf16[2,256,512]{2,1,0:T(8,128)(2,1)S(1)} collective-permute-done((bf16[2,256,512]{2,1,0:T(8,128)(2,1)}, bf16[2,256,512]{2,1,0:T(8,128)(2,1)S(1)}, u32[]{:S(2)}, u32[]{:S(2)}) %collective-permute-start.8) | collective-permute-done | bytes 524320 | tf_op jit(solution)/shard_map/ppermute | solution.py:100
  123.9 1.1 constant_dynamic-update-slice_fusion.8
  125.0 1.1 constant_dynamic-update-slice_fusion.7
  126.2 1.7 slice_bitcast_fusion
  127.9 6.3 %shard_map.152 = (bf16[256,256]{1,0:T(8,128)(2,1)}, bf16[1024,128]{1,0:T(8,128)(2,1)}, bf16[1024,128]{1,0:T(8,128)(2,1)}, f32[256,128]{1,0:T(8,128)}, f32[256,128]{1,0:T(8,128)}) custom-call(s32[2]{0:T(128)} %constant.39.clone.at_ref, bf16[256,2048]{1,0:T(8,128)(2,1)} %bitcast.103, bf16[256,2048]{1,0:T(8,128)(2,1)} %bitcast.111, ...), custom_call_target="tpu_custom_call" | custom-call | tf_op jit(solution)/shard_map/pallas_call | solution.py:78
  134.2 1.6 fusion.10
  135.8 2.0 add_convert_fusion.5
  137.8 2.3 collective-permute-start.10
  140.1 1.7 slice_bitcast_fusion.8
  142.4 6.3 %shard_map.153 = (bf16[256,256]{1,0:T(8,128)(2,1)}, bf16[1024,128]{1,0:T(8,128)(2,1)}, bf16[1024,128]{1,0:T(8,128)(2,1)}, f32[256,128]{1,0:T(8,128)}, f32[256,128]{1,0:T(8,128)}) custom-call(s32[2]{0:T(128)} %constant.40.clone.at_ref, bf16[256,2048]{1,0:T(8,128)(2,1)} %bitcast.104, bf16[256,2048]{1,0:T(8,128)(2,1)} %bitcast.112, ...), custom_call_target="tpu_custom_call" | custom-call | tf_op jit(solution)/shard_map/pallas_call | solution.py:78
  148.8 1.6 fusion.11
  150.4 1.6 fusion.15
  152.0 2.0 add_convert_fusion.4
  154.0 1.9 collective-permute-start.11
  155.9 1.7 slice_bitcast_fusion.6
  157.6 6.2 %shard_map.154 = (bf16[256,256]{1,0:T(8,128)(2,1)}, bf16[1024,128]{1,0:T(8,128)(2,1)}, bf16[1024,128]{1,0:T(8,128)(2,1)}, f32[256,128]{1,0:T(8,128)}, f32[256,128]{1,0:T(8,128)}) custom-call(s32[2]{0:T(128)} %constant.41.clone.at_ref, bf16[256,2048]{1,0:T(8,128)(2,1)} %bitcast.105, bf16[256,2048]{1,0:T(8,128)(2,1)} %bitcast.113, ...), custom_call_target="tpu_custom_call" | custom-call | tf_op jit(solution)/shard_map/pallas_call | solution.py:78
  163.8 1.6 fusion.12
  165.4 1.6 fusion.16
  167.6 1.2 add_convert_fusion.3
  168.8 1.7 slice_bitcast_fusion.4
  170.4 6.3 %shard_map.155 = (bf16[256,256]{1,0:T(8,128)(2,1)}, bf16[1024,128]{1,0:T(8,128)(2,1)}, bf16[1024,128]{1,0:T(8,128)(2,1)}, f32[256,128]{1,0:T(8,128)}, f32[256,128]{1,0:T(8,128)}) custom-call(s32[2]{0:T(128)} %constant.42.clone.at_ref, bf16[256,2048]{1,0:T(8,128)(2,1)} %bitcast.106, bf16[256,2048]{1,0:T(8,128)(2,1)} %bitcast.114, ...), custom_call_target="tpu_custom_call" | custom-call | tf_op jit(solution)/shard_map/pallas_call | solution.py:78
  176.8 1.0 fusion.13
  177.8 1.0 fusion.17
  179.0 1.9 collective-permute-start.13
  181.2 10.6 %collective-permute-done.13 = bf16[2,256,512]{2,1,0:T(8,128)(2,1)S(1)} collective-permute-done((bf16[2,256,512]{2,1,0:T(8,128)(2,1)S(1)}, bf16[2,256,512]{2,1,0:T(8,128)(2,1)S(1)}, u32[]{:S(2)}, u32[]{:S(2)}) %collective-permute-start.13) | collective-permute-done | bytes 524320 | tf_op jit(solution)/shard_map/ppermute | solution.py:100
  191.9 1.9 collective-permute-start.14
  194.1 10.4 %collective-permute-done.14 = bf16[2,256,512]{2,1,0:T(8,128)(2,1)S(1)} collective-permute-done((bf16[2,256,512]{2,1,0:T(8,128)(2,1)S(1)}, bf16[2,256,512]{2,1,0:T(8,128)(2,1)S(1)}, u32[]{:S(2)}, u32[]{:S(2)}) %collective-permute-start.14) | collective-permute-done | bytes 524320 | tf_op jit(solution)/shard_map/ppermute | solution.py:100
  204.6 1.9 collective-permute-start.15
  206.7 1.9 collective-permute-start.12
  208.7 8.5 %collective-permute-done.15 = bf16[2,256,512]{2,1,0:T(8,128)(2,1)S(1)} collective-permute-done((bf16[2,256,512]{2,1,0:T(8,128)(2,1)S(1)}, bf16[2,256,512]{2,1,0:T(8,128)(2,1)S(1)}, u32[]{:S(2)}, u32[]{:S(2)}) %collective-permute-start.15) | collective-permute-done | bytes 524320 | tf_op jit(solution)/shard_map/ppermute | solution.py:100
  217.5 2.1 collective-permute-start.16
  219.6 3.2 %collective-permute-done.12 = bf16[2,256,512]{2,1,0:T(8,128)(2,1)S(1)} collective-permute-done((bf16[2,256,512]{2,1,0:T(8,128)(2,1)S(1)}, bf16[2,256,512]{2,1,0:T(8,128)(2,1)S(1)}, u32[]{:S(2)}, u32[]{:S(2)}) %collective-permute-start.12) | collective-permute-done | bytes 524320 | tf_op jit(solution)/shard_map/ppermute | solution.py:100
  223.3 6.9 %collective-permute-done.16 = bf16[2,256,512]{2,1,0:T(8,128)(2,1)S(1)} collective-permute-done((bf16[2,256,512]{2,1,0:T(8,128)(2,1)S(1)}, bf16[2,256,512]{2,1,0:T(8,128)(2,1)S(1)}, u32[]{:S(2)}, u32[]{:S(2)}) %collective-permute-start.16) | collective-permute-done | bytes 524320 | tf_op jit(solution)/shard_map/ppermute | solution.py:100
  (206 shorter events, 15.3 us)
Async XLA Ops:
  1.9 32.3 %copy-start.70 = (s32[4]{0:T(128)S(1)}, s32[4]{0:T(128)}, u32[]{:S(2)}) copy-start(s32[4]{0:T(128)} %param.17) | copy-start | bytes 52
  2.0 9.4 %collective-permute-start.1 = (bf16[2,256,512]{2,1,0:T(8,128)(2,1)S(1)}, bf16[2,256,512]{2,1,0:T(8,128)(2,1)S(1)}, u32[]{:S(2)}, u32[]{:S(2)}) collective-permute-start(bf16[2,256,512]{2,1,0:T(8,128)(2,1)S(1)} %pad_maximum_fusion), channel_id=1, source_target_pairs={{0,1},{1,2},{2,3},{3,4},{4,5},{5,6},{6,7},{7,8},{8,9},{9,10},{10,1... | collective-permute-start | bytes 1572872 | tf_op jit(solution)/shard_map/ppermute | solution.py:100
  12.2 12.6 %collective-permute-start.2 = (bf16[2,256,512]{2,1,0:T(8,128)(2,1)S(1)}, bf16[2,256,512]{2,1,0:T(8,128)(2,1)}, u32[]{:S(2)}, u32[]{:S(2)}) collective-permute-start(bf16[2,256,512]{2,1,0:T(8,128)(2,1)S(1)} %collective-permute-done.1), channel_id=1, source_target_pairs={{0,1},{1,2},{2,3},{3,4},{4,5},{5,6},{6,7},{7,8},{8,9},{9,10},{10,1... | collective-permute-start | bytes 1572872 | tf_op jit(solution)/shard_map/ppermute | solution.py:100
  18.7 36.6 %collective-permute-start = (bf16[1,256,2048]{2,1,0:T(8,128)(2,1)}, bf16[1,256,2048]{2,1,0:T(8,128)(2,1)S(1)}, u32[]{:S(2)}, u32[]{:S(2)}) collective-permute-start(bf16[1,256,2048]{2,1,0:T(8,128)(2,1)} %param.16), channel_id=1, source_target_pairs={{0,224},{32,0},{64,32},{96,64},{128,96},{160,128},{192,160},{224,1... | collective-permute-start | bytes 3145736 | tf_op jit(solution)/shard_map/ppermute | solution.py:94
  24.8 13.0 %collective-permute-start.3 = (bf16[2,256,512]{2,1,0:T(8,128)(2,1)}, bf16[2,256,512]{2,1,0:T(8,128)(2,1)}, u32[]{:S(2)}, u32[]{:S(2)}) collective-permute-start(bf16[2,256,512]{2,1,0:T(8,128)(2,1)} %collective-permute-done.2), channel_id=1, source_target_pairs={{0,1},{1,2},{2,3},{3,4},{4,5},{5,6},{6,7},{7,8},{8,9},{9,10},{10,1... | collective-permute-start | bytes 1572872 | tf_op jit(solution)/shard_map/ppermute | solution.py:100
  32.3 31.2 %collective-permute-start.5 = (bf16[2,256,512]{2,1,0:T(8,128)(2,1)}, bf16[2,256,512]{2,1,0:T(8,128)(2,1)S(1)}, u32[]{:S(2)}, u32[]{:S(2)}) collective-permute-start(bf16[2,256,512]{2,1,0:T(8,128)(2,1)} %pad_maximum_fusion.1), channel_id=1, source_target_pairs={{0,1},{1,2},{2,3},{3,4},{4,5},{5,6},{6,7},{7,8},{8,9},{9,10},{10,1... | collective-permute-start | bytes 1572872 | tf_op jit(solution)/shard_map/ppermute | solution.py:100
  37.9 12.9 %collective-permute-start.4 = (bf16[2,256,512]{2,1,0:T(8,128)(2,1)}, bf16[2,256,512]{2,1,0:T(8,128)(2,1)S(1)}, u32[]{:S(2)}, u32[]{:S(2)}) collective-permute-start(bf16[2,256,512]{2,1,0:T(8,128)(2,1)} %collective-permute-done.3), channel_id=1, source_target_pairs={{0,1},{1,2},{2,3},{3,4},{4,5},{5,6},{6,7},{7,8},{8,9},{9,10},{10,1... | collective-permute-start | bytes 1572872 | tf_op jit(solution)/shard_map/ppermute | solution.py:100
  46.0 7.0 %copy-start.9 = (bf16[2,256,512]{2,1,0:T(8,128)(2,1)S(1)}, bf16[2,256,512]{2,1,0:T(8,128)(2,1)}, u32[]{:S(2)}) copy-start(bf16[2,256,512]{2,1,0:T(8,128)(2,1)} %copy-done.8) | copy-start | bytes 1572868
  63.5 10.0 %copy-start.11 = (bf16[1024,128]{1,0:T(8,128)(2,1)S(1)}, bf16[1024,128]{1,0:T(8,128)(2,1)}, u32[]{:S(2)}) copy-start(bf16[1024,128]{1,0:T(8,128)(2,1)} %get-tuple-element.71) | copy-start | bytes 786436
  67.1 17.2 %collective-permute-start.6 = (bf16[2,256,512]{2,1,0:T(8,128)(2,1)S(1)}, bf16[2,256,512]{2,1,0:T(8,128)(2,1)}, u32[]{:S(2)}, u32[]{:S(2)}) collective-permute-start(bf16[2,256,512]{2,1,0:T(8,128)(2,1)S(1)} %collective-permute-done.5), channel_id=1, source_target_pairs={{0,1},{1,2},{2,3},{3,4},{4,5},{5,6},{6,7},{7,8},{8,9},{9,10},{10,1... | collective-permute-start | bytes 1572872 | tf_op jit(solution)/shard_map/ppermute | solution.py:100
  74.7 11.7 %copy-start.2 = (bf16[2,1280,512]{2,1,0:T(8,128)(2,1)S(1)}, bf16[2,1280,512]{2,1,0:T(8,128)(2,1)}, u32[]{:S(2)}) copy-start(bf16[2,1280,512]{2,1,0:T(8,128)(2,1)} %copy-done.1) | copy-start | bytes 7864324
  84.3 13.8 %collective-permute-start.7 = (bf16[2,256,512]{2,1,0:T(8,128)(2,1)}, bf16[2,256,512]{2,1,0:T(8,128)(2,1)}, u32[]{:S(2)}, u32[]{:S(2)}) collective-permute-start(bf16[2,256,512]{2,1,0:T(8,128)(2,1)} %collective-permute-done.6), channel_id=1, source_target_pairs={{0,1},{1,2},{2,3},{3,4},{4,5},{5,6},{6,7},{7,8},{8,9},{9,10},{10,1... | collective-permute-start | bytes 1572872 | tf_op jit(solution)/shard_map/ppermute | solution.py:100
  100.3 8.3 %copy-start.36 = (bf16[256,128]{1,0:T(8,128)(2,1)S(1)}, bf16[256,128]{1,0:T(8,128)(2,1)}, u32[]{:S(2)}) copy-start(bf16[256,128]{1,0:T(8,128)(2,1)} %get-tuple-element.198) | copy-start | bytes 196612
  107.6 9.8 %copy-start.28 = (bf16[256,128]{1,0:T(8,128)(2,1)S(1)}, bf16[256,128]{1,0:T(8,128)(2,1)}, u32[]{:S(2)}) copy-start(bf16[256,128]{1,0:T(8,128)(2,1)} %get-tuple-element.195) | copy-start | bytes 196612
  108.6 8.9 %copy-start.29 = (bf16[256,128]{1,0:T(8,128)(2,1)S(1)}, bf16[256,128]{1,0:T(8,128)(2,1)}, u32[]{:S(2)}) copy-start(bf16[256,128]{1,0:T(8,128)(2,1)} %get-tuple-element.211) | copy-start | bytes 196612
  108.6 8.9 %copy-start.42 = (bf16[256,128]{1,0:T(8,128)(2,1)S(1)}, bf16[256,128]{1,0:T(8,128)(2,1)}, u32[]{:S(2)}) copy-start(bf16[256,128]{1,0:T(8,128)(2,1)} %get-tuple-element.215) | copy-start | bytes 196612
  108.7 8.9 %copy-start.23 = (bf16[256,128]{1,0:T(8,128)(2,1)S(1)}, bf16[256,128]{1,0:T(8,128)(2,1)}, u32[]{:S(2)}) copy-start(bf16[256,128]{1,0:T(8,128)(2,1)} %get-tuple-element.196) | copy-start | bytes 196612
  108.7 8.9 %copy-start.38 = (bf16[256,128]{1,0:T(8,128)(2,1)S(1)}, bf16[256,128]{1,0:T(8,128)(2,1)}, u32[]{:S(2)}) copy-start(bf16[256,128]{1,0:T(8,128)(2,1)} %get-tuple-element.200) | copy-start | bytes 196612
  108.8 8.9 %copy-start.16 = (bf16[256,128]{1,0:T(8,128)(2,1)S(1)}, bf16[256,128]{1,0:T(8,128)(2,1)}, u32[]{:S(2)}) copy-start(bf16[256,128]{1,0:T(8,128)(2,1)} %get-tuple-element.208) | copy-start | bytes 196612
  108.8 8.9 %copy-start.24 = (bf16[256,128]{1,0:T(8,128)(2,1)S(1)}, bf16[256,128]{1,0:T(8,128)(2,1)}, u32[]{:S(2)}) copy-start(bf16[256,128]{1,0:T(8,128)(2,1)} %get-tuple-element.212) | copy-start | bytes 196612
  108.8 8.9 %copy-start.39 = (bf16[256,128]{1,0:T(8,128)(2,1)S(1)}, bf16[256,128]{1,0:T(8,128)(2,1)}, u32[]{:S(2)}) copy-start(bf16[256,128]{1,0:T(8,128)(2,1)} %get-tuple-element.216) | copy-start | bytes 196612
  109.6 8.8 %copy-start.22 = (bf16[256,128]{1,0:T(8,128)(2,1)S(1)}, bf16[256,128]{1,0:T(8,128)(2,1)}, u32[]{:S(2)}) copy-start(bf16[256,128]{1,0:T(8,128)(2,1)} %get-tuple-element.197) | copy-start | bytes 196612
  109.6 8.8 %copy-start.34 = (bf16[256,128]{1,0:T(8,128)(2,1)S(1)}, bf16[256,128]{1,0:T(8,128)(2,1)}, u32[]{:S(2)}) copy-start(bf16[256,128]{1,0:T(8,128)(2,1)} %get-tuple-element.201) | copy-start | bytes 196612
  109.6 26.2 %collective-permute-start.9 = (bf16[2,256,512]{2,1,0:T(8,128)(2,1)}, bf16[2,256,512]{2,1,0:T(8,128)(2,1)}, u32[]{:S(2)}, u32[]{:S(2)}) collective-permute-start(bf16[2,256,512]{2,1,0:T(8,128)(2,1)} %pad_maximum_fusion.2), channel_id=1, source_target_pairs={{1,0},{2,1},{3,2},{4,3},{5,4},{6,5},{7,6},{8,7},{9,8},{10,9},{11,1... | collective-permute-start | bytes 1572872 | tf_op jit(solution)/shard_map/ppermute | solution.py:100
  112.2 11.7 %collective-permute-start.8 = (bf16[2,256,512]{2,1,0:T(8,128)(2,1)}, bf16[2,256,512]{2,1,0:T(8,128)(2,1)S(1)}, u32[]{:S(2)}, u32[]{:S(2)}) collective-permute-start(bf16[2,256,512]{2,1,0:T(8,128)(2,1)} %collective-permute-done.7), channel_id=1, source_target_pairs={{0,1},{1,2},{2,3},{3,4},{4,5},{5,6},{6,7},{7,8},{8,9},{9,10},{10,1... | collective-permute-start | bytes 1572872 | tf_op jit(solution)/shard_map/ppermute | solution.py:100
  127.9 8.0 %copy-start.4 = (bf16[1,256,512]{2,1,0:T(8,128)(2,1)S(1)}, bf16[1,256,512]{2,1,0:T(8,128)(2,1)}, u32[]{:S(2)}) copy-start(bf16[1,256,512]{2,1,0:T(8,128)(2,1)} %maximum_bitcast_fusion.4) | copy-start | bytes 786436
  127.9 8.0 %copy-start.5 = (bf16[1,256,512]{2,1,0:T(8,128)(2,1)S(1)}, bf16[1,256,512]{2,1,0:T(8,128)(2,1)}, u32[]{:S(2)}) copy-start(bf16[1,256,512]{2,1,0:T(8,128)(2,1)} %maximum_bitcast_fusion.5) | copy-start | bytes 786436
  137.8 14.2 %collective-permute-start.10 = (bf16[2,256,512]{2,1,0:T(8,128)(2,1)}, bf16[2,256,512]{2,1,0:T(8,128)(2,1)}, u32[]{:S(2)}, u32[]{:S(2)}) collective-permute-start(bf16[2,256,512]{2,1,0:T(8,128)(2,1)} %add_convert_fusion.5), channel_id=1, source_target_pairs={{1,0},{2,1},{3,2},{4,3},{5,4},{6,5},{7,6},{8,7},{9,8},{10,9},{11,1... | collective-permute-start | bytes 1572872 | tf_op jit(solution)/shard_map/ppermute | solution.py:100
  142.4 9.6 %copy-start.3 = (bf16[1,256,512]{2,1,0:T(8,128)(2,1)S(1)}, bf16[1,256,512]{2,1,0:T(8,128)(2,1)}, u32[]{:S(2)}) copy-start(bf16[1,256,512]{2,1,0:T(8,128)(2,1)} %maximum_bitcast_fusion.7) | copy-start | bytes 786436
  154.0 13.6 %collective-permute-start.11 = (bf16[2,256,512]{2,1,0:T(8,128)(2,1)}, bf16[2,256,512]{2,1,0:T(8,128)(2,1)}, u32[]{:S(2)}, u32[]{:S(2)}) collective-permute-start(bf16[2,256,512]{2,1,0:T(8,128)(2,1)} %add_convert_fusion.4), channel_id=1, source_target_pairs={{1,0},{2,1},{3,2},{4,3},{5,4},{6,5},{7,6},{8,7},{9,8},{10,9},{11,1... | collective-permute-start | bytes 1572872 | tf_op jit(solution)/shard_map/ppermute | solution.py:100
  170.4 8.4 %copy-start.19 = (bf16[256,128]{1,0:T(8,128)(2,1)S(1)}, bf16[256,128]{1,0:T(8,128)(2,1)}, u32[]{:S(2)}) copy-start(bf16[256,128]{1,0:T(8,128)(2,1)} %get-tuple-element.162) | copy-start | bytes 196612
  170.4 8.4 %copy-start.33 = (bf16[256,128]{1,0:T(8,128)(2,1)S(1)}, bf16[256,128]{1,0:T(8,128)(2,1)}, u32[]{:S(2)}) copy-start(bf16[256,128]{1,0:T(8,128)(2,1)} %get-tuple-element.166) | copy-start | bytes 196612
  170.4 8.4 %copy-start.43 = (bf16[256,128]{1,0:T(8,128)(2,1)S(1)}, bf16[256,128]{1,0:T(8,128)(2,1)}, u32[]{:S(2)}) copy-start(bf16[256,128]{1,0:T(8,128)(2,1)} %get-tuple-element.170) | copy-start | bytes 196612
  179.0 12.7 %collective-permute-start.13 = (bf16[2,256,512]{2,1,0:T(8,128)(2,1)S(1)}, bf16[2,256,512]{2,1,0:T(8,128)(2,1)S(1)}, u32[]{:S(2)}, u32[]{:S(2)}) collective-permute-start(bf16[2,256,512]{2,1,0:T(8,128)(2,1)S(1)} %pad_maximum_fusion.3), channel_id=1, source_target_pairs={{1,0},{2,1},{3,2},{4,3},{5,4},{6,5},{7,6},{8,7},{9,8},{10,9},{11,1... | collective-permute-start | bytes 1572872 | tf_op jit(solution)/shard_map/ppermute | solution.py:100
  181.0 12.8 %copy-start.61 = (bf16[256,256]{1,0:T(8,128)(2,1)S(1)}, bf16[256,256]{1,0:T(8,128)(2,1)}, u32[]{:S(2)}) copy-start(bf16[256,256]{1,0:T(8,128)(2,1)} %get-tuple-element.69) | copy-start | bytes 393220
  181.0 12.8 %copy-start.62 = (bf16[256,256]{1,0:T(8,128)(2,1)S(1)}, bf16[256,256]{1,0:T(8,128)(2,1)}, u32[]{:S(2)}) copy-start(bf16[256,256]{1,0:T(8,128)(2,1)} %get-tuple-element.77) | copy-start | bytes 393220
  181.1 12.8 %copy-start.12 = (bf16[256,128]{1,0:T(8,128)(2,1)S(1)}, bf16[256,128]{1,0:T(8,128)(2,1)}, u32[]{:S(2)}) copy-start(bf16[256,128]{1,0:T(8,128)(2,1)} %get-tuple-element.160) | copy-start | bytes 196612
  181.1 12.8 %copy-start.17 = (bf16[256,128]{1,0:T(8,128)(2,1)S(1)}, bf16[256,128]{1,0:T(8,128)(2,1)}, u32[]{:S(2)}) copy-start(bf16[256,128]{1,0:T(8,128)(2,1)} %get-tuple-element.164) | copy-start | bytes 196612
  181.1 12.8 %copy-start.30 = (bf16[256,128]{1,0:T(8,128)(2,1)S(1)}, bf16[256,128]{1,0:T(8,128)(2,1)}, u32[]{:S(2)}) copy-start(bf16[256,128]{1,0:T(8,128)(2,1)} %get-tuple-element.168) | copy-start | bytes 196612
  181.1 12.8 %copy-start.14 = (bf16[256,128]{1,0:T(8,128)(2,1)S(1)}, bf16[256,128]{1,0:T(8,128)(2,1)}, u32[]{:S(2)}) copy-start(bf16[256,128]{1,0:T(8,128)(2,1)} %get-tuple-element.176) | copy-start | bytes 196612
  181.2 12.8 %copy-start.18 = (bf16[256,128]{1,0:T(8,128)(2,1)S(1)}, bf16[256,128]{1,0:T(8,128)(2,1)}, u32[]{:S(2)}) copy-start(bf16[256,128]{1,0:T(8,128)(2,1)} %get-tuple-element.180) | copy-start | bytes 196612
  181.2 12.8 %copy-start.31 = (bf16[256,128]{1,0:T(8,128)(2,1)S(1)}, bf16[256,128]{1,0:T(8,128)(2,1)}, u32[]{:S(2)}) copy-start(bf16[256,128]{1,0:T(8,128)(2,1)} %get-tuple-element.184) | copy-start | bytes 196612
  191.9 12.6 %collective-permute-start.14 = (bf16[2,256,512]{2,1,0:T(8,128)(2,1)S(1)}, bf16[2,256,512]{2,1,0:T(8,128)(2,1)S(1)}, u32[]{:S(2)}, u32[]{:S(2)}) collective-permute-start(bf16[2,256,512]{2,1,0:T(8,128)(2,1)S(1)} %add_convert_fusion.2), channel_id=1, source_target_pairs={{1,0},{2,1},{3,2},{4,3},{5,4},{6,5},{7,6},{8,7},{9,8},{10,9},{11,1... | collective-permute-start | bytes 1572872 | tf_op jit(solution)/shard_map/ppermute | solution.py:100
  193.9 12.7 %copy-start.63 = (bf16[256,256]{1,0:T(8,128)(2,1)S(1)}, bf16[256,256]{1,0:T(8,128)(2,1)}, u32[]{:S(2)}) copy-start(bf16[256,256]{1,0:T(8,128)(2,1)} %get-tuple-element.86) | copy-start | bytes 393220
  194.0 12.6 %copy-start.64 = (bf16[256,256]{1,0:T(8,128)(2,1)S(1)}, bf16[256,256]{1,0:T(8,128)(2,1)}, u32[]{:S(2)}) copy-start(bf16[256,256]{1,0:T(8,128)(2,1)} %get-tuple-element.95) | copy-start | bytes 393220
  194.0 12.6 %copy-start.65 = (bf16[256,256]{1,0:T(8,128)(2,1)S(1)}, bf16[256,256]{1,0:T(8,128)(2,1)}, u32[]{:S(2)}) copy-start(bf16[256,256]{1,0:T(8,128)(2,1)} %get-tuple-element.102) | copy-start | bytes 393220
  194.1 14.5 %copy-start.13 = (bf16[256,128]{1,0:T(8,128)(2,1)S(1)}, bf16[256,128]{1,0:T(8,128)(2,1)}, u32[]{:S(2)}) copy-start(bf16[256,128]{1,0:T(8,128)(2,1)} %get-tuple-element.163) | copy-start | bytes 196612
  204.6 12.6 %collective-permute-start.15 = (bf16[2,256,512]{2,1,0:T(8,128)(2,1)S(1)}, bf16[2,256,512]{2,1,0:T(8,128)(2,1)S(1)}, u32[]{:S(2)}, u32[]{:S(2)}) collective-permute-start(bf16[2,256,512]{2,1,0:T(8,128)(2,1)S(1)} %add_convert_fusion.1), channel_id=1, source_target_pairs={{1,0},{2,1},{3,2},{4,3},{5,4},{6,5},{7,6},{8,7},{9,8},{10,9},{11,1... | collective-permute-start | bytes 1572872 | tf_op jit(solution)/shard_map/ppermute | solution.py:100
  206.7 16.2 %collective-permute-start.12 = (bf16[2,256,512]{2,1,0:T(8,128)(2,1)S(1)}, bf16[2,256,512]{2,1,0:T(8,128)(2,1)S(1)}, u32[]{:S(2)}, u32[]{:S(2)}) collective-permute-start(bf16[2,256,512]{2,1,0:T(8,128)(2,1)S(1)} %add_convert_fusion.3), channel_id=1, source_target_pairs={{1,0},{2,1},{3,2},{4,3},{5,4},{6,5},{7,6},{8,7},{9,8},{10,9},{11,1... | collective-permute-start | bytes 1572872 | tf_op jit(solution)/shard_map/ppermute | solution.py:100
  208.6 10.9 %copy-start.66 = (bf16[256,256]{1,0:T(8,128)(2,1)S(1)}, bf16[256,256]{1,0:T(8,128)(2,1)}, u32[]{:S(2)}) copy-start(bf16[256,256]{1,0:T(8,128)(2,1)} %get-tuple-element.110) | copy-start | bytes 393220
  208.7 10.9 %copy-start.67 = (bf16[256,256]{1,0:T(8,128)(2,1)S(1)}, bf16[256,256]{1,0:T(8,128)(2,1)}, u32[]{:S(2)}) copy-start(bf16[256,256]{1,0:T(8,128)(2,1)} %get-tuple-element.119) | copy-start | bytes 393220
  208.7 10.9 %copy-start.68 = (bf16[256,256]{1,0:T(8,128)(2,1)S(1)}, bf16[256,256]{1,0:T(8,128)(2,1)}, u32[]{:S(2)}) copy-start(bf16[256,256]{1,0:T(8,128)(2,1)} %get-tuple-element.128) | copy-start | bytes 393220
  217.4 5.6 %copy-start.45 = (f32[256,128]{1,0:T(8,128)S(1)}, f32[256,128]{1,0:T(8,128)}, u32[]{:S(2)}) copy-start(f32[256,128]{1,0:T(8,128)} %get-tuple-element.72) | copy-start | bytes 393220
  217.4 5.6 %copy-start.46 = (f32[256,128]{1,0:T(8,128)S(1)}, f32[256,128]{1,0:T(8,128)}, u32[]{:S(2)}) copy-start(f32[256,128]{1,0:T(8,128)} %get-tuple-element.73) | copy-start | bytes 393220
  217.4 5.6 %copy-start.47 = (f32[256,128]{1,0:T(8,128)S(1)}, f32[256,128]{1,0:T(8,128)}, u32[]{:S(2)}) copy-start(f32[256,128]{1,0:T(8,128)} %get-tuple-element.81) | copy-start | bytes 393220
  217.5 12.7 %collective-permute-start.16 = (bf16[2,256,512]{2,1,0:T(8,128)(2,1)S(1)}, bf16[2,256,512]{2,1,0:T(8,128)(2,1)S(1)}, u32[]{:S(2)}, u32[]{:S(2)}) collective-permute-start(bf16[2,256,512]{2,1,0:T(8,128)(2,1)S(1)} %add_convert_fusion), channel_id=1, source_target_pairs={{1,0},{2,1},{3,2},{4,3},{5,4},{6,5},{7,6},{8,7},{9,8},{10,9},{11,1... | collective-permute-start | bytes 1572872 | tf_op jit(solution)/shard_map/ppermute | solution.py:100
  223.3 7.1 %copy-start.53 = (f32[256,128]{1,0:T(8,128)S(1)}, f32[256,128]{1,0:T(8,128)}, u32[]{:S(2)}) copy-start(f32[256,128]{1,0:T(8,128)} %get-tuple-element.105) | copy-start | bytes 393220
  223.3 7.1 %copy-start.54 = (f32[256,128]{1,0:T(8,128)S(1)}, f32[256,128]{1,0:T(8,128)}, u32[]{:S(2)}) copy-start(f32[256,128]{1,0:T(8,128)} %get-tuple-element.106) | copy-start | bytes 393220
  223.3 7.1 %copy-start.55 = (f32[256,128]{1,0:T(8,128)S(1)}, f32[256,128]{1,0:T(8,128)}, u32[]{:S(2)}) copy-start(f32[256,128]{1,0:T(8,128)} %get-tuple-element.114) | copy-start | bytes 393220
  223.3 7.1 %copy-start.56 = (f32[256,128]{1,0:T(8,128)S(1)}, f32[256,128]{1,0:T(8,128)}, u32[]{:S(2)}) copy-start(f32[256,128]{1,0:T(8,128)} %get-tuple-element.115) | copy-start | bytes 393220
  223.3 7.1 %copy-start.57 = (f32[256,128]{1,0:T(8,128)S(1)}, f32[256,128]{1,0:T(8,128)}, u32[]{:S(2)}) copy-start(f32[256,128]{1,0:T(8,128)} %get-tuple-element.123) | copy-start | bytes 393220
  223.3 7.1 %copy-start.58 = (f32[256,128]{1,0:T(8,128)S(1)}, f32[256,128]{1,0:T(8,128)}, u32[]{:S(2)}) copy-start(f32[256,128]{1,0:T(8,128)} %get-tuple-element.124) | copy-start | bytes 393220
  223.3 7.1 %copy-start.59 = (f32[256,128]{1,0:T(8,128)S(1)}, f32[256,128]{1,0:T(8,128)}, u32[]{:S(2)}) copy-start(f32[256,128]{1,0:T(8,128)} %get-tuple-element.132) | copy-start | bytes 393220
  223.3 7.1 %copy-start.60 = (f32[256,128]{1,0:T(8,128)S(1)}, f32[256,128]{1,0:T(8,128)}, u32[]{:S(2)}) copy-start(f32[256,128]{1,0:T(8,128)} %get-tuple-element.133) | copy-start | bytes 393220
  (24 other events, 73.7 us)

commit v5 on v4

v5 whole, which is shorter than its diff:
```python
import jax
import jax.numpy as jnp
from jax import lax
from jax.experimental import pallas as pl
from jax.experimental.pallas import tpu as pltpu
from jax.sharding import PartitionSpec as P


WINDOW = 1024
KV_HEADS = 8
CHUNKS = 2
GROUP = 2


SCORE_SCALE = 168.0 ** (-0.5)


def product(a, b, dims):
    return lax.dot_general(a, b, dims, preferred_element_type=jnp.float32)


def attention_back_kernel(at_ref, q_ref, do_ref, *refs):
    blocks = len(refs) - 7
    piece_refs = refs[:blocks]
    mask_ref = refs[blocks]
    dq_ref, far_ref, own_ref = refs[-3:]
    head_size = piece_refs[0].shape[2]
    heads = q_ref.shape[1] // head_size
    rows = q_ref.shape[0]
    allowed = mask_ref[...] > 0
    keys = jnp.concatenate([ref[0] for ref in piece_refs], axis=0)
    values = jnp.concatenate([ref[1] for ref in piece_refs], axis=0)
    queries = jnp.concatenate([q_ref[:, h * head_size:(h + 1) * head_size] for h in range(heads)], axis=0)
    grads = jnp.concatenate([do_ref[:, h * head_size:(h + 1) * head_size] for h in range(heads)], axis=0)
    allowed = jnp.concatenate([allowed] * heads, axis=0)
    nt = (((1,), (1,)), ((), ()))
    tn = (((0,), (0,)), ((), ()))
    nn = (((1,), (0,)), ((), ()))
    scores = SCORE_SCALE * product(queries, keys, nt)
    scores = jnp.where(allowed, scores, -jnp.inf)
    highest = jnp.max(scores, axis=-1, keepdims=True)
    log_total = highest + jnp.log(jnp.sum(jnp.exp(scores - highest), axis=-1, keepdims=True))
    weights = jnp.exp(scores - log_total)
    weight_half = weights.astype(jnp.bfloat16)
    attended = product(weight_half, values, nn).astype(jnp.bfloat16)
    row_dot = jnp.sum(attended.astype(jnp.float32) * grads.astype(jnp.float32), axis=-1, keepdims=True)
    weight_grad = product(grads, values, nt)
    score_grad = (weights * (weight_grad - row_dot)).astype(jnp.bfloat16)
    query_back = SCORE_SCALE * product(score_grad, keys, nn)
    for h in range(heads):
        dq_ref[:, h * head_size:(h + 1) * head_size] = query_back[h * rows:(h + 1) * rows].astype(dq_ref.dtype)
    key_back = SCORE_SCALE * product(score_grad, queries, tn)
    value_back = product(weight_half, grads, tn)
    for block in range(blocks - 1):
        lines = slice(block * rows, (block + 1) * rows)
        far_ref[block, 0] = key_back[lines].astype(far_ref.dtype)
        far_ref[block, 1] = value_back[lines].astype(far_ref.dtype)
    own_ref[0] = key_back[(blocks - 1) * rows:]
    own_ref[1] = value_back[(blocks - 1) * rows:]


def attention_back(queries, grads, window_pieces, allowed, buffers, query_group, kv_group):
    rows, width = queries.shape
    head_size = width // (GROUP * KV_HEADS)
    group_width = GROUP * head_size
    span = rows * len(window_pieces)
    q_spec = pl.BlockSpec((rows, group_width), lambda g, at: (0, at[0]))
    piece_spec = pl.BlockSpec((2, rows, head_size), lambda g, at: (0, 0, at[1]))
    mask_spec = pl.BlockSpec((rows, span), lambda g, at: (0, 0))
    any_spec = pl.BlockSpec(memory_space=pl.ANY)
    far_spec = pl.BlockSpec((len(window_pieces) - 1, 2, rows, head_size), lambda g, at: (0, 0, 0, at[1]))
    own_spec = pl.BlockSpec((2, rows, head_size), lambda g, at: (0, 0, at[1]))
    inputs = [queries, grads, *window_pieces, allowed, *buffers]
    first_buffer = 1 + len(inputs) - len(buffers)
    grid_spec = pltpu.PrefetchScalarGridSpec(
        num_scalar_prefetch=1,
        grid=(1,),
        in_specs=[q_spec, q_spec] + [piece_spec] * len(window_pieces) + [mask_spec] + [any_spec] * 3,
        out_specs=[q_spec, far_spec, own_spec],
    )
    return pl.pallas_call(
        attention_back_kernel,
        grid_spec=grid_spec,
        out_shape=[jax.ShapeDtypeStruct(b.shape, b.dtype) for b in buffers],
        input_output_aliases={first_buffer + i: i for i in range(3)},
        compiler_params=pltpu.CompilerParams(vmem_limit_bytes=60 * 1024 * 1024),
    )(jnp.array([query_group, kv_group], jnp.int32), *inputs)


def passed_along(shard, axis, by):
    count = lax.axis_size(axis)
    return lax.ppermute(shard, axis, [(i, (i + by) % count) for i in range(count)])


def shifted(value, axis, steps):
    count = lax.axis_size(axis)
    initial, last = (max(0, -steps), min(count, count - steps))
    return lax.ppermute(value, axis, [(source, source + steps) for source in range(initial, last)])


def doc_number(positions, doc_lengths):
    ends = jnp.cumsum(doc_lengths)
    return jnp.sum((positions[:, None] >= ends[None, :]).astype(jnp.int32), axis=1)


def window_mask(query_pos, key_pos, doc_lengths):
    same_doc = (
        doc_number(query_pos, doc_lengths)[:, None] == doc_number(key_pos, doc_lengths)[None, :]
    )
    spacing = query_pos[:, None] - key_pos[None, :]
    return same_doc & (spacing >= 0) & (spacing < WINDOW) & (key_pos[None, :] >= 0)


def local_body(query_rows, key_rows, value_rows, finished_grad, doc_lengths):
    queries = query_rows[0]
    keys_here = key_rows[0]
    values_here = value_rows[0]
    count_rows = queries.shape[0]
    reach_blocks = WINDOW // count_rows
    pair_width = keys_here.shape[1]
    head_size = pair_width // KV_HEADS
    rank_here = lax.axis_index("ctx")
    first_pos = rank_here * count_rows
    arriving = passed_along(finished_grad, "section", -1)[0]
    query_pos = first_pos + jnp.arange(count_rows, dtype=jnp.int32)
    key_pos = first_pos - WINDOW + jnp.arange(WINDOW + count_rows, dtype=jnp.int32)
    allowed = window_mask(query_pos, key_pos, doc_lengths).astype(jnp.float32)
    chunk_groups = KV_HEADS // CHUNKS
    chunk_width = chunk_groups * head_size
    mask = allowed.astype(jnp.bfloat16)

    def own_pair_of(chunk):
        cols = slice(chunk * chunk_width, (chunk + 1) * chunk_width)
        return jnp.stack([keys_here[:, cols], values_here[:, cols]])

    def return_hop(partial, far, block):
        arrived = shifted(partial, "ctx", -1).astype(jnp.float32)
        return (arrived + far[block].astype(jnp.float32)).astype(jnp.bfloat16)

    def run_chunk(chunk, window_pieces, query_back, side_step, side_value):
        far = jnp.zeros((reach_blocks, 2, count_rows, chunk_width), jnp.bfloat16)
        own = jnp.zeros((2, count_rows, chunk_width), jnp.float32)
        for group in range(chunk_groups):
            side_value = side_step(group, side_value)
            query_back, far, own = attention_back(
                queries, arriving, window_pieces, mask, (query_back, far, own),
                chunk * chunk_groups + group, group,
            )
        return query_back, far, own, side_value

    query_back = jnp.zeros(queries.shape, jnp.bfloat16)

    relayed = own_pair_of(0)
    window_a = [relayed]
    for _ in range(reach_blocks):
        relayed = shifted(relayed, "ctx", 1)
        window_a.insert(0, relayed)

    window_b = []

    def forward_step(group, relayed_b):
        window_b.insert(0, relayed_b)
        return shifted(relayed_b, "ctx", 1)

    query_back, far_a, own_a, relayed_b = run_chunk(0, window_a, query_back, forward_step, own_pair_of(1))
    window_b.insert(0, relayed_b)

    def return_step(group, partial):
        if group + 1 < reach_blocks:
            return return_hop(partial, far_a, group + 1)
        return shifted(partial, "ctx", -1).astype(jnp.float32)

    query_back, far_b, own_b, arrived_a = run_chunk(1, window_b, query_back, return_step, far_a[0])

    partial_b = far_b[0]
    for block in range(1, reach_blocks):
        partial_b = return_hop(partial_b, far_b, block)
    arrived_b = shifted(partial_b, "ctx", -1).astype(jnp.float32)

    totals = [(own_a + arrived_a).astype(jnp.bfloat16), (own_b + arrived_b).astype(jnp.bfloat16)]
    return (
        query_back[None],
        jnp.concatenate([total[0] for total in totals], axis=1)[None],
        jnp.concatenate([total[1] for total in totals], axis=1)[None],
    )


def solution(mesh):
    return jax.shard_map(
        local_body,
        mesh=mesh,
        in_specs=(
            P("section", "ctx", None),
            P("section", "ctx", None),
            P("section", "ctx", None),
            P("section", "ctx", None),
            P(),
        ),
        out_specs=(P("section", "ctx", None), P("section", "ctx", None), P("section", "ctx", None)),
        check_vma=False,
    )
```

time: 234 us -> 173 us (0.74)
  local copies, waits for them, and re-layouts: 46.3 us -> 12.2 us
  waiting for transfers between devices: 58.8 us -> 44.3 us
  other arithmetic: 14.4 us -> 4.76 us
    slice x16 -> x0, local copies, waits for them, and re-layouts: 20.9 us -> none  [the longest x8 11.1 us: far_payload(): piece[1][rows]]
    ppermute x16, waiting for transfers between devices: 58.8 us -> 41.3 us  [shifted(): lax.ppermute(value, axis, [(source, source + steps) for source in range(i...]
    squeeze x8 -> x4, local copies, waits for them, and re-layouts: 15.3 us -> 2.37 us  [the longest x1 1.22 us: local_body(): partial_b = far_b[0]]
    unnamed x157 -> x22, local copies, waits for them, and re-layouts: 6.48 us -> 0.05 us
    convert_element_type x11 -> x9, other arithmetic: 7.71 us -> 2.56 us  [the longest x1 1.44 us: local_body(): mask = allowed.astype(jnp.bfloat16)]
    another operation x4 -> x8, local copies, waits for them, and re-layouts: 2.31 us -> 7.38 us
    another operation x19 -> x1, other arithmetic: 3.78 us -> 0.18 us  [the longest x18 3.6 us: far_payload(): jnp.stack([jnp.concatenate([piece[1][rows] for piece in pieces], axis=1),...]
    ppermute x1, waiting for transfers between devices: 0.01 us -> 2.94 us  [passed_along(): lax.ppermute(shard, axis, [(i, (i + by) % count) for i in range(count)])]
  transfers between devices with their start and end apart: 17 -> 17, of which waited for: 11 -> 11; matrix products, arithmetic and copies ran while one was open for 16% -> 8% of each run, Pallas kernels for 16% -> 29%
where the time goes in v5:
time: 173 us; the launch traced here: 172 us
  starting transfers between devices  59.2 us (34%)
  Pallas kernels  50.6 us (29%)
  waiting for transfers between devices  44.3 us (26%)
  local copies, waits for them, and re-layouts  12.2 us (7%)
  other arithmetic  4.76 us (3%)
    ppermute x16, starting transfers between devices, shifted(): lax.ppermute(value, axis, [(source, source + steps) for source in range(i...  53.6 us
    pallas_call x8, Pallas kernels, attention_back(): pl.pallas_call(attention_back_kernel, grid_spec=grid_spec, out_shape=[jax...  50.6 us
    ppermute x16, waiting for transfers between devices, shifted(): lax.ppermute(value, axis, [(source, source + steps) for source in range(i...  41.3 us
    another operation x8, local copies, waits for them, and re-layouts  7.38 us
    ppermute x1, starting transfers between devices, passed_along(): lax.ppermute(shard, axis, [(i, (i + by) % count) for i in range(count)])  5.65 us
  transfers between devices with their start and end apart: 17, of which 11 were waited for; matrix products, arithmetic and copies ran while one was open for 8% of the time, Pallas kernels for 29%

profile of v5, /device:TPU:25, one launch (start us, length us, event | category | flops | bytes accessed | tf_op | source)
XLA Modules:
  0.0 172.1 jit_solution(5169181806594767078)
XLA Ops:
  0.6 1.3 slice_bitcast_fusion.6
  1.9 0.1 pad_maximum_fusion.1.refs_4_
  2.0 3.3 %collective-permute-start.5 = (bf16[2,256,512]{2,1,0:T(8,128)(2,1)S(1)}, bf16[2,256,512]{2,1,0:T(8,128)(2,1)S(1)}, u32[]{:S(2)}, u32[]{:S(2)}) collective-permute-start(bf16[2,256,512]{2,1,0:T(8,128)(2,1)S(1)} %pad_maximum_fusion.1.refs_4_), channel_id=1, source_target_pairs={{0,1},{1,2},{2,3},{3,4},{4,5},{5,6},{6,7},{7,8},{8,9},{9,10},{10,1... | collective-permute-start | bytes 1572872 | tf_op jit(solution)/shard_map/ppermute | solution.py:98
  5.3 0.1 pad_maximum_fusion.refs_4_
  5.4 1.9 %collective-permute-start.1 = (bf16[2,256,512]{2,1,0:T(8,128)(2,1)S(1)}, bf16[2,256,512]{2,1,0:T(8,128)(2,1)S(1)}, u32[]{:S(2)}, u32[]{:S(2)}) collective-permute-start(bf16[2,256,512]{2,1,0:T(8,128)(2,1)S(1)} %pad_maximum_fusion.refs_4_), channel_id=1, source_target_pairs={{0,1},{1,2},{2,3},{3,4},{4,5},{5,6},{6,7},{7,8},{8,9},{9,10},{10,1... | collective-permute-start | bytes 1572872 | tf_op jit(solution)/shard_map/ppermute | solution.py:98
  7.3 4.1 %collective-permute-done.5.refs_3_ = bf16[2,256,512]{2,1,0:T(8,128)(2,1)S(1)} collective-permute-done((bf16[2,256,512]{2,1,0:T(8,128)(2,1)S(1)}, bf16[2,256,512]{2,1,0:T(8,128)(2,1)S(1)}, u32[]{:S(2)}, u32[]{:S(2)}) %collective-permute-start.5) | collective-permute-done | bytes 524320 | tf_op jit(solution)/shard_map/ppermute | solution.py:98
  11.4 6.5 %collective-permute-start.6 = (bf16[2,256,512]{2,1,0:T(8,128)(2,1)S(1)}, bf16[2,256,512]{2,1,0:T(8,128)(2,1)}, u32[]{:S(2)}, u32[]{:S(2)}) collective-permute-start(bf16[2,256,512]{2,1,0:T(8,128)(2,1)S(1)} %collective-permute-done.5.refs_3_), channel_id=1, source_target_pairs={{0,1},{1,2},{2,3},{3,4},{4,5},{5,6},{6,7},{7,8},{8,9},{9,10},{10,1... | collective-permute-start | bytes 1572872 | tf_op jit(solution)/shard_map/ppermute | solution.py:98
  18.0 5.6 %collective-permute-start.2 = (bf16[2,256,512]{2,1,0:T(8,128)(2,1)S(1)}, bf16[2,256,512]{2,1,0:T(8,128)(2,1)}, u32[]{:S(2)}, u32[]{:S(2)}) collective-permute-start(bf16[2,256,512]{2,1,0:T(8,128)(2,1)S(1)} %collective-permute-done.1.refs_3_), channel_id=1, source_target_pairs={{0,1},{1,2},{2,3},{3,4},{4,5},{5,6},{6,7},{7,8},{8,9},{9,10},{10,1... | collective-permute-start | bytes 1572872 | tf_op jit(solution)/shard_map/ppermute | solution.py:98
  23.6 0.5 collective-permute-done.6.refs_2_
  24.1 6.6 %collective-permute-start.7 = (bf16[2,256,512]{2,1,0:T(8,128)(2,1)}, bf16[2,256,512]{2,1,0:T(8,128)(2,1)}, u32[]{:S(2)}, u32[]{:S(2)}) collective-permute-start(bf16[2,256,512]{2,1,0:T(8,128)(2,1)} %collective-permute-done.6.refs_2_), channel_id=1, source_target_pairs={{0,1},{1,2},{2,3},{3,4},{4,5},{5,6},{6,7},{7,8},{8,9},{9,10},{10,1... | collective-permute-start | bytes 1572872 | tf_op jit(solution)/shard_map/ppermute | solution.py:98
  30.7 5.7 %collective-permute-start = (bf16[1,256,2048]{2,1,0:T(8,128)(2,1)}, bf16[1,256,2048]{2,1,0:T(8,128)(2,1)S(1)}, u32[]{:S(2)}, u32[]{:S(2)}) collective-permute-start(bf16[1,256,2048]{2,1,0:T(8,128)(2,1)} %param.16), channel_id=1, source_target_pairs={{0,224},{32,0},{64,32},{96,64},{128,96},{160,128},{192,160},{224,1... | collective-permute-start | bytes 3145736 | tf_op jit(solution)/shard_map/ppermute | solution.py:92
  36.3 0.2 reduce-window.8
  36.5 2.2 %collective-permute-start.3 = (bf16[2,256,512]{2,1,0:T(8,128)(2,1)}, bf16[2,256,512]{2,1,0:T(8,128)(2,1)S(1)}, u32[]{:S(2)}, u32[]{:S(2)}) collective-permute-start(bf16[2,256,512]{2,1,0:T(8,128)(2,1)} %collective-permute-done.2.refs_2_), channel_id=1, source_target_pairs={{0,1},{1,2},{2,3},{3,4},{4,5},{5,6},{6,7},{7,8},{8,9},{9,10},{10,1... | collective-permute-start | bytes 1572872 | tf_op jit(solution)/shard_map/ppermute | solution.py:98
  38.7 0.1 convert_reduce_fusion.1
  38.8 0.1 convert_reduce_fusion
  38.9 4.7 %collective-permute-start.8 = (bf16[2,256,512]{2,1,0:T(8,128)(2,1)}, bf16[2,256,512]{2,1,0:T(8,128)(2,1)}, u32[]{:S(2)}, u32[]{:S(2)}) collective-permute-start(bf16[2,256,512]{2,1,0:T(8,128)(2,1)} %collective-permute-done.7.refs_1_), channel_id=1, source_target_pairs={{0,1},{1,2},{2,3},{3,4},{4,5},{5,6},{6,7},{7,8},{8,9},{9,10},{10,1... | collective-permute-start | bytes 1572872 | tf_op jit(solution)/shard_map/ppermute | solution.py:98
  43.6 1.5 collective-permute-done.3.refs_1_
  45.1 6.4 %collective-permute-start.4 = (bf16[2,256,512]{2,1,0:T(8,128)(2,1)S(1)}, bf16[2,256,512]{2,1,0:T(8,128)(2,1)}, u32[]{:S(2)}, u32[]{:S(2)}) collective-permute-start(bf16[2,256,512]{2,1,0:T(8,128)(2,1)S(1)} %collective-permute-done.3.refs_1_), channel_id=1, source_target_pairs={{0,1},{1,2},{2,3},{3,4},{4,5},{5,6},{6,7},{7,8},{8,9},{9,10},{10,1... | collective-permute-start | bytes 1572872 | tf_op jit(solution)/shard_map/ppermute | solution.py:98
  51.5 1.4 convert_convert_fusion.refs_5_
  52.9 2.9 %collective-permute-done = bf16[1,256,2048]{2,1,0:T(8,128)(2,1)S(1)} collective-permute-done((bf16[1,256,2048]{2,1,0:T(8,128)(2,1)}, bf16[1,256,2048]{2,1,0:T(8,128)(2,1)S(1)}, u32[]{:S(2)}, u32[]{:S(2)}) %collective-permute-start) | collective-permute-done | bytes 1048608 | tf_op jit(solution)/shard_map/ppermute | solution.py:92
  55.9 1.6 broadcast_7_refs_7_.2.clone.refs_7_
  57.5 1.1 broadcast_6_refs_8_.2.clone.refs_8_
  58.6 1.1 broadcast_in_dim.8.refs_6_
  59.7 0.5 call_exported.0.at_ref
  60.3 6.3 %shard_map.148 = (bf16[256,2048]{1,0:T(8,128)(2,1)}, bf16[4,2,256,512]{3,2,1,0:T(8,128)(2,1)}, f32[2,256,512]{2,1,0:T(8,128)}) custom-call(s32[2]{0:T(128)} %call_exported.0.at_ref, bf16[256,2048]{1,0:T(8,128)(2,1)} %bitcast.50, bf16[256,2048]{1,0:T(8,128)(2,1)} %bitcast.58, ...), custom_call_target="tpu_custom_call", output_to_operand_aliasing={{0}: (9, {}), {1}: (10, {}), {2}: (11, {})} | custom-call | tf_op jit(solution)/shard_map/pallas_call | solution.py:81
  66.5 0.5 call_exported.1.at_ref
  67.0 6.3 %shard_map.149 = (bf16[256,2048]{1,0:T(8,128)(2,1)}, bf16[4,2,256,512]{3,2,1,0:T(8,128)(2,1)}, f32[2,256,512]{2,1,0:T(8,128)}) custom-call(s32[2]{0:T(128)} %call_exported.1.at_ref, bf16[256,2048]{1,0:T(8,128)(2,1)} %bitcast.51, bf16[256,2048]{1,0:T(8,128)(2,1)} %bitcast.59, ...), custom_call_target="tpu_custom_call", output_to_operand_aliasing={{0}: (9, {}), {1}: (10, {}), {2}: (11, {})} | custom-call | tf_op jit(solution)/shard_map/pallas_call | solution.py:81
  73.3 0.5 call_exported.2.at_ref
  73.8 6.3 %shard_map.150 = (bf16[256,2048]{1,0:T(8,128)(2,1)}, bf16[4,2,256,512]{3,2,1,0:T(8,128)(2,1)}, f32[2,256,512]{2,1,0:T(8,128)}) custom-call(s32[2]{0:T(128)} %call_exported.2.at_ref, bf16[256,2048]{1,0:T(8,128)(2,1)} %bitcast.52, bf16[256,2048]{1,0:T(8,128)(2,1)} %bitcast.60, ...), custom_call_target="tpu_custom_call", output_to_operand_aliasing={{0}: (9, {}), {1}: (10, {}), {2}: (11, {})} | custom-call | tf_op jit(solution)/shard_map/pallas_call | solution.py:81
  80.1 0.5 call_exported.3.at_ref
  80.6 6.5 %shard_map.151 = (bf16[256,2048]{1,0:T(8,128)(2,1)}, bf16[4,2,256,512]{3,2,1,0:T(8,128)(2,1)}, f32[2,256,512]{2,1,0:T(8,128)}) custom-call(s32[2]{0:T(128)} %call_exported.3.at_ref, bf16[256,2048]{1,0:T(8,128)(2,1)} %bitcast.53, bf16[256,2048]{1,0:T(8,128)(2,1)} %bitcast.61, ...), custom_call_target="tpu_custom_call", output_to_operand_aliasing={{0}: (9, {}), {1}: (10, {}), {2}: (11, {})} | custom-call | tf_op jit(solution)/shard_map/pallas_call | solution.py:81
  87.1 1.1 slice_bitcast_fusion.1
  88.2 1.9 %collective-permute-start.9 = (bf16[2,256,512]{2,1,0:T(8,128)(2,1)S(1)}, bf16[2,256,512]{2,1,0:T(8,128)(2,1)S(1)}, u32[]{:S(2)}, u32[]{:S(2)}) collective-permute-start(bf16[2,256,512]{2,1,0:T(8,128)(2,1)S(1)} %slice_bitcast_fusion.1), channel_id=1, source_target_pairs={{1,0},{2,1},{3,2},{4,3},{5,4},{6,5},{7,6},{8,7},{9,8},{10,9},{11,1... | collective-permute-start | bytes 1572872 | tf_op jit(solution)/shard_map/ppermute | solution.py:98
  90.1 1.5 broadcast_7_refs_7_.2.refs_7_
  91.6 1.1 broadcast_6_refs_8_.2.refs_8_
  92.7 6.2 %shard_map.152 = (bf16[256,2048]{1,0:T(8,128)(2,1)}, bf16[4,2,256,512]{3,2,1,0:T(8,128)(2,1)}, f32[2,256,512]{2,1,0:T(8,128)}) custom-call(s32[2]{0:T(128)} %constant.44.clone.at_ref, bf16[256,2048]{1,0:T(8,128)(2,1)} %bitcast.54, bf16[256,2048]{1,0:T(8,128)(2,1)} %bitcast.62, ...), custom_call_target="tpu_custom_call", output_to_operand_aliasing={{0}: (9, {}), {1}: (10, {}), {2}: (11, {})} | custom-call | tf_op jit(solution)/shard_map/pallas_call | solution.py:81
  98.9 6.2 %shard_map.153 = (bf16[256,2048]{1,0:T(8,128)(2,1)}, bf16[4,2,256,512]{3,2,1,0:T(8,128)(2,1)}, f32[2,256,512]{2,1,0:T(8,128)}) custom-call(s32[2]{0:T(128)} %constant.45.clone.at_ref, bf16[256,2048]{1,0:T(8,128)(2,1)} %bitcast.55, bf16[256,2048]{1,0:T(8,128)(2,1)} %bitcast.63, ...), custom_call_target="tpu_custom_call", output_to_operand_aliasing={{0}: (9, {}), {1}: (10, {}), {2}: (11, {})} | custom-call | tf_op jit(solution)/shard_map/pallas_call | solution.py:81
  105.2 6.2 %shard_map.154 = (bf16[256,2048]{1,0:T(8,128)(2,1)}, bf16[4,2,256,512]{3,2,1,0:T(8,128)(2,1)}, f32[2,256,512]{2,1,0:T(8,128)}) custom-call(s32[2]{0:T(128)} %constant.46.clone.at_ref, bf16[256,2048]{1,0:T(8,128)(2,1)} %bitcast.56, bf16[256,2048]{1,0:T(8,128)(2,1)} %bitcast.64, ...), custom_call_target="tpu_custom_call", output_to_operand_aliasing={{0}: (9, {}), {1}: (10, {}), {2}: (11, {})} | custom-call | tf_op jit(solution)/shard_map/pallas_call | solution.py:81
  111.4 6.6 %shard_map.155 = (bf16[256,2048]{1,0:T(8,128)(2,1)}, bf16[4,2,256,512]{3,2,1,0:T(8,128)(2,1)}, f32[2,256,512]{2,1,0:T(8,128)}) custom-call(s32[2]{0:T(128)} %constant.47.clone.at_ref, bf16[256,2048]{1,0:T(8,128)(2,1)} %bitcast.57, bf16[256,2048]{1,0:T(8,128)(2,1)} %bitcast.65, ...), custom_call_target="tpu_custom_call", output_to_operand_aliasing={{0}: (9, {}), {1}: (10, {}), {2}: (11, {})} | custom-call | tf_op jit(solution)/shard_map/pallas_call | solution.py:81
  118.0 1.2 slice_bitcast_fusion
  119.3 2.7 %collective-permute-start.13 = (bf16[2,256,512]{2,1,0:T(8,128)(2,1)S(1)}, bf16[2,256,512]{2,1,0:T(8,128)(2,1)S(1)}, u32[]{:S(2)}, u32[]{:S(2)}) collective-permute-start(bf16[2,256,512]{2,1,0:T(8,128)(2,1)S(1)} %slice_bitcast_fusion), channel_id=1, source_target_pairs={{1,0},{2,1},{3,2},{4,3},{5,4},{6,5},{7,6},{8,7},{9,8},{10,9},{11,1... | collective-permute-start | bytes 1572872 | tf_op jit(solution)/shard_map/ppermute | solution.py:98
  122.0 0.1 fusion.8
  122.2 1.9 %collective-permute-start.10 = (bf16[2,256,512]{2,1,0:T(8,128)(2,1)S(1)}, bf16[2,256,512]{2,1,0:T(8,128)(2,1)S(1)}, u32[]{:S(2)}, u32[]{:S(2)}) collective-permute-start(bf16[2,256,512]{2,1,0:T(8,128)(2,1)S(1)} %fusion.8), channel_id=1, source_target_pairs={{1,0},{2,1},{3,2},{4,3},{5,4},{6,5},{7,6},{8,7},{9,8},{10,9},{11,1... | collective-permute-start | bytes 1572872 | tf_op jit(solution)/shard_map/ppermute | solution.py:98
  124.1 7.8 %collective-permute-done.13 = bf16[2,256,512]{2,1,0:T(8,128)(2,1)S(1)} collective-permute-done((bf16[2,256,512]{2,1,0:T(8,128)(2,1)S(1)}, bf16[2,256,512]{2,1,0:T(8,128)(2,1)S(1)}, u32[]{:S(2)}, u32[]{:S(2)}) %collective-permute-start.13) | collective-permute-done | bytes 524320 | tf_op jit(solution)/shard_map/ppermute | solution.py:98
  131.9 0.1 fusion.5
  132.0 1.9 %collective-permute-start.14 = (bf16[2,256,512]{2,1,0:T(8,128)(2,1)S(1)}, bf16[2,256,512]{2,1,0:T(8,128)(2,1)S(1)}, u32[]{:S(2)}, u32[]{:S(2)}) collective-permute-start(bf16[2,256,512]{2,1,0:T(8,128)(2,1)S(1)} %fusion.5), channel_id=1, source_target_pairs={{1,0},{2,1},{3,2},{4,3},{5,4},{6,5},{7,6},{8,7},{9,8},{10,9},{11,1... | collective-permute-start | bytes 1572872 | tf_op jit(solution)/shard_map/ppermute | solution.py:98
  133.9 3.5 %collective-permute-done.10 = bf16[2,256,512]{2,1,0:T(8,128)(2,1)S(1)} collective-permute-done((bf16[2,256,512]{2,1,0:T(8,128)(2,1)S(1)}, bf16[2,256,512]{2,1,0:T(8,128)(2,1)S(1)}, u32[]{:S(2)}, u32[]{:S(2)}) %collective-permute-start.10) | collective-permute-done | bytes 524320 | tf_op jit(solution)/shard_map/ppermute | solution.py:98
  137.5 0.1 fusion.7
  137.6 2.1 %collective-permute-start.11 = (bf16[2,256,512]{2,1,0:T(8,128)(2,1)S(1)}, bf16[2,256,512]{2,1,0:T(8,128)(2,1)S(1)}, u32[]{:S(2)}, u32[]{:S(2)}) collective-permute-start(bf16[2,256,512]{2,1,0:T(8,128)(2,1)S(1)} %fusion.7), channel_id=1, source_target_pairs={{1,0},{2,1},{3,2},{4,3},{5,4},{6,5},{7,6},{8,7},{9,8},{10,9},{11,1... | collective-permute-start | bytes 1572872 | tf_op jit(solution)/shard_map/ppermute | solution.py:98
  139.7 4.9 %collective-permute-done.14 = bf16[2,256,512]{2,1,0:T(8,128)(2,1)S(1)} collective-permute-done((bf16[2,256,512]{2,1,0:T(8,128)(2,1)S(1)}, bf16[2,256,512]{2,1,0:T(8,128)(2,1)S(1)}, u32[]{:S(2)}, u32[]{:S(2)}) %collective-permute-start.14) | collective-permute-done | bytes 524320 | tf_op jit(solution)/shard_map/ppermute | solution.py:98
  144.6 0.1 fusion.4
  144.8 1.9 %collective-permute-start.15 = (bf16[2,256,512]{2,1,0:T(8,128)(2,1)S(1)}, bf16[2,256,512]{2,1,0:T(8,128)(2,1)S(1)}, u32[]{:S(2)}, u32[]{:S(2)}) collective-permute-start(bf16[2,256,512]{2,1,0:T(8,128)(2,1)S(1)} %fusion.4), channel_id=1, source_target_pairs={{1,0},{2,1},{3,2},{4,3},{5,4},{6,5},{7,6},{8,7},{9,8},{10,9},{11,1... | collective-permute-start | bytes 1572872 | tf_op jit(solution)/shard_map/ppermute | solution.py:98
  146.7 3.7 %collective-permute-done.11 = bf16[2,256,512]{2,1,0:T(8,128)(2,1)S(1)} collective-permute-done((bf16[2,256,512]{2,1,0:T(8,128)(2,1)S(1)}, bf16[2,256,512]{2,1,0:T(8,128)(2,1)S(1)}, u32[]{:S(2)}, u32[]{:S(2)}) %collective-permute-start.11) | collective-permute-done | bytes 524320 | tf_op jit(solution)/shard_map/ppermute | solution.py:98
  150.4 0.1 fusion.6
  150.5 2.1 %collective-permute-start.12 = (bf16[2,256,512]{2,1,0:T(8,128)(2,1)S(1)}, bf16[2,256,512]{2,1,0:T(8,128)(2,1)S(1)}, u32[]{:S(2)}, u32[]{:S(2)}) collective-permute-start(bf16[2,256,512]{2,1,0:T(8,128)(2,1)S(1)} %fusion.6), channel_id=1, source_target_pairs={{1,0},{2,1},{3,2},{4,3},{5,4},{6,5},{7,6},{8,7},{9,8},{10,9},{11,1... | collective-permute-start | bytes 1572872 | tf_op jit(solution)/shard_map/ppermute | solution.py:98
  152.6 4.8 %collective-permute-done.15 = bf16[2,256,512]{2,1,0:T(8,128)(2,1)S(1)} collective-permute-done((bf16[2,256,512]{2,1,0:T(8,128)(2,1)S(1)}, bf16[2,256,512]{2,1,0:T(8,128)(2,1)S(1)}, u32[]{:S(2)}, u32[]{:S(2)}) %collective-permute-start.15) | collective-permute-done | bytes 524320 | tf_op jit(solution)/shard_map/ppermute | solution.py:98
  157.4 0.1 fusion.3
  157.5 1.9 %collective-permute-start.16 = (bf16[2,256,512]{2,1,0:T(8,128)(2,1)S(1)}, bf16[2,256,512]{2,1,0:T(8,128)(2,1)S(1)}, u32[]{:S(2)}, u32[]{:S(2)}) collective-permute-start(bf16[2,256,512]{2,1,0:T(8,128)(2,1)S(1)} %fusion.3), channel_id=1, source_target_pairs={{1,0},{2,1},{3,2},{4,3},{5,4},{6,5},{7,6},{8,7},{9,8},{10,9},{11,1... | collective-permute-start | bytes 1572872 | tf_op jit(solution)/shard_map/ppermute | solution.py:98
  159.4 3.8 %collective-permute-done.12 = bf16[2,256,512]{2,1,0:T(8,128)(2,1)S(1)} collective-permute-done((bf16[2,256,512]{2,1,0:T(8,128)(2,1)S(1)}, bf16[2,256,512]{2,1,0:T(8,128)(2,1)S(1)}, u32[]{:S(2)}, u32[]{:S(2)}) %collective-permute-start.12) | collective-permute-done | bytes 524320 | tf_op jit(solution)/shard_map/ppermute | solution.py:98
  163.3 0.2 add_convert_fusion.1
  163.5 6.6 %collective-permute-done.16 = bf16[2,256,512]{2,1,0:T(8,128)(2,1)S(1)} collective-permute-done((bf16[2,256,512]{2,1,0:T(8,128)(2,1)S(1)}, bf16[2,256,512]{2,1,0:T(8,128)(2,1)S(1)}, u32[]{:S(2)}, u32[]{:S(2)}) %collective-permute-start.16) | collective-permute-done | bytes 524320 | tf_op jit(solution)/shard_map/ppermute | solution.py:98
  170.1 0.2 add_convert_fusion
  170.3 0.9 maximum_bitcast_fusion.1
  171.2 0.9 maximum_bitcast_fusion
  (33 shorter events, 0.2 us)
Async XLA Ops:
  0.6 35.7 %copy-start.10 = (s32[4]{0:T(128)S(1)}, s32[4]{0:T(128)}, u32[]{:S(2)}) copy-start(s32[4]{0:T(128)} %param.17) | copy-start | bytes 52
  2.0 56.7 %copy-start.6 = (bf16[2,256,512]{2,1,0:T(8,128)(2,1)}, bf16[2,256,512]{2,1,0:T(8,128)(2,1)S(1)}, u32[]{:S(2)}) copy-start(bf16[2,256,512]{2,1,0:T(8,128)(2,1)S(1)} %pad_maximum_fusion.1.refs_4_) | copy-start | bytes 1572868
  2.0 9.4 %collective-permute-start.5 = (bf16[2,256,512]{2,1,0:T(8,128)(2,1)S(1)}, bf16[2,256,512]{2,1,0:T(8,128)(2,1)S(1)}, u32[]{:S(2)}, u32[]{:S(2)}) collective-permute-start(bf16[2,256,512]{2,1,0:T(8,128)(2,1)S(1)} %pad_maximum_fusion.1.refs_4_), channel_id=1, source_target_pairs={{0,1},{1,2},{2,3},{3,4},{4,5},{5,6},{6,7},{7,8},{8,9},{9,10},{10,1... | collective-permute-start | bytes 1572872 | tf_op jit(solution)/shard_map/ppermute | solution.py:98
  5.4 54.3 %copy-start.5 = (bf16[2,256,512]{2,1,0:T(8,128)(2,1)}, bf16[2,256,512]{2,1,0:T(8,128)(2,1)S(1)}, u32[]{:S(2)}) copy-start(bf16[2,256,512]{2,1,0:T(8,128)(2,1)S(1)} %pad_maximum_fusion.refs_4_) | copy-start | bytes 1572868
  5.4 12.5 %collective-permute-start.1 = (bf16[2,256,512]{2,1,0:T(8,128)(2,1)S(1)}, bf16[2,256,512]{2,1,0:T(8,128)(2,1)S(1)}, u32[]{:S(2)}, u32[]{:S(2)}) collective-permute-start(bf16[2,256,512]{2,1,0:T(8,128)(2,1)S(1)} %pad_maximum_fusion.refs_4_), channel_id=1, source_target_pairs={{0,1},{1,2},{2,3},{3,4},{4,5},{5,6},{6,7},{7,8},{8,9},{9,10},{10,1... | collective-permute-start | bytes 1572872 | tf_op jit(solution)/shard_map/ppermute | solution.py:98
  11.4 12.6 %copy-start.9 = (bf16[2,256,512]{2,1,0:T(8,128)(2,1)}, bf16[2,256,512]{2,1,0:T(8,128)(2,1)S(1)}, u32[]{:S(2)}) copy-start(bf16[2,256,512]{2,1,0:T(8,128)(2,1)S(1)} %collective-permute-done.5.refs_3_) | copy-start | bytes 1572868
  11.4 12.6 %collective-permute-start.6 = (bf16[2,256,512]{2,1,0:T(8,128)(2,1)S(1)}, bf16[2,256,512]{2,1,0:T(8,128)(2,1)}, u32[]{:S(2)}, u32[]{:S(2)}) collective-permute-start(bf16[2,256,512]{2,1,0:T(8,128)(2,1)S(1)} %collective-permute-done.5.refs_3_), channel_id=1, source_target_pairs={{0,1},{1,2},{2,3},{3,4},{4,5},{5,6},{6,7},{7,8},{8,9},{9,10},{10,1... | collective-permute-start | bytes 1572872 | tf_op jit(solution)/shard_map/ppermute | solution.py:98
  18.0 41.8 %copy-start.7 = (bf16[2,256,512]{2,1,0:T(8,128)(2,1)}, bf16[2,256,512]{2,1,0:T(8,128)(2,1)S(1)}, u32[]{:S(2)}) copy-start(bf16[2,256,512]{2,1,0:T(8,128)(2,1)S(1)} %collective-permute-done.1.refs_3_) | copy-start | bytes 1572868
  18.0 18.5 %collective-permute-start.2 = (bf16[2,256,512]{2,1,0:T(8,128)(2,1)S(1)}, bf16[2,256,512]{2,1,0:T(8,128)(2,1)}, u32[]{:S(2)}, u32[]{:S(2)}) collective-permute-start(bf16[2,256,512]{2,1,0:T(8,128)(2,1)S(1)} %collective-permute-done.1.refs_3_), channel_id=1, source_target_pairs={{0,1},{1,2},{2,3},{3,4},{4,5},{5,6},{6,7},{7,8},{8,9},{9,10},{10,1... | collective-permute-start | bytes 1572872 | tf_op jit(solution)/shard_map/ppermute | solution.py:98
  24.1 14.8 %collective-permute-start.7 = (bf16[2,256,512]{2,1,0:T(8,128)(2,1)}, bf16[2,256,512]{2,1,0:T(8,128)(2,1)}, u32[]{:S(2)}, u32[]{:S(2)}) collective-permute-start(bf16[2,256,512]{2,1,0:T(8,128)(2,1)} %collective-permute-done.6.refs_2_), channel_id=1, source_target_pairs={{0,1},{1,2},{2,3},{3,4},{4,5},{5,6},{6,7},{7,8},{8,9},{9,10},{10,1... | collective-permute-start | bytes 1572872 | tf_op jit(solution)/shard_map/ppermute | solution.py:98
  30.7 25.2 %collective-permute-start = (bf16[1,256,2048]{2,1,0:T(8,128)(2,1)}, bf16[1,256,2048]{2,1,0:T(8,128)(2,1)S(1)}, u32[]{:S(2)}, u32[]{:S(2)}) collective-permute-start(bf16[1,256,2048]{2,1,0:T(8,128)(2,1)} %param.16), channel_id=1, source_target_pairs={{0,224},{32,0},{64,32},{96,64},{128,96},{160,128},{192,160},{224,1... | collective-permute-start | bytes 3145736 | tf_op jit(solution)/shard_map/ppermute | solution.py:92
  36.5 8.6 %collective-permute-start.3 = (bf16[2,256,512]{2,1,0:T(8,128)(2,1)}, bf16[2,256,512]{2,1,0:T(8,128)(2,1)S(1)}, u32[]{:S(2)}, u32[]{:S(2)}) collective-permute-start(bf16[2,256,512]{2,1,0:T(8,128)(2,1)} %collective-permute-done.2.refs_2_), channel_id=1, source_target_pairs={{0,1},{1,2},{2,3},{3,4},{4,5},{5,6},{6,7},{7,8},{8,9},{9,10},{10,1... | collective-permute-start | bytes 1572872 | tf_op jit(solution)/shard_map/ppermute | solution.py:98
  38.9 17.0 %collective-permute-start.8 = (bf16[2,256,512]{2,1,0:T(8,128)(2,1)}, bf16[2,256,512]{2,1,0:T(8,128)(2,1)}, u32[]{:S(2)}, u32[]{:S(2)}) collective-permute-start(bf16[2,256,512]{2,1,0:T(8,128)(2,1)} %collective-permute-done.7.refs_1_), channel_id=1, source_target_pairs={{0,1},{1,2},{2,3},{3,4},{4,5},{5,6},{6,7},{7,8},{8,9},{9,10},{10,1... | collective-permute-start | bytes 1572872 | tf_op jit(solution)/shard_map/ppermute | solution.py:98
  45.1 14.6 %copy-start.8 = (bf16[2,256,512]{2,1,0:T(8,128)(2,1)}, bf16[2,256,512]{2,1,0:T(8,128)(2,1)S(1)}, u32[]{:S(2)}) copy-start(bf16[2,256,512]{2,1,0:T(8,128)(2,1)S(1)} %collective-permute-done.3.refs_1_) | copy-start | bytes 1572868
  45.1 45.0 %collective-permute-start.4 = (bf16[2,256,512]{2,1,0:T(8,128)(2,1)S(1)}, bf16[2,256,512]{2,1,0:T(8,128)(2,1)}, u32[]{:S(2)}, u32[]{:S(2)}) collective-permute-start(bf16[2,256,512]{2,1,0:T(8,128)(2,1)S(1)} %collective-permute-done.3.refs_1_), channel_id=1, source_target_pairs={{0,1},{1,2},{2,3},{3,4},{4,5},{5,6},{6,7},{7,8},{8,9},{9,10},{10,1... | collective-permute-start | bytes 1572872 | tf_op jit(solution)/shard_map/ppermute | solution.py:98
  55.9 3.9 %copy-start.2 = (bf16[1,256,2048]{2,1,0:T(8,128)(2,1)}, bf16[1,256,2048]{2,1,0:T(8,128)(2,1)S(1)}, u32[]{:S(2)}) copy-start(bf16[1,256,2048]{2,1,0:T(8,128)(2,1)S(1)} %collective-permute-done) | copy-start | bytes 3145732
  88.2 33.8 %collective-permute-start.9 = (bf16[2,256,512]{2,1,0:T(8,128)(2,1)S(1)}, bf16[2,256,512]{2,1,0:T(8,128)(2,1)S(1)}, u32[]{:S(2)}, u32[]{:S(2)}) collective-permute-start(bf16[2,256,512]{2,1,0:T(8,128)(2,1)S(1)} %slice_bitcast_fusion.1), channel_id=1, source_target_pairs={{1,0},{2,1},{3,2},{4,3},{5,4},{6,5},{7,6},{8,7},{9,8},{10,9},{11,1... | collective-permute-start | bytes 1572872 | tf_op jit(solution)/shard_map/ppermute | solution.py:98
  111.4 10.6 %copy-start.1 = (bf16[4,2,256,512]{3,2,1,0:T(8,128)(2,1)S(1)}, bf16[4,2,256,512]{3,2,1,0:T(8,128)(2,1)}, u32[]{:S(2)}) copy-start(bf16[4,2,256,512]{3,2,1,0:T(8,128)(2,1)} %get-tuple-element.48) | copy-start | bytes 6291460
  118.0 13.8 %copy-start = (bf16[4,2,256,512]{3,2,1,0:T(8,128)(2,1)S(1)}, bf16[4,2,256,512]{3,2,1,0:T(8,128)(2,1)}, u32[]{:S(2)}) copy-start(bf16[4,2,256,512]{3,2,1,0:T(8,128)(2,1)} %get-tuple-element.50) | copy-start | bytes 6291460
  119.3 12.6 %collective-permute-start.13 = (bf16[2,256,512]{2,1,0:T(8,128)(2,1)S(1)}, bf16[2,256,512]{2,1,0:T(8,128)(2,1)S(1)}, u32[]{:S(2)}, u32[]{:S(2)}) collective-permute-start(bf16[2,256,512]{2,1,0:T(8,128)(2,1)S(1)} %slice_bitcast_fusion), channel_id=1, source_target_pairs={{1,0},{2,1},{3,2},{4,3},{5,4},{6,5},{7,6},{8,7},{9,8},{10,9},{11,1... | collective-permute-start | bytes 1572872 | tf_op jit(solution)/shard_map/ppermute | solution.py:98
  122.2 15.3 %collective-permute-start.10 = (bf16[2,256,512]{2,1,0:T(8,128)(2,1)S(1)}, bf16[2,256,512]{2,1,0:T(8,128)(2,1)S(1)}, u32[]{:S(2)}, u32[]{:S(2)}) collective-permute-start(bf16[2,256,512]{2,1,0:T(8,128)(2,1)S(1)} %fusion.8), channel_id=1, source_target_pairs={{1,0},{2,1},{3,2},{4,3},{5,4},{6,5},{7,6},{8,7},{9,8},{10,9},{11,1... | collective-permute-start | bytes 1572872 | tf_op jit(solution)/shard_map/ppermute | solution.py:98
  132.0 12.6 %collective-permute-start.14 = (bf16[2,256,512]{2,1,0:T(8,128)(2,1)S(1)}, bf16[2,256,512]{2,1,0:T(8,128)(2,1)S(1)}, u32[]{:S(2)}, u32[]{:S(2)}) collective-permute-start(bf16[2,256,512]{2,1,0:T(8,128)(2,1)S(1)} %fusion.5), channel_id=1, source_target_pairs={{1,0},{2,1},{3,2},{4,3},{5,4},{6,5},{7,6},{8,7},{9,8},{10,9},{11,1... | collective-permute-start | bytes 1572872 | tf_op jit(solution)/shard_map/ppermute | solution.py:98
  137.6 25.6 %copy-start.3 = (f32[2,256,512]{2,1,0:T(8,128)S(1)}, f32[2,256,512]{2,1,0:T(8,128)}, u32[]{:S(2)}) copy-start(f32[2,256,512]{2,1,0:T(8,128)} %get-tuple-element.47) | copy-start | bytes 3145732
  137.6 12.7 %collective-permute-start.11 = (bf16[2,256,512]{2,1,0:T(8,128)(2,1)S(1)}, bf16[2,256,512]{2,1,0:T(8,128)(2,1)S(1)}, u32[]{:S(2)}, u32[]{:S(2)}) collective-permute-start(bf16[2,256,512]{2,1,0:T(8,128)(2,1)S(1)} %fusion.7), channel_id=1, source_target_pairs={{1,0},{2,1},{3,2},{4,3},{5,4},{6,5},{7,6},{8,7},{9,8},{10,9},{11,1... | collective-permute-start | bytes 1572872 | tf_op jit(solution)/shard_map/ppermute | solution.py:98
  144.8 12.6 %collective-permute-start.15 = (bf16[2,256,512]{2,1,0:T(8,128)(2,1)S(1)}, bf16[2,256,512]{2,1,0:T(8,128)(2,1)S(1)}, u32[]{:S(2)}, u32[]{:S(2)}) collective-permute-start(bf16[2,256,512]{2,1,0:T(8,128)(2,1)S(1)} %fusion.4), channel_id=1, source_target_pairs={{1,0},{2,1},{3,2},{4,3},{5,4},{6,5},{7,6},{8,7},{9,8},{10,9},{11,1... | collective-permute-start | bytes 1572872 | tf_op jit(solution)/shard_map/ppermute | solution.py:98
  150.5 19.6 %copy-start.4 = (f32[2,256,512]{2,1,0:T(8,128)S(1)}, f32[2,256,512]{2,1,0:T(8,128)}, u32[]{:S(2)}) copy-start(f32[2,256,512]{2,1,0:T(8,128)} %get-tuple-element.49) | copy-start | bytes 3145732
  150.5 12.7 %collective-permute-start.12 = (bf16[2,256,512]{2,1,0:T(8,128)(2,1)S(1)}, bf16[2,256,512]{2,1,0:T(8,128)(2,1)S(1)}, u32[]{:S(2)}, u32[]{:S(2)}) collective-permute-start(bf16[2,256,512]{2,1,0:T(8,128)(2,1)S(1)} %fusion.6), channel_id=1, source_target_pairs={{1,0},{2,1},{3,2},{4,3},{5,4},{6,5},{7,6},{8,7},{9,8},{10,9},{11,1... | collective-permute-start | bytes 1572872 | tf_op jit(solution)/shard_map/ppermute | solution.py:98
  157.5 12.6 %collective-permute-start.16 = (bf16[2,256,512]{2,1,0:T(8,128)(2,1)S(1)}, bf16[2,256,512]{2,1,0:T(8,128)(2,1)S(1)}, u32[]{:S(2)}, u32[]{:S(2)}) collective-permute-start(bf16[2,256,512]{2,1,0:T(8,128)(2,1)S(1)} %fusion.3), channel_id=1, source_target_pairs={{1,0},{2,1},{3,2},{4,3},{5,4},{6,5},{7,6},{8,7},{9,8},{10,9},{11,1... | collective-permute-start | bytes 1572872 | tf_op jit(solution)/shard_map/ppermute | solution.py:98

commit v6 on v5

--- a/solution.py
+++ b/solution.py
@@ -8,7 +8,7 @@
 
 WINDOW = 1024
 KV_HEADS = 8
-CHUNKS = 2
+CHUNKS = 4
 GROUP = 2
 
 
@@ -133,53 +133,64 @@
         cols = slice(chunk * chunk_width, (chunk + 1) * chunk_width)
         return jnp.stack([keys_here[:, cols], values_here[:, cols]])
 
-    def return_hop(partial, far, block):
+    def relay_step(step, state):
+        window, relayed = state
+        relayed = shifted(relayed, "ctx", 1)
+        return [relayed] + window, relayed
+
+    def return_step(step, state):
+        far, partial = state
         arrived = shifted(partial, "ctx", -1).astype(jnp.float32)
-        return (arrived + far[block].astype(jnp.float32)).astype(jnp.bfloat16)
-
-    def run_chunk(chunk, window_pieces, query_back, side_step, side_value):
-        far = jnp.zeros((reach_blocks, 2, count_rows, chunk_width), jnp.bfloat16)
-        own = jnp.zeros((2, count_rows, chunk_width), jnp.float32)
-        for group in range(chunk_groups):
-            side_value = side_step(group, side_value)
-            query_back, far, own = attention_back(
-                queries, arriving, window_pieces, mask, (query_back, far, own),
-                chunk * chunk_groups + group, group,
-            )
-        return query_back, far, own, side_value
-
-    query_back = jnp.zeros(queries.shape, jnp.bfloat16)
-
-    relayed = own_pair_of(0)
-    window_a = [relayed]
-    for _ in range(reach_blocks):
-        relayed = shifted(relayed, "ctx", 1)
-        window_a.insert(0, relayed)
-
-    window_b = []
-
-    def forward_step(group, relayed_b):
-        window_b.insert(0, relayed_b)
-        return shifted(relayed_b, "ctx", 1)
-
-    query_back, far_a, own_a, relayed_b = run_chunk(0, window_a, query_back, forward_step, own_pair_of(1))
-    window_b.insert(0, relayed_b)
-
-    def return_step(group, partial):
-        if group + 1 < reach_blocks:
-            return return_hop(partial, far_a, group + 1)
-        return shifted(partial, "ctx", -1).astype(jnp.float32)
-
-    query_back, far_b, own_b, arrived_a = run_chunk(1, window_b, query_back, return_step, far_a[0])
-
-    partial_b = far_b[0]
-    for block in range(1, reach_blocks):
-        partial_b = return_hop(partial_b, far_b, block)
-    arrived_b = shifted(partial_b, "ctx", -1).astype(jnp.float32)
-
-    totals = [(own_a + arrived_a).astype(jnp.bfloat16), (own_b + arrived_b).astype(jnp.bfloat16)]
+        if step + 1 < reach_blocks:
+            return far, (arrived + far[step + 1].astype(jnp.float32)).astype(jnp.bfloat16)
+        return far, arrived
+
+    buffers = {}
+    query_back = [jnp.zeros(queries.shape, jnp.bfloat16)]
+
+    def run_pieces(chunks, windows, chains):
+        index = 0
+        for chunk in chunks:
+            far = jnp.zeros((reach_blocks, 2, count_rows, chunk_width), jnp.bfloat16)
+            own = jnp.zeros((2, count_rows, chunk_width), jnp.float32)
+            for group in range(chunk_groups):
+                for name in chains:
+                    step_fn, state = chains[name]
+                    chains[name] = (step_fn, step_fn(index, state))
+                query_back[0], far, own = attention_back(
+                    queries, arriving, windows[chunk], mask, (query_back[0], far, own),
+                    chunk * chunk_groups + group, group,
+                )
+                index += 1
+            buffers[chunk] = (far, own)
+        return {name: chains[name][1] for name in chains}
+
+    half = CHUNKS // 2
+    states = {chunk: ([own_pair_of(chunk)], own_pair_of(chunk)) for chunk in range(half)}
+    for step in range(reach_blocks):
+        for chunk in range(half):
+            states[chunk] = relay_step(step, states[chunk])
+    windows = {chunk: states[chunk][0] for chunk in range(half)}
+
+    chains = {f"c{chunk}": (relay_step, ([own_pair_of(chunk)], own_pair_of(chunk))) for chunk in range(half, CHUNKS)}
+    done = run_pieces(range(half), windows, chains)
+    for chunk in range(half, CHUNKS):
+        windows[chunk] = done[f"c{chunk}"][0]
+
+    chains = {f"c{chunk}": (return_step, (buffers[chunk][0], buffers[chunk][0][0])) for chunk in range(half)}
+    done = run_pieces(range(half, CHUNKS), windows, chains)
+    arrived = {chunk: done[f"c{chunk}"][1] for chunk in range(half)}
+
+    states = {chunk: (buffers[chunk][0], buffers[chunk][0][0]) for chunk in range(half, CHUNKS)}
+    for step in range(reach_blocks):
+        for chunk in range(half, CHUNKS):
+            states[chunk] = return_step(step, states[chunk])
+    for chunk in range(half, CHUNKS):
+        arrived[chunk] = states[chunk][1]
+
+    totals = [(buffers[chunk][1] + arrived[chunk]).astype(jnp.bfloat16) for chunk in range(CHUNKS)]
     return (
-        query_back[None],
+        query_back[0][None],
         jnp.concatenate([total[0] for total in totals], axis=1)[None],
         jnp.concatenate([total[1] for total in totals], axis=1)[None],
     )

time: 173 us -> 172 us (level)
  waiting for transfers between devices: 44.3 us -> 15.9 us
  starting transfers between devices: 59.2 us -> 82.9 us
  local copies, waits for them, and re-layouts: 12.2 us -> 16 us
    ppermute x16 -> x32, waiting for transfers between devices: 41.3 us -> 15.9 us  [shifted(): lax.ppermute(value, axis, [(source, source + steps) for source in range(i...]
    ppermute x16 -> x32, starting transfers between devices: 53.6 us -> 77.3 us  [shifted(): lax.ppermute(value, axis, [(source, source + steps) for source in range(i...]
    ppermute x1, waiting for transfers between devices: 2.94 us -> 0.01 us  [passed_along(): lax.ppermute(shard, axis, [(i, (i + by) % count) for i in range(count)])]
    squeeze x2 -> x4, local copies, waits for them, and re-layouts: 2.3 us -> 3.96 us  [local_body(): buffers[chunk][0][0]]
    another operation x8 -> x10, local copies, waits for them, and re-layouts: 7.38 us -> 8.7 us
  transfers between devices with their start and end apart: 17 -> 33, of which waited for: 11 -> 13; matrix products, arithmetic and copies ran while one was open for 8% -> 10% of each run, Pallas kernels for 29% -> 29%
where the time goes in v6:
time: 172 us; the launch traced here: 171 us
  starting transfers between devices  82.9 us (48%)
  Pallas kernels  49.8 us (29%)
  local copies, waits for them, and re-layouts  16 us (9%)
  waiting for transfers between devices  15.9 us (9%)
  other arithmetic  4.61 us (3%)
    ppermute x32, starting transfers between devices, shifted(): lax.ppermute(value, axis, [(source, source + steps) for source in range(i...  77.3 us
    pallas_call x8, Pallas kernels, attention_back(): pl.pallas_call(attention_back_kernel, grid_spec=grid_spec, out_shape=[jax...  49.8 us
    ppermute x32, waiting for transfers between devices, shifted(): lax.ppermute(value, axis, [(source, source + steps) for source in range(i...  15.9 us
    another operation x10, local copies, waits for them, and re-layouts  8.7 us
    ppermute x1, starting transfers between devices, passed_along(): lax.ppermute(shard, axis, [(i, (i + by) % count) for i in range(count)])  5.65 us
    squeeze x4, local copies, waits for them, and re-layouts, local_body(): buffers[chunk][0][0]  3.96 us
  transfers between devices with their start and end apart: 33, of which 13 were waited for; matrix products, arithmetic and copies ran while one was open for 10% of the time, Pallas kernels for 29%

profile of v6, /device:TPU:25, one launch (start us, length us, event | category | flops | bytes accessed | tf_op | source)
XLA Modules:
  0.0 170.6 jit_solution(14458422925217939789)
XLA Ops:
  0.6 1.4 slice_bitcast_fusion.12
  2.1 3.3 %collective-permute-start.13 = (bf16[2,256,256]{2,1,0:T(8,128)(2,1)S(1)}, bf16[2,256,256]{2,1,0:T(8,128)(2,1)}, u32[]{:S(2)}, u32[]{:S(2)}) collective-permute-start(bf16[2,256,256]{2,1,0:T(8,128)(2,1)S(1)} %pad_maximum_fusion.3.refs_4_), channel_id=1, source_target_pairs={{0,1},{1,2},{2,3},{3,4},{4,5},{5,6},{6,7},{7,8},{8,9},{9,10},{10,1... | collective-permute-start | bytes 786440 | tf_op jit(solution)/shard_map/ppermute | solution.py:98
  5.5 1.9 %collective-permute-start.9 = (bf16[2,256,256]{2,1,0:T(8,128)(2,1)S(1)}, bf16[2,256,256]{2,1,0:T(8,128)(2,1)S(1)}, u32[]{:S(2)}, u32[]{:S(2)}) collective-permute-start(bf16[2,256,256]{2,1,0:T(8,128)(2,1)S(1)} %pad_maximum_fusion.2.refs_4_), channel_id=1, source_target_pairs={{0,1},{1,2},{2,3},{3,4},{4,5},{5,6},{6,7},{7,8},{8,9},{9,10},{10,1... | collective-permute-start | bytes 786440 | tf_op jit(solution)/shard_map/ppermute | solution.py:98
  7.4 3.6 %collective-permute-start.5 = (bf16[2,256,256]{2,1,0:T(8,128)(2,1)S(1)}, bf16[2,256,256]{2,1,0:T(8,128)(2,1)S(1)}, u32[]{:S(2)}, u32[]{:S(2)}) collective-permute-start(bf16[2,256,256]{2,1,0:T(8,128)(2,1)S(1)} %pad_maximum_fusion.1.refs_4_), channel_id=1, source_target_pairs={{0,1},{1,2},{2,3},{3,4},{4,5},{5,6},{6,7},{7,8},{8,9},{9,10},{10,1... | collective-permute-start | bytes 786440 | tf_op jit(solution)/shard_map/ppermute | solution.py:98
  11.1 1.9 %collective-permute-start.1 = (bf16[2,256,256]{2,1,0:T(8,128)(2,1)S(1)}, bf16[2,256,256]{2,1,0:T(8,128)(2,1)S(1)}, u32[]{:S(2)}, u32[]{:S(2)}) collective-permute-start(bf16[2,256,256]{2,1,0:T(8,128)(2,1)S(1)} %pad_maximum_fusion.refs_4_), channel_id=1, source_target_pairs={{0,1},{1,2},{2,3},{3,4},{4,5},{5,6},{6,7},{7,8},{8,9},{9,10},{10,1... | collective-permute-start | bytes 786440 | tf_op jit(solution)/shard_map/ppermute | solution.py:98
  13.0 3.6 %collective-permute-start.14 = (bf16[2,256,256]{2,1,0:T(8,128)(2,1)}, bf16[2,256,256]{2,1,0:T(8,128)(2,1)}, u32[]{:S(2)}, u32[]{:S(2)}) collective-permute-start(bf16[2,256,256]{2,1,0:T(8,128)(2,1)} %collective-permute-done.13.refs_3_), channel_id=1, source_target_pairs={{0,1},{1,2},{2,3},{3,4},{4,5},{5,6},{6,7},{7,8},{8,9},{9,10},{10,1... | collective-permute-start | bytes 786440 | tf_op jit(solution)/shard_map/ppermute | solution.py:98
  16.6 1.9 %collective-permute-start.10 = (bf16[2,256,256]{2,1,0:T(8,128)(2,1)S(1)}, bf16[2,256,256]{2,1,0:T(8,128)(2,1)}, u32[]{:S(2)}, u32[]{:S(2)}) collective-permute-start(bf16[2,256,256]{2,1,0:T(8,128)(2,1)S(1)} %collective-permute-done.9.refs_3_), channel_id=1, source_target_pairs={{0,1},{1,2},{2,3},{3,4},{4,5},{5,6},{6,7},{7,8},{8,9},{9,10},{10,1... | collective-permute-start | bytes 786440 | tf_op jit(solution)/shard_map/ppermute | solution.py:98
  18.6 5.7 %collective-permute-start = (bf16[1,256,2048]{2,1,0:T(8,128)(2,1)}, bf16[1,256,2048]{2,1,0:T(8,128)(2,1)S(1)}, u32[]{:S(2)}, u32[]{:S(2)}) collective-permute-start(bf16[1,256,2048]{2,1,0:T(8,128)(2,1)} %param.16), channel_id=1, source_target_pairs={{0,224},{32,0},{64,32},{96,64},{128,96},{160,128},{192,160},{224,1... | collective-permute-start | bytes 3145736 | tf_op jit(solution)/shard_map/ppermute | solution.py:92
  24.2 3.6 %collective-permute-start.6 = (bf16[2,256,256]{2,1,0:T(8,128)(2,1)S(1)}, bf16[2,256,256]{2,1,0:T(8,128)(2,1)}, u32[]{:S(2)}, u32[]{:S(2)}) collective-permute-start(bf16[2,256,256]{2,1,0:T(8,128)(2,1)S(1)} %collective-permute-done.5.refs_3_), channel_id=1, source_target_pairs={{0,1},{1,2},{2,3},{3,4},{4,5},{5,6},{6,7},{7,8},{8,9},{9,10},{10,1... | collective-permute-start | bytes 786440 | tf_op jit(solution)/shard_map/ppermute | solution.py:98
  27.8 1.9 %collective-permute-start.2 = (bf16[2,256,256]{2,1,0:T(8,128)(2,1)S(1)}, bf16[2,256,256]{2,1,0:T(8,128)(2,1)S(1)}, u32[]{:S(2)}, u32[]{:S(2)}) collective-permute-start(bf16[2,256,256]{2,1,0:T(8,128)(2,1)S(1)} %collective-permute-done.1.refs_3_), channel_id=1, source_target_pairs={{0,1},{1,2},{2,3},{3,4},{4,5},{5,6},{6,7},{7,8},{8,9},{9,10},{10,1... | collective-permute-start | bytes 786440 | tf_op jit(solution)/shard_map/ppermute | solution.py:98
  29.8 3.2 %collective-permute-start.15 = (bf16[2,256,256]{2,1,0:T(8,128)(2,1)}, bf16[2,256,256]{2,1,0:T(8,128)(2,1)}, u32[]{:S(2)}, u32[]{:S(2)}) collective-permute-start(bf16[2,256,256]{2,1,0:T(8,128)(2,1)} %collective-permute-done.14.refs_2_), channel_id=1, source_target_pairs={{0,1},{1,2},{2,3},{3,4},{4,5},{5,6},{6,7},{7,8},{8,9},{9,10},{10,1... | collective-permute-start | bytes 786440 | tf_op jit(solution)/shard_map/ppermute | solution.py:98
  33.0 1.9 %collective-permute-start.11 = (bf16[2,256,256]{2,1,0:T(8,128)(2,1)}, bf16[2,256,256]{2,1,0:T(8,128)(2,1)}, u32[]{:S(2)}, u32[]{:S(2)}) collective-permute-start(bf16[2,256,256]{2,1,0:T(8,128)(2,1)} %collective-permute-done.10.refs_2_), channel_id=1, source_target_pairs={{0,1},{1,2},{2,3},{3,4},{4,5},{5,6},{6,7},{7,8},{8,9},{9,10},{10,1... | collective-permute-start | bytes 786440 | tf_op jit(solution)/shard_map/ppermute | solution.py:98
  35.3 3.6 %collective-permute-start.7 = (bf16[2,256,256]{2,1,0:T(8,128)(2,1)}, bf16[2,256,256]{2,1,0:T(8,128)(2,1)S(1)}, u32[]{:S(2)}, u32[]{:S(2)}) collective-permute-start(bf16[2,256,256]{2,1,0:T(8,128)(2,1)} %collective-permute-done.6.refs_2_), channel_id=1, source_target_pairs={{0,1},{1,2},{2,3},{3,4},{4,5},{5,6},{6,7},{7,8},{8,9},{9,10},{10,1... | collective-permute-start | bytes 786440 | tf_op jit(solution)/shard_map/ppermute | solution.py:98
  38.9 1.9 %collective-permute-start.3 = (bf16[2,256,256]{2,1,0:T(8,128)(2,1)S(1)}, bf16[2,256,256]{2,1,0:T(8,128)(2,1)S(1)}, u32[]{:S(2)}, u32[]{:S(2)}) collective-permute-start(bf16[2,256,256]{2,1,0:T(8,128)(2,1)S(1)} %collective-permute-done.2.refs_2_), channel_id=1, source_target_pairs={{0,1},{1,2},{2,3},{3,4},{4,5},{5,6},{6,7},{7,8},{8,9},{9,10},{10,1... | collective-permute-start | bytes 786440 | tf_op jit(solution)/shard_map/ppermute | solution.py:98
  40.8 3.6 %collective-permute-start.16 = (bf16[2,256,256]{2,1,0:T(8,128)(2,1)}, bf16[2,256,256]{2,1,0:T(8,128)(2,1)S(1)}, u32[]{:S(2)}, u32[]{:S(2)}) collective-permute-start(bf16[2,256,256]{2,1,0:T(8,128)(2,1)} %collective-permute-done.15.refs_1_), channel_id=1, source_target_pairs={{0,1},{1,2},{2,3},{3,4},{4,5},{5,6},{6,7},{7,8},{8,9},{9,10},{10,1... | collective-permute-start | bytes 786440 | tf_op jit(solution)/shard_map/ppermute | solution.py:98
  44.4 1.9 %collective-permute-start.12 = (bf16[2,256,256]{2,1,0:T(8,128)(2,1)}, bf16[2,256,256]{2,1,0:T(8,128)(2,1)}, u32[]{:S(2)}, u32[]{:S(2)}) collective-permute-start(bf16[2,256,256]{2,1,0:T(8,128)(2,1)} %collective-permute-done.11.refs_1_), channel_id=1, source_target_pairs={{0,1},{1,2},{2,3},{3,4},{4,5},{5,6},{6,7},{7,8},{8,9},{9,10},{10,1... | collective-permute-start | bytes 786440 | tf_op jit(solution)/shard_map/ppermute | solution.py:98
  46.4 1.4 convert_convert_fusion.refs_5_
  47.8 3.3 %collective-permute-start.8 = (bf16[2,256,256]{2,1,0:T(8,128)(2,1)S(1)}, bf16[2,256,256]{2,1,0:T(8,128)(2,1)}, u32[]{:S(2)}, u32[]{:S(2)}) collective-permute-start(bf16[2,256,256]{2,1,0:T(8,128)(2,1)S(1)} %collective-permute-done.7.refs_1_), channel_id=1, source_target_pairs={{0,1},{1,2},{2,3},{3,4},{4,5},{5,6},{6,7},{7,8},{8,9},{9,10},{10,1... | collective-permute-start | bytes 786440 | tf_op jit(solution)/shard_map/ppermute | solution.py:98
  51.1 1.9 %collective-permute-start.4 = (bf16[2,256,256]{2,1,0:T(8,128)(2,1)S(1)}, bf16[2,256,256]{2,1,0:T(8,128)(2,1)S(1)}, u32[]{:S(2)}, u32[]{:S(2)}) collective-permute-start(bf16[2,256,256]{2,1,0:T(8,128)(2,1)S(1)} %collective-permute-done.3.refs_1_), channel_id=1, source_target_pairs={{0,1},{1,2},{2,3},{3,4},{4,5},{5,6},{6,7},{7,8},{8,9},{9,10},{10,1... | collective-permute-start | bytes 786440 | tf_op jit(solution)/shard_map/ppermute | solution.py:98
  53.7 1.1 broadcast_5_refs_7_.2.clone.refs_7_
  54.9 1.1 broadcast_in_dim.8.refs_6_
  56.0 0.8 broadcast_4_refs_8_.2.clone.refs_8_
  57.3 6.2 %shard_map.148 = (bf16[256,2048]{1,0:T(8,128)(2,1)}, bf16[4,2,256,256]{3,2,1,0:T(8,128)(2,1)}, f32[2,256,256]{2,1,0:T(8,128)}) custom-call(s32[2]{0:T(128)} %call_exported.0.at_ref, bf16[256,2048]{1,0:T(8,128)(2,1)} %bitcast.88, bf16[256,2048]{1,0:T(8,128)(2,1)} %bitcast.96, ...), custom_call_target="tpu_custom_call", output_to_operand_aliasing={{0}: (9, {}), {1}: (10, {}), {2}: (11, {})} | custom-call | tf_op jit(solution)/shard_map/pallas_call | solution.py:81
  64.1 6.2 %shard_map.149 = (bf16[256,2048]{1,0:T(8,128)(2,1)}, bf16[4,2,256,256]{3,2,1,0:T(8,128)(2,1)}, f32[2,256,256]{2,1,0:T(8,128)}) custom-call(s32[2]{0:T(128)} %call_exported.1.at_ref, bf16[256,2048]{1,0:T(8,128)(2,1)} %bitcast.89, bf16[256,2048]{1,0:T(8,128)(2,1)} %bitcast.97, ...), custom_call_target="tpu_custom_call", output_to_operand_aliasing={{0}: (9, {}), {1}: (10, {}), {2}: (11, {})} | custom-call | tf_op jit(solution)/shard_map/pallas_call | solution.py:81
  70.3 1.0 slice_bitcast_fusion.3
  71.2 2.6 %collective-permute-start.17 = (bf16[2,256,256]{2,1,0:T(8,128)(2,1)S(1)}, bf16[2,256,256]{2,1,0:T(8,128)(2,1)S(1)}, u32[]{:S(2)}, u32[]{:S(2)}) collective-permute-start(bf16[2,256,256]{2,1,0:T(8,128)(2,1)S(1)} %slice_bitcast_fusion.3), channel_id=1, source_target_pairs={{1,0},{2,1},{3,2},{4,3},{5,4},{6,5},{7,6},{8,7},{9,8},{10,9},{11,1... | collective-permute-start | bytes 786440 | tf_op jit(solution)/shard_map/ppermute | solution.py:98
  73.8 1.1 broadcast_5_refs_7_.2.clone.1.refs_7_
  74.9 0.8 broadcast_4_refs_8_.2.clone.1.refs_8_
  75.7 6.2 %shard_map.150 = (bf16[256,2048]{1,0:T(8,128)(2,1)}, bf16[4,2,256,256]{3,2,1,0:T(8,128)(2,1)}, f32[2,256,256]{2,1,0:T(8,128)}) custom-call(s32[2]{0:T(128)} %constant.42.clone.at_ref, bf16[256,2048]{1,0:T(8,128)(2,1)} %bitcast.90, bf16[256,2048]{1,0:T(8,128)(2,1)} %bitcast.98, ...), custom_call_target="tpu_custom_call", output_to_operand_aliasing={{0}: (9, {}), {1}: (10, {}), {2}: (11, {})} | custom-call | tf_op jit(solution)/shard_map/pallas_call | solution.py:81
  81.9 6.2 %shard_map.151 = (bf16[256,2048]{1,0:T(8,128)(2,1)}, bf16[4,2,256,256]{3,2,1,0:T(8,128)(2,1)}, f32[2,256,256]{2,1,0:T(8,128)}) custom-call(s32[2]{0:T(128)} %constant.43.clone.at_ref, bf16[256,2048]{1,0:T(8,128)(2,1)} %bitcast.91, bf16[256,2048]{1,0:T(8,128)(2,1)} %bitcast.99, ...), custom_call_target="tpu_custom_call", output_to_operand_aliasing={{0}: (9, {}), {1}: (10, {}), {2}: (11, {})} | custom-call | tf_op jit(solution)/shard_map/pallas_call | solution.py:81
  88.1 1.0 slice_bitcast_fusion.2
  89.1 2.5 %collective-permute-start.21 = (bf16[2,256,256]{2,1,0:T(8,128)(2,1)S(1)}, bf16[2,256,256]{2,1,0:T(8,128)(2,1)S(1)}, u32[]{:S(2)}, u32[]{:S(2)}) collective-permute-start(bf16[2,256,256]{2,1,0:T(8,128)(2,1)S(1)} %slice_bitcast_fusion.2), channel_id=1, source_target_pairs={{1,0},{2,1},{3,2},{4,3},{5,4},{6,5},{7,6},{8,7},{9,8},{10,9},{11,1... | collective-permute-start | bytes 786440 | tf_op jit(solution)/shard_map/ppermute | solution.py:98
  91.6 1.1 broadcast_5_refs_7_.2.clone.2.refs_7_
  92.7 0.8 broadcast_4_refs_8_.2.clone.2.refs_8_
  93.5 6.2 %shard_map.152 = (bf16[256,2048]{1,0:T(8,128)(2,1)}, bf16[4,2,256,256]{3,2,1,0:T(8,128)(2,1)}, f32[2,256,256]{2,1,0:T(8,128)}) custom-call(s32[2]{0:T(128)} %constant.44.clone.at_ref, bf16[256,2048]{1,0:T(8,128)(2,1)} %bitcast.92, bf16[256,2048]{1,0:T(8,128)(2,1)} %bitcast.100, ...), custom_call_target="tpu_custom_call", output_to_operand_aliasing={{0}: (9, {}), {1}: (10, {}), {2}: (11, {})} | custom-call | tf_op jit(solution)/shard_map/pallas_call | solution.py:81
  99.7 6.2 %shard_map.153 = (bf16[256,2048]{1,0:T(8,128)(2,1)}, bf16[4,2,256,256]{3,2,1,0:T(8,128)(2,1)}, f32[2,256,256]{2,1,0:T(8,128)}) custom-call(s32[2]{0:T(128)} %constant.45.clone.at_ref, bf16[256,2048]{1,0:T(8,128)(2,1)} %bitcast.93, bf16[256,2048]{1,0:T(8,128)(2,1)} %bitcast.101, ...), custom_call_target="tpu_custom_call", output_to_operand_aliasing={{0}: (9, {}), {1}: (10, {}), {2}: (11, {})} | custom-call | tf_op jit(solution)/shard_map/pallas_call | solution.py:81
  106.0 1.0 slice_bitcast_fusion.1
  106.9 2.7 %collective-permute-start.25 = (bf16[2,256,256]{2,1,0:T(8,128)(2,1)S(1)}, bf16[2,256,256]{2,1,0:T(8,128)(2,1)S(1)}, u32[]{:S(2)}, u32[]{:S(2)}) collective-permute-start(bf16[2,256,256]{2,1,0:T(8,128)(2,1)S(1)} %slice_bitcast_fusion.1), channel_id=1, source_target_pairs={{1,0},{2,1},{3,2},{4,3},{5,4},{6,5},{7,6},{8,7},{9,8},{10,9},{11,1... | collective-permute-start | bytes 786440 | tf_op jit(solution)/shard_map/ppermute | solution.py:98
  109.6 1.1 broadcast_5_refs_7_.2.refs_7_
  110.7 0.8 broadcast_4_refs_8_.2.refs_8_
  111.6 6.2 %shard_map.154 = (bf16[256,2048]{1,0:T(8,128)(2,1)}, bf16[4,2,256,256]{3,2,1,0:T(8,128)(2,1)}, f32[2,256,256]{2,1,0:T(8,128)}) custom-call(s32[2]{0:T(128)} %constant.46.clone.at_ref, bf16[256,2048]{1,0:T(8,128)(2,1)} %bitcast.94, bf16[256,2048]{1,0:T(8,128)(2,1)} %bitcast.102, ...), custom_call_target="tpu_custom_call", output_to_operand_aliasing={{0}: (9, {}), {1}: (10, {}), {2}: (11, {})} | custom-call | tf_op jit(solution)/shard_map/pallas_call | solution.py:81
  117.8 6.3 %shard_map.155 = (bf16[256,2048]{1,0:T(8,128)(2,1)}, bf16[4,2,256,256]{3,2,1,0:T(8,128)(2,1)}, f32[2,256,256]{2,1,0:T(8,128)}) custom-call(s32[2]{0:T(128)} %constant.47.clone.at_ref, bf16[256,2048]{1,0:T(8,128)(2,1)} %bitcast.95, bf16[256,2048]{1,0:T(8,128)(2,1)} %bitcast.103, ...), custom_call_target="tpu_custom_call", output_to_operand_aliasing={{0}: (9, {}), {1}: (10, {}), {2}: (11, {})} | custom-call | tf_op jit(solution)/shard_map/pallas_call | solution.py:81
  124.1 1.1 slice_bitcast_fusion
  125.2 2.1 %collective-permute-start.29 = (bf16[2,256,256]{2,1,0:T(8,128)(2,1)S(1)}, bf16[2,256,256]{2,1,0:T(8,128)(2,1)S(1)}, u32[]{:S(2)}, u32[]{:S(2)}) collective-permute-start(bf16[2,256,256]{2,1,0:T(8,128)(2,1)S(1)} %slice_bitcast_fusion), channel_id=1, source_target_pairs={{1,0},{2,1},{3,2},{4,3},{5,4},{6,5},{7,6},{8,7},{9,8},{10,9},{11,1... | collective-permute-start | bytes 786440 | tf_op jit(solution)/shard_map/ppermute | solution.py:98
  127.4 2.4 %collective-permute-start.18 = (bf16[2,256,256]{2,1,0:T(8,128)(2,1)S(1)}, bf16[2,256,256]{2,1,0:T(8,128)(2,1)S(1)}, u32[]{:S(2)}, u32[]{:S(2)}) collective-permute-start(bf16[2,256,256]{2,1,0:T(8,128)(2,1)S(1)} %fusion.14), channel_id=1, source_target_pairs={{1,0},{2,1},{3,2},{4,3},{5,4},{6,5},{7,6},{8,7},{9,8},{10,9},{11,1... | collective-permute-start | bytes 786440 | tf_op jit(solution)/shard_map/ppermute | solution.py:98
  129.9 2.0 %collective-permute-start.22 = (bf16[2,256,256]{2,1,0:T(8,128)(2,1)S(1)}, bf16[2,256,256]{2,1,0:T(8,128)(2,1)S(1)}, u32[]{:S(2)}, u32[]{:S(2)}) collective-permute-start(bf16[2,256,256]{2,1,0:T(8,128)(2,1)S(1)} %fusion.11), channel_id=1, source_target_pairs={{1,0},{2,1},{3,2},{4,3},{5,4},{6,5},{7,6},{8,7},{9,8},{10,9},{11,1... | collective-permute-start | bytes 786440 | tf_op jit(solution)/shard_map/ppermute | solution.py:98
  132.0 2.4 %collective-permute-start.26 = (bf16[2,256,256]{2,1,0:T(8,128)(2,1)S(1)}, bf16[2,256,256]{2,1,0:T(8,128)(2,1)S(1)}, u32[]{:S(2)}, u32[]{:S(2)}) collective-permute-start(bf16[2,256,256]{2,1,0:T(8,128)(2,1)S(1)} %fusion.8), channel_id=1, source_target_pairs={{1,0},{2,1},{3,2},{4,3},{5,4},{6,5},{7,6},{8,7},{9,8},{10,9},{11,1... | collective-permute-start | bytes 786440 | tf_op jit(solution)/shard_map/ppermute | solution.py:98
  135.2 1.9 %collective-permute-start.30 = (bf16[2,256,256]{2,1,0:T(8,128)(2,1)S(1)}, bf16[2,256,256]{2,1,0:T(8,128)(2,1)S(1)}, u32[]{:S(2)}, u32[]{:S(2)}) collective-permute-start(bf16[2,256,256]{2,1,0:T(8,128)(2,1)S(1)} %fusion.5), channel_id=1, source_target_pairs={{1,0},{2,1},{3,2},{4,3},{5,4},{6,5},{7,6},{8,7},{9,8},{10,9},{11,1... | collective-permute-start | bytes 786440 | tf_op jit(solution)/shard_map/ppermute | solution.py:98
  138.0 1.9 %collective-permute-start.19 = (bf16[2,256,256]{2,1,0:T(8,128)(2,1)S(1)}, bf16[2,256,256]{2,1,0:T(8,128)(2,1)S(1)}, u32[]{:S(2)}, u32[]{:S(2)}) collective-permute-start(bf16[2,256,256]{2,1,0:T(8,128)(2,1)S(1)} %fusion.13), channel_id=1, source_target_pairs={{1,0},{2,1},{3,2},{4,3},{5,4},{6,5},{7,6},{8,7},{9,8},{10,9},{11,1... | collective-permute-start | bytes 786440 | tf_op jit(solution)/shard_map/ppermute | solution.py:98
  139.9 0.8 collective-permute-done.22
  140.8 1.9 %collective-permute-start.23 = (bf16[2,256,256]{2,1,0:T(8,128)(2,1)S(1)}, bf16[2,256,256]{2,1,0:T(8,128)(2,1)S(1)}, u32[]{:S(2)}, u32[]{:S(2)}) collective-permute-start(bf16[2,256,256]{2,1,0:T(8,128)(2,1)S(1)} %fusion.10), channel_id=1, source_target_pairs={{1,0},{2,1},{3,2},{4,3},{5,4},{6,5},{7,6},{8,7},{9,8},{10,9},{11,1... | collective-permute-start | bytes 786440 | tf_op jit(solution)/shard_map/ppermute | solution.py:98
  142.7 0.8 collective-permute-done.26
  143.6 1.9 %collective-permute-start.27 = (bf16[2,256,256]{2,1,0:T(8,128)(2,1)S(1)}, bf16[2,256,256]{2,1,0:T(8,128)(2,1)S(1)}, u32[]{:S(2)}, u32[]{:S(2)}) collective-permute-start(bf16[2,256,256]{2,1,0:T(8,128)(2,1)S(1)} %fusion.7), channel_id=1, source_target_pairs={{1,0},{2,1},{3,2},{4,3},{5,4},{6,5},{7,6},{8,7},{9,8},{10,9},{11,1... | collective-permute-start | bytes 786440 | tf_op jit(solution)/shard_map/ppermute | solution.py:98
  145.5 0.8 collective-permute-done.30
  146.4 1.9 %collective-permute-start.31 = (bf16[2,256,256]{2,1,0:T(8,128)(2,1)S(1)}, bf16[2,256,256]{2,1,0:T(8,128)(2,1)S(1)}, u32[]{:S(2)}, u32[]{:S(2)}) collective-permute-start(bf16[2,256,256]{2,1,0:T(8,128)(2,1)S(1)} %fusion.4), channel_id=1, source_target_pairs={{1,0},{2,1},{3,2},{4,3},{5,4},{6,5},{7,6},{8,7},{9,8},{10,9},{11,1... | collective-permute-start | bytes 786440 | tf_op jit(solution)/shard_map/ppermute | solution.py:98
  149.2 2.1 %collective-permute-start.20 = (bf16[2,256,256]{2,1,0:T(8,128)(2,1)S(1)}, bf16[2,256,256]{2,1,0:T(8,128)(2,1)S(1)}, u32[]{:S(2)}, u32[]{:S(2)}) collective-permute-start(bf16[2,256,256]{2,1,0:T(8,128)(2,1)S(1)} %fusion.12), channel_id=1, source_target_pairs={{1,0},{2,1},{3,2},{4,3},{5,4},{6,5},{7,6},{8,7},{9,8},{10,9},{11,1... | collective-permute-start | bytes 786440 | tf_op jit(solution)/shard_map/ppermute | solution.py:98
  152.0 1.9 %collective-permute-start.24 = (bf16[2,256,256]{2,1,0:T(8,128)(2,1)S(1)}, bf16[2,256,256]{2,1,0:T(8,128)(2,1)S(1)}, u32[]{:S(2)}, u32[]{:S(2)}) collective-permute-start(bf16[2,256,256]{2,1,0:T(8,128)(2,1)S(1)} %fusion.9), channel_id=1, source_target_pairs={{1,0},{2,1},{3,2},{4,3},{5,4},{6,5},{7,6},{8,7},{9,8},{10,9},{11,1... | collective-permute-start | bytes 786440 | tf_op jit(solution)/shard_map/ppermute | solution.py:98
  154.9 2.1 %collective-permute-start.28 = (bf16[2,256,256]{2,1,0:T(8,128)(2,1)S(1)}, bf16[2,256,256]{2,1,0:T(8,128)(2,1)S(1)}, u32[]{:S(2)}, u32[]{:S(2)}) collective-permute-start(bf16[2,256,256]{2,1,0:T(8,128)(2,1)S(1)} %fusion.6), channel_id=1, source_target_pairs={{1,0},{2,1},{3,2},{4,3},{5,4},{6,5},{7,6},{8,7},{9,8},{10,9},{11,1... | collective-permute-start | bytes 786440 | tf_op jit(solution)/shard_map/ppermute | solution.py:98
  157.7 1.9 %collective-permute-start.32 = (bf16[2,256,256]{2,1,0:T(8,128)(2,1)S(1)}, bf16[2,256,256]{2,1,0:T(8,128)(2,1)S(1)}, u32[]{:S(2)}, u32[]{:S(2)}) collective-permute-start(bf16[2,256,256]{2,1,0:T(8,128)(2,1)S(1)} %fusion.3), channel_id=1, source_target_pairs={{1,0},{2,1},{3,2},{4,3},{5,4},{6,5},{7,6},{8,7},{9,8},{10,9},{11,1... | collective-permute-start | bytes 786440 | tf_op jit(solution)/shard_map/ppermute | solution.py:98
  160.5 2.7 %collective-permute-done.24 = bf16[2,256,256]{2,1,0:T(8,128)(2,1)S(1)} collective-permute-done((bf16[2,256,256]{2,1,0:T(8,128)(2,1)S(1)}, bf16[2,256,256]{2,1,0:T(8,128)(2,1)S(1)}, u32[]{:S(2)}, u32[]{:S(2)}) %collective-permute-start.24) | collective-permute-done | bytes 262176 | tf_op jit(solution)/shard_map/ppermute | solution.py:98
  163.3 2.7 %collective-permute-done.28 = bf16[2,256,256]{2,1,0:T(8,128)(2,1)S(1)} collective-permute-done((bf16[2,256,256]{2,1,0:T(8,128)(2,1)S(1)}, bf16[2,256,256]{2,1,0:T(8,128)(2,1)S(1)}, u32[]{:S(2)}, u32[]{:S(2)}) %collective-permute-start.28) | collective-permute-done | bytes 262176 | tf_op jit(solution)/shard_map/ppermute | solution.py:98
  166.1 2.7 %collective-permute-done.32 = bf16[2,256,256]{2,1,0:T(8,128)(2,1)S(1)} collective-permute-done((bf16[2,256,256]{2,1,0:T(8,128)(2,1)S(1)}, bf16[2,256,256]{2,1,0:T(8,128)(2,1)S(1)}, u32[]{:S(2)}, u32[]{:S(2)}) %collective-permute-start.32) | collective-permute-done | bytes 262176 | tf_op jit(solution)/shard_map/ppermute | solution.py:98
  168.9 0.9 maximum_bitcast_fusion.1
  169.8 0.9 maximum_bitcast_fusion
  (103 shorter events, 8.7 us)
Async XLA Ops:
  2.0 32.9 %copy-start.21 = (s32[4]{0:T(128)S(1)}, s32[4]{0:T(128)}, u32[]{:S(2)}) copy-start(s32[4]{0:T(128)} %param.17) | copy-start | bytes 52
  2.1 45.7 %copy-start.12 = (bf16[2,256,256]{2,1,0:T(8,128)(2,1)}, bf16[2,256,256]{2,1,0:T(8,128)(2,1)S(1)}, u32[]{:S(2)}) copy-start(bf16[2,256,256]{2,1,0:T(8,128)(2,1)S(1)} %pad_maximum_fusion.3.refs_4_) | copy-start | bytes 786436
  2.1 10.9 %collective-permute-start.13 = (bf16[2,256,256]{2,1,0:T(8,128)(2,1)S(1)}, bf16[2,256,256]{2,1,0:T(8,128)(2,1)}, u32[]{:S(2)}, u32[]{:S(2)}) collective-permute-start(bf16[2,256,256]{2,1,0:T(8,128)(2,1)S(1)} %pad_maximum_fusion.3.refs_4_), channel_id=1, source_target_pairs={{0,1},{1,2},{2,3},{3,4},{4,5},{5,6},{6,7},{7,8},{8,9},{9,10},{10,1... | collective-permute-start | bytes 786440 | tf_op jit(solution)/shard_map/ppermute | solution.py:98
  5.4 49.4 %copy-start.11 = (bf16[2,256,256]{2,1,0:T(8,128)(2,1)}, bf16[2,256,256]{2,1,0:T(8,128)(2,1)S(1)}, u32[]{:S(2)}) copy-start(bf16[2,256,256]{2,1,0:T(8,128)(2,1)S(1)} %pad_maximum_fusion.2.refs_4_) | copy-start | bytes 786436
  5.5 11.2 %collective-permute-start.9 = (bf16[2,256,256]{2,1,0:T(8,128)(2,1)S(1)}, bf16[2,256,256]{2,1,0:T(8,128)(2,1)S(1)}, u32[]{:S(2)}, u32[]{:S(2)}) collective-permute-start(bf16[2,256,256]{2,1,0:T(8,128)(2,1)S(1)} %pad_maximum_fusion.2.refs_4_), channel_id=1, source_target_pairs={{0,1},{1,2},{2,3},{3,4},{4,5},{5,6},{6,7},{7,8},{8,9},{9,10},{10,1... | collective-permute-start | bytes 786440 | tf_op jit(solution)/shard_map/ppermute | solution.py:98
  7.4 47.4 %copy-start.10 = (bf16[2,256,256]{2,1,0:T(8,128)(2,1)}, bf16[2,256,256]{2,1,0:T(8,128)(2,1)S(1)}, u32[]{:S(2)}) copy-start(bf16[2,256,256]{2,1,0:T(8,128)(2,1)S(1)} %pad_maximum_fusion.1.refs_4_) | copy-start | bytes 786436
  7.4 16.8 %collective-permute-start.5 = (bf16[2,256,256]{2,1,0:T(8,128)(2,1)S(1)}, bf16[2,256,256]{2,1,0:T(8,128)(2,1)S(1)}, u32[]{:S(2)}, u32[]{:S(2)}) collective-permute-start(bf16[2,256,256]{2,1,0:T(8,128)(2,1)S(1)} %pad_maximum_fusion.1.refs_4_), channel_id=1, source_target_pairs={{0,1},{1,2},{2,3},{3,4},{4,5},{5,6},{6,7},{7,8},{8,9},{9,10},{10,1... | collective-permute-start | bytes 786440 | tf_op jit(solution)/shard_map/ppermute | solution.py:98
  11.1 44.9 %copy-start.9 = (bf16[2,256,256]{2,1,0:T(8,128)(2,1)}, bf16[2,256,256]{2,1,0:T(8,128)(2,1)S(1)}, u32[]{:S(2)}) copy-start(bf16[2,256,256]{2,1,0:T(8,128)(2,1)S(1)} %pad_maximum_fusion.refs_4_) | copy-start | bytes 786436
  11.1 16.8 %collective-permute-start.1 = (bf16[2,256,256]{2,1,0:T(8,128)(2,1)S(1)}, bf16[2,256,256]{2,1,0:T(8,128)(2,1)S(1)}, u32[]{:S(2)}, u32[]{:S(2)}) collective-permute-start(bf16[2,256,256]{2,1,0:T(8,128)(2,1)S(1)} %pad_maximum_fusion.refs_4_), channel_id=1, source_target_pairs={{0,1},{1,2},{2,3},{3,4},{4,5},{5,6},{6,7},{7,8},{8,9},{9,10},{10,1... | collective-permute-start | bytes 786440 | tf_op jit(solution)/shard_map/ppermute | solution.py:98
  13.0 16.8 %collective-permute-start.14 = (bf16[2,256,256]{2,1,0:T(8,128)(2,1)}, bf16[2,256,256]{2,1,0:T(8,128)(2,1)}, u32[]{:S(2)}, u32[]{:S(2)}) collective-permute-start(bf16[2,256,256]{2,1,0:T(8,128)(2,1)} %collective-permute-done.13.refs_3_), channel_id=1, source_target_pairs={{0,1},{1,2},{2,3},{3,4},{4,5},{5,6},{6,7},{7,8},{8,9},{9,10},{10,1... | collective-permute-start | bytes 786440 | tf_op jit(solution)/shard_map/ppermute | solution.py:98
  16.6 39.3 %copy-start.16 = (bf16[2,256,256]{2,1,0:T(8,128)(2,1)}, bf16[2,256,256]{2,1,0:T(8,128)(2,1)S(1)}, u32[]{:S(2)}) copy-start(bf16[2,256,256]{2,1,0:T(8,128)(2,1)S(1)} %collective-permute-done.9.refs_3_) | copy-start | bytes 786436
  16.6 16.3 %collective-permute-start.10 = (bf16[2,256,256]{2,1,0:T(8,128)(2,1)S(1)}, bf16[2,256,256]{2,1,0:T(8,128)(2,1)}, u32[]{:S(2)}, u32[]{:S(2)}) collective-permute-start(bf16[2,256,256]{2,1,0:T(8,128)(2,1)S(1)} %collective-permute-done.9.refs_3_), channel_id=1, source_target_pairs={{0,1},{1,2},{2,3},{3,4},{4,5},{5,6},{6,7},{7,8},{8,9},{9,10},{10,1... | collective-permute-start | bytes 786440 | tf_op jit(solution)/shard_map/ppermute | solution.py:98
  18.6 34.5 %collective-permute-start = (bf16[1,256,2048]{2,1,0:T(8,128)(2,1)}, bf16[1,256,2048]{2,1,0:T(8,128)(2,1)S(1)}, u32[]{:S(2)}, u32[]{:S(2)}) collective-permute-start(bf16[1,256,2048]{2,1,0:T(8,128)(2,1)} %param.16), channel_id=1, source_target_pairs={{0,224},{32,0},{64,32},{96,64},{128,96},{160,128},{192,160},{224,1... | collective-permute-start | bytes 3145736 | tf_op jit(solution)/shard_map/ppermute | solution.py:92
  24.2 31.7 %copy-start.14 = (bf16[2,256,256]{2,1,0:T(8,128)(2,1)}, bf16[2,256,256]{2,1,0:T(8,128)(2,1)S(1)}, u32[]{:S(2)}) copy-start(bf16[2,256,256]{2,1,0:T(8,128)(2,1)S(1)} %collective-permute-done.5.refs_3_) | copy-start | bytes 786436
  24.2 11.0 %collective-permute-start.6 = (bf16[2,256,256]{2,1,0:T(8,128)(2,1)S(1)}, bf16[2,256,256]{2,1,0:T(8,128)(2,1)}, u32[]{:S(2)}, u32[]{:S(2)}) collective-permute-start(bf16[2,256,256]{2,1,0:T(8,128)(2,1)S(1)} %collective-permute-done.5.refs_3_), channel_id=1, source_target_pairs={{0,1},{1,2},{2,3},{3,4},{4,5},{5,6},{6,7},{7,8},{8,9},{9,10},{10,1... | collective-permute-start | bytes 786440 | tf_op jit(solution)/shard_map/ppermute | solution.py:98
  27.8 28.1 %copy-start.13 = (bf16[2,256,256]{2,1,0:T(8,128)(2,1)}, bf16[2,256,256]{2,1,0:T(8,128)(2,1)S(1)}, u32[]{:S(2)}) copy-start(bf16[2,256,256]{2,1,0:T(8,128)(2,1)S(1)} %collective-permute-done.1.refs_3_) | copy-start | bytes 786436
  27.8 11.0 %collective-permute-start.2 = (bf16[2,256,256]{2,1,0:T(8,128)(2,1)S(1)}, bf16[2,256,256]{2,1,0:T(8,128)(2,1)S(1)}, u32[]{:S(2)}, u32[]{:S(2)}) collective-permute-start(bf16[2,256,256]{2,1,0:T(8,128)(2,1)S(1)} %collective-permute-done.1.refs_3_), channel_id=1, source_target_pairs={{0,1},{1,2},{2,3},{3,4},{4,5},{5,6},{6,7},{7,8},{8,9},{9,10},{10,1... | collective-permute-start | bytes 786440 | tf_op jit(solution)/shard_map/ppermute | solution.py:98
  29.8 11.0 %collective-permute-start.15 = (bf16[2,256,256]{2,1,0:T(8,128)(2,1)}, bf16[2,256,256]{2,1,0:T(8,128)(2,1)}, u32[]{:S(2)}, u32[]{:S(2)}) collective-permute-start(bf16[2,256,256]{2,1,0:T(8,128)(2,1)} %collective-permute-done.14.refs_2_), channel_id=1, source_target_pairs={{0,1},{1,2},{2,3},{3,4},{4,5},{5,6},{6,7},{7,8},{8,9},{9,10},{10,1... | collective-permute-start | bytes 786440 | tf_op jit(solution)/shard_map/ppermute | solution.py:98
  33.0 11.5 %collective-permute-start.11 = (bf16[2,256,256]{2,1,0:T(8,128)(2,1)}, bf16[2,256,256]{2,1,0:T(8,128)(2,1)}, u32[]{:S(2)}, u32[]{:S(2)}) collective-permute-start(bf16[2,256,256]{2,1,0:T(8,128)(2,1)} %collective-permute-done.10.refs_2_), channel_id=1, source_target_pairs={{0,1},{1,2},{2,3},{3,4},{4,5},{5,6},{6,7},{7,8},{8,9},{9,10},{10,1... | collective-permute-start | bytes 786440 | tf_op jit(solution)/shard_map/ppermute | solution.py:98
  35.3 12.5 %collective-permute-start.7 = (bf16[2,256,256]{2,1,0:T(8,128)(2,1)}, bf16[2,256,256]{2,1,0:T(8,128)(2,1)S(1)}, u32[]{:S(2)}, u32[]{:S(2)}) collective-permute-start(bf16[2,256,256]{2,1,0:T(8,128)(2,1)} %collective-permute-done.6.refs_2_), channel_id=1, source_target_pairs={{0,1},{1,2},{2,3},{3,4},{4,5},{5,6},{6,7},{7,8},{8,9},{9,10},{10,1... | collective-permute-start | bytes 786440 | tf_op jit(solution)/shard_map/ppermute | solution.py:98
  38.9 17.1 %copy-start.15 = (bf16[2,256,256]{2,1,0:T(8,128)(2,1)}, bf16[2,256,256]{2,1,0:T(8,128)(2,1)S(1)}, u32[]{:S(2)}) copy-start(bf16[2,256,256]{2,1,0:T(8,128)(2,1)S(1)} %collective-permute-done.2.refs_2_) | copy-start | bytes 786436
  38.9 12.2 %collective-permute-start.3 = (bf16[2,256,256]{2,1,0:T(8,128)(2,1)S(1)}, bf16[2,256,256]{2,1,0:T(8,128)(2,1)S(1)}, u32[]{:S(2)}, u32[]{:S(2)}) collective-permute-start(bf16[2,256,256]{2,1,0:T(8,128)(2,1)S(1)} %collective-permute-done.2.refs_2_), channel_id=1, source_target_pairs={{0,1},{1,2},{2,3},{3,4},{4,5},{5,6},{6,7},{7,8},{8,9},{9,10},{10,1... | collective-permute-start | bytes 786440 | tf_op jit(solution)/shard_map/ppermute | solution.py:98
  40.8 12.2 %collective-permute-start.16 = (bf16[2,256,256]{2,1,0:T(8,128)(2,1)}, bf16[2,256,256]{2,1,0:T(8,128)(2,1)S(1)}, u32[]{:S(2)}, u32[]{:S(2)}) collective-permute-start(bf16[2,256,256]{2,1,0:T(8,128)(2,1)} %collective-permute-done.15.refs_1_), channel_id=1, source_target_pairs={{0,1},{1,2},{2,3},{3,4},{4,5},{5,6},{6,7},{7,8},{8,9},{9,10},{10,1... | collective-permute-start | bytes 786440 | tf_op jit(solution)/shard_map/ppermute | solution.py:98
  44.4 29.4 %collective-permute-start.12 = (bf16[2,256,256]{2,1,0:T(8,128)(2,1)}, bf16[2,256,256]{2,1,0:T(8,128)(2,1)}, u32[]{:S(2)}, u32[]{:S(2)}) collective-permute-start(bf16[2,256,256]{2,1,0:T(8,128)(2,1)} %collective-permute-done.11.refs_1_), channel_id=1, source_target_pairs={{0,1},{1,2},{2,3},{3,4},{4,5},{5,6},{6,7},{7,8},{8,9},{9,10},{10,1... | collective-permute-start | bytes 786440 | tf_op jit(solution)/shard_map/ppermute | solution.py:98
  47.8 15.8 %copy-start.18 = (bf16[2,256,256]{2,1,0:T(8,128)(2,1)}, bf16[2,256,256]{2,1,0:T(8,128)(2,1)S(1)}, u32[]{:S(2)}) copy-start(bf16[2,256,256]{2,1,0:T(8,128)(2,1)S(1)} %collective-permute-done.7.refs_1_) | copy-start | bytes 786436
  47.8 43.8 %collective-permute-start.8 = (bf16[2,256,256]{2,1,0:T(8,128)(2,1)S(1)}, bf16[2,256,256]{2,1,0:T(8,128)(2,1)}, u32[]{:S(2)}, u32[]{:S(2)}) collective-permute-start(bf16[2,256,256]{2,1,0:T(8,128)(2,1)S(1)} %collective-permute-done.7.refs_1_), channel_id=1, source_target_pairs={{0,1},{1,2},{2,3},{3,4},{4,5},{5,6},{6,7},{7,8},{8,9},{9,10},{10,1... | collective-permute-start | bytes 786440 | tf_op jit(solution)/shard_map/ppermute | solution.py:98
  51.1 4.9 %copy-start.17 = (bf16[2,256,256]{2,1,0:T(8,128)(2,1)}, bf16[2,256,256]{2,1,0:T(8,128)(2,1)S(1)}, u32[]{:S(2)}) copy-start(bf16[2,256,256]{2,1,0:T(8,128)(2,1)S(1)} %collective-permute-done.3.refs_1_) | copy-start | bytes 786436
  51.1 58.5 %collective-permute-start.4 = (bf16[2,256,256]{2,1,0:T(8,128)(2,1)S(1)}, bf16[2,256,256]{2,1,0:T(8,128)(2,1)S(1)}, u32[]{:S(2)}, u32[]{:S(2)}) collective-permute-start(bf16[2,256,256]{2,1,0:T(8,128)(2,1)S(1)} %collective-permute-done.3.refs_1_), channel_id=1, source_target_pairs={{0,1},{1,2},{2,3},{3,4},{4,5},{5,6},{6,7},{7,8},{8,9},{9,10},{10,1... | collective-permute-start | bytes 786440 | tf_op jit(solution)/shard_map/ppermute | solution.py:98
  53.0 0.7 copy-start.20
  53.7 2.2 %copy-start = (bf16[1,256,2048]{2,1,0:T(8,128)(2,1)}, bf16[1,256,2048]{2,1,0:T(8,128)(2,1)S(1)}, u32[]{:S(2)}) copy-start(bf16[1,256,2048]{2,1,0:T(8,128)(2,1)S(1)} %collective-permute-done) | copy-start | bytes 3145732
  71.2 56.1 %collective-permute-start.17 = (bf16[2,256,256]{2,1,0:T(8,128)(2,1)S(1)}, bf16[2,256,256]{2,1,0:T(8,128)(2,1)S(1)}, u32[]{:S(2)}, u32[]{:S(2)}) collective-permute-start(bf16[2,256,256]{2,1,0:T(8,128)(2,1)S(1)} %slice_bitcast_fusion.3), channel_id=1, source_target_pairs={{1,0},{2,1},{3,2},{4,3},{5,4},{6,5},{7,6},{8,7},{9,8},{10,9},{11,1... | collective-permute-start | bytes 786440 | tf_op jit(solution)/shard_map/ppermute | solution.py:98
  89.1 40.7 %collective-permute-start.21 = (bf16[2,256,256]{2,1,0:T(8,128)(2,1)S(1)}, bf16[2,256,256]{2,1,0:T(8,128)(2,1)S(1)}, u32[]{:S(2)}, u32[]{:S(2)}) collective-permute-start(bf16[2,256,256]{2,1,0:T(8,128)(2,1)S(1)} %slice_bitcast_fusion.2), channel_id=1, source_target_pairs={{1,0},{2,1},{3,2},{4,3},{5,4},{6,5},{7,6},{8,7},{9,8},{10,9},{11,1... | collective-permute-start | bytes 786440 | tf_op jit(solution)/shard_map/ppermute | solution.py:98
  106.9 24.9 %collective-permute-start.25 = (bf16[2,256,256]{2,1,0:T(8,128)(2,1)S(1)}, bf16[2,256,256]{2,1,0:T(8,128)(2,1)S(1)}, u32[]{:S(2)}, u32[]{:S(2)}) collective-permute-start(bf16[2,256,256]{2,1,0:T(8,128)(2,1)S(1)} %slice_bitcast_fusion.1), channel_id=1, source_target_pairs={{1,0},{2,1},{3,2},{4,3},{5,4},{6,5},{7,6},{8,7},{9,8},{10,9},{11,1... | collective-permute-start | bytes 786440 | tf_op jit(solution)/shard_map/ppermute | solution.py:98
  109.6 1.9 %copy-start.19 = (bf16[2,256,256]{2,1,0:T(8,128)(2,1)}, bf16[2,256,256]{2,1,0:T(8,128)(2,1)S(1)}, u32[]{:S(2)}) copy-start(bf16[2,256,256]{2,1,0:T(8,128)(2,1)S(1)} %collective-permute-done.4.refs_0_) | copy-start | bytes 786436
  117.8 9.5 %copy-start.2 = (bf16[4,2,256,256]{3,2,1,0:T(8,128)(2,1)S(1)}, bf16[4,2,256,256]{3,2,1,0:T(8,128)(2,1)}, u32[]{:S(2)}) copy-start(bf16[4,2,256,256]{3,2,1,0:T(8,128)(2,1)} %get-tuple-element.44) | copy-start | bytes 3145732
  117.8 14.1 %copy-start.4 = (bf16[4,2,256,256]{3,2,1,0:T(8,128)(2,1)S(1)}, bf16[4,2,256,256]{3,2,1,0:T(8,128)(2,1)}, u32[]{:S(2)}) copy-start(bf16[4,2,256,256]{3,2,1,0:T(8,128)(2,1)} %get-tuple-element.48) | copy-start | bytes 3145732
  124.1 5.7 %copy-start.3 = (bf16[4,2,256,256]{3,2,1,0:T(8,128)(2,1)S(1)}, bf16[4,2,256,256]{3,2,1,0:T(8,128)(2,1)}, u32[]{:S(2)}) copy-start(bf16[4,2,256,256]{3,2,1,0:T(8,128)(2,1)} %get-tuple-element.46) | copy-start | bytes 3145732
  125.2 9.9 %copy-start.1 = (bf16[4,2,256,256]{3,2,1,0:T(8,128)(2,1)S(1)}, bf16[4,2,256,256]{3,2,1,0:T(8,128)(2,1)}, u32[]{:S(2)}) copy-start(bf16[4,2,256,256]{3,2,1,0:T(8,128)(2,1)} %get-tuple-element.50) | copy-start | bytes 3145732
  125.2 9.9 %collective-permute-start.29 = (bf16[2,256,256]{2,1,0:T(8,128)(2,1)S(1)}, bf16[2,256,256]{2,1,0:T(8,128)(2,1)S(1)}, u32[]{:S(2)}, u32[]{:S(2)}) collective-permute-start(bf16[2,256,256]{2,1,0:T(8,128)(2,1)S(1)} %slice_bitcast_fusion), channel_id=1, source_target_pairs={{1,0},{2,1},{3,2},{4,3},{5,4},{6,5},{7,6},{8,7},{9,8},{10,9},{11,1... | collective-permute-start | bytes 786440 | tf_op jit(solution)/shard_map/ppermute | solution.py:98
  127.4 10.5 %collective-permute-start.18 = (bf16[2,256,256]{2,1,0:T(8,128)(2,1)S(1)}, bf16[2,256,256]{2,1,0:T(8,128)(2,1)S(1)}, u32[]{:S(2)}, u32[]{:S(2)}) collective-permute-start(bf16[2,256,256]{2,1,0:T(8,128)(2,1)S(1)} %fusion.14), channel_id=1, source_target_pairs={{1,0},{2,1},{3,2},{4,3},{5,4},{6,5},{7,6},{8,7},{9,8},{10,9},{11,1... | collective-permute-start | bytes 786440 | tf_op jit(solution)/shard_map/ppermute | solution.py:98
  129.9 10.8 %collective-permute-start.22 = (bf16[2,256,256]{2,1,0:T(8,128)(2,1)S(1)}, bf16[2,256,256]{2,1,0:T(8,128)(2,1)S(1)}, u32[]{:S(2)}, u32[]{:S(2)}) collective-permute-start(bf16[2,256,256]{2,1,0:T(8,128)(2,1)S(1)} %fusion.11), channel_id=1, source_target_pairs={{1,0},{2,1},{3,2},{4,3},{5,4},{6,5},{7,6},{8,7},{9,8},{10,9},{11,1... | collective-permute-start | bytes 786440 | tf_op jit(solution)/shard_map/ppermute | solution.py:98
  132.0 11.6 %collective-permute-start.26 = (bf16[2,256,256]{2,1,0:T(8,128)(2,1)S(1)}, bf16[2,256,256]{2,1,0:T(8,128)(2,1)S(1)}, u32[]{:S(2)}, u32[]{:S(2)}) collective-permute-start(bf16[2,256,256]{2,1,0:T(8,128)(2,1)S(1)} %fusion.8), channel_id=1, source_target_pairs={{1,0},{2,1},{3,2},{4,3},{5,4},{6,5},{7,6},{8,7},{9,8},{10,9},{11,1... | collective-permute-start | bytes 786440 | tf_op jit(solution)/shard_map/ppermute | solution.py:98
  135.2 11.2 %collective-permute-start.30 = (bf16[2,256,256]{2,1,0:T(8,128)(2,1)S(1)}, bf16[2,256,256]{2,1,0:T(8,128)(2,1)S(1)}, u32[]{:S(2)}, u32[]{:S(2)}) collective-permute-start(bf16[2,256,256]{2,1,0:T(8,128)(2,1)S(1)} %fusion.5), channel_id=1, source_target_pairs={{1,0},{2,1},{3,2},{4,3},{5,4},{6,5},{7,6},{8,7},{9,8},{10,9},{11,1... | collective-permute-start | bytes 786440 | tf_op jit(solution)/shard_map/ppermute | solution.py:98
  138.0 11.2 %collective-permute-start.19 = (bf16[2,256,256]{2,1,0:T(8,128)(2,1)S(1)}, bf16[2,256,256]{2,1,0:T(8,128)(2,1)S(1)}, u32[]{:S(2)}, u32[]{:S(2)}) collective-permute-start(bf16[2,256,256]{2,1,0:T(8,128)(2,1)S(1)} %fusion.13), channel_id=1, source_target_pairs={{1,0},{2,1},{3,2},{4,3},{5,4},{6,5},{7,6},{8,7},{9,8},{10,9},{11,1... | collective-permute-start | bytes 786440 | tf_op jit(solution)/shard_map/ppermute | solution.py:98
  140.8 11.2 %collective-permute-start.23 = (bf16[2,256,256]{2,1,0:T(8,128)(2,1)S(1)}, bf16[2,256,256]{2,1,0:T(8,128)(2,1)S(1)}, u32[]{:S(2)}, u32[]{:S(2)}) collective-permute-start(bf16[2,256,256]{2,1,0:T(8,128)(2,1)S(1)} %fusion.10), channel_id=1, source_target_pairs={{1,0},{2,1},{3,2},{4,3},{5,4},{6,5},{7,6},{8,7},{9,8},{10,9},{11,1... | collective-permute-start | bytes 786440 | tf_op jit(solution)/shard_map/ppermute | solution.py:98
  143.6 11.2 %collective-permute-start.27 = (bf16[2,256,256]{2,1,0:T(8,128)(2,1)S(1)}, bf16[2,256,256]{2,1,0:T(8,128)(2,1)S(1)}, u32[]{:S(2)}, u32[]{:S(2)}) collective-permute-start(bf16[2,256,256]{2,1,0:T(8,128)(2,1)S(1)} %fusion.7), channel_id=1, source_target_pairs={{1,0},{2,1},{3,2},{4,3},{5,4},{6,5},{7,6},{8,7},{9,8},{10,9},{11,1... | collective-permute-start | bytes 786440 | tf_op jit(solution)/shard_map/ppermute | solution.py:98
  146.4 11.2 %collective-permute-start.31 = (bf16[2,256,256]{2,1,0:T(8,128)(2,1)S(1)}, bf16[2,256,256]{2,1,0:T(8,128)(2,1)S(1)}, u32[]{:S(2)}, u32[]{:S(2)}) collective-permute-start(bf16[2,256,256]{2,1,0:T(8,128)(2,1)S(1)} %fusion.4), channel_id=1, source_target_pairs={{1,0},{2,1},{3,2},{4,3},{5,4},{6,5},{7,6},{8,7},{9,8},{10,9},{11,1... | collective-permute-start | bytes 786440 | tf_op jit(solution)/shard_map/ppermute | solution.py:98
  149.2 11.2 %copy-start.5 = (f32[2,256,256]{2,1,0:T(8,128)S(1)}, f32[2,256,256]{2,1,0:T(8,128)}, u32[]{:S(2)}) copy-start(f32[2,256,256]{2,1,0:T(8,128)} %get-tuple-element.43) | copy-start | bytes 1572868
  149.2 11.2 %collective-permute-start.20 = (bf16[2,256,256]{2,1,0:T(8,128)(2,1)S(1)}, bf16[2,256,256]{2,1,0:T(8,128)(2,1)S(1)}, u32[]{:S(2)}, u32[]{:S(2)}) collective-permute-start(bf16[2,256,256]{2,1,0:T(8,128)(2,1)S(1)} %fusion.12), channel_id=1, source_target_pairs={{1,0},{2,1},{3,2},{4,3},{5,4},{6,5},{7,6},{8,7},{9,8},{10,9},{11,1... | collective-permute-start | bytes 786440 | tf_op jit(solution)/shard_map/ppermute | solution.py:98
  152.0 11.2 %collective-permute-start.24 = (bf16[2,256,256]{2,1,0:T(8,128)(2,1)S(1)}, bf16[2,256,256]{2,1,0:T(8,128)(2,1)S(1)}, u32[]{:S(2)}, u32[]{:S(2)}) collective-permute-start(bf16[2,256,256]{2,1,0:T(8,128)(2,1)S(1)} %fusion.9), channel_id=1, source_target_pairs={{1,0},{2,1},{3,2},{4,3},{5,4},{6,5},{7,6},{8,7},{9,8},{10,9},{11,1... | collective-permute-start | bytes 786440 | tf_op jit(solution)/shard_map/ppermute | solution.py:98
  154.9 8.4 %copy-start.7 = (f32[2,256,256]{2,1,0:T(8,128)S(1)}, f32[2,256,256]{2,1,0:T(8,128)}, u32[]{:S(2)}) copy-start(f32[2,256,256]{2,1,0:T(8,128)} %get-tuple-element.45) | copy-start | bytes 1572868
  154.9 11.1 %collective-permute-start.28 = (bf16[2,256,256]{2,1,0:T(8,128)(2,1)S(1)}, bf16[2,256,256]{2,1,0:T(8,128)(2,1)S(1)}, u32[]{:S(2)}, u32[]{:S(2)}) collective-permute-start(bf16[2,256,256]{2,1,0:T(8,128)(2,1)S(1)} %fusion.6), channel_id=1, source_target_pairs={{1,0},{2,1},{3,2},{4,3},{5,4},{6,5},{7,6},{8,7},{9,8},{10,9},{11,1... | collective-permute-start | bytes 786440 | tf_op jit(solution)/shard_map/ppermute | solution.py:98
  157.7 11.2 %collective-permute-start.32 = (bf16[2,256,256]{2,1,0:T(8,128)(2,1)S(1)}, bf16[2,256,256]{2,1,0:T(8,128)(2,1)S(1)}, u32[]{:S(2)}, u32[]{:S(2)}) collective-permute-start(bf16[2,256,256]{2,1,0:T(8,128)(2,1)S(1)} %fusion.3), channel_id=1, source_target_pairs={{1,0},{2,1},{3,2},{4,3},{5,4},{6,5},{7,6},{8,7},{9,8},{10,9},{11,1... | collective-permute-start | bytes 786440 | tf_op jit(solution)/shard_map/ppermute | solution.py:98
  160.5 5.6 %copy-start.8 = (f32[2,256,256]{2,1,0:T(8,128)S(1)}, f32[2,256,256]{2,1,0:T(8,128)}, u32[]{:S(2)}) copy-start(f32[2,256,256]{2,1,0:T(8,128)} %get-tuple-element.47) | copy-start | bytes 1572868
  166.0 2.8 %copy-start.6 = (f32[2,256,256]{2,1,0:T(8,128)S(1)}, f32[2,256,256]{2,1,0:T(8,128)}, u32[]{:S(2)}) copy-start(f32[2,256,256]{2,1,0:T(8,128)} %get-tuple-element.49) | copy-start | bytes 1572868

commit v7 on v5

--- a/solution.py
+++ b/solution.py
@@ -59,22 +59,22 @@
     own_ref[1] = value_back[(blocks - 1) * rows:]
 
 
-def attention_back(queries, grads, window_pieces, allowed, buffers, query_group, kv_group):
+def attention_back(queries, grads, window_pieces, allowed, buffers, query_group, kv_group, groups):
     rows, width = queries.shape
     head_size = width // (GROUP * KV_HEADS)
     group_width = GROUP * head_size
     span = rows * len(window_pieces)
-    q_spec = pl.BlockSpec((rows, group_width), lambda g, at: (0, at[0]))
-    piece_spec = pl.BlockSpec((2, rows, head_size), lambda g, at: (0, 0, at[1]))
+    q_spec = pl.BlockSpec((rows, group_width), lambda g, at: (0, g + at[0]))
+    piece_spec = pl.BlockSpec((2, rows, head_size), lambda g, at: (0, 0, g + at[1]))
     mask_spec = pl.BlockSpec((rows, span), lambda g, at: (0, 0))
     any_spec = pl.BlockSpec(memory_space=pl.ANY)
-    far_spec = pl.BlockSpec((len(window_pieces) - 1, 2, rows, head_size), lambda g, at: (0, 0, 0, at[1]))
-    own_spec = pl.BlockSpec((2, rows, head_size), lambda g, at: (0, 0, at[1]))
+    far_spec = pl.BlockSpec((len(window_pieces) - 1, 2, rows, head_size), lambda g, at: (0, 0, 0, g))
+    own_spec = pl.BlockSpec((2, rows, head_size), lambda g, at: (0, 0, g))
     inputs = [queries, grads, *window_pieces, allowed, *buffers]
     first_buffer = 1 + len(inputs) - len(buffers)
     grid_spec = pltpu.PrefetchScalarGridSpec(
         num_scalar_prefetch=1,
-        grid=(1,),
+        grid=(groups,),
         in_specs=[q_spec, q_spec] + [piece_spec] * len(window_pieces) + [mask_spec] + [any_spec] * 3,
         out_specs=[q_spec, far_spec, own_spec],
     )
@@ -133,51 +133,33 @@
         cols = slice(chunk * chunk_width, (chunk + 1) * chunk_width)
         return jnp.stack([keys_here[:, cols], values_here[:, cols]])
 
-    def return_hop(partial, far, block):
-        arrived = shifted(partial, "ctx", -1).astype(jnp.float32)
-        return (arrived + far[block].astype(jnp.float32)).astype(jnp.bfloat16)
+    windows = [[own_pair_of(chunk)] for chunk in range(CHUNKS)]
+    for _ in range(reach_blocks):
+        for chunk in range(CHUNKS):
+            windows[chunk].insert(0, shifted(windows[chunk][0], "ctx", 1))
 
-    def run_chunk(chunk, window_pieces, query_back, side_step, side_value):
+    query_back = jnp.zeros(queries.shape, jnp.bfloat16)
+    results = []
+    for chunk in range(CHUNKS):
         far = jnp.zeros((reach_blocks, 2, count_rows, chunk_width), jnp.bfloat16)
         own = jnp.zeros((2, count_rows, chunk_width), jnp.float32)
-        for group in range(chunk_groups):
-            side_value = side_step(group, side_value)
-            query_back, far, own = attention_back(
-                queries, arriving, window_pieces, mask, (query_back, far, own),
-                chunk * chunk_groups + group, group,
-            )
-        return query_back, far, own, side_value
+        query_back, far, own = attention_back(
+            queries, arriving, windows[chunk], mask, (query_back, far, own),
+            chunk * chunk_groups, 0, chunk_groups,
+        )
+        results.append((far, own))
 
-    query_back = jnp.zeros(queries.shape, jnp.bfloat16)
+    partials = [far[0] for far, _ in results]
+    for step in range(reach_blocks):
+        for chunk in range(CHUNKS):
+            far = results[chunk][0]
+            arrived = shifted(partials[chunk], "ctx", -1).astype(jnp.float32)
+            if step + 1 < reach_blocks:
+                partials[chunk] = (arrived + far[step + 1].astype(jnp.float32)).astype(jnp.bfloat16)
+            else:
+                partials[chunk] = arrived
 
-    relayed = own_pair_of(0)
-    window_a = [relayed]
-    for _ in range(reach_blocks):
-        relayed = shifted(relayed, "ctx", 1)
-        window_a.insert(0, relayed)
-
-    window_b = []
-
-    def forward_step(group, relayed_b):
-        window_b.insert(0, relayed_b)
-        return shifted(relayed_b, "ctx", 1)
-
-    query_back, far_a, own_a, relayed_b = run_chunk(0, window_a, query_back, forward_step, own_pair_of(1))
-    window_b.insert(0, relayed_b)
-
-    def return_step(group, partial):
-        if group + 1 < reach_blocks:
-            return return_hop(partial, far_a, group + 1)
-        return shifted(partial, "ctx", -1).astype(jnp.float32)
-
-    query_back, far_b, own_b, arrived_a = run_chunk(1, window_b, query_back, return_step, far_a[0])
-
-    partial_b = far_b[0]
-    for block in range(1, reach_blocks):
-        partial_b = return_hop(partial_b, far_b, block)
-    arrived_b = shifted(partial_b, "ctx", -1).astype(jnp.float32)
-
-    totals = [(own_a + arrived_a).astype(jnp.bfloat16), (own_b + arrived_b).astype(jnp.bfloat16)]
+    totals = [(own + arrived).astype(jnp.bfloat16) for (_, own), arrived in zip(results, partials)]
     return (
         query_back[None],
         jnp.concatenate([total[0] for total in totals], axis=1)[None],

time: 173 us -> 154 us (0.89)
  Pallas kernels: 50.6 us -> 32.9 us
    pallas_call x8 -> x2, Pallas kernels: 50.6 us -> 32.9 us  [attention_back(): pl.pallas_call(attention_back_kernel, grid_spec=grid_spec, out_shape=[jax...]
    another operation x8 -> x5, local copies, waits for them, and re-layouts: 7.38 us -> 5.88 us
  transfers between devices with their start and end apart: 17 -> 17, of which waited for: 11 -> 11; matrix products, arithmetic and copies ran while one was open for 8% -> 8% of each run, Pallas kernels for 29% -> 22%
where the time goes in v7:
time: 154 us; the launch traced here: 153 us
  starting transfers between devices  59.2 us (38%)
  waiting for transfers between devices  44.3 us (29%)
  Pallas kernels  32.9 us (21%)
  local copies, waits for them, and re-layouts  10.7 us (7%)
  other arithmetic  4.74 us (3%)
    ppermute x16, starting transfers between devices, shifted(): lax.ppermute(value, axis, [(source, source + steps) for source in range(i...  53.6 us
    ppermute x16, waiting for transfers between devices, shifted(): lax.ppermute(value, axis, [(source, source + steps) for source in range(i...  41.3 us
    pallas_call x2, Pallas kernels, attention_back(): pl.pallas_call(attention_back_kernel, grid_spec=grid_spec, out_shape=[jax...  32.9 us
    another operation x5, local copies, waits for them, and re-layouts  5.88 us
    ppermute x1, starting transfers between devices, passed_along(): lax.ppermute(shard, axis, [(i, (i + by) % count) for i in range(count)])  5.65 us
  transfers between devices with their start and end apart: 17, of which 11 were waited for; matrix products, arithmetic and copies ran while one was open for 8% of the time, Pallas kernels for 22%

profile of v7, /device:TPU:25, one launch (start us, length us, event | category | flops | bytes accessed | tf_op | source)
XLA Modules:
  0.0 152.8 jit_solution(2661370992703411141)
XLA Ops:
  0.6 1.3 slice_bitcast_fusion.6
  1.9 0.1 pad_maximum_fusion.1.refs_4_
  2.0 3.3 %collective-permute-start.5 = (bf16[2,256,512]{2,1,0:T(8,128)(2,1)S(1)}, bf16[2,256,512]{2,1,0:T(8,128)(2,1)S(1)}, u32[]{:S(2)}, u32[]{:S(2)}) collective-permute-start(bf16[2,256,512]{2,1,0:T(8,128)(2,1)S(1)} %pad_maximum_fusion.1.refs_4_), channel_id=1, source_target_pairs={{0,1},{1,2},{2,3},{3,4},{4,5},{5,6},{6,7},{7,8},{8,9},{9,10},{10,1... | collective-permute-start | bytes 1572872 | tf_op jit(solution)/shard_map/ppermute | solution.py:98
  5.3 0.1 pad_maximum_fusion.refs_4_
  5.4 1.9 %collective-permute-start.1 = (bf16[2,256,512]{2,1,0:T(8,128)(2,1)S(1)}, bf16[2,256,512]{2,1,0:T(8,128)(2,1)S(1)}, u32[]{:S(2)}, u32[]{:S(2)}) collective-permute-start(bf16[2,256,512]{2,1,0:T(8,128)(2,1)S(1)} %pad_maximum_fusion.refs_4_), channel_id=1, source_target_pairs={{0,1},{1,2},{2,3},{3,4},{4,5},{5,6},{6,7},{7,8},{8,9},{9,10},{10,1... | collective-permute-start | bytes 1572872 | tf_op jit(solution)/shard_map/ppermute | solution.py:98
  7.3 4.1 %collective-permute-done.5.refs_3_ = bf16[2,256,512]{2,1,0:T(8,128)(2,1)S(1)} collective-permute-done((bf16[2,256,512]{2,1,0:T(8,128)(2,1)S(1)}, bf16[2,256,512]{2,1,0:T(8,128)(2,1)S(1)}, u32[]{:S(2)}, u32[]{:S(2)}) %collective-permute-start.5) | collective-permute-done | bytes 524320 | tf_op jit(solution)/shard_map/ppermute | solution.py:98
  11.4 6.5 %collective-permute-start.6 = (bf16[2,256,512]{2,1,0:T(8,128)(2,1)S(1)}, bf16[2,256,512]{2,1,0:T(8,128)(2,1)}, u32[]{:S(2)}, u32[]{:S(2)}) collective-permute-start(bf16[2,256,512]{2,1,0:T(8,128)(2,1)S(1)} %collective-permute-done.5.refs_3_), channel_id=1, source_target_pairs={{0,1},{1,2},{2,3},{3,4},{4,5},{5,6},{6,7},{7,8},{8,9},{9,10},{10,1... | collective-permute-start | bytes 1572872 | tf_op jit(solution)/shard_map/ppermute | solution.py:98
  17.9 0.0 collective-permute-done.1.refs_3_
  18.0 0.0 copy-start.7
  18.0 5.6 %collective-permute-start.2 = (bf16[2,256,512]{2,1,0:T(8,128)(2,1)S(1)}, bf16[2,256,512]{2,1,0:T(8,128)(2,1)}, u32[]{:S(2)}, u32[]{:S(2)}) collective-permute-start(bf16[2,256,512]{2,1,0:T(8,128)(2,1)S(1)} %collective-permute-done.1.refs_3_), channel_id=1, source_target_pairs={{0,1},{1,2},{2,3},{3,4},{4,5},{5,6},{6,7},{7,8},{8,9},{9,10},{10,1... | collective-permute-start | bytes 1572872 | tf_op jit(solution)/shard_map/ppermute | solution.py:98
  23.6 0.5 collective-permute-done.6.refs_2_
  24.0 0.0 copy-done.8
  24.1 6.6 %collective-permute-start.7 = (bf16[2,256,512]{2,1,0:T(8,128)(2,1)}, bf16[2,256,512]{2,1,0:T(8,128)(2,1)}, u32[]{:S(2)}, u32[]{:S(2)}) collective-permute-start(bf16[2,256,512]{2,1,0:T(8,128)(2,1)} %collective-permute-done.6.refs_2_), channel_id=1, source_target_pairs={{0,1},{1,2},{2,3},{3,4},{4,5},{5,6},{6,7},{7,8},{8,9},{9,10},{10,1... | collective-permute-start | bytes 1572872 | tf_op jit(solution)/shard_map/ppermute | solution.py:98
  30.7 5.7 %collective-permute-start = (bf16[1,256,2048]{2,1,0:T(8,128)(2,1)}, bf16[1,256,2048]{2,1,0:T(8,128)(2,1)S(1)}, u32[]{:S(2)}, u32[]{:S(2)}) collective-permute-start(bf16[1,256,2048]{2,1,0:T(8,128)(2,1)} %param.10), channel_id=1, source_target_pairs={{0,224},{32,0},{64,32},{96,64},{128,96},{160,128},{192,160},{224,1... | collective-permute-start | bytes 3145736 | tf_op jit(solution)/shard_map/ppermute | solution.py:92
  36.3 0.0 copy-done.10
  36.3 0.2 reduce-window.8
  36.5 0.0 collective-permute-done.2.refs_2_
  36.5 2.2 %collective-permute-start.3 = (bf16[2,256,512]{2,1,0:T(8,128)(2,1)}, bf16[2,256,512]{2,1,0:T(8,128)(2,1)S(1)}, u32[]{:S(2)}, u32[]{:S(2)}) collective-permute-start(bf16[2,256,512]{2,1,0:T(8,128)(2,1)} %collective-permute-done.2.refs_2_), channel_id=1, source_target_pairs={{0,1},{1,2},{2,3},{3,4},{4,5},{5,6},{6,7},{7,8},{8,9},{9,10},{10,1... | collective-permute-start | bytes 1572872 | tf_op jit(solution)/shard_map/ppermute | solution.py:98
  38.7 0.1 convert_reduce_fusion.1
  38.8 0.1 convert_reduce_fusion
  38.9 0.0 collective-permute-done.7.refs_1_
  38.9 4.7 %collective-permute-start.8 = (bf16[2,256,512]{2,1,0:T(8,128)(2,1)}, bf16[2,256,512]{2,1,0:T(8,128)(2,1)}, u32[]{:S(2)}, u32[]{:S(2)}) collective-permute-start(bf16[2,256,512]{2,1,0:T(8,128)(2,1)} %collective-permute-done.7.refs_1_), channel_id=1, source_target_pairs={{0,1},{1,2},{2,3},{3,4},{4,5},{5,6},{6,7},{7,8},{8,9},{9,10},{10,1... | collective-permute-start | bytes 1572872 | tf_op jit(solution)/shard_map/ppermute | solution.py:98
  43.6 1.5 collective-permute-done.3.refs_1_
  45.1 6.4 %collective-permute-start.4 = (bf16[2,256,512]{2,1,0:T(8,128)(2,1)S(1)}, bf16[2,256,512]{2,1,0:T(8,128)(2,1)}, u32[]{:S(2)}, u32[]{:S(2)}) collective-permute-start(bf16[2,256,512]{2,1,0:T(8,128)(2,1)S(1)} %collective-permute-done.3.refs_1_), channel_id=1, source_target_pairs={{0,1},{1,2},{2,3},{3,4},{4,5},{5,6},{6,7},{7,8},{8,9},{9,10},{10,1... | collective-permute-start | bytes 1572872 | tf_op jit(solution)/shard_map/ppermute | solution.py:98
  51.5 1.4 convert_convert_fusion.refs_5_
  52.9 3.0 %collective-permute-done = bf16[1,256,2048]{2,1,0:T(8,128)(2,1)S(1)} collective-permute-done((bf16[1,256,2048]{2,1,0:T(8,128)(2,1)}, bf16[1,256,2048]{2,1,0:T(8,128)(2,1)S(1)}, u32[]{:S(2)}, u32[]{:S(2)}) %collective-permute-start) | collective-permute-done | bytes 1048608 | tf_op jit(solution)/shard_map/ppermute | solution.py:92
  55.9 0.0 collective-permute-done.8.refs_0_
  55.9 1.6 %broadcast_4_refs_7_.2.clone.refs_7_ = bf16[4,2,256,512]{3,2,1,0:T(8,128)(2,1)} broadcast(bf16[]{:T(256)} %constant.7.clone.1), dimensions={} | broadcast | bytes 2097154 | tf_op jit(solution)/shard_map/broadcast.4.refs_7_
  57.5 1.1 broadcast_3_refs_8_.2.clone.refs_8_
  58.6 1.1 broadcast_in_dim.8.refs_6_
  59.7 0.5 call_exported.0.at_ref
  60.3 16.4 %shard_map.94 = (bf16[256,2048]{1,0:T(8,128)(2,1)}, bf16[4,2,256,512]{3,2,1,0:T(8,128)(2,1)}, f32[2,256,512]{2,1,0:T(8,128)}) custom-call(s32[2]{0:T(128)} %call_exported.0.at_ref, bf16[256,2048]{1,0:T(8,128)(2,1)} %bitcast.50, bf16[256,2048]{1,0:T(8,128)(2,1)} %bitcast.52, ...), custom_call_target="tpu_custom_call", output_to_operand_aliasing={{0}: (9, {}), {1}: (10, {}), {2}: (11, {})} | custom-call | tf_op jit(solution)/shard_map/pallas_call | solution.py:81
  76.6 1.1 slice_bitcast_fusion.1
  77.7 1.9 %collective-permute-start.9 = (bf16[2,256,512]{2,1,0:T(8,128)(2,1)S(1)}, bf16[2,256,512]{2,1,0:T(8,128)(2,1)S(1)}, u32[]{:S(2)}, u32[]{:S(2)}) collective-permute-start(bf16[2,256,512]{2,1,0:T(8,128)(2,1)S(1)} %slice_bitcast_fusion.1), channel_id=1, source_target_pairs={{1,0},{2,1},{3,2},{4,3},{5,4},{6,5},{7,6},{8,7},{9,8},{10,9},{11,1... | collective-permute-start | bytes 1572872 | tf_op jit(solution)/shard_map/ppermute | solution.py:98
  79.7 0.0 collective-permute-done.4.refs_0_
  79.7 1.5 broadcast_4_refs_7_.2.refs_7_
  81.2 1.1 broadcast_3_refs_8_.2.refs_8_
  82.3 16.5 %shard_map.95 = (bf16[256,2048]{1,0:T(8,128)(2,1)}, bf16[4,2,256,512]{3,2,1,0:T(8,128)(2,1)}, f32[2,256,512]{2,1,0:T(8,128)}) custom-call(s32[2]{0:T(128)} %constant.29.clone.at_ref, bf16[256,2048]{1,0:T(8,128)(2,1)} %bitcast.51, bf16[256,2048]{1,0:T(8,128)(2,1)} %bitcast.53, ...), custom_call_target="tpu_custom_call", output_to_operand_aliasing={{0}: (9, {}), {1}: (10, {}), {2}: (11, {})} | custom-call | tf_op jit(solution)/shard_map/pallas_call | solution.py:81
  98.8 1.2 slice_bitcast_fusion
  100.0 2.7 %collective-permute-start.13 = (bf16[2,256,512]{2,1,0:T(8,128)(2,1)S(1)}, bf16[2,256,512]{2,1,0:T(8,128)(2,1)S(1)}, u32[]{:S(2)}, u32[]{:S(2)}) collective-permute-start(bf16[2,256,512]{2,1,0:T(8,128)(2,1)S(1)} %slice_bitcast_fusion), channel_id=1, source_target_pairs={{1,0},{2,1},{3,2},{4,3},{5,4},{6,5},{7,6},{8,7},{9,8},{10,9},{11,1... | collective-permute-start | bytes 1572872 | tf_op jit(solution)/shard_map/ppermute | solution.py:98
  102.8 0.0 collective-permute-done.9
  102.8 0.1 fusion.8
  102.9 1.9 %collective-permute-start.10 = (bf16[2,256,512]{2,1,0:T(8,128)(2,1)S(1)}, bf16[2,256,512]{2,1,0:T(8,128)(2,1)S(1)}, u32[]{:S(2)}, u32[]{:S(2)}) collective-permute-start(bf16[2,256,512]{2,1,0:T(8,128)(2,1)S(1)} %fusion.8), channel_id=1, source_target_pairs={{1,0},{2,1},{3,2},{4,3},{5,4},{6,5},{7,6},{8,7},{9,8},{10,9},{11,1... | collective-permute-start | bytes 1572872 | tf_op jit(solution)/shard_map/ppermute | solution.py:98
  104.8 7.8 %collective-permute-done.13 = bf16[2,256,512]{2,1,0:T(8,128)(2,1)S(1)} collective-permute-done((bf16[2,256,512]{2,1,0:T(8,128)(2,1)S(1)}, bf16[2,256,512]{2,1,0:T(8,128)(2,1)S(1)}, u32[]{:S(2)}, u32[]{:S(2)}) %collective-permute-start.13) | collective-permute-done | bytes 524320 | tf_op jit(solution)/shard_map/ppermute | solution.py:98
  112.6 0.1 fusion.5
  112.8 1.9 %collective-permute-start.14 = (bf16[2,256,512]{2,1,0:T(8,128)(2,1)S(1)}, bf16[2,256,512]{2,1,0:T(8,128)(2,1)S(1)}, u32[]{:S(2)}, u32[]{:S(2)}) collective-permute-start(bf16[2,256,512]{2,1,0:T(8,128)(2,1)S(1)} %fusion.5), channel_id=1, source_target_pairs={{1,0},{2,1},{3,2},{4,3},{5,4},{6,5},{7,6},{8,7},{9,8},{10,9},{11,1... | collective-permute-start | bytes 1572872 | tf_op jit(solution)/shard_map/ppermute | solution.py:98
  114.7 3.5 %collective-permute-done.10 = bf16[2,256,512]{2,1,0:T(8,128)(2,1)S(1)} collective-permute-done((bf16[2,256,512]{2,1,0:T(8,128)(2,1)S(1)}, bf16[2,256,512]{2,1,0:T(8,128)(2,1)S(1)}, u32[]{:S(2)}, u32[]{:S(2)}) %collective-permute-start.10) | collective-permute-done | bytes 524320 | tf_op jit(solution)/shard_map/ppermute | solution.py:98
  118.3 0.1 fusion.7
  118.4 2.1 %collective-permute-start.11 = (bf16[2,256,512]{2,1,0:T(8,128)(2,1)S(1)}, bf16[2,256,512]{2,1,0:T(8,128)(2,1)S(1)}, u32[]{:S(2)}, u32[]{:S(2)}) collective-permute-start(bf16[2,256,512]{2,1,0:T(8,128)(2,1)S(1)} %fusion.7), channel_id=1, source_target_pairs={{1,0},{2,1},{3,2},{4,3},{5,4},{6,5},{7,6},{8,7},{9,8},{10,9},{11,1... | collective-permute-start | bytes 1572872 | tf_op jit(solution)/shard_map/ppermute | solution.py:98
  120.5 4.9 %collective-permute-done.14 = bf16[2,256,512]{2,1,0:T(8,128)(2,1)S(1)} collective-permute-done((bf16[2,256,512]{2,1,0:T(8,128)(2,1)S(1)}, bf16[2,256,512]{2,1,0:T(8,128)(2,1)S(1)}, u32[]{:S(2)}, u32[]{:S(2)}) %collective-permute-start.14) | collective-permute-done | bytes 524320 | tf_op jit(solution)/shard_map/ppermute | solution.py:98
  125.4 0.1 fusion.4
  125.5 1.9 %collective-permute-start.15 = (bf16[2,256,512]{2,1,0:T(8,128)(2,1)S(1)}, bf16[2,256,512]{2,1,0:T(8,128)(2,1)S(1)}, u32[]{:S(2)}, u32[]{:S(2)}) collective-permute-start(bf16[2,256,512]{2,1,0:T(8,128)(2,1)S(1)} %fusion.4), channel_id=1, source_target_pairs={{1,0},{2,1},{3,2},{4,3},{5,4},{6,5},{7,6},{8,7},{9,8},{10,9},{11,1... | collective-permute-start | bytes 1572872 | tf_op jit(solution)/shard_map/ppermute | solution.py:98
  127.5 3.7 %collective-permute-done.11 = bf16[2,256,512]{2,1,0:T(8,128)(2,1)S(1)} collective-permute-done((bf16[2,256,512]{2,1,0:T(8,128)(2,1)S(1)}, bf16[2,256,512]{2,1,0:T(8,128)(2,1)S(1)}, u32[]{:S(2)}, u32[]{:S(2)}) %collective-permute-start.11) | collective-permute-done | bytes 524320 | tf_op jit(solution)/shard_map/ppermute | solution.py:98
  131.1 0.1 fusion.6
  131.3 2.1 %collective-permute-start.12 = (bf16[2,256,512]{2,1,0:T(8,128)(2,1)S(1)}, bf16[2,256,512]{2,1,0:T(8,128)(2,1)S(1)}, u32[]{:S(2)}, u32[]{:S(2)}) collective-permute-start(bf16[2,256,512]{2,1,0:T(8,128)(2,1)S(1)} %fusion.6), channel_id=1, source_target_pairs={{1,0},{2,1},{3,2},{4,3},{5,4},{6,5},{7,6},{8,7},{9,8},{10,9},{11,1... | collective-permute-start | bytes 1572872 | tf_op jit(solution)/shard_map/ppermute | solution.py:98
  133.3 4.8 %collective-permute-done.15 = bf16[2,256,512]{2,1,0:T(8,128)(2,1)S(1)} collective-permute-done((bf16[2,256,512]{2,1,0:T(8,128)(2,1)S(1)}, bf16[2,256,512]{2,1,0:T(8,128)(2,1)S(1)}, u32[]{:S(2)}, u32[]{:S(2)}) %collective-permute-start.15) | collective-permute-done | bytes 524320 | tf_op jit(solution)/shard_map/ppermute | solution.py:98
  138.1 0.1 fusion.3
  138.3 1.9 %collective-permute-start.16 = (bf16[2,256,512]{2,1,0:T(8,128)(2,1)S(1)}, bf16[2,256,512]{2,1,0:T(8,128)(2,1)S(1)}, u32[]{:S(2)}, u32[]{:S(2)}) collective-permute-start(bf16[2,256,512]{2,1,0:T(8,128)(2,1)S(1)} %fusion.3), channel_id=1, source_target_pairs={{1,0},{2,1},{3,2},{4,3},{5,4},{6,5},{7,6},{8,7},{9,8},{10,9},{11,1... | collective-permute-start | bytes 1572872 | tf_op jit(solution)/shard_map/ppermute | solution.py:98
  140.2 3.8 %collective-permute-done.12 = bf16[2,256,512]{2,1,0:T(8,128)(2,1)S(1)} collective-permute-done((bf16[2,256,512]{2,1,0:T(8,128)(2,1)S(1)}, bf16[2,256,512]{2,1,0:T(8,128)(2,1)S(1)}, u32[]{:S(2)}, u32[]{:S(2)}) %collective-permute-start.12) | collective-permute-done | bytes 524320 | tf_op jit(solution)/shard_map/ppermute | solution.py:98
  144.0 0.2 add_convert_fusion.1
  144.2 6.6 %collective-permute-done.16 = bf16[2,256,512]{2,1,0:T(8,128)(2,1)S(1)} collective-permute-done((bf16[2,256,512]{2,1,0:T(8,128)(2,1)S(1)}, bf16[2,256,512]{2,1,0:T(8,128)(2,1)S(1)}, u32[]{:S(2)}, u32[]{:S(2)}) %collective-permute-start.16) | collective-permute-done | bytes 524320 | tf_op jit(solution)/shard_map/ppermute | solution.py:98
  150.9 0.2 add_convert_fusion
  151.1 0.9 maximum_bitcast_fusion.1
  152.0 0.9 maximum_bitcast_fusion
  (24 shorter events, 0.1 us)
Async XLA Ops:
  0.6 35.7 %copy-start.10 = (s32[4]{0:T(128)S(1)}, s32[4]{0:T(128)}, u32[]{:S(2)}) copy-start(s32[4]{0:T(128)} %param.11) | copy-start | bytes 52
  2.0 56.6 %copy-start.6 = (bf16[2,256,512]{2,1,0:T(8,128)(2,1)}, bf16[2,256,512]{2,1,0:T(8,128)(2,1)S(1)}, u32[]{:S(2)}) copy-start(bf16[2,256,512]{2,1,0:T(8,128)(2,1)S(1)} %pad_maximum_fusion.1.refs_4_) | copy-start | bytes 1572868
  2.0 9.4 %collective-permute-start.5 = (bf16[2,256,512]{2,1,0:T(8,128)(2,1)S(1)}, bf16[2,256,512]{2,1,0:T(8,128)(2,1)S(1)}, u32[]{:S(2)}, u32[]{:S(2)}) collective-permute-start(bf16[2,256,512]{2,1,0:T(8,128)(2,1)S(1)} %pad_maximum_fusion.1.refs_4_), channel_id=1, source_target_pairs={{0,1},{1,2},{2,3},{3,4},{4,5},{5,6},{6,7},{7,8},{8,9},{9,10},{10,1... | collective-permute-start | bytes 1572872 | tf_op jit(solution)/shard_map/ppermute | solution.py:98
  5.4 54.3 %copy-start.5 = (bf16[2,256,512]{2,1,0:T(8,128)(2,1)}, bf16[2,256,512]{2,1,0:T(8,128)(2,1)S(1)}, u32[]{:S(2)}) copy-start(bf16[2,256,512]{2,1,0:T(8,128)(2,1)S(1)} %pad_maximum_fusion.refs_4_) | copy-start | bytes 1572868
  5.4 12.5 %collective-permute-start.1 = (bf16[2,256,512]{2,1,0:T(8,128)(2,1)S(1)}, bf16[2,256,512]{2,1,0:T(8,128)(2,1)S(1)}, u32[]{:S(2)}, u32[]{:S(2)}) collective-permute-start(bf16[2,256,512]{2,1,0:T(8,128)(2,1)S(1)} %pad_maximum_fusion.refs_4_), channel_id=1, source_target_pairs={{0,1},{1,2},{2,3},{3,4},{4,5},{5,6},{6,7},{7,8},{8,9},{9,10},{10,1... | collective-permute-start | bytes 1572872 | tf_op jit(solution)/shard_map/ppermute | solution.py:98
  11.4 12.6 %copy-start.8 = (bf16[2,256,512]{2,1,0:T(8,128)(2,1)}, bf16[2,256,512]{2,1,0:T(8,128)(2,1)S(1)}, u32[]{:S(2)}) copy-start(bf16[2,256,512]{2,1,0:T(8,128)(2,1)S(1)} %collective-permute-done.5.refs_3_) | copy-start | bytes 1572868
  11.4 12.6 %collective-permute-start.6 = (bf16[2,256,512]{2,1,0:T(8,128)(2,1)S(1)}, bf16[2,256,512]{2,1,0:T(8,128)(2,1)}, u32[]{:S(2)}, u32[]{:S(2)}) collective-permute-start(bf16[2,256,512]{2,1,0:T(8,128)(2,1)S(1)} %collective-permute-done.5.refs_3_), channel_id=1, source_target_pairs={{0,1},{1,2},{2,3},{3,4},{4,5},{5,6},{6,7},{7,8},{8,9},{9,10},{10,1... | collective-permute-start | bytes 1572872 | tf_op jit(solution)/shard_map/ppermute | solution.py:98
  18.0 41.8 %copy-start.7 = (bf16[2,256,512]{2,1,0:T(8,128)(2,1)}, bf16[2,256,512]{2,1,0:T(8,128)(2,1)S(1)}, u32[]{:S(2)}) copy-start(bf16[2,256,512]{2,1,0:T(8,128)(2,1)S(1)} %collective-permute-done.1.refs_3_) | copy-start | bytes 1572868
  18.0 18.5 %collective-permute-start.2 = (bf16[2,256,512]{2,1,0:T(8,128)(2,1)S(1)}, bf16[2,256,512]{2,1,0:T(8,128)(2,1)}, u32[]{:S(2)}, u32[]{:S(2)}) collective-permute-start(bf16[2,256,512]{2,1,0:T(8,128)(2,1)S(1)} %collective-permute-done.1.refs_3_), channel_id=1, source_target_pairs={{0,1},{1,2},{2,3},{3,4},{4,5},{5,6},{6,7},{7,8},{8,9},{9,10},{10,1... | collective-permute-start | bytes 1572872 | tf_op jit(solution)/shard_map/ppermute | solution.py:98
  24.1 14.8 %collective-permute-start.7 = (bf16[2,256,512]{2,1,0:T(8,128)(2,1)}, bf16[2,256,512]{2,1,0:T(8,128)(2,1)}, u32[]{:S(2)}, u32[]{:S(2)}) collective-permute-start(bf16[2,256,512]{2,1,0:T(8,128)(2,1)} %collective-permute-done.6.refs_2_), channel_id=1, source_target_pairs={{0,1},{1,2},{2,3},{3,4},{4,5},{5,6},{6,7},{7,8},{8,9},{9,10},{10,1... | collective-permute-start | bytes 1572872 | tf_op jit(solution)/shard_map/ppermute | solution.py:98
  30.7 25.2 %collective-permute-start = (bf16[1,256,2048]{2,1,0:T(8,128)(2,1)}, bf16[1,256,2048]{2,1,0:T(8,128)(2,1)S(1)}, u32[]{:S(2)}, u32[]{:S(2)}) collective-permute-start(bf16[1,256,2048]{2,1,0:T(8,128)(2,1)} %param.10), channel_id=1, source_target_pairs={{0,224},{32,0},{64,32},{96,64},{128,96},{160,128},{192,160},{224,1... | collective-permute-start | bytes 3145736 | tf_op jit(solution)/shard_map/ppermute | solution.py:92
  36.5 8.6 %collective-permute-start.3 = (bf16[2,256,512]{2,1,0:T(8,128)(2,1)}, bf16[2,256,512]{2,1,0:T(8,128)(2,1)S(1)}, u32[]{:S(2)}, u32[]{:S(2)}) collective-permute-start(bf16[2,256,512]{2,1,0:T(8,128)(2,1)} %collective-permute-done.2.refs_2_), channel_id=1, source_target_pairs={{0,1},{1,2},{2,3},{3,4},{4,5},{5,6},{6,7},{7,8},{8,9},{9,10},{10,1... | collective-permute-start | bytes 1572872 | tf_op jit(solution)/shard_map/ppermute | solution.py:98
  38.9 17.0 %collective-permute-start.8 = (bf16[2,256,512]{2,1,0:T(8,128)(2,1)}, bf16[2,256,512]{2,1,0:T(8,128)(2,1)}, u32[]{:S(2)}, u32[]{:S(2)}) collective-permute-start(bf16[2,256,512]{2,1,0:T(8,128)(2,1)} %collective-permute-done.7.refs_1_), channel_id=1, source_target_pairs={{0,1},{1,2},{2,3},{3,4},{4,5},{5,6},{6,7},{7,8},{8,9},{9,10},{10,1... | collective-permute-start | bytes 1572872 | tf_op jit(solution)/shard_map/ppermute | solution.py:98
  45.1 14.6 %copy-start.9 = (bf16[2,256,512]{2,1,0:T(8,128)(2,1)}, bf16[2,256,512]{2,1,0:T(8,128)(2,1)S(1)}, u32[]{:S(2)}) copy-start(bf16[2,256,512]{2,1,0:T(8,128)(2,1)S(1)} %collective-permute-done.3.refs_1_) | copy-start | bytes 1572868
  45.1 34.5 %collective-permute-start.4 = (bf16[2,256,512]{2,1,0:T(8,128)(2,1)S(1)}, bf16[2,256,512]{2,1,0:T(8,128)(2,1)}, u32[]{:S(2)}, u32[]{:S(2)}) collective-permute-start(bf16[2,256,512]{2,1,0:T(8,128)(2,1)S(1)} %collective-permute-done.3.refs_1_), channel_id=1, source_target_pairs={{0,1},{1,2},{2,3},{3,4},{4,5},{5,6},{6,7},{7,8},{8,9},{9,10},{10,1... | collective-permute-start | bytes 1572872 | tf_op jit(solution)/shard_map/ppermute | solution.py:98
  55.9 3.9 %copy-start.4 = (bf16[1,256,2048]{2,1,0:T(8,128)(2,1)}, bf16[1,256,2048]{2,1,0:T(8,128)(2,1)S(1)}, u32[]{:S(2)}) copy-start(bf16[1,256,2048]{2,1,0:T(8,128)(2,1)S(1)} %collective-permute-done) | copy-start | bytes 3145732
  77.7 25.0 %collective-permute-start.9 = (bf16[2,256,512]{2,1,0:T(8,128)(2,1)S(1)}, bf16[2,256,512]{2,1,0:T(8,128)(2,1)S(1)}, u32[]{:S(2)}, u32[]{:S(2)}) collective-permute-start(bf16[2,256,512]{2,1,0:T(8,128)(2,1)S(1)} %slice_bitcast_fusion.1), channel_id=1, source_target_pairs={{1,0},{2,1},{3,2},{4,3},{5,4},{6,5},{7,6},{8,7},{9,8},{10,9},{11,1... | collective-permute-start | bytes 1572872 | tf_op jit(solution)/shard_map/ppermute | solution.py:98
  82.3 20.5 %copy-start.1 = (bf16[4,2,256,512]{3,2,1,0:T(8,128)(2,1)S(1)}, bf16[4,2,256,512]{3,2,1,0:T(8,128)(2,1)}, u32[]{:S(2)}) copy-start(bf16[4,2,256,512]{3,2,1,0:T(8,128)(2,1)} %get-tuple-element.12) | copy-start | bytes 6291460
  98.8 13.8 %copy-start = (bf16[4,2,256,512]{3,2,1,0:T(8,128)(2,1)S(1)}, bf16[4,2,256,512]{3,2,1,0:T(8,128)(2,1)}, u32[]{:S(2)}) copy-start(bf16[4,2,256,512]{3,2,1,0:T(8,128)(2,1)} %get-tuple-element.14) | copy-start | bytes 6291460
  100.0 12.6 %collective-permute-start.13 = (bf16[2,256,512]{2,1,0:T(8,128)(2,1)S(1)}, bf16[2,256,512]{2,1,0:T(8,128)(2,1)S(1)}, u32[]{:S(2)}, u32[]{:S(2)}) collective-permute-start(bf16[2,256,512]{2,1,0:T(8,128)(2,1)S(1)} %slice_bitcast_fusion), channel_id=1, source_target_pairs={{1,0},{2,1},{3,2},{4,3},{5,4},{6,5},{7,6},{8,7},{9,8},{10,9},{11,1... | collective-permute-start | bytes 1572872 | tf_op jit(solution)/shard_map/ppermute | solution.py:98
  102.9 15.3 %collective-permute-start.10 = (bf16[2,256,512]{2,1,0:T(8,128)(2,1)S(1)}, bf16[2,256,512]{2,1,0:T(8,128)(2,1)S(1)}, u32[]{:S(2)}, u32[]{:S(2)}) collective-permute-start(bf16[2,256,512]{2,1,0:T(8,128)(2,1)S(1)} %fusion.8), channel_id=1, source_target_pairs={{1,0},{2,1},{3,2},{4,3},{5,4},{6,5},{7,6},{8,7},{9,8},{10,9},{11,1... | collective-permute-start | bytes 1572872 | tf_op jit(solution)/shard_map/ppermute | solution.py:98
  112.8 12.6 %collective-permute-start.14 = (bf16[2,256,512]{2,1,0:T(8,128)(2,1)S(1)}, bf16[2,256,512]{2,1,0:T(8,128)(2,1)S(1)}, u32[]{:S(2)}, u32[]{:S(2)}) collective-permute-start(bf16[2,256,512]{2,1,0:T(8,128)(2,1)S(1)} %fusion.5), channel_id=1, source_target_pairs={{1,0},{2,1},{3,2},{4,3},{5,4},{6,5},{7,6},{8,7},{9,8},{10,9},{11,1... | collective-permute-start | bytes 1572872 | tf_op jit(solution)/shard_map/ppermute | solution.py:98
  118.4 25.6 %copy-start.3 = (f32[2,256,512]{2,1,0:T(8,128)S(1)}, f32[2,256,512]{2,1,0:T(8,128)}, u32[]{:S(2)}) copy-start(f32[2,256,512]{2,1,0:T(8,128)} %get-tuple-element.11) | copy-start | bytes 3145732
  118.4 12.7 %collective-permute-start.11 = (bf16[2,256,512]{2,1,0:T(8,128)(2,1)S(1)}, bf16[2,256,512]{2,1,0:T(8,128)(2,1)S(1)}, u32[]{:S(2)}, u32[]{:S(2)}) collective-permute-start(bf16[2,256,512]{2,1,0:T(8,128)(2,1)S(1)} %fusion.7), channel_id=1, source_target_pairs={{1,0},{2,1},{3,2},{4,3},{5,4},{6,5},{7,6},{8,7},{9,8},{10,9},{11,1... | collective-permute-start | bytes 1572872 | tf_op jit(solution)/shard_map/ppermute | solution.py:98
  125.5 12.6 %collective-permute-start.15 = (bf16[2,256,512]{2,1,0:T(8,128)(2,1)S(1)}, bf16[2,256,512]{2,1,0:T(8,128)(2,1)S(1)}, u32[]{:S(2)}, u32[]{:S(2)}) collective-permute-start(bf16[2,256,512]{2,1,0:T(8,128)(2,1)S(1)} %fusion.4), channel_id=1, source_target_pairs={{1,0},{2,1},{3,2},{4,3},{5,4},{6,5},{7,6},{8,7},{9,8},{10,9},{11,1... | collective-permute-start | bytes 1572872 | tf_op jit(solution)/shard_map/ppermute | solution.py:98
  131.3 19.6 %copy-start.2 = (f32[2,256,512]{2,1,0:T(8,128)S(1)}, f32[2,256,512]{2,1,0:T(8,128)}, u32[]{:S(2)}) copy-start(f32[2,256,512]{2,1,0:T(8,128)} %get-tuple-element.13) | copy-start | bytes 3145732
  131.3 12.7 %collective-permute-start.12 = (bf16[2,256,512]{2,1,0:T(8,128)(2,1)S(1)}, bf16[2,256,512]{2,1,0:T(8,128)(2,1)S(1)}, u32[]{:S(2)}, u32[]{:S(2)}) collective-permute-start(bf16[2,256,512]{2,1,0:T(8,128)(2,1)S(1)} %fusion.6), channel_id=1, source_target_pairs={{1,0},{2,1},{3,2},{4,3},{5,4},{6,5},{7,6},{8,7},{9,8},{10,9},{11,1... | collective-permute-start | bytes 1572872 | tf_op jit(solution)/shard_map/ppermute | solution.py:98
  138.3 12.6 %collective-permute-start.16 = (bf16[2,256,512]{2,1,0:T(8,128)(2,1)S(1)}, bf16[2,256,512]{2,1,0:T(8,128)(2,1)S(1)}, u32[]{:S(2)}, u32[]{:S(2)}) collective-permute-start(bf16[2,256,512]{2,1,0:T(8,128)(2,1)S(1)} %fusion.3), channel_id=1, source_target_pairs={{1,0},{2,1},{3,2},{4,3},{5,4},{6,5},{7,6},{8,7},{9,8},{10,9},{11,1... | collective-permute-start | bytes 1572872 | tf_op jit(solution)/shard_map/ppermute | solution.py:98

commit v8 on v7

--- a/solution.py
+++ b/solution.py
@@ -20,7 +20,7 @@
 
 
 def attention_back_kernel(at_ref, q_ref, do_ref, *refs):
-    blocks = len(refs) - 7
+    blocks = len(refs) - 4
     piece_refs = refs[:blocks]
     mask_ref = refs[blocks]
     dq_ref, far_ref, own_ref = refs[-3:]
@@ -39,8 +39,8 @@
     scores = SCORE_SCALE * product(queries, keys, nt)
     scores = jnp.where(allowed, scores, -jnp.inf)
     highest = jnp.max(scores, axis=-1, keepdims=True)
-    log_total = highest + jnp.log(jnp.sum(jnp.exp(scores - highest), axis=-1, keepdims=True))
-    weights = jnp.exp(scores - log_total)
+    shifted_exp = jnp.exp(scores - highest)
+    weights = shifted_exp * (1.0 / jnp.sum(shifted_exp, axis=-1, keepdims=True))
     weight_half = weights.astype(jnp.bfloat16)
     attended = product(weight_half, values, nn).astype(jnp.bfloat16)
     row_dot = jnp.sum(attended.astype(jnp.float32) * grads.astype(jnp.float32), axis=-1, keepdims=True)
@@ -59,7 +59,7 @@
     own_ref[1] = value_back[(blocks - 1) * rows:]
 
 
-def attention_back(queries, grads, window_pieces, allowed, buffers, query_group, kv_group, groups):
+def attention_back(queries, grads, window_pieces, allowed, query_group, kv_group, groups):
     rows, width = queries.shape
     head_size = width // (GROUP * KV_HEADS)
     group_width = GROUP * head_size
@@ -67,22 +67,25 @@
     q_spec = pl.BlockSpec((rows, group_width), lambda g, at: (0, g + at[0]))
     piece_spec = pl.BlockSpec((2, rows, head_size), lambda g, at: (0, 0, g + at[1]))
     mask_spec = pl.BlockSpec((rows, span), lambda g, at: (0, 0))
-    any_spec = pl.BlockSpec(memory_space=pl.ANY)
     far_spec = pl.BlockSpec((len(window_pieces) - 1, 2, rows, head_size), lambda g, at: (0, 0, 0, g))
     own_spec = pl.BlockSpec((2, rows, head_size), lambda g, at: (0, 0, g))
-    inputs = [queries, grads, *window_pieces, allowed, *buffers]
-    first_buffer = 1 + len(inputs) - len(buffers)
+    inputs = [queries, grads, *window_pieces, allowed]
+    dq_spec = pl.BlockSpec((rows, group_width), lambda g, at: (0, g))
     grid_spec = pltpu.PrefetchScalarGridSpec(
         num_scalar_prefetch=1,
         grid=(groups,),
-        in_specs=[q_spec, q_spec] + [piece_spec] * len(window_pieces) + [mask_spec] + [any_spec] * 3,
-        out_specs=[q_spec, far_spec, own_spec],
+        in_specs=[q_spec, q_spec] + [piece_spec] * len(window_pieces) + [mask_spec],
+        out_specs=[dq_spec, far_spec, own_spec],
     )
+    chunk_width = groups * head_size
     return pl.pallas_call(
         attention_back_kernel,
         grid_spec=grid_spec,
-        out_shape=[jax.ShapeDtypeStruct(b.shape, b.dtype) for b in buffers],
-        input_output_aliases={first_buffer + i: i for i in range(3)},
+        out_shape=[
+            jax.ShapeDtypeStruct((rows, groups * group_width), jnp.bfloat16),
+            jax.ShapeDtypeStruct((len(window_pieces) - 1, 2, rows, chunk_width), jnp.bfloat16),
+            jax.ShapeDtypeStruct((2, rows, chunk_width), jnp.float32),
+        ],
         compiler_params=pltpu.CompilerParams(vmem_limit_bytes=60 * 1024 * 1024),
     )(jnp.array([query_group, kv_group], jnp.int32), *inputs)
 
@@ -138,16 +141,15 @@
         for chunk in range(CHUNKS):
             windows[chunk].insert(0, shifted(windows[chunk][0], "ctx", 1))
 
-    query_back = jnp.zeros(queries.shape, jnp.bfloat16)
+    query_parts = []
     results = []
     for chunk in range(CHUNKS):
-        far = jnp.zeros((reach_blocks, 2, count_rows, chunk_width), jnp.bfloat16)
-        own = jnp.zeros((2, count_rows, chunk_width), jnp.float32)
-        query_back, far, own = attention_back(
-            queries, arriving, windows[chunk], mask, (query_back, far, own),
-            chunk * chunk_groups, 0, chunk_groups,
+        query_part, far, own = attention_back(
+            queries, arriving, windows[chunk], mask, chunk * chunk_groups, 0, chunk_groups
         )
+        query_parts.append(query_part)
         results.append((far, own))
+    query_back = jnp.concatenate(query_parts, axis=1)
 
     partials = [far[0] for far, _ in results]
     for step in range(reach_blocks):

time: 154 us -> 148 us (0.961)
  local copies, waits for them, and re-layouts: 10.7 us -> 4.83 us
    another operation x5 -> x1, local copies, waits for them, and re-layouts: 5.88 us -> 0.62 us
  transfers between devices with their start and end apart: 17 -> 17, of which waited for: 11 -> 11; matrix products, arithmetic and copies ran while one was open for 8% -> 5% of each run, Pallas kernels for 22% -> 22%
where the time goes in v8:
time: 148 us; the launch traced here: 147 us
  starting transfers between devices  59.5 us (40%)
  waiting for transfers between devices  43.1 us (29%)
  Pallas kernels  32.7 us (22%)
  other arithmetic  5.84 us (4%)
  local copies, waits for them, and re-layouts  4.83 us (3%)
    ppermute x16, starting transfers between devices, shifted(): lax.ppermute(value, axis, [(source, source + steps) for source in range(i...  53.8 us
    ppermute x16, waiting for transfers between devices, shifted(): lax.ppermute(value, axis, [(source, source + steps) for source in range(i...  40.2 us
    pallas_call x2, Pallas kernels, attention_back(): pl.pallas_call(attention_back_kernel, grid_spec=grid_spec, out_shape=[jax...  32.7 us
    ppermute x1, starting transfers between devices, passed_along(): lax.ppermute(shard, axis, [(i, (i + by) % count) for i in range(count)])  5.65 us
  transfers between devices with their start and end apart: 17, of which 11 were waited for; matrix products, arithmetic and copies ran while one was open for 5% of the time, Pallas kernels for 22%

profile of v8, /device:TPU:25, one launch (start us, length us, event | category | flops | bytes accessed | tf_op | source)
XLA Modules:
  0.0 146.9 jit_solution(18300352982948334518)
XLA Ops:
  0.6 0.0 copy-start.12
  0.6 1.3 slice_bitcast_fusion.8
  1.9 0.1 pad_maximum_fusion.refs_4_
  2.0 3.3 %collective-permute-start.1 = (bf16[2,256,512]{2,1,0:T(8,128)(2,1)S(1)}, bf16[2,256,512]{2,1,0:T(8,128)(2,1)S(1)}, u32[]{:S(2)}, u32[]{:S(2)}) collective-permute-start(bf16[2,256,512]{2,1,0:T(8,128)(2,1)S(1)} %pad_maximum_fusion.refs_4_), channel_id=1, source_target_pairs={{0,1},{1,2},{2,3},{3,4},{4,5},{5,6},{6,7},{7,8},{8,9},{9,10},{10,1... | collective-permute-start | bytes 1572872 | tf_op jit(solution)/shard_map/ppermute | solution.py:101
  5.3 0.1 pad_maximum_fusion.1.refs_4_
  5.4 0.0 copy-start.3
  5.4 1.9 %collective-permute-start.5 = (bf16[2,256,512]{2,1,0:T(8,128)(2,1)S(1)}, bf16[2,256,512]{2,1,0:T(8,128)(2,1)S(1)}, u32[]{:S(2)}, u32[]{:S(2)}) collective-permute-start(bf16[2,256,512]{2,1,0:T(8,128)(2,1)S(1)} %pad_maximum_fusion.1.refs_4_), channel_id=1, source_target_pairs={{0,1},{1,2},{2,3},{3,4},{4,5},{5,6},{6,7},{7,8},{8,9},{9,10},{10,1... | collective-permute-start | bytes 1572872 | tf_op jit(solution)/shard_map/ppermute | solution.py:101
  7.3 4.1 %collective-permute-done.1.refs_3_ = bf16[2,256,512]{2,1,0:T(8,128)(2,1)S(1)} collective-permute-done((bf16[2,256,512]{2,1,0:T(8,128)(2,1)S(1)}, bf16[2,256,512]{2,1,0:T(8,128)(2,1)S(1)}, u32[]{:S(2)}, u32[]{:S(2)}) %collective-permute-start.1) | collective-permute-done | bytes 524320 | tf_op jit(solution)/shard_map/ppermute | solution.py:101
  11.4 6.5 %collective-permute-start.2 = (bf16[2,256,512]{2,1,0:T(8,128)(2,1)S(1)}, bf16[2,256,512]{2,1,0:T(8,128)(2,1)}, u32[]{:S(2)}, u32[]{:S(2)}) collective-permute-start(bf16[2,256,512]{2,1,0:T(8,128)(2,1)S(1)} %collective-permute-done.1.refs_3_), channel_id=1, source_target_pairs={{0,1},{1,2},{2,3},{3,4},{4,5},{5,6},{6,7},{7,8},{8,9},{9,10},{10,1... | collective-permute-start | bytes 1572872 | tf_op jit(solution)/shard_map/ppermute | solution.py:101
  17.9 0.0 collective-permute-done.5.refs_3_
  17.9 0.0 copy-start.9
  17.9 5.6 %collective-permute-start.6 = (bf16[2,256,512]{2,1,0:T(8,128)(2,1)S(1)}, bf16[2,256,512]{2,1,0:T(8,128)(2,1)}, u32[]{:S(2)}, u32[]{:S(2)}) collective-permute-start(bf16[2,256,512]{2,1,0:T(8,128)(2,1)S(1)} %collective-permute-done.5.refs_3_), channel_id=1, source_target_pairs={{0,1},{1,2},{2,3},{3,4},{4,5},{5,6},{6,7},{7,8},{8,9},{9,10},{10,1... | collective-permute-start | bytes 1572872 | tf_op jit(solution)/shard_map/ppermute | solution.py:101
  23.5 0.5 collective-permute-done.2.refs_2_
  24.0 6.6 %collective-permute-start.3 = (bf16[2,256,512]{2,1,0:T(8,128)(2,1)}, bf16[2,256,512]{2,1,0:T(8,128)(2,1)}, u32[]{:S(2)}, u32[]{:S(2)}) collective-permute-start(bf16[2,256,512]{2,1,0:T(8,128)(2,1)} %collective-permute-done.2.refs_2_), channel_id=1, source_target_pairs={{0,1},{1,2},{2,3},{3,4},{4,5},{5,6},{6,7},{7,8},{8,9},{9,10},{10,1... | collective-permute-start | bytes 1572872 | tf_op jit(solution)/shard_map/ppermute | solution.py:101
  30.6 5.7 %collective-permute-start = (bf16[1,256,2048]{2,1,0:T(8,128)(2,1)}, bf16[1,256,2048]{2,1,0:T(8,128)(2,1)S(1)}, u32[]{:S(2)}, u32[]{:S(2)}) collective-permute-start(bf16[1,256,2048]{2,1,0:T(8,128)(2,1)} %param.10), channel_id=1, source_target_pairs={{0,224},{32,0},{64,32},{96,64},{128,96},{160,128},{192,160},{224,1... | collective-permute-start | bytes 3145736 | tf_op jit(solution)/shard_map/ppermute | solution.py:95
  36.3 0.2 reduce-window.8
  36.5 0.0 collective-permute-done.6.refs_2_
  36.5 2.2 %collective-permute-start.7 = (bf16[2,256,512]{2,1,0:T(8,128)(2,1)}, bf16[2,256,512]{2,1,0:T(8,128)(2,1)}, u32[]{:S(2)}, u32[]{:S(2)}) collective-permute-start(bf16[2,256,512]{2,1,0:T(8,128)(2,1)} %collective-permute-done.6.refs_2_), channel_id=1, source_target_pairs={{0,1},{1,2},{2,3},{3,4},{4,5},{5,6},{6,7},{7,8},{8,9},{9,10},{10,1... | collective-permute-start | bytes 1572872 | tf_op jit(solution)/shard_map/ppermute | solution.py:101
  38.7 0.1 convert_reduce_fusion.1
  38.8 0.1 convert_reduce_fusion
  38.9 0.0 collective-permute-done.3.refs_1_
  38.9 4.7 %collective-permute-start.4 = (bf16[2,256,512]{2,1,0:T(8,128)(2,1)}, bf16[2,256,512]{2,1,0:T(8,128)(2,1)S(1)}, u32[]{:S(2)}, u32[]{:S(2)}) collective-permute-start(bf16[2,256,512]{2,1,0:T(8,128)(2,1)} %collective-permute-done.3.refs_1_), channel_id=1, source_target_pairs={{0,1},{1,2},{2,3},{3,4},{4,5},{5,6},{6,7},{7,8},{8,9},{9,10},{10,1... | collective-permute-start | bytes 1572872 | tf_op jit(solution)/shard_map/ppermute | solution.py:101
  43.6 1.5 %collective-permute-done.7.refs_1_ = bf16[2,256,512]{2,1,0:T(8,128)(2,1)} collective-permute-done((bf16[2,256,512]{2,1,0:T(8,128)(2,1)}, bf16[2,256,512]{2,1,0:T(8,128)(2,1)}, u32[]{:S(2)}, u32[]{:S(2)}) %collective-permute-start.7) | collective-permute-done | bytes 524320 | tf_op jit(solution)/shard_map/ppermute | solution.py:101
  45.1 6.5 %collective-permute-start.8 = (bf16[2,256,512]{2,1,0:T(8,128)(2,1)}, bf16[2,256,512]{2,1,0:T(8,128)(2,1)}, u32[]{:S(2)}, u32[]{:S(2)}) collective-permute-start(bf16[2,256,512]{2,1,0:T(8,128)(2,1)} %collective-permute-done.7.refs_1_), channel_id=1, source_target_pairs={{0,1},{1,2},{2,3},{3,4},{4,5},{5,6},{6,7},{7,8},{8,9},{9,10},{10,1... | collective-permute-start | bytes 1572872 | tf_op jit(solution)/shard_map/ppermute | solution.py:101
  51.6 1.4 convert_convert_fusion.refs_5_
  53.0 2.9 %collective-permute-done = bf16[1,256,2048]{2,1,0:T(8,128)(2,1)S(1)} collective-permute-done((bf16[1,256,2048]{2,1,0:T(8,128)(2,1)}, bf16[1,256,2048]{2,1,0:T(8,128)(2,1)S(1)}, u32[]{:S(2)}, u32[]{:S(2)}) %collective-permute-start) | collective-permute-done | bytes 1048608 | tf_op jit(solution)/shard_map/ppermute | solution.py:95
  55.9 0.0 collective-permute-done.4.refs_0_
  55.9 0.6 call_exported.0.at_ref
  56.5 0.3 copy-done
  56.8 0.2 copy-done.11
  57.0 16.3 %shard_map.94 = (bf16[256,1024]{1,0:T(8,128)(2,1)}, bf16[4,2,256,512]{3,2,1,0:T(8,128)(2,1)}, f32[2,256,512]{2,1,0:T(8,128)}) custom-call(s32[2]{0:T(128)} %call_exported.0.at_ref, bf16[256,2048]{1,0:T(8,128)(2,1)} %bitcast.50, bf16[256,2048]{1,0:T(8,128)(2,1)} %bitcast.52, bf16[2,256,512]{2,1,0:T(8,128)(2,1)} %copy-done.11, ...), custom_call_target="tpu_custom_call" | custom-call | tf_op jit(solution)/shard_map/pallas_call | solution.py:81
  73.3 1.1 slice_bitcast_fusion.1
  74.4 2.1 %collective-permute-start.9 = (bf16[2,256,512]{2,1,0:T(8,128)(2,1)S(1)}, bf16[2,256,512]{2,1,0:T(8,128)(2,1)S(1)}, u32[]{:S(2)}, u32[]{:S(2)}) collective-permute-start(bf16[2,256,512]{2,1,0:T(8,128)(2,1)S(1)} %slice_bitcast_fusion.1), channel_id=1, source_target_pairs={{1,0},{2,1},{3,2},{4,3},{5,4},{6,5},{7,6},{8,7},{9,8},{10,9},{11,1... | collective-permute-start | bytes 1572872 | tf_op jit(solution)/shard_map/ppermute | solution.py:101
  76.5 0.0 collective-permute-done.8.refs_0_
  76.5 16.3 %shard_map.95 = (bf16[256,1024]{1,0:T(8,128)(2,1)}, bf16[4,2,256,512]{3,2,1,0:T(8,128)(2,1)}, f32[2,256,512]{2,1,0:T(8,128)}) custom-call(s32[2]{0:T(128)} %constant.24.clone.at_ref, bf16[256,2048]{1,0:T(8,128)(2,1)} %bitcast.51, bf16[256,2048]{1,0:T(8,128)(2,1)} %bitcast.53, bf16[2,256,512]{2,1,0:T(8,128)(2,1)} %collective-permute-done.8.refs_0_, ...), custom_call_target="tpu_custom_call" | custom-call | tf_op jit(solution)/shard_map/pallas_call | solution.py:81
  92.8 1.2 slice_bitcast_fusion
  94.1 2.7 %collective-permute-start.13 = (bf16[2,256,512]{2,1,0:T(8,128)(2,1)S(1)}, bf16[2,256,512]{2,1,0:T(8,128)(2,1)S(1)}, u32[]{:S(2)}, u32[]{:S(2)}) collective-permute-start(bf16[2,256,512]{2,1,0:T(8,128)(2,1)S(1)} %slice_bitcast_fusion), channel_id=1, source_target_pairs={{1,0},{2,1},{3,2},{4,3},{5,4},{6,5},{7,6},{8,7},{9,8},{10,9},{11,1... | collective-permute-start | bytes 1572872 | tf_op jit(solution)/shard_map/ppermute | solution.py:101
  96.8 0.0 collective-permute-done.9
  96.8 0.1 fusion.8
  97.0 1.9 %collective-permute-start.10 = (bf16[2,256,512]{2,1,0:T(8,128)(2,1)S(1)}, bf16[2,256,512]{2,1,0:T(8,128)(2,1)S(1)}, u32[]{:S(2)}, u32[]{:S(2)}) collective-permute-start(bf16[2,256,512]{2,1,0:T(8,128)(2,1)S(1)} %fusion.8), channel_id=1, source_target_pairs={{1,0},{2,1},{3,2},{4,3},{5,4},{6,5},{7,6},{8,7},{9,8},{10,9},{11,1... | collective-permute-start | bytes 1572872 | tf_op jit(solution)/shard_map/ppermute | solution.py:101
  98.9 7.8 %collective-permute-done.13 = bf16[2,256,512]{2,1,0:T(8,128)(2,1)S(1)} collective-permute-done((bf16[2,256,512]{2,1,0:T(8,128)(2,1)S(1)}, bf16[2,256,512]{2,1,0:T(8,128)(2,1)S(1)}, u32[]{:S(2)}, u32[]{:S(2)}) %collective-permute-start.13) | collective-permute-done | bytes 524320 | tf_op jit(solution)/shard_map/ppermute | solution.py:101
  106.7 0.1 fusion.5
  106.8 1.9 %collective-permute-start.14 = (bf16[2,256,512]{2,1,0:T(8,128)(2,1)S(1)}, bf16[2,256,512]{2,1,0:T(8,128)(2,1)S(1)}, u32[]{:S(2)}, u32[]{:S(2)}) collective-permute-start(bf16[2,256,512]{2,1,0:T(8,128)(2,1)S(1)} %fusion.5), channel_id=1, source_target_pairs={{1,0},{2,1},{3,2},{4,3},{5,4},{6,5},{7,6},{8,7},{9,8},{10,9},{11,1... | collective-permute-start | bytes 1572872 | tf_op jit(solution)/shard_map/ppermute | solution.py:101
  108.7 3.5 %collective-permute-done.10 = bf16[2,256,512]{2,1,0:T(8,128)(2,1)S(1)} collective-permute-done((bf16[2,256,512]{2,1,0:T(8,128)(2,1)S(1)}, bf16[2,256,512]{2,1,0:T(8,128)(2,1)S(1)}, u32[]{:S(2)}, u32[]{:S(2)}) %collective-permute-start.10) | collective-permute-done | bytes 524320 | tf_op jit(solution)/shard_map/ppermute | solution.py:101
  112.3 0.1 fusion.7
  112.4 2.1 %collective-permute-start.11 = (bf16[2,256,512]{2,1,0:T(8,128)(2,1)S(1)}, bf16[2,256,512]{2,1,0:T(8,128)(2,1)S(1)}, u32[]{:S(2)}, u32[]{:S(2)}) collective-permute-start(bf16[2,256,512]{2,1,0:T(8,128)(2,1)S(1)} %fusion.7), channel_id=1, source_target_pairs={{1,0},{2,1},{3,2},{4,3},{5,4},{6,5},{7,6},{8,7},{9,8},{10,9},{11,1... | collective-permute-start | bytes 1572872 | tf_op jit(solution)/shard_map/ppermute | solution.py:101
  114.5 4.9 %collective-permute-done.14 = bf16[2,256,512]{2,1,0:T(8,128)(2,1)S(1)} collective-permute-done((bf16[2,256,512]{2,1,0:T(8,128)(2,1)S(1)}, bf16[2,256,512]{2,1,0:T(8,128)(2,1)S(1)}, u32[]{:S(2)}, u32[]{:S(2)}) %collective-permute-start.14) | collective-permute-done | bytes 524320 | tf_op jit(solution)/shard_map/ppermute | solution.py:101
  119.4 0.1 fusion.4
  119.6 1.9 %collective-permute-start.15 = (bf16[2,256,512]{2,1,0:T(8,128)(2,1)S(1)}, bf16[2,256,512]{2,1,0:T(8,128)(2,1)S(1)}, u32[]{:S(2)}, u32[]{:S(2)}) collective-permute-start(bf16[2,256,512]{2,1,0:T(8,128)(2,1)S(1)} %fusion.4), channel_id=1, source_target_pairs={{1,0},{2,1},{3,2},{4,3},{5,4},{6,5},{7,6},{8,7},{9,8},{10,9},{11,1... | collective-permute-start | bytes 1572872 | tf_op jit(solution)/shard_map/ppermute | solution.py:101
  121.5 3.7 %collective-permute-done.11 = bf16[2,256,512]{2,1,0:T(8,128)(2,1)S(1)} collective-permute-done((bf16[2,256,512]{2,1,0:T(8,128)(2,1)S(1)}, bf16[2,256,512]{2,1,0:T(8,128)(2,1)S(1)}, u32[]{:S(2)}, u32[]{:S(2)}) %collective-permute-start.11) | collective-permute-done | bytes 524320 | tf_op jit(solution)/shard_map/ppermute | solution.py:101
  125.2 0.1 fusion.6
  125.3 0.0 copy-start.5
  125.3 2.1 %collective-permute-start.12 = (bf16[2,256,512]{2,1,0:T(8,128)(2,1)S(1)}, bf16[2,256,512]{2,1,0:T(8,128)(2,1)S(1)}, u32[]{:S(2)}, u32[]{:S(2)}) collective-permute-start(bf16[2,256,512]{2,1,0:T(8,128)(2,1)S(1)} %fusion.6), channel_id=1, source_target_pairs={{1,0},{2,1},{3,2},{4,3},{5,4},{6,5},{7,6},{8,7},{9,8},{10,9},{11,1... | collective-permute-start | bytes 1572872 | tf_op jit(solution)/shard_map/ppermute | solution.py:101
  127.4 4.8 %collective-permute-done.15 = bf16[2,256,512]{2,1,0:T(8,128)(2,1)S(1)} collective-permute-done((bf16[2,256,512]{2,1,0:T(8,128)(2,1)S(1)}, bf16[2,256,512]{2,1,0:T(8,128)(2,1)S(1)}, u32[]{:S(2)}, u32[]{:S(2)}) %collective-permute-start.15) | collective-permute-done | bytes 524320 | tf_op jit(solution)/shard_map/ppermute | solution.py:101
  132.2 0.1 fusion.3
  132.3 1.9 %collective-permute-start.16 = (bf16[2,256,512]{2,1,0:T(8,128)(2,1)S(1)}, bf16[2,256,512]{2,1,0:T(8,128)(2,1)S(1)}, u32[]{:S(2)}, u32[]{:S(2)}) collective-permute-start(bf16[2,256,512]{2,1,0:T(8,128)(2,1)S(1)} %fusion.3), channel_id=1, source_target_pairs={{1,0},{2,1},{3,2},{4,3},{5,4},{6,5},{7,6},{8,7},{9,8},{10,9},{11,1... | collective-permute-start | bytes 1572872 | tf_op jit(solution)/shard_map/ppermute | solution.py:101
  134.3 1.1 maximum_bitcast_fusion
  135.3 2.8 %collective-permute-done.12 = bf16[2,256,512]{2,1,0:T(8,128)(2,1)S(1)} collective-permute-done((bf16[2,256,512]{2,1,0:T(8,128)(2,1)S(1)}, bf16[2,256,512]{2,1,0:T(8,128)(2,1)S(1)}, u32[]{:S(2)}, u32[]{:S(2)}) %collective-permute-start.12) | collective-permute-done | bytes 524320 | tf_op jit(solution)/shard_map/ppermute | solution.py:101
  138.1 0.0 copy-done.5
  138.1 0.2 add_convert_fusion.1
  138.3 6.6 %collective-permute-done.16 = bf16[2,256,512]{2,1,0:T(8,128)(2,1)S(1)} collective-permute-done((bf16[2,256,512]{2,1,0:T(8,128)(2,1)S(1)}, bf16[2,256,512]{2,1,0:T(8,128)(2,1)S(1)}, u32[]{:S(2)}, u32[]{:S(2)}) %collective-permute-start.16) | collective-permute-done | bytes 524320 | tf_op jit(solution)/shard_map/ppermute | solution.py:101
  144.9 0.2 add_convert_fusion
  145.2 0.9 maximum_bitcast_fusion.2
  146.0 0.9 maximum_bitcast_fusion.1
  (24 shorter events, 0.1 us)
Async XLA Ops:
  0.6 35.7 %copy-start.12 = (s32[4]{0:T(128)S(1)}, s32[4]{0:T(128)}, u32[]{:S(2)}) copy-start(s32[4]{0:T(128)} %param.11) | copy-start | bytes 52
  2.0 54.5 %copy-start.4 = (bf16[2,256,512]{2,1,0:T(8,128)(2,1)}, bf16[2,256,512]{2,1,0:T(8,128)(2,1)S(1)}, u32[]{:S(2)}) copy-start(bf16[2,256,512]{2,1,0:T(8,128)(2,1)S(1)} %pad_maximum_fusion.refs_4_) | copy-start | bytes 1572868
  2.0 9.4 %collective-permute-start.1 = (bf16[2,256,512]{2,1,0:T(8,128)(2,1)S(1)}, bf16[2,256,512]{2,1,0:T(8,128)(2,1)S(1)}, u32[]{:S(2)}, u32[]{:S(2)}) collective-permute-start(bf16[2,256,512]{2,1,0:T(8,128)(2,1)S(1)} %pad_maximum_fusion.refs_4_), channel_id=1, source_target_pairs={{0,1},{1,2},{2,3},{3,4},{4,5},{5,6},{6,7},{7,8},{8,9},{9,10},{10,1... | collective-permute-start | bytes 1572872 | tf_op jit(solution)/shard_map/ppermute | solution.py:101
  5.4 67.9 %copy-start.3 = (bf16[2,256,512]{2,1,0:T(8,128)(2,1)}, bf16[2,256,512]{2,1,0:T(8,128)(2,1)S(1)}, u32[]{:S(2)}) copy-start(bf16[2,256,512]{2,1,0:T(8,128)(2,1)S(1)} %pad_maximum_fusion.1.refs_4_) | copy-start | bytes 1572868
  5.4 12.5 %collective-permute-start.5 = (bf16[2,256,512]{2,1,0:T(8,128)(2,1)S(1)}, bf16[2,256,512]{2,1,0:T(8,128)(2,1)S(1)}, u32[]{:S(2)}, u32[]{:S(2)}) collective-permute-start(bf16[2,256,512]{2,1,0:T(8,128)(2,1)S(1)} %pad_maximum_fusion.1.refs_4_), channel_id=1, source_target_pairs={{0,1},{1,2},{2,3},{3,4},{4,5},{5,6},{6,7},{7,8},{8,9},{9,10},{10,1... | collective-permute-start | bytes 1572872 | tf_op jit(solution)/shard_map/ppermute | solution.py:101
  11.4 12.6 %copy-start.10 = (bf16[2,256,512]{2,1,0:T(8,128)(2,1)}, bf16[2,256,512]{2,1,0:T(8,128)(2,1)S(1)}, u32[]{:S(2)}) copy-start(bf16[2,256,512]{2,1,0:T(8,128)(2,1)S(1)} %collective-permute-done.1.refs_3_) | copy-start | bytes 1572868
  11.4 12.6 %collective-permute-start.2 = (bf16[2,256,512]{2,1,0:T(8,128)(2,1)S(1)}, bf16[2,256,512]{2,1,0:T(8,128)(2,1)}, u32[]{:S(2)}, u32[]{:S(2)}) collective-permute-start(bf16[2,256,512]{2,1,0:T(8,128)(2,1)S(1)} %collective-permute-done.1.refs_3_), channel_id=1, source_target_pairs={{0,1},{1,2},{2,3},{3,4},{4,5},{5,6},{6,7},{7,8},{8,9},{9,10},{10,1... | collective-permute-start | bytes 1572872 | tf_op jit(solution)/shard_map/ppermute | solution.py:101
  17.9 58.5 %copy-start.9 = (bf16[2,256,512]{2,1,0:T(8,128)(2,1)}, bf16[2,256,512]{2,1,0:T(8,128)(2,1)S(1)}, u32[]{:S(2)}) copy-start(bf16[2,256,512]{2,1,0:T(8,128)(2,1)S(1)} %collective-permute-done.5.refs_3_) | copy-start | bytes 1572868
  17.9 18.5 %collective-permute-start.6 = (bf16[2,256,512]{2,1,0:T(8,128)(2,1)S(1)}, bf16[2,256,512]{2,1,0:T(8,128)(2,1)}, u32[]{:S(2)}, u32[]{:S(2)}) collective-permute-start(bf16[2,256,512]{2,1,0:T(8,128)(2,1)S(1)} %collective-permute-done.5.refs_3_), channel_id=1, source_target_pairs={{0,1},{1,2},{2,3},{3,4},{4,5},{5,6},{6,7},{7,8},{8,9},{9,10},{10,1... | collective-permute-start | bytes 1572872 | tf_op jit(solution)/shard_map/ppermute | solution.py:101
  24.0 14.8 %collective-permute-start.3 = (bf16[2,256,512]{2,1,0:T(8,128)(2,1)}, bf16[2,256,512]{2,1,0:T(8,128)(2,1)}, u32[]{:S(2)}, u32[]{:S(2)}) collective-permute-start(bf16[2,256,512]{2,1,0:T(8,128)(2,1)} %collective-permute-done.2.refs_2_), channel_id=1, source_target_pairs={{0,1},{1,2},{2,3},{3,4},{4,5},{5,6},{6,7},{7,8},{8,9},{9,10},{10,1... | collective-permute-start | bytes 1572872 | tf_op jit(solution)/shard_map/ppermute | solution.py:101
  30.6 25.2 %collective-permute-start = (bf16[1,256,2048]{2,1,0:T(8,128)(2,1)}, bf16[1,256,2048]{2,1,0:T(8,128)(2,1)S(1)}, u32[]{:S(2)}, u32[]{:S(2)}) collective-permute-start(bf16[1,256,2048]{2,1,0:T(8,128)(2,1)} %param.10), channel_id=1, source_target_pairs={{0,224},{32,0},{64,32},{96,64},{128,96},{160,128},{192,160},{224,1... | collective-permute-start | bytes 3145736 | tf_op jit(solution)/shard_map/ppermute | solution.py:95
  36.5 8.6 %collective-permute-start.7 = (bf16[2,256,512]{2,1,0:T(8,128)(2,1)}, bf16[2,256,512]{2,1,0:T(8,128)(2,1)}, u32[]{:S(2)}, u32[]{:S(2)}) collective-permute-start(bf16[2,256,512]{2,1,0:T(8,128)(2,1)} %collective-permute-done.6.refs_2_), channel_id=1, source_target_pairs={{0,1},{1,2},{2,3},{3,4},{4,5},{5,6},{6,7},{7,8},{8,9},{9,10},{10,1... | collective-permute-start | bytes 1572872 | tf_op jit(solution)/shard_map/ppermute | solution.py:101
  38.9 17.0 %collective-permute-start.4 = (bf16[2,256,512]{2,1,0:T(8,128)(2,1)}, bf16[2,256,512]{2,1,0:T(8,128)(2,1)S(1)}, u32[]{:S(2)}, u32[]{:S(2)}) collective-permute-start(bf16[2,256,512]{2,1,0:T(8,128)(2,1)} %collective-permute-done.3.refs_1_), channel_id=1, source_target_pairs={{0,1},{1,2},{2,3},{3,4},{4,5},{5,6},{6,7},{7,8},{8,9},{9,10},{10,1... | collective-permute-start | bytes 1572872 | tf_op jit(solution)/shard_map/ppermute | solution.py:101
  45.1 31.4 %collective-permute-start.8 = (bf16[2,256,512]{2,1,0:T(8,128)(2,1)}, bf16[2,256,512]{2,1,0:T(8,128)(2,1)}, u32[]{:S(2)}, u32[]{:S(2)}) collective-permute-start(bf16[2,256,512]{2,1,0:T(8,128)(2,1)} %collective-permute-done.7.refs_1_), channel_id=1, source_target_pairs={{0,1},{1,2},{2,3},{3,4},{4,5},{5,6},{6,7},{7,8},{8,9},{9,10},{10,1... | collective-permute-start | bytes 1572872 | tf_op jit(solution)/shard_map/ppermute | solution.py:101
  55.9 1.0 copy-start
  55.9 1.1 copy-start.11
  74.4 22.4 %copy-start.1 = (bf16[4,2,256,512]{3,2,1,0:T(8,128)(2,1)S(1)}, bf16[4,2,256,512]{3,2,1,0:T(8,128)(2,1)}, u32[]{:S(2)}) copy-start(bf16[4,2,256,512]{3,2,1,0:T(8,128)(2,1)} %get-tuple-element.12) | copy-start | bytes 6291460
  74.4 22.4 %collective-permute-start.9 = (bf16[2,256,512]{2,1,0:T(8,128)(2,1)S(1)}, bf16[2,256,512]{2,1,0:T(8,128)(2,1)S(1)}, u32[]{:S(2)}, u32[]{:S(2)}) collective-permute-start(bf16[2,256,512]{2,1,0:T(8,128)(2,1)S(1)} %slice_bitcast_fusion.1), channel_id=1, source_target_pairs={{1,0},{2,1},{3,2},{4,3},{5,4},{6,5},{7,6},{8,7},{9,8},{10,9},{11,1... | collective-permute-start | bytes 1572872 | tf_op jit(solution)/shard_map/ppermute | solution.py:101
  92.8 13.8 %copy-start.2 = (bf16[4,2,256,512]{3,2,1,0:T(8,128)(2,1)S(1)}, bf16[4,2,256,512]{3,2,1,0:T(8,128)(2,1)}, u32[]{:S(2)}) copy-start(bf16[4,2,256,512]{3,2,1,0:T(8,128)(2,1)} %get-tuple-element.14) | copy-start | bytes 6291460
  94.1 12.6 %collective-permute-start.13 = (bf16[2,256,512]{2,1,0:T(8,128)(2,1)S(1)}, bf16[2,256,512]{2,1,0:T(8,128)(2,1)S(1)}, u32[]{:S(2)}, u32[]{:S(2)}) collective-permute-start(bf16[2,256,512]{2,1,0:T(8,128)(2,1)S(1)} %slice_bitcast_fusion), channel_id=1, source_target_pairs={{1,0},{2,1},{3,2},{4,3},{5,4},{6,5},{7,6},{8,7},{9,8},{10,9},{11,1... | collective-permute-start | bytes 1572872 | tf_op jit(solution)/shard_map/ppermute | solution.py:101
  97.0 15.3 %collective-permute-start.10 = (bf16[2,256,512]{2,1,0:T(8,128)(2,1)S(1)}, bf16[2,256,512]{2,1,0:T(8,128)(2,1)S(1)}, u32[]{:S(2)}, u32[]{:S(2)}) collective-permute-start(bf16[2,256,512]{2,1,0:T(8,128)(2,1)S(1)} %fusion.8), channel_id=1, source_target_pairs={{1,0},{2,1},{3,2},{4,3},{5,4},{6,5},{7,6},{8,7},{9,8},{10,9},{11,1... | collective-permute-start | bytes 1572872 | tf_op jit(solution)/shard_map/ppermute | solution.py:101
  106.8 12.6 %collective-permute-start.14 = (bf16[2,256,512]{2,1,0:T(8,128)(2,1)S(1)}, bf16[2,256,512]{2,1,0:T(8,128)(2,1)S(1)}, u32[]{:S(2)}, u32[]{:S(2)}) collective-permute-start(bf16[2,256,512]{2,1,0:T(8,128)(2,1)S(1)} %fusion.5), channel_id=1, source_target_pairs={{1,0},{2,1},{3,2},{4,3},{5,4},{6,5},{7,6},{8,7},{9,8},{10,9},{11,1... | collective-permute-start | bytes 1572872 | tf_op jit(solution)/shard_map/ppermute | solution.py:101
  112.4 21.8 %copy-start.7 = (bf16[256,1024]{1,0:T(8,128)(2,1)S(1)}, bf16[256,1024]{1,0:T(8,128)(2,1)}, u32[]{:S(2)}) copy-start(bf16[256,1024]{1,0:T(8,128)(2,1)} %get-tuple-element.9) | copy-start | bytes 1572868
  112.4 21.8 %copy-start.8 = (bf16[256,1024]{1,0:T(8,128)(2,1)S(1)}, bf16[256,1024]{1,0:T(8,128)(2,1)}, u32[]{:S(2)}) copy-start(bf16[256,1024]{1,0:T(8,128)(2,1)} %get-tuple-element.10) | copy-start | bytes 1572868
  112.4 12.7 %collective-permute-start.11 = (bf16[2,256,512]{2,1,0:T(8,128)(2,1)S(1)}, bf16[2,256,512]{2,1,0:T(8,128)(2,1)S(1)}, u32[]{:S(2)}, u32[]{:S(2)}) collective-permute-start(bf16[2,256,512]{2,1,0:T(8,128)(2,1)S(1)} %fusion.7), channel_id=1, source_target_pairs={{1,0},{2,1},{3,2},{4,3},{5,4},{6,5},{7,6},{8,7},{9,8},{10,9},{11,1... | collective-permute-start | bytes 1572872 | tf_op jit(solution)/shard_map/ppermute | solution.py:101
  119.6 12.6 %collective-permute-start.15 = (bf16[2,256,512]{2,1,0:T(8,128)(2,1)S(1)}, bf16[2,256,512]{2,1,0:T(8,128)(2,1)S(1)}, u32[]{:S(2)}, u32[]{:S(2)}) collective-permute-start(bf16[2,256,512]{2,1,0:T(8,128)(2,1)S(1)} %fusion.4), channel_id=1, source_target_pairs={{1,0},{2,1},{3,2},{4,3},{5,4},{6,5},{7,6},{8,7},{9,8},{10,9},{11,1... | collective-permute-start | bytes 1572872 | tf_op jit(solution)/shard_map/ppermute | solution.py:101
  125.3 12.8 %copy-start.5 = (f32[2,256,512]{2,1,0:T(8,128)S(1)}, f32[2,256,512]{2,1,0:T(8,128)}, u32[]{:S(2)}) copy-start(f32[2,256,512]{2,1,0:T(8,128)} %get-tuple-element.11) | copy-start | bytes 3145732
  125.3 12.7 %collective-permute-start.12 = (bf16[2,256,512]{2,1,0:T(8,128)(2,1)S(1)}, bf16[2,256,512]{2,1,0:T(8,128)(2,1)S(1)}, u32[]{:S(2)}, u32[]{:S(2)}) collective-permute-start(bf16[2,256,512]{2,1,0:T(8,128)(2,1)S(1)} %fusion.6), channel_id=1, source_target_pairs={{1,0},{2,1},{3,2},{4,3},{5,4},{6,5},{7,6},{8,7},{9,8},{10,9},{11,1... | collective-permute-start | bytes 1572872 | tf_op jit(solution)/shard_map/ppermute | solution.py:101
  132.3 12.6 %collective-permute-start.16 = (bf16[2,256,512]{2,1,0:T(8,128)(2,1)S(1)}, bf16[2,256,512]{2,1,0:T(8,128)(2,1)S(1)}, u32[]{:S(2)}, u32[]{:S(2)}) collective-permute-start(bf16[2,256,512]{2,1,0:T(8,128)(2,1)S(1)} %fusion.3), channel_id=1, source_target_pairs={{1,0},{2,1},{3,2},{4,3},{5,4},{6,5},{7,6},{8,7},{9,8},{10,9},{11,1... | collective-permute-start | bytes 1572872 | tf_op jit(solution)/shard_map/ppermute | solution.py:101
  135.3 9.6 %copy-start.6 = (f32[2,256,512]{2,1,0:T(8,128)S(1)}, f32[2,256,512]{2,1,0:T(8,128)}, u32[]{:S(2)}) copy-start(f32[2,256,512]{2,1,0:T(8,128)} %get-tuple-element.13) | copy-start | bytes 3145732

commit v9 on v8

--- a/solution.py
+++ b/solution.py
@@ -34,7 +34,6 @@
     grads = jnp.concatenate([do_ref[:, h * head_size:(h + 1) * head_size] for h in range(heads)], axis=0)
     allowed = jnp.concatenate([allowed] * heads, axis=0)
     nt = (((1,), (1,)), ((), ()))
-    tn = (((0,), (0,)), ((), ()))
     nn = (((1,), (0,)), ((), ()))
     scores = SCORE_SCALE * product(queries, keys, nt)
     scores = jnp.where(allowed, scores, -jnp.inf)
@@ -49,8 +48,8 @@
     query_back = SCORE_SCALE * product(score_grad, keys, nn)
     for h in range(heads):
         dq_ref[:, h * head_size:(h + 1) * head_size] = query_back[h * rows:(h + 1) * rows].astype(dq_ref.dtype)
-    key_back = SCORE_SCALE * product(score_grad, queries, tn)
-    value_back = product(weight_half, grads, tn)
+    key_back = (SCORE_SCALE * product(queries.T, score_grad, nn)).T
+    value_back = product(grads.T, weight_half, nn).T
     for block in range(blocks - 1):
         lines = slice(block * rows, (block + 1) * rows)
         far_ref[block, 0] = key_back[lines].astype(far_ref.dtype)

time: 148 us -> 146 us (0.986)
  Pallas kernels: 32.7 us -> 30.5 us
    pallas_call x2, Pallas kernels: 32.7 us -> 30.5 us  [attention_back(): pl.pallas_call(attention_back_kernel, grid_spec=grid_spec, out_shape=[jax...]
  transfers between devices with their start and end apart: 17 -> 17, of which waited for: 11 -> 11; matrix products, arithmetic and copies ran while one was open for 5% -> 5% of each run, Pallas kernels for 22% -> 21%
where the time goes in v9:
time: 146 us; the launch traced here: 145 us
  starting transfers between devices  59.5 us (41%)
  waiting for transfers between devices  43.1 us (30%)
  Pallas kernels  30.5 us (21%)
  other arithmetic  5.84 us (4%)
  local copies, waits for them, and re-layouts  4.83 us (3%)
    ppermute x16, starting transfers between devices, shifted(): lax.ppermute(value, axis, [(source, source + steps) for source in range(i...  53.8 us
    ppermute x16, waiting for transfers between devices, shifted(): lax.ppermute(value, axis, [(source, source + steps) for source in range(i...  40.2 us
    pallas_call x2, Pallas kernels, attention_back(): pl.pallas_call(attention_back_kernel, grid_spec=grid_spec, out_shape=[jax...  30.5 us
    ppermute x1, starting transfers between devices, passed_along(): lax.ppermute(shard, axis, [(i, (i + by) % count) for i in range(count)])  5.65 us
  transfers between devices with their start and end apart: 17, of which 11 were waited for; matrix products, arithmetic and copies ran while one was open for 5% of the time, Pallas kernels for 21%

profile of v9, /device:TPU:25, one launch (start us, length us, event | category | flops | bytes accessed | tf_op | source)
XLA Modules:
  0.0 144.8 jit_solution(6833840322491159864)
XLA Ops:
  0.6 0.0 copy-start.12
  0.6 1.3 slice_bitcast_fusion.8
  1.9 0.1 pad_maximum_fusion.refs_4_
  2.0 3.3 %collective-permute-start.1 = (bf16[2,256,512]{2,1,0:T(8,128)(2,1)S(1)}, bf16[2,256,512]{2,1,0:T(8,128)(2,1)S(1)}, u32[]{:S(2)}, u32[]{:S(2)}) collective-permute-start(bf16[2,256,512]{2,1,0:T(8,128)(2,1)S(1)} %pad_maximum_fusion.refs_4_), channel_id=1, source_target_pairs={{0,1},{1,2},{2,3},{3,4},{4,5},{5,6},{6,7},{7,8},{8,9},{9,10},{10,1... | collective-permute-start | bytes 1572872 | tf_op jit(solution)/shard_map/ppermute | solution.py:100
  5.3 0.1 pad_maximum_fusion.1.refs_4_
  5.4 0.0 copy-start.3
  5.4 1.9 %collective-permute-start.5 = (bf16[2,256,512]{2,1,0:T(8,128)(2,1)S(1)}, bf16[2,256,512]{2,1,0:T(8,128)(2,1)S(1)}, u32[]{:S(2)}, u32[]{:S(2)}) collective-permute-start(bf16[2,256,512]{2,1,0:T(8,128)(2,1)S(1)} %pad_maximum_fusion.1.refs_4_), channel_id=1, source_target_pairs={{0,1},{1,2},{2,3},{3,4},{4,5},{5,6},{6,7},{7,8},{8,9},{9,10},{10,1... | collective-permute-start | bytes 1572872 | tf_op jit(solution)/shard_map/ppermute | solution.py:100
  7.3 4.1 %collective-permute-done.1.refs_3_ = bf16[2,256,512]{2,1,0:T(8,128)(2,1)S(1)} collective-permute-done((bf16[2,256,512]{2,1,0:T(8,128)(2,1)S(1)}, bf16[2,256,512]{2,1,0:T(8,128)(2,1)S(1)}, u32[]{:S(2)}, u32[]{:S(2)}) %collective-permute-start.1) | collective-permute-done | bytes 524320 | tf_op jit(solution)/shard_map/ppermute | solution.py:100
  11.4 6.5 %collective-permute-start.2 = (bf16[2,256,512]{2,1,0:T(8,128)(2,1)S(1)}, bf16[2,256,512]{2,1,0:T(8,128)(2,1)}, u32[]{:S(2)}, u32[]{:S(2)}) collective-permute-start(bf16[2,256,512]{2,1,0:T(8,128)(2,1)S(1)} %collective-permute-done.1.refs_3_), channel_id=1, source_target_pairs={{0,1},{1,2},{2,3},{3,4},{4,5},{5,6},{6,7},{7,8},{8,9},{9,10},{10,1... | collective-permute-start | bytes 1572872 | tf_op jit(solution)/shard_map/ppermute | solution.py:100
  17.9 0.0 collective-permute-done.5.refs_3_
  17.9 0.0 copy-start.9
  17.9 5.6 %collective-permute-start.6 = (bf16[2,256,512]{2,1,0:T(8,128)(2,1)S(1)}, bf16[2,256,512]{2,1,0:T(8,128)(2,1)}, u32[]{:S(2)}, u32[]{:S(2)}) collective-permute-start(bf16[2,256,512]{2,1,0:T(8,128)(2,1)S(1)} %collective-permute-done.5.refs_3_), channel_id=1, source_target_pairs={{0,1},{1,2},{2,3},{3,4},{4,5},{5,6},{6,7},{7,8},{8,9},{9,10},{10,1... | collective-permute-start | bytes 1572872 | tf_op jit(solution)/shard_map/ppermute | solution.py:100
  23.5 0.5 collective-permute-done.2.refs_2_
  24.0 6.6 %collective-permute-start.3 = (bf16[2,256,512]{2,1,0:T(8,128)(2,1)}, bf16[2,256,512]{2,1,0:T(8,128)(2,1)}, u32[]{:S(2)}, u32[]{:S(2)}) collective-permute-start(bf16[2,256,512]{2,1,0:T(8,128)(2,1)} %collective-permute-done.2.refs_2_), channel_id=1, source_target_pairs={{0,1},{1,2},{2,3},{3,4},{4,5},{5,6},{6,7},{7,8},{8,9},{9,10},{10,1... | collective-permute-start | bytes 1572872 | tf_op jit(solution)/shard_map/ppermute | solution.py:100
  30.6 5.7 %collective-permute-start = (bf16[1,256,2048]{2,1,0:T(8,128)(2,1)}, bf16[1,256,2048]{2,1,0:T(8,128)(2,1)S(1)}, u32[]{:S(2)}, u32[]{:S(2)}) collective-permute-start(bf16[1,256,2048]{2,1,0:T(8,128)(2,1)} %param.10), channel_id=1, source_target_pairs={{0,224},{32,0},{64,32},{96,64},{128,96},{160,128},{192,160},{224,1... | collective-permute-start | bytes 3145736 | tf_op jit(solution)/shard_map/ppermute | solution.py:94
  36.3 0.2 reduce-window.8
  36.5 0.0 collective-permute-done.6.refs_2_
  36.5 2.2 %collective-permute-start.7 = (bf16[2,256,512]{2,1,0:T(8,128)(2,1)}, bf16[2,256,512]{2,1,0:T(8,128)(2,1)}, u32[]{:S(2)}, u32[]{:S(2)}) collective-permute-start(bf16[2,256,512]{2,1,0:T(8,128)(2,1)} %collective-permute-done.6.refs_2_), channel_id=1, source_target_pairs={{0,1},{1,2},{2,3},{3,4},{4,5},{5,6},{6,7},{7,8},{8,9},{9,10},{10,1... | collective-permute-start | bytes 1572872 | tf_op jit(solution)/shard_map/ppermute | solution.py:100
  38.7 0.1 convert_reduce_fusion.1
  38.8 0.1 convert_reduce_fusion
  38.9 0.0 collective-permute-done.3.refs_1_
  38.9 4.7 %collective-permute-start.4 = (bf16[2,256,512]{2,1,0:T(8,128)(2,1)}, bf16[2,256,512]{2,1,0:T(8,128)(2,1)S(1)}, u32[]{:S(2)}, u32[]{:S(2)}) collective-permute-start(bf16[2,256,512]{2,1,0:T(8,128)(2,1)} %collective-permute-done.3.refs_1_), channel_id=1, source_target_pairs={{0,1},{1,2},{2,3},{3,4},{4,5},{5,6},{6,7},{7,8},{8,9},{9,10},{10,1... | collective-permute-start | bytes 1572872 | tf_op jit(solution)/shard_map/ppermute | solution.py:100
  43.6 1.5 %collective-permute-done.7.refs_1_ = bf16[2,256,512]{2,1,0:T(8,128)(2,1)} collective-permute-done((bf16[2,256,512]{2,1,0:T(8,128)(2,1)}, bf16[2,256,512]{2,1,0:T(8,128)(2,1)}, u32[]{:S(2)}, u32[]{:S(2)}) %collective-permute-start.7) | collective-permute-done | bytes 524320 | tf_op jit(solution)/shard_map/ppermute | solution.py:100
  45.1 6.5 %collective-permute-start.8 = (bf16[2,256,512]{2,1,0:T(8,128)(2,1)}, bf16[2,256,512]{2,1,0:T(8,128)(2,1)}, u32[]{:S(2)}, u32[]{:S(2)}) collective-permute-start(bf16[2,256,512]{2,1,0:T(8,128)(2,1)} %collective-permute-done.7.refs_1_), channel_id=1, source_target_pairs={{0,1},{1,2},{2,3},{3,4},{4,5},{5,6},{6,7},{7,8},{8,9},{9,10},{10,1... | collective-permute-start | bytes 1572872 | tf_op jit(solution)/shard_map/ppermute | solution.py:100
  51.6 1.4 convert_convert_fusion.refs_5_
  53.0 2.9 %collective-permute-done = bf16[1,256,2048]{2,1,0:T(8,128)(2,1)S(1)} collective-permute-done((bf16[1,256,2048]{2,1,0:T(8,128)(2,1)}, bf16[1,256,2048]{2,1,0:T(8,128)(2,1)S(1)}, u32[]{:S(2)}, u32[]{:S(2)}) %collective-permute-start) | collective-permute-done | bytes 1048608 | tf_op jit(solution)/shard_map/ppermute | solution.py:94
  55.9 0.0 collective-permute-done.4.refs_0_
  55.9 0.6 call_exported.0.at_ref
  56.5 0.3 copy-done
  56.8 0.2 copy-done.11
  57.0 15.3 %shard_map.94 = (bf16[256,1024]{1,0:T(8,128)(2,1)}, bf16[4,2,256,512]{3,2,1,0:T(8,128)(2,1)}, f32[2,256,512]{2,1,0:T(8,128)}) custom-call(s32[2]{0:T(128)} %call_exported.0.at_ref, bf16[256,2048]{1,0:T(8,128)(2,1)} %bitcast.50, bf16[256,2048]{1,0:T(8,128)(2,1)} %bitcast.52, bf16[2,256,512]{2,1,0:T(8,128)(2,1)} %copy-done.11, ...), custom_call_target="tpu_custom_call" | custom-call | tf_op jit(solution)/shard_map/pallas_call | solution.py:80
  72.3 1.1 slice_bitcast_fusion.1
  73.4 2.1 %collective-permute-start.9 = (bf16[2,256,512]{2,1,0:T(8,128)(2,1)S(1)}, bf16[2,256,512]{2,1,0:T(8,128)(2,1)S(1)}, u32[]{:S(2)}, u32[]{:S(2)}) collective-permute-start(bf16[2,256,512]{2,1,0:T(8,128)(2,1)S(1)} %slice_bitcast_fusion.1), channel_id=1, source_target_pairs={{1,0},{2,1},{3,2},{4,3},{5,4},{6,5},{7,6},{8,7},{9,8},{10,9},{11,1... | collective-permute-start | bytes 1572872 | tf_op jit(solution)/shard_map/ppermute | solution.py:100
  75.4 0.0 collective-permute-done.8.refs_0_
  75.4 15.3 %shard_map.95 = (bf16[256,1024]{1,0:T(8,128)(2,1)}, bf16[4,2,256,512]{3,2,1,0:T(8,128)(2,1)}, f32[2,256,512]{2,1,0:T(8,128)}) custom-call(s32[2]{0:T(128)} %constant.24.clone.at_ref, bf16[256,2048]{1,0:T(8,128)(2,1)} %bitcast.51, bf16[256,2048]{1,0:T(8,128)(2,1)} %bitcast.53, bf16[2,256,512]{2,1,0:T(8,128)(2,1)} %collective-permute-done.8.refs_0_, ...), custom_call_target="tpu_custom_call" | custom-call | tf_op jit(solution)/shard_map/pallas_call | solution.py:80
  90.7 1.2 slice_bitcast_fusion
  91.9 2.7 %collective-permute-start.13 = (bf16[2,256,512]{2,1,0:T(8,128)(2,1)S(1)}, bf16[2,256,512]{2,1,0:T(8,128)(2,1)S(1)}, u32[]{:S(2)}, u32[]{:S(2)}) collective-permute-start(bf16[2,256,512]{2,1,0:T(8,128)(2,1)S(1)} %slice_bitcast_fusion), channel_id=1, source_target_pairs={{1,0},{2,1},{3,2},{4,3},{5,4},{6,5},{7,6},{8,7},{9,8},{10,9},{11,1... | collective-permute-start | bytes 1572872 | tf_op jit(solution)/shard_map/ppermute | solution.py:100
  94.7 0.0 collective-permute-done.9
  94.7 0.0 copy-done.1
  94.7 0.1 fusion.8
  94.8 1.9 %collective-permute-start.10 = (bf16[2,256,512]{2,1,0:T(8,128)(2,1)S(1)}, bf16[2,256,512]{2,1,0:T(8,128)(2,1)S(1)}, u32[]{:S(2)}, u32[]{:S(2)}) collective-permute-start(bf16[2,256,512]{2,1,0:T(8,128)(2,1)S(1)} %fusion.8), channel_id=1, source_target_pairs={{1,0},{2,1},{3,2},{4,3},{5,4},{6,5},{7,6},{8,7},{9,8},{10,9},{11,1... | collective-permute-start | bytes 1572872 | tf_op jit(solution)/shard_map/ppermute | solution.py:100
  96.8 7.8 %collective-permute-done.13 = bf16[2,256,512]{2,1,0:T(8,128)(2,1)S(1)} collective-permute-done((bf16[2,256,512]{2,1,0:T(8,128)(2,1)S(1)}, bf16[2,256,512]{2,1,0:T(8,128)(2,1)S(1)}, u32[]{:S(2)}, u32[]{:S(2)}) %collective-permute-start.13) | collective-permute-done | bytes 524320 | tf_op jit(solution)/shard_map/ppermute | solution.py:100
  104.6 0.1 fusion.5
  104.7 1.9 %collective-permute-start.14 = (bf16[2,256,512]{2,1,0:T(8,128)(2,1)S(1)}, bf16[2,256,512]{2,1,0:T(8,128)(2,1)S(1)}, u32[]{:S(2)}, u32[]{:S(2)}) collective-permute-start(bf16[2,256,512]{2,1,0:T(8,128)(2,1)S(1)} %fusion.5), channel_id=1, source_target_pairs={{1,0},{2,1},{3,2},{4,3},{5,4},{6,5},{7,6},{8,7},{9,8},{10,9},{11,1... | collective-permute-start | bytes 1572872 | tf_op jit(solution)/shard_map/ppermute | solution.py:100
  106.6 3.5 %collective-permute-done.10 = bf16[2,256,512]{2,1,0:T(8,128)(2,1)S(1)} collective-permute-done((bf16[2,256,512]{2,1,0:T(8,128)(2,1)S(1)}, bf16[2,256,512]{2,1,0:T(8,128)(2,1)S(1)}, u32[]{:S(2)}, u32[]{:S(2)}) %collective-permute-start.10) | collective-permute-done | bytes 524320 | tf_op jit(solution)/shard_map/ppermute | solution.py:100
  110.2 0.1 fusion.7
  110.3 2.1 %collective-permute-start.11 = (bf16[2,256,512]{2,1,0:T(8,128)(2,1)S(1)}, bf16[2,256,512]{2,1,0:T(8,128)(2,1)S(1)}, u32[]{:S(2)}, u32[]{:S(2)}) collective-permute-start(bf16[2,256,512]{2,1,0:T(8,128)(2,1)S(1)} %fusion.7), channel_id=1, source_target_pairs={{1,0},{2,1},{3,2},{4,3},{5,4},{6,5},{7,6},{8,7},{9,8},{10,9},{11,1... | collective-permute-start | bytes 1572872 | tf_op jit(solution)/shard_map/ppermute | solution.py:100
  112.4 4.9 %collective-permute-done.14 = bf16[2,256,512]{2,1,0:T(8,128)(2,1)S(1)} collective-permute-done((bf16[2,256,512]{2,1,0:T(8,128)(2,1)S(1)}, bf16[2,256,512]{2,1,0:T(8,128)(2,1)S(1)}, u32[]{:S(2)}, u32[]{:S(2)}) %collective-permute-start.14) | collective-permute-done | bytes 524320 | tf_op jit(solution)/shard_map/ppermute | solution.py:100
  117.3 0.1 fusion.4
  117.4 1.9 %collective-permute-start.15 = (bf16[2,256,512]{2,1,0:T(8,128)(2,1)S(1)}, bf16[2,256,512]{2,1,0:T(8,128)(2,1)S(1)}, u32[]{:S(2)}, u32[]{:S(2)}) collective-permute-start(bf16[2,256,512]{2,1,0:T(8,128)(2,1)S(1)} %fusion.4), channel_id=1, source_target_pairs={{1,0},{2,1},{3,2},{4,3},{5,4},{6,5},{7,6},{8,7},{9,8},{10,9},{11,1... | collective-permute-start | bytes 1572872 | tf_op jit(solution)/shard_map/ppermute | solution.py:100
  119.4 3.7 %collective-permute-done.11 = bf16[2,256,512]{2,1,0:T(8,128)(2,1)S(1)} collective-permute-done((bf16[2,256,512]{2,1,0:T(8,128)(2,1)S(1)}, bf16[2,256,512]{2,1,0:T(8,128)(2,1)S(1)}, u32[]{:S(2)}, u32[]{:S(2)}) %collective-permute-start.11) | collective-permute-done | bytes 524320 | tf_op jit(solution)/shard_map/ppermute | solution.py:100
  123.1 0.1 fusion.6
  123.2 2.1 %collective-permute-start.12 = (bf16[2,256,512]{2,1,0:T(8,128)(2,1)S(1)}, bf16[2,256,512]{2,1,0:T(8,128)(2,1)S(1)}, u32[]{:S(2)}, u32[]{:S(2)}) collective-permute-start(bf16[2,256,512]{2,1,0:T(8,128)(2,1)S(1)} %fusion.6), channel_id=1, source_target_pairs={{1,0},{2,1},{3,2},{4,3},{5,4},{6,5},{7,6},{8,7},{9,8},{10,9},{11,1... | collective-permute-start | bytes 1572872 | tf_op jit(solution)/shard_map/ppermute | solution.py:100
  125.3 4.8 %collective-permute-done.15 = bf16[2,256,512]{2,1,0:T(8,128)(2,1)S(1)} collective-permute-done((bf16[2,256,512]{2,1,0:T(8,128)(2,1)S(1)}, bf16[2,256,512]{2,1,0:T(8,128)(2,1)S(1)}, u32[]{:S(2)}, u32[]{:S(2)}) %collective-permute-start.15) | collective-permute-done | bytes 524320 | tf_op jit(solution)/shard_map/ppermute | solution.py:100
  130.0 0.1 fusion.3
  130.2 1.9 %collective-permute-start.16 = (bf16[2,256,512]{2,1,0:T(8,128)(2,1)S(1)}, bf16[2,256,512]{2,1,0:T(8,128)(2,1)S(1)}, u32[]{:S(2)}, u32[]{:S(2)}) collective-permute-start(bf16[2,256,512]{2,1,0:T(8,128)(2,1)S(1)} %fusion.3), channel_id=1, source_target_pairs={{1,0},{2,1},{3,2},{4,3},{5,4},{6,5},{7,6},{8,7},{9,8},{10,9},{11,1... | collective-permute-start | bytes 1572872 | tf_op jit(solution)/shard_map/ppermute | solution.py:100
  132.1 1.1 maximum_bitcast_fusion
  133.2 2.8 %collective-permute-done.12 = bf16[2,256,512]{2,1,0:T(8,128)(2,1)S(1)} collective-permute-done((bf16[2,256,512]{2,1,0:T(8,128)(2,1)S(1)}, bf16[2,256,512]{2,1,0:T(8,128)(2,1)S(1)}, u32[]{:S(2)}, u32[]{:S(2)}) %collective-permute-start.12) | collective-permute-done | bytes 524320 | tf_op jit(solution)/shard_map/ppermute | solution.py:100
  136.0 0.0 copy-done.5
  136.0 0.2 add_convert_fusion.1
  136.2 6.6 %collective-permute-done.16 = bf16[2,256,512]{2,1,0:T(8,128)(2,1)S(1)} collective-permute-done((bf16[2,256,512]{2,1,0:T(8,128)(2,1)S(1)}, bf16[2,256,512]{2,1,0:T(8,128)(2,1)S(1)}, u32[]{:S(2)}, u32[]{:S(2)}) %collective-permute-start.16) | collective-permute-done | bytes 524320 | tf_op jit(solution)/shard_map/ppermute | solution.py:100
  142.8 0.2 add_convert_fusion
  143.0 0.9 maximum_bitcast_fusion.2
  143.9 0.9 maximum_bitcast_fusion.1
  (24 shorter events, 0.1 us)
Async XLA Ops:
  0.6 35.7 %copy-start.12 = (s32[4]{0:T(128)S(1)}, s32[4]{0:T(128)}, u32[]{:S(2)}) copy-start(s32[4]{0:T(128)} %param.11) | copy-start | bytes 52
  2.0 54.5 %copy-start.4 = (bf16[2,256,512]{2,1,0:T(8,128)(2,1)}, bf16[2,256,512]{2,1,0:T(8,128)(2,1)S(1)}, u32[]{:S(2)}) copy-start(bf16[2,256,512]{2,1,0:T(8,128)(2,1)S(1)} %pad_maximum_fusion.refs_4_) | copy-start | bytes 1572868
  2.0 9.4 %collective-permute-start.1 = (bf16[2,256,512]{2,1,0:T(8,128)(2,1)S(1)}, bf16[2,256,512]{2,1,0:T(8,128)(2,1)S(1)}, u32[]{:S(2)}, u32[]{:S(2)}) collective-permute-start(bf16[2,256,512]{2,1,0:T(8,128)(2,1)S(1)} %pad_maximum_fusion.refs_4_), channel_id=1, source_target_pairs={{0,1},{1,2},{2,3},{3,4},{4,5},{5,6},{6,7},{7,8},{8,9},{9,10},{10,1... | collective-permute-start | bytes 1572872 | tf_op jit(solution)/shard_map/ppermute | solution.py:100
  5.4 66.9 %copy-start.3 = (bf16[2,256,512]{2,1,0:T(8,128)(2,1)}, bf16[2,256,512]{2,1,0:T(8,128)(2,1)S(1)}, u32[]{:S(2)}) copy-start(bf16[2,256,512]{2,1,0:T(8,128)(2,1)S(1)} %pad_maximum_fusion.1.refs_4_) | copy-start | bytes 1572868
  5.4 12.5 %collective-permute-start.5 = (bf16[2,256,512]{2,1,0:T(8,128)(2,1)S(1)}, bf16[2,256,512]{2,1,0:T(8,128)(2,1)S(1)}, u32[]{:S(2)}, u32[]{:S(2)}) collective-permute-start(bf16[2,256,512]{2,1,0:T(8,128)(2,1)S(1)} %pad_maximum_fusion.1.refs_4_), channel_id=1, source_target_pairs={{0,1},{1,2},{2,3},{3,4},{4,5},{5,6},{6,7},{7,8},{8,9},{9,10},{10,1... | collective-permute-start | bytes 1572872 | tf_op jit(solution)/shard_map/ppermute | solution.py:100
  11.4 12.6 %copy-start.10 = (bf16[2,256,512]{2,1,0:T(8,128)(2,1)}, bf16[2,256,512]{2,1,0:T(8,128)(2,1)S(1)}, u32[]{:S(2)}) copy-start(bf16[2,256,512]{2,1,0:T(8,128)(2,1)S(1)} %collective-permute-done.1.refs_3_) | copy-start | bytes 1572868
  11.4 12.6 %collective-permute-start.2 = (bf16[2,256,512]{2,1,0:T(8,128)(2,1)S(1)}, bf16[2,256,512]{2,1,0:T(8,128)(2,1)}, u32[]{:S(2)}, u32[]{:S(2)}) collective-permute-start(bf16[2,256,512]{2,1,0:T(8,128)(2,1)S(1)} %collective-permute-done.1.refs_3_), channel_id=1, source_target_pairs={{0,1},{1,2},{2,3},{3,4},{4,5},{5,6},{6,7},{7,8},{8,9},{9,10},{10,1... | collective-permute-start | bytes 1572872 | tf_op jit(solution)/shard_map/ppermute | solution.py:100
  17.9 57.5 %copy-start.9 = (bf16[2,256,512]{2,1,0:T(8,128)(2,1)}, bf16[2,256,512]{2,1,0:T(8,128)(2,1)S(1)}, u32[]{:S(2)}) copy-start(bf16[2,256,512]{2,1,0:T(8,128)(2,1)S(1)} %collective-permute-done.5.refs_3_) | copy-start | bytes 1572868
  17.9 18.5 %collective-permute-start.6 = (bf16[2,256,512]{2,1,0:T(8,128)(2,1)S(1)}, bf16[2,256,512]{2,1,0:T(8,128)(2,1)}, u32[]{:S(2)}, u32[]{:S(2)}) collective-permute-start(bf16[2,256,512]{2,1,0:T(8,128)(2,1)S(1)} %collective-permute-done.5.refs_3_), channel_id=1, source_target_pairs={{0,1},{1,2},{2,3},{3,4},{4,5},{5,6},{6,7},{7,8},{8,9},{9,10},{10,1... | collective-permute-start | bytes 1572872 | tf_op jit(solution)/shard_map/ppermute | solution.py:100
  24.0 14.8 %collective-permute-start.3 = (bf16[2,256,512]{2,1,0:T(8,128)(2,1)}, bf16[2,256,512]{2,1,0:T(8,128)(2,1)}, u32[]{:S(2)}, u32[]{:S(2)}) collective-permute-start(bf16[2,256,512]{2,1,0:T(8,128)(2,1)} %collective-permute-done.2.refs_2_), channel_id=1, source_target_pairs={{0,1},{1,2},{2,3},{3,4},{4,5},{5,6},{6,7},{7,8},{8,9},{9,10},{10,1... | collective-permute-start | bytes 1572872 | tf_op jit(solution)/shard_map/ppermute | solution.py:100
  30.6 25.2 %collective-permute-start = (bf16[1,256,2048]{2,1,0:T(8,128)(2,1)}, bf16[1,256,2048]{2,1,0:T(8,128)(2,1)S(1)}, u32[]{:S(2)}, u32[]{:S(2)}) collective-permute-start(bf16[1,256,2048]{2,1,0:T(8,128)(2,1)} %param.10), channel_id=1, source_target_pairs={{0,224},{32,0},{64,32},{96,64},{128,96},{160,128},{192,160},{224,1... | collective-permute-start | bytes 3145736 | tf_op jit(solution)/shard_map/ppermute | solution.py:94
  36.5 8.6 %collective-permute-start.7 = (bf16[2,256,512]{2,1,0:T(8,128)(2,1)}, bf16[2,256,512]{2,1,0:T(8,128)(2,1)}, u32[]{:S(2)}, u32[]{:S(2)}) collective-permute-start(bf16[2,256,512]{2,1,0:T(8,128)(2,1)} %collective-permute-done.6.refs_2_), channel_id=1, source_target_pairs={{0,1},{1,2},{2,3},{3,4},{4,5},{5,6},{6,7},{7,8},{8,9},{9,10},{10,1... | collective-permute-start | bytes 1572872 | tf_op jit(solution)/shard_map/ppermute | solution.py:100
  38.9 17.0 %collective-permute-start.4 = (bf16[2,256,512]{2,1,0:T(8,128)(2,1)}, bf16[2,256,512]{2,1,0:T(8,128)(2,1)S(1)}, u32[]{:S(2)}, u32[]{:S(2)}) collective-permute-start(bf16[2,256,512]{2,1,0:T(8,128)(2,1)} %collective-permute-done.3.refs_1_), channel_id=1, source_target_pairs={{0,1},{1,2},{2,3},{3,4},{4,5},{5,6},{6,7},{7,8},{8,9},{9,10},{10,1... | collective-permute-start | bytes 1572872 | tf_op jit(solution)/shard_map/ppermute | solution.py:100
  45.1 30.3 %collective-permute-start.8 = (bf16[2,256,512]{2,1,0:T(8,128)(2,1)}, bf16[2,256,512]{2,1,0:T(8,128)(2,1)}, u32[]{:S(2)}, u32[]{:S(2)}) collective-permute-start(bf16[2,256,512]{2,1,0:T(8,128)(2,1)} %collective-permute-done.7.refs_1_), channel_id=1, source_target_pairs={{0,1},{1,2},{2,3},{3,4},{4,5},{5,6},{6,7},{7,8},{8,9},{9,10},{10,1... | collective-permute-start | bytes 1572872 | tf_op jit(solution)/shard_map/ppermute | solution.py:100
  55.9 1.0 copy-start
  55.9 1.1 copy-start.11
  73.3 21.3 %copy-start.1 = (bf16[4,2,256,512]{3,2,1,0:T(8,128)(2,1)S(1)}, bf16[4,2,256,512]{3,2,1,0:T(8,128)(2,1)}, u32[]{:S(2)}) copy-start(bf16[4,2,256,512]{3,2,1,0:T(8,128)(2,1)} %get-tuple-element.12) | copy-start | bytes 6291460
  73.4 21.3 %collective-permute-start.9 = (bf16[2,256,512]{2,1,0:T(8,128)(2,1)S(1)}, bf16[2,256,512]{2,1,0:T(8,128)(2,1)S(1)}, u32[]{:S(2)}, u32[]{:S(2)}) collective-permute-start(bf16[2,256,512]{2,1,0:T(8,128)(2,1)S(1)} %slice_bitcast_fusion.1), channel_id=1, source_target_pairs={{1,0},{2,1},{3,2},{4,3},{5,4},{6,5},{7,6},{8,7},{9,8},{10,9},{11,1... | collective-permute-start | bytes 1572872 | tf_op jit(solution)/shard_map/ppermute | solution.py:100
  90.7 13.8 %copy-start.2 = (bf16[4,2,256,512]{3,2,1,0:T(8,128)(2,1)S(1)}, bf16[4,2,256,512]{3,2,1,0:T(8,128)(2,1)}, u32[]{:S(2)}) copy-start(bf16[4,2,256,512]{3,2,1,0:T(8,128)(2,1)} %get-tuple-element.14) | copy-start | bytes 6291460
  91.9 12.6 %collective-permute-start.13 = (bf16[2,256,512]{2,1,0:T(8,128)(2,1)S(1)}, bf16[2,256,512]{2,1,0:T(8,128)(2,1)S(1)}, u32[]{:S(2)}, u32[]{:S(2)}) collective-permute-start(bf16[2,256,512]{2,1,0:T(8,128)(2,1)S(1)} %slice_bitcast_fusion), channel_id=1, source_target_pairs={{1,0},{2,1},{3,2},{4,3},{5,4},{6,5},{7,6},{8,7},{9,8},{10,9},{11,1... | collective-permute-start | bytes 1572872 | tf_op jit(solution)/shard_map/ppermute | solution.py:100
  94.8 15.3 %collective-permute-start.10 = (bf16[2,256,512]{2,1,0:T(8,128)(2,1)S(1)}, bf16[2,256,512]{2,1,0:T(8,128)(2,1)S(1)}, u32[]{:S(2)}, u32[]{:S(2)}) collective-permute-start(bf16[2,256,512]{2,1,0:T(8,128)(2,1)S(1)} %fusion.8), channel_id=1, source_target_pairs={{1,0},{2,1},{3,2},{4,3},{5,4},{6,5},{7,6},{8,7},{9,8},{10,9},{11,1... | collective-permute-start | bytes 1572872 | tf_op jit(solution)/shard_map/ppermute | solution.py:100
  104.7 12.6 %collective-permute-start.14 = (bf16[2,256,512]{2,1,0:T(8,128)(2,1)S(1)}, bf16[2,256,512]{2,1,0:T(8,128)(2,1)S(1)}, u32[]{:S(2)}, u32[]{:S(2)}) collective-permute-start(bf16[2,256,512]{2,1,0:T(8,128)(2,1)S(1)} %fusion.5), channel_id=1, source_target_pairs={{1,0},{2,1},{3,2},{4,3},{5,4},{6,5},{7,6},{8,7},{9,8},{10,9},{11,1... | collective-permute-start | bytes 1572872 | tf_op jit(solution)/shard_map/ppermute | solution.py:100
  110.3 21.8 %copy-start.7 = (bf16[256,1024]{1,0:T(8,128)(2,1)S(1)}, bf16[256,1024]{1,0:T(8,128)(2,1)}, u32[]{:S(2)}) copy-start(bf16[256,1024]{1,0:T(8,128)(2,1)} %get-tuple-element.9) | copy-start | bytes 1572868
  110.3 21.8 %copy-start.8 = (bf16[256,1024]{1,0:T(8,128)(2,1)S(1)}, bf16[256,1024]{1,0:T(8,128)(2,1)}, u32[]{:S(2)}) copy-start(bf16[256,1024]{1,0:T(8,128)(2,1)} %get-tuple-element.10) | copy-start | bytes 1572868
  110.3 12.7 %collective-permute-start.11 = (bf16[2,256,512]{2,1,0:T(8,128)(2,1)S(1)}, bf16[2,256,512]{2,1,0:T(8,128)(2,1)S(1)}, u32[]{:S(2)}, u32[]{:S(2)}) collective-permute-start(bf16[2,256,512]{2,1,0:T(8,128)(2,1)S(1)} %fusion.7), channel_id=1, source_target_pairs={{1,0},{2,1},{3,2},{4,3},{5,4},{6,5},{7,6},{8,7},{9,8},{10,9},{11,1... | collective-permute-start | bytes 1572872 | tf_op jit(solution)/shard_map/ppermute | solution.py:100
  117.4 12.6 %collective-permute-start.15 = (bf16[2,256,512]{2,1,0:T(8,128)(2,1)S(1)}, bf16[2,256,512]{2,1,0:T(8,128)(2,1)S(1)}, u32[]{:S(2)}, u32[]{:S(2)}) collective-permute-start(bf16[2,256,512]{2,1,0:T(8,128)(2,1)S(1)} %fusion.4), channel_id=1, source_target_pairs={{1,0},{2,1},{3,2},{4,3},{5,4},{6,5},{7,6},{8,7},{9,8},{10,9},{11,1... | collective-permute-start | bytes 1572872 | tf_op jit(solution)/shard_map/ppermute | solution.py:100
  123.2 12.8 %copy-start.5 = (f32[2,256,512]{2,1,0:T(8,128)S(1)}, f32[2,256,512]{2,1,0:T(8,128)}, u32[]{:S(2)}) copy-start(f32[2,256,512]{2,1,0:T(8,128)} %get-tuple-element.11) | copy-start | bytes 3145732
  123.2 12.7 %collective-permute-start.12 = (bf16[2,256,512]{2,1,0:T(8,128)(2,1)S(1)}, bf16[2,256,512]{2,1,0:T(8,128)(2,1)S(1)}, u32[]{:S(2)}, u32[]{:S(2)}) collective-permute-start(bf16[2,256,512]{2,1,0:T(8,128)(2,1)S(1)} %fusion.6), channel_id=1, source_target_pairs={{1,0},{2,1},{3,2},{4,3},{5,4},{6,5},{7,6},{8,7},{9,8},{10,9},{11,1... | collective-permute-start | bytes 1572872 | tf_op jit(solution)/shard_map/ppermute | solution.py:100
  130.2 12.6 %collective-permute-start.16 = (bf16[2,256,512]{2,1,0:T(8,128)(2,1)S(1)}, bf16[2,256,512]{2,1,0:T(8,128)(2,1)S(1)}, u32[]{:S(2)}, u32[]{:S(2)}) collective-permute-start(bf16[2,256,512]{2,1,0:T(8,128)(2,1)S(1)} %fusion.3), channel_id=1, source_target_pairs={{1,0},{2,1},{3,2},{4,3},{5,4},{6,5},{7,6},{8,7},{9,8},{10,9},{11,1... | collective-permute-start | bytes 1572872 | tf_op jit(solution)/shard_map/ppermute | solution.py:100
  133.2 9.6 %copy-start.6 = (f32[2,256,512]{2,1,0:T(8,128)S(1)}, f32[2,256,512]{2,1,0:T(8,128)}, u32[]{:S(2)}) copy-start(f32[2,256,512]{2,1,0:T(8,128)} %get-tuple-element.13) | copy-start | bytes 3145732

commit v10 on v9

--- a/solution.py
+++ b/solution.py
@@ -20,16 +20,17 @@
 
 
 def attention_back_kernel(at_ref, q_ref, do_ref, *refs):
-    blocks = len(refs) - 4
-    piece_refs = refs[:blocks]
-    mask_ref = refs[blocks]
+    blocks = (len(refs) - 4) // 2
+    key_refs = refs[:blocks]
+    value_refs = refs[blocks:2 * blocks]
+    mask_ref = refs[2 * blocks]
     dq_ref, far_ref, own_ref = refs[-3:]
-    head_size = piece_refs[0].shape[2]
+    head_size = key_refs[0].shape[1]
     heads = q_ref.shape[1] // head_size
     rows = q_ref.shape[0]
     allowed = mask_ref[...] > 0
-    keys = jnp.concatenate([ref[0] for ref in piece_refs], axis=0)
-    values = jnp.concatenate([ref[1] for ref in piece_refs], axis=0)
+    keys = jnp.concatenate([ref[...] for ref in key_refs], axis=0)
+    values = jnp.concatenate([ref[...] for ref in value_refs], axis=0)
     queries = jnp.concatenate([q_ref[:, h * head_size:(h + 1) * head_size] for h in range(heads)], axis=0)
     grads = jnp.concatenate([do_ref[:, h * head_size:(h + 1) * head_size] for h in range(heads)], axis=0)
     allowed = jnp.concatenate([allowed] * heads, axis=0)
@@ -58,22 +59,23 @@
     own_ref[1] = value_back[(blocks - 1) * rows:]
 
 
-def attention_back(queries, grads, window_pieces, allowed, query_group, kv_group, groups):
+def attention_back(queries, grads, key_pieces, value_pieces, allowed, query_group, kv_group, groups):
+    window_pieces = key_pieces
     rows, width = queries.shape
     head_size = width // (GROUP * KV_HEADS)
     group_width = GROUP * head_size
     span = rows * len(window_pieces)
     q_spec = pl.BlockSpec((rows, group_width), lambda g, at: (0, g + at[0]))
-    piece_spec = pl.BlockSpec((2, rows, head_size), lambda g, at: (0, 0, g + at[1]))
+    piece_spec = pl.BlockSpec((rows, head_size), lambda g, at: (0, g + at[1]))
     mask_spec = pl.BlockSpec((rows, span), lambda g, at: (0, 0))
     far_spec = pl.BlockSpec((len(window_pieces) - 1, 2, rows, head_size), lambda g, at: (0, 0, 0, g))
     own_spec = pl.BlockSpec((2, rows, head_size), lambda g, at: (0, 0, g))
-    inputs = [queries, grads, *window_pieces, allowed]
+    inputs = [queries, grads, *key_pieces, *value_pieces, allowed]
     dq_spec = pl.BlockSpec((rows, group_width), lambda g, at: (0, g))
     grid_spec = pltpu.PrefetchScalarGridSpec(
         num_scalar_prefetch=1,
         grid=(groups,),
-        in_specs=[q_spec, q_spec] + [piece_spec] * len(window_pieces) + [mask_spec],
+        in_specs=[q_spec, q_spec] + [piece_spec] * (2 * len(window_pieces)) + [mask_spec],
         out_specs=[dq_spec, far_spec, own_spec],
     )
     chunk_width = groups * head_size
@@ -118,7 +120,6 @@
     keys_here = key_rows[0]
     values_here = value_rows[0]
     count_rows = queries.shape[0]
-    reach_blocks = WINDOW // count_rows
     pair_width = keys_here.shape[1]
     head_size = pair_width // KV_HEADS
     rank_here = lax.axis_index("ctx")
@@ -133,34 +134,53 @@
 
     def own_pair_of(chunk):
         cols = slice(chunk * chunk_width, (chunk + 1) * chunk_width)
-        return jnp.stack([keys_here[:, cols], values_here[:, cols]])
-
-    windows = [[own_pair_of(chunk)] for chunk in range(CHUNKS)]
-    for _ in range(reach_blocks):
-        for chunk in range(CHUNKS):
-            windows[chunk].insert(0, shifted(windows[chunk][0], "ctx", 1))
+        return [keys_here[:, cols], values_here[:, cols]]
+
+    odd = (rank_here % 2) == 1
+
+    def partner(value):
+        count = lax.axis_size("ctx")
+        return lax.ppermute(value, "ctx", [(i, i ^ 1) for i in range(count)])
+
+    def forward(own):
+        minus_two = [shifted(half, "ctx", 2) for half in own]
+        minus_one = [partner(jnp.where(odd, a, b)) for a, b in zip(minus_two, own)]
+        minus_four = [shifted(half, "ctx", 2) for half in minus_two]
+        minus_three = [partner(jnp.where(odd, a, b)) for a, b in zip(minus_four, minus_two)]
+        return [minus_four, minus_three, minus_two, minus_one, own]
+
+    def backward(far, own):
+        passed = [partner(jnp.stack([far[3, h], far[1, h]])).astype(jnp.float32) for h in range(2)]
+        to_four, to_two, direct = [], [], []
+        for h in range(2):
+            zero = jnp.zeros_like(passed[h][0])
+            to_four.append(far[0, h].astype(jnp.float32) + jnp.where(odd, passed[h][1], zero))
+            to_two.append(far[2, h].astype(jnp.float32) + jnp.where(odd, passed[h][0], passed[h][1]))
+            direct.append(jnp.where(odd, zero, passed[h][0]))
+        arrived = [shifted(x.astype(jnp.bfloat16), "ctx", -2).astype(jnp.float32) for x in to_four]
+        arrived = [
+            shifted((a + t).astype(jnp.bfloat16), "ctx", -2).astype(jnp.float32)
+            for a, t in zip(arrived, to_two)
+        ]
+        return [(own[h] + (arrived[h] + direct[h])).astype(jnp.bfloat16) for h in range(2)]
+
+    window_a = forward(own_pair_of(0))
+    own_b = list(lax.optimization_barrier((own_pair_of(1), window_a[0]))[0])
+    window_b = forward(own_b)
+    windows = [window_a, window_b]
 
     query_parts = []
     results = []
     for chunk in range(CHUNKS):
         query_part, far, own = attention_back(
-            queries, arriving, windows[chunk], mask, chunk * chunk_groups, 0, chunk_groups
+            queries, arriving, [w[0] for w in windows[chunk]], [w[1] for w in windows[chunk]],
+            mask, chunk * chunk_groups, 0, chunk_groups,
         )
         query_parts.append(query_part)
         results.append((far, own))
     query_back = jnp.concatenate(query_parts, axis=1)
 
-    partials = [far[0] for far, _ in results]
-    for step in range(reach_blocks):
-        for chunk in range(CHUNKS):
-            far = results[chunk][0]
-            arrived = shifted(partials[chunk], "ctx", -1).astype(jnp.float32)
-            if step + 1 < reach_blocks:
-                partials[chunk] = (arrived + far[step + 1].astype(jnp.float32)).astype(jnp.bfloat16)
-            else:
-                partials[chunk] = arrived
-
-    totals = [(own + arrived).astype(jnp.bfloat16) for (_, own), arrived in zip(results, partials)]
+    totals = [backward(far, own) for far, own in results]
     return (
         query_back[None],
         jnp.concatenate([total[0] for total in totals], axis=1)[None],

time: 146 us -> 156 us (1.068)
  local copies, waits for them, and re-layouts: 4.83 us -> 9.22 us
  other arithmetic: 5.84 us -> 8.89 us
  starting transfers between devices: 59.5 us -> 62.4 us
    ppermute x0 -> x12, starting transfers between devices: none -> 13.1 us  [partner(): return lax.ppermute(value, 'ctx', [(i, i ^ 1) for i in range(count)])]
    ppermute x16, starting transfers between devices: 53.8 us -> 43.7 us  [shifted(): lax.ppermute(value, axis, [(source, source + steps) for source in range(i...]
    unnamed x26 -> x52, local copies, waits for them, and re-layouts: 0.57 us -> 3.88 us
    ppermute x1, waiting for transfers between devices: 2.86 us -> 0.01 us  [passed_along(): lax.ppermute(shard, axis, [(i, (i + by) % count) for i in range(count)])]
    squeeze x4 -> x0, local copies, waits for them, and re-layouts: 2.38 us -> none  [the longest x2 2.3 us: local_body(): partials = [far[0] for far, _ in results]]
    select_n x0 -> x4, other arithmetic: none -> 2.04 us  [forward(): minus_one = [partner(jnp.where(odd, a, b)) for a, b in zip(minus_two, own)]]
    slice x0 -> x2, local copies, waits for them, and re-layouts: none -> 2 us  [own_pair_of(): return [keys_here[:, cols], values_here[:, cols]]]
    ppermute x16, waiting for transfers between devices: 40.2 us -> 42.1 us  [shifted(): lax.ppermute(value, axis, [(source, source + steps) for source in range(i...]
  transfers between devices with their start and end apart: 17 -> 29, of which waited for: 11 -> 12; matrix products, arithmetic and copies ran while one was open for 5% -> 8% of each run, Pallas kernels for 21% -> 20%
where the time goes in v10:
time: 156 us; the launch traced here: 155 us
  starting transfers between devices  62.4 us (40%)
  waiting for transfers between devices  42.1 us (27%)
  Pallas kernels  30.9 us (20%)
  local copies, waits for them, and re-layouts  9.22 us (6%)
  other arithmetic  8.89 us (6%)
    ppermute x16, starting transfers between devices, shifted(): lax.ppermute(value, axis, [(source, source + steps) for source in range(i...  43.7 us
    ppermute x16, waiting for transfers between devices, shifted(): lax.ppermute(value, axis, [(source, source + steps) for source in range(i...  42.1 us
    pallas_call x2, Pallas kernels, attention_back(): pl.pallas_call(attention_back_kernel, grid_spec=grid_spec, out_shape=[jax...  30.9 us
    ppermute x12, starting transfers between devices, partner(): return lax.ppermute(value, 'ctx', [(i, i ^ 1) for i in range(count)])  13.1 us
    ppermute x1, starting transfers between devices, passed_along(): lax.ppermute(shard, axis, [(i, (i + by) % count) for i in range(count)])  5.65 us
    unnamed x52, local copies, waits for them, and re-layouts  3.88 us
  transfers between devices with their start and end apart: 29, of which 12 were waited for; matrix products, arithmetic and copies ran while one was open for 8% of the time, Pallas kernels for 20%

profile of v10, /device:TPU:25, one launch (start us, length us, event | category | flops | bytes accessed | tf_op | source)
XLA Modules:
  0.0 154.7 jit_solution(16733878498689729072)
XLA Ops:
  0.6 1.0 slice.136.refs_4_
  1.7 2.8 %collective-permute-start.1 = (bf16[256,512]{1,0:T(8,128)(2,1)S(1)}, bf16[256,512]{1,0:T(8,128)(2,1)S(1)}, u32[]{:S(2)}, u32[]{:S(2)}) collective-permute-start(bf16[256,512]{1,0:T(8,128)(2,1)S(1)} %slice.136.refs_4_), channel_id=1, source_target_pairs={{0,2},{1,3},{2,4},{3,5},{4,6},{5,7},{6,8},{7,9},{8,10},{9,11},{10,... | collective-permute-start | bytes 786440 | tf_op jit(solution)/shard_map/ppermute | solution.py:102
  4.5 1.0 slice.137.refs_9_
  5.5 3.2 %collective-permute-start.5 = (bf16[256,512]{1,0:T(8,128)(2,1)S(1)}, bf16[256,512]{1,0:T(8,128)(2,1)S(1)}, u32[]{:S(2)}, u32[]{:S(2)}) collective-permute-start(bf16[256,512]{1,0:T(8,128)(2,1)S(1)} %slice.137.refs_9_), channel_id=1, source_target_pairs={{0,2},{1,3},{2,4},{3,5},{4,6},{5,7},{6,8},{7,9},{8,10},{9,11},{10,... | collective-permute-start | bytes 786440 | tf_op jit(solution)/shard_map/ppermute | solution.py:102
  8.7 2.1 %collective-permute-done.1.refs_2_ = bf16[256,512]{1,0:T(8,128)(2,1)S(1)} collective-permute-done((bf16[256,512]{1,0:T(8,128)(2,1)S(1)}, bf16[256,512]{1,0:T(8,128)(2,1)S(1)}, u32[]{:S(2)}, u32[]{:S(2)}) %collective-permute-start.1) | collective-permute-done | bytes 262176 | tf_op jit(solution)/shard_map/ppermute | solution.py:102
  10.8 4.9 %collective-permute-start.2 = (bf16[256,512]{1,0:T(8,128)(2,1)S(1)}, bf16[256,512]{1,0:T(8,128)(2,1)S(1)}, u32[]{:S(2)}, u32[]{:S(2)}) collective-permute-start(bf16[256,512]{1,0:T(8,128)(2,1)S(1)} %collective-permute-done.1.refs_2_), channel_id=1, source_target_pairs={{0,2},{1,3},{2,4},{3,5},{4,6},{5,7},{6,8},{7,9},{8,10},{9,11},{10,... | collective-permute-start | bytes 786440 | tf_op jit(solution)/shard_map/ppermute | solution.py:102
  15.7 5.7 %collective-permute-start = (bf16[1,256,2048]{2,1,0:T(8,128)(2,1)}, bf16[1,256,2048]{2,1,0:T(8,128)(2,1)S(1)}, u32[]{:S(2)}, u32[]{:S(2)}) collective-permute-start(bf16[1,256,2048]{2,1,0:T(8,128)(2,1)} %param.10), channel_id=1, source_target_pairs={{0,224},{32,0},{64,32},{96,64},{128,96},{160,128},{192,160},{224,1... | collective-permute-start | bytes 3145736 | tf_op jit(solution)/shard_map/ppermute | solution.py:96
  21.3 0.8 reduce-window.8
  22.2 1.9 %collective-permute-start.6 = (bf16[256,512]{1,0:T(8,128)(2,1)S(1)}, bf16[256,512]{1,0:T(8,128)(2,1)S(1)}, u32[]{:S(2)}, u32[]{:S(2)}) collective-permute-start(bf16[256,512]{1,0:T(8,128)(2,1)S(1)} %collective-permute-done.5.refs_7_), channel_id=1, source_target_pairs={{0,2},{1,3},{2,4},{3,5},{4,6},{5,7},{6,8},{7,9},{8,10},{9,11},{10,... | collective-permute-start | bytes 786440 | tf_op jit(solution)/shard_map/ppermute | solution.py:102
  24.2 1.2 broadcast_select_fusion.6
  25.4 4.3 %collective-permute-done.6.refs_5_ = bf16[256,512]{1,0:T(8,128)(2,1)S(1)} collective-permute-done((bf16[256,512]{1,0:T(8,128)(2,1)S(1)}, bf16[256,512]{1,0:T(8,128)(2,1)S(1)}, u32[]{:S(2)}, u32[]{:S(2)}) %collective-permute-start.6) | collective-permute-done | bytes 262176 | tf_op jit(solution)/shard_map/ppermute | solution.py:102
  29.7 3.7 %collective-permute-start.13 = (bf16[256,512]{1,0:T(8,128)(2,1)S(1)}, bf16[256,512]{1,0:T(8,128)(2,1)S(1)}, u32[]{:S(2)}, u32[]{:S(2)}) collective-permute-start(bf16[256,512]{1,0:T(8,128)(2,1)S(1)} %get-tuple-element.13.refs_9_), channel_id=1, source_target_pairs={{0,2},{1,3},{2,4},{3,5},{4,6},{5,7},{6,8},{7,9},{8,10},{9,11},{10,... | collective-permute-start | bytes 786440 | tf_op jit(solution)/shard_map/ppermute | solution.py:102
  33.5 1.9 %collective-permute-start.9 = (bf16[256,512]{1,0:T(8,128)(2,1)S(1)}, bf16[256,512]{1,0:T(8,128)(2,1)S(1)}, u32[]{:S(2)}, u32[]{:S(2)}) collective-permute-start(bf16[256,512]{1,0:T(8,128)(2,1)S(1)} %get-tuple-element.12.refs_4_), channel_id=1, source_target_pairs={{0,2},{1,3},{2,4},{3,5},{4,6},{5,7},{6,8},{7,9},{8,10},{9,11},{10,... | collective-permute-start | bytes 786440 | tf_op jit(solution)/shard_map/ppermute | solution.py:102
  35.5 1.6 %collective-permute-done.13.refs_7_ = bf16[256,512]{1,0:T(8,128)(2,1)S(1)} collective-permute-done((bf16[256,512]{1,0:T(8,128)(2,1)S(1)}, bf16[256,512]{1,0:T(8,128)(2,1)S(1)}, u32[]{:S(2)}, u32[]{:S(2)}) %collective-permute-start.13) | collective-permute-done | bytes 262176 | tf_op jit(solution)/shard_map/ppermute | solution.py:102
  37.1 5.5 %collective-permute-start.14 = (bf16[256,512]{1,0:T(8,128)(2,1)S(1)}, bf16[256,512]{1,0:T(8,128)(2,1)S(1)}, u32[]{:S(2)}, u32[]{:S(2)}) collective-permute-start(bf16[256,512]{1,0:T(8,128)(2,1)S(1)} %collective-permute-done.13.refs_7_), channel_id=1, source_target_pairs={{0,2},{1,3},{2,4},{3,5},{4,6},{5,7},{6,8},{7,9},{8,10},{9,11},{10,... | collective-permute-start | bytes 786440 | tf_op jit(solution)/shard_map/ppermute | solution.py:102
  42.7 0.2 collective-permute-done.9.refs_2_
  42.9 3.9 %collective-permute-start.10 = (bf16[256,512]{1,0:T(8,128)(2,1)S(1)}, bf16[256,512]{1,0:T(8,128)(2,1)S(1)}, u32[]{:S(2)}, u32[]{:S(2)}) collective-permute-start(bf16[256,512]{1,0:T(8,128)(2,1)S(1)} %collective-permute-done.9.refs_2_), channel_id=1, source_target_pairs={{0,2},{1,3},{2,4},{3,5},{4,6},{5,7},{6,8},{7,9},{8,10},{9,11},{10,... | collective-permute-start | bytes 786440 | tf_op jit(solution)/shard_map/ppermute | solution.py:102
  46.9 1.4 convert_convert_fusion.refs_10_
  48.2 7.3 %collective-permute-start.3 = (bf16[256,512]{1,0:T(8,128)(2,1)S(1)}, bf16[256,512]{1,0:T(8,128)(2,1)S(1)}, u32[]{:S(2)}, u32[]{:S(2)}) collective-permute-start(bf16[256,512]{1,0:T(8,128)(2,1)S(1)} %get-tuple-element.44), channel_id=1, source_target_pairs={{0,1},{1,0},{2,3},{3,2},{4,5},{5,4},{6,7},{7,6},{8,9},{9,8},{10,11... | collective-permute-start | bytes 786440 | tf_op jit(solution)/shard_map/ppermute | solution.py:143
  55.7 0.4 collective-permute-start.7
  56.1 2.7 %collective-permute-start.8 = (bf16[256,512]{1,0:T(8,128)(2,1)S(1)}, bf16[256,512]{1,0:T(8,128)(2,1)S(1)}, u32[]{:S(2)}, u32[]{:S(2)}) collective-permute-start(bf16[256,512]{1,0:T(8,128)(2,1)S(1)} %get-tuple-element.39), channel_id=1, source_target_pairs={{0,1},{1,0},{2,3},{3,2},{4,5},{5,4},{6,7},{7,6},{8,9},{9,8},{10,11... | collective-permute-start | bytes 786440 | tf_op jit(solution)/shard_map/ppermute | solution.py:143
  58.8 0.7 broadcast_select_fusion
  59.6 0.7 copy-done.22
  60.3 0.7 copy-done.23
  61.0 0.5 collective-permute-start.16
  61.6 0.4 collective-permute-start.12
  62.0 0.2 copy-done.24
  62.3 0.7 call_exported.0.at_ref
  63.2 15.5 %shard_map.94 = (bf16[256,1024]{1,0:T(8,128)(2,1)}, bf16[4,2,256,512]{3,2,1,0:T(8,128)(2,1)}, f32[2,256,512]{2,1,0:T(8,128)}) custom-call(s32[2]{0:T(128)} %call_exported.0.at_ref, bf16[256,2048]{1,0:T(8,128)(2,1)} %bitcast.100, bf16[256,2048]{1,0:T(8,128)(2,1)} %bitcast.102, bf16[256,512]{1,0:T(8,128)(2,1)} %copy-done.16, bf16[256,512]{1,0:T(8,128)(2,1)} %copy-done.22, ...), custom_call_target="tpu_custom_call" | custom-call | tf_op jit(solution)/shard_map/pallas_call | solution.py:82
  78.7 1.3 slice_bitcast_fusion.3
  80.0 0.2 collective-permute-start.17
  80.3 0.7 collective-permute-start.23
  81.0 0.7 copy-done.21
  81.6 15.5 %shard_map.95 = (bf16[256,1024]{1,0:T(8,128)(2,1)}, bf16[4,2,256,512]{3,2,1,0:T(8,128)(2,1)}, f32[2,256,512]{2,1,0:T(8,128)}) custom-call(s32[2]{0:T(128)} %constant.39.clone.at_ref, bf16[256,2048]{1,0:T(8,128)(2,1)} %bitcast.101, bf16[256,2048]{1,0:T(8,128)(2,1)} %bitcast.103, bf16[256,512]{1,0:T(8,128)(2,1)} %copy-done.9, ...), custom_call_target="tpu_custom_call" | custom-call | tf_op jit(solution)/shard_map/pallas_call | solution.py:82
  97.1 1.3 slice_bitcast_fusion.1
  98.5 0.2 collective-permute-start.20
  98.8 0.5 collective-permute-start.26
  99.3 1.1 maximum_bitcast_fusion
  100.6 1.3 copy-done.3
  101.9 0.2 fusion.8
  102.1 2.1 %collective-permute-start.18 = (bf16[256,512]{1,0:T(8,128)(2,1)S(1)}, bf16[256,512]{1,0:T(8,128)(2,1)S(1)}, u32[]{:S(2)}, u32[]{:S(2)}) collective-permute-start(bf16[256,512]{1,0:T(8,128)(2,1)S(1)} %get-tuple-element.22), channel_id=1, source_target_pairs={{2,0},{3,1},{4,2},{5,3},{6,4},{7,5},{8,6},{9,7},{10,8},{11,9},{12,... | collective-permute-start | bytes 786440 | tf_op jit(solution)/shard_map/ppermute | solution.py:102
  104.2 1.9 %collective-permute-start.24 = (bf16[256,512]{1,0:T(8,128)(2,1)S(1)}, bf16[256,512]{1,0:T(8,128)(2,1)S(1)}, u32[]{:S(2)}, u32[]{:S(2)}) collective-permute-start(bf16[256,512]{1,0:T(8,128)(2,1)S(1)} %get-tuple-element.21), channel_id=1, source_target_pairs={{2,0},{3,1},{4,2},{5,3},{6,4},{7,5},{8,6},{9,7},{10,8},{11,9},{12,... | collective-permute-start | bytes 786440 | tf_op jit(solution)/shard_map/ppermute | solution.py:102
  106.1 0.1 convert_element_type.148
  106.3 0.1 convert_element_type.168
  106.4 0.2 fusion.5
  106.6 1.9 %collective-permute-start.21 = (bf16[256,512]{1,0:T(8,128)(2,1)S(1)}, bf16[256,512]{1,0:T(8,128)(2,1)S(1)}, u32[]{:S(2)}, u32[]{:S(2)}) collective-permute-start(bf16[256,512]{1,0:T(8,128)(2,1)S(1)} %get-tuple-element.30), channel_id=1, source_target_pairs={{2,0},{3,1},{4,2},{5,3},{6,4},{7,5},{8,6},{9,7},{10,8},{11,9},{12,... | collective-permute-start | bytes 786440 | tf_op jit(solution)/shard_map/ppermute | solution.py:102
  108.5 1.9 %collective-permute-start.27 = (bf16[256,512]{1,0:T(8,128)(2,1)S(1)}, bf16[256,512]{1,0:T(8,128)(2,1)S(1)}, u32[]{:S(2)}, u32[]{:S(2)}) collective-permute-start(bf16[256,512]{1,0:T(8,128)(2,1)S(1)} %get-tuple-element.29), channel_id=1, source_target_pairs={{2,0},{3,1},{4,2},{5,3},{6,4},{7,5},{8,6},{9,7},{10,8},{11,9},{12,... | collective-permute-start | bytes 786440 | tf_op jit(solution)/shard_map/ppermute | solution.py:102
  110.4 3.6 %collective-permute-done.18 = bf16[256,512]{1,0:T(8,128)(2,1)S(1)} collective-permute-done((bf16[256,512]{1,0:T(8,128)(2,1)S(1)}, bf16[256,512]{1,0:T(8,128)(2,1)S(1)}, u32[]{:S(2)}, u32[]{:S(2)}) %collective-permute-start.18) | collective-permute-done | bytes 262176 | tf_op jit(solution)/shard_map/ppermute | solution.py:102
  114.0 5.6 %collective-permute-done.24 = bf16[256,512]{1,0:T(8,128)(2,1)S(1)} collective-permute-done((bf16[256,512]{1,0:T(8,128)(2,1)S(1)}, bf16[256,512]{1,0:T(8,128)(2,1)S(1)}, u32[]{:S(2)}, u32[]{:S(2)}) %collective-permute-start.24) | collective-permute-done | bytes 262176 | tf_op jit(solution)/shard_map/ppermute | solution.py:102
  119.6 0.3 fusion.7
  120.0 2.1 %collective-permute-start.19 = (bf16[256,512]{1,0:T(8,128)(2,1)S(1)}, bf16[256,512]{1,0:T(8,128)(2,1)S(1)}, u32[]{:S(2)}, u32[]{:S(2)}) collective-permute-start(bf16[256,512]{1,0:T(8,128)(2,1)S(1)} %get-tuple-element.20), channel_id=1, source_target_pairs={{2,0},{3,1},{4,2},{5,3},{6,4},{7,5},{8,6},{9,7},{10,8},{11,9},{12,... | collective-permute-start | bytes 786440 | tf_op jit(solution)/shard_map/ppermute | solution.py:102
  122.0 1.9 %collective-permute-start.25 = (bf16[256,512]{1,0:T(8,128)(2,1)S(1)}, bf16[256,512]{1,0:T(8,128)(2,1)S(1)}, u32[]{:S(2)}, u32[]{:S(2)}) collective-permute-start(bf16[256,512]{1,0:T(8,128)(2,1)S(1)} %get-tuple-element.19), channel_id=1, source_target_pairs={{2,0},{3,1},{4,2},{5,3},{6,4},{7,5},{8,6},{9,7},{10,8},{11,9},{12,... | collective-permute-start | bytes 786440 | tf_op jit(solution)/shard_map/ppermute | solution.py:102
  124.0 1.3 collective-permute-done.21
  125.2 5.6 %collective-permute-done.27 = bf16[256,512]{1,0:T(8,128)(2,1)S(1)} collective-permute-done((bf16[256,512]{1,0:T(8,128)(2,1)S(1)}, bf16[256,512]{1,0:T(8,128)(2,1)S(1)}, u32[]{:S(2)}, u32[]{:S(2)}) %collective-permute-start.27) | collective-permute-done | bytes 262176 | tf_op jit(solution)/shard_map/ppermute | solution.py:102
  130.9 0.3 fusion.4
  131.2 2.1 %collective-permute-start.22 = (bf16[256,512]{1,0:T(8,128)(2,1)S(1)}, bf16[256,512]{1,0:T(8,128)(2,1)S(1)}, u32[]{:S(2)}, u32[]{:S(2)}) collective-permute-start(bf16[256,512]{1,0:T(8,128)(2,1)S(1)} %get-tuple-element.28), channel_id=1, source_target_pairs={{2,0},{3,1},{4,2},{5,3},{6,4},{7,5},{8,6},{9,7},{10,8},{11,9},{12,... | collective-permute-start | bytes 786440 | tf_op jit(solution)/shard_map/ppermute | solution.py:102
  133.3 1.9 %collective-permute-start.28 = (bf16[256,512]{1,0:T(8,128)(2,1)S(1)}, bf16[256,512]{1,0:T(8,128)(2,1)S(1)}, u32[]{:S(2)}, u32[]{:S(2)}) collective-permute-start(bf16[256,512]{1,0:T(8,128)(2,1)S(1)} %get-tuple-element.27), channel_id=1, source_target_pairs={{2,0},{3,1},{4,2},{5,3},{6,4},{7,5},{8,6},{9,7},{10,8},{11,9},{12,... | collective-permute-start | bytes 786440 | tf_op jit(solution)/shard_map/ppermute | solution.py:102
  135.2 1.3 collective-permute-done.19
  136.5 5.6 %collective-permute-done.25 = bf16[256,512]{1,0:T(8,128)(2,1)S(1)} collective-permute-done((bf16[256,512]{1,0:T(8,128)(2,1)S(1)}, bf16[256,512]{1,0:T(8,128)(2,1)S(1)}, u32[]{:S(2)}, u32[]{:S(2)}) %collective-permute-start.25) | collective-permute-done | bytes 262176 | tf_op jit(solution)/shard_map/ppermute | solution.py:102
  142.1 0.3 fusion.18
  142.4 5.3 %collective-permute-done.22 = bf16[256,512]{1,0:T(8,128)(2,1)S(1)} collective-permute-done((bf16[256,512]{1,0:T(8,128)(2,1)S(1)}, bf16[256,512]{1,0:T(8,128)(2,1)S(1)}, u32[]{:S(2)}, u32[]{:S(2)}) %collective-permute-start.22) | collective-permute-done | bytes 262176 | tf_op jit(solution)/shard_map/ppermute | solution.py:102
  147.7 5.6 %collective-permute-done.28 = bf16[256,512]{1,0:T(8,128)(2,1)S(1)} collective-permute-done((bf16[256,512]{1,0:T(8,128)(2,1)S(1)}, bf16[256,512]{1,0:T(8,128)(2,1)S(1)}, u32[]{:S(2)}, u32[]{:S(2)}) %collective-permute-start.28) | collective-permute-done | bytes 262176 | tf_op jit(solution)/shard_map/ppermute | solution.py:102
  153.3 0.3 fusion.16
  153.6 1.1 maximum_bitcast_fusion.1
  (80 shorter events, 1.3 us)
Async XLA Ops:
  0.6 29.0 %copy-start.5 = (bf16[1,256,1024]{2,1,0:T(8,128)(2,1)S(1)}, bf16[1,256,1024]{2,1,0:T(8,128)(2,1)}, u32[]{:S(2)}) copy-start(bf16[1,256,1024]{2,1,0:T(8,128)(2,1)} %param.9) | copy-start | bytes 1572868
  1.7 28.0 %copy-start.10 = (bf16[256,512]{1,0:T(8,128)(2,1)}, bf16[256,512]{1,0:T(8,128)(2,1)S(1)}, u32[]{:S(2)}) copy-start(bf16[256,512]{1,0:T(8,128)(2,1)S(1)} %slice.136.refs_4_) | copy-start | bytes 786436
  1.7 9.1 %collective-permute-start.1 = (bf16[256,512]{1,0:T(8,128)(2,1)S(1)}, bf16[256,512]{1,0:T(8,128)(2,1)S(1)}, u32[]{:S(2)}, u32[]{:S(2)}) collective-permute-start(bf16[256,512]{1,0:T(8,128)(2,1)S(1)} %slice.136.refs_4_), channel_id=1, source_target_pairs={{0,2},{1,3},{2,4},{3,5},{4,6},{5,7},{6,8},{7,9},{8,10},{9,11},{10,... | collective-permute-start | bytes 786440 | tf_op jit(solution)/shard_map/ppermute | solution.py:102
  5.4 42.8 %copy-start.11 = (bf16[256,512]{1,0:T(8,128)(2,1)}, bf16[256,512]{1,0:T(8,128)(2,1)S(1)}, u32[]{:S(2)}) copy-start(bf16[256,512]{1,0:T(8,128)(2,1)S(1)} %slice.137.refs_9_) | copy-start | bytes 786436
  5.5 16.8 %collective-permute-start.5 = (bf16[256,512]{1,0:T(8,128)(2,1)S(1)}, bf16[256,512]{1,0:T(8,128)(2,1)S(1)}, u32[]{:S(2)}, u32[]{:S(2)}) collective-permute-start(bf16[256,512]{1,0:T(8,128)(2,1)S(1)} %slice.137.refs_9_), channel_id=1, source_target_pairs={{0,2},{1,3},{2,4},{3,5},{4,6},{5,7},{6,8},{7,9},{8,10},{9,11},{10,... | collective-permute-start | bytes 786440 | tf_op jit(solution)/shard_map/ppermute | solution.py:102
  10.8 37.5 %copy-start.14 = (bf16[256,512]{1,0:T(8,128)(2,1)}, bf16[256,512]{1,0:T(8,128)(2,1)S(1)}, u32[]{:S(2)}) copy-start(bf16[256,512]{1,0:T(8,128)(2,1)S(1)} %collective-permute-done.1.refs_2_) | copy-start | bytes 786436
  10.8 13.4 %collective-permute-start.2 = (bf16[256,512]{1,0:T(8,128)(2,1)S(1)}, bf16[256,512]{1,0:T(8,128)(2,1)S(1)}, u32[]{:S(2)}, u32[]{:S(2)}) collective-permute-start(bf16[256,512]{1,0:T(8,128)(2,1)S(1)} %collective-permute-done.1.refs_2_), channel_id=1, source_target_pairs={{0,2},{1,3},{2,4},{3,5},{4,6},{5,7},{6,8},{7,9},{8,10},{9,11},{10,... | collective-permute-start | bytes 786440 | tf_op jit(solution)/shard_map/ppermute | solution.py:102
  15.7 46.4 %collective-permute-start = (bf16[1,256,2048]{2,1,0:T(8,128)(2,1)}, bf16[1,256,2048]{2,1,0:T(8,128)(2,1)S(1)}, u32[]{:S(2)}, u32[]{:S(2)}) collective-permute-start(bf16[1,256,2048]{2,1,0:T(8,128)(2,1)} %param.10), channel_id=1, source_target_pairs={{0,224},{32,0},{64,32},{96,64},{128,96},{160,128},{192,160},{224,1... | collective-permute-start | bytes 3145736 | tf_op jit(solution)/shard_map/ppermute | solution.py:96
  22.2 26.0 %copy-start.15 = (bf16[256,512]{1,0:T(8,128)(2,1)}, bf16[256,512]{1,0:T(8,128)(2,1)S(1)}, u32[]{:S(2)}) copy-start(bf16[256,512]{1,0:T(8,128)(2,1)S(1)} %collective-permute-done.5.refs_7_) | copy-start | bytes 786436
  22.2 7.4 %collective-permute-start.6 = (bf16[256,512]{1,0:T(8,128)(2,1)S(1)}, bf16[256,512]{1,0:T(8,128)(2,1)S(1)}, u32[]{:S(2)}, u32[]{:S(2)}) collective-permute-start(bf16[256,512]{1,0:T(8,128)(2,1)S(1)} %collective-permute-done.5.refs_7_), channel_id=1, source_target_pairs={{0,2},{1,3},{2,4},{3,5},{4,6},{5,7},{6,8},{7,9},{8,10},{9,11},{10,... | collective-permute-start | bytes 786440 | tf_op jit(solution)/shard_map/ppermute | solution.py:102
  24.2 24.1 %copy-start.16 = (bf16[256,512]{1,0:T(8,128)(2,1)}, bf16[256,512]{1,0:T(8,128)(2,1)S(1)}, u32[]{:S(2)}) copy-start(bf16[256,512]{1,0:T(8,128)(2,1)S(1)} %collective-permute-done.2.refs_0_) | copy-start | bytes 786436
  25.4 34.2 %copy-start.1 = (bf16[256,512]{1,0:T(8,128)(2,1)}, bf16[256,512]{1,0:T(8,128)(2,1)S(1)}, u32[]{:S(2)}) copy-start(bf16[256,512]{1,0:T(8,128)(2,1)S(1)} %get-tuple-element.12.refs_4_) | copy-start | bytes 786436
  29.6 5.9 %copy-start.17 = (bf16[256,512]{1,0:T(8,128)(2,1)}, bf16[256,512]{1,0:T(8,128)(2,1)S(1)}, u32[]{:S(2)}) copy-start(bf16[256,512]{1,0:T(8,128)(2,1)S(1)} %collective-permute-done.6.refs_5_) | copy-start | bytes 786436
  29.7 48.9 %copy-start.2 = (bf16[256,512]{1,0:T(8,128)(2,1)}, bf16[256,512]{1,0:T(8,128)(2,1)S(1)}, u32[]{:S(2)}) copy-start(bf16[256,512]{1,0:T(8,128)(2,1)S(1)} %get-tuple-element.13.refs_9_) | copy-start | bytes 786436
  29.7 7.4 %collective-permute-start.13 = (bf16[256,512]{1,0:T(8,128)(2,1)S(1)}, bf16[256,512]{1,0:T(8,128)(2,1)S(1)}, u32[]{:S(2)}, u32[]{:S(2)}) collective-permute-start(bf16[256,512]{1,0:T(8,128)(2,1)S(1)} %get-tuple-element.13.refs_9_), channel_id=1, source_target_pairs={{0,2},{1,3},{2,4},{3,5},{4,6},{5,7},{6,8},{7,9},{8,10},{9,11},{10,... | collective-permute-start | bytes 786440 | tf_op jit(solution)/shard_map/ppermute | solution.py:102
  33.5 9.4 %collective-permute-start.9 = (bf16[256,512]{1,0:T(8,128)(2,1)S(1)}, bf16[256,512]{1,0:T(8,128)(2,1)S(1)}, u32[]{:S(2)}, u32[]{:S(2)}) collective-permute-start(bf16[256,512]{1,0:T(8,128)(2,1)S(1)} %get-tuple-element.12.refs_4_), channel_id=1, source_target_pairs={{0,2},{1,3},{2,4},{3,5},{4,6},{5,7},{6,8},{7,9},{8,10},{9,11},{10,... | collective-permute-start | bytes 786440 | tf_op jit(solution)/shard_map/ppermute | solution.py:102
  37.1 41.5 %copy-start.6 = (bf16[256,512]{1,0:T(8,128)(2,1)}, bf16[256,512]{1,0:T(8,128)(2,1)S(1)}, u32[]{:S(2)}) copy-start(bf16[256,512]{1,0:T(8,128)(2,1)S(1)} %collective-permute-done.13.refs_7_) | copy-start | bytes 786436
  37.1 18.5 %collective-permute-start.14 = (bf16[256,512]{1,0:T(8,128)(2,1)S(1)}, bf16[256,512]{1,0:T(8,128)(2,1)S(1)}, u32[]{:S(2)}, u32[]{:S(2)}) collective-permute-start(bf16[256,512]{1,0:T(8,128)(2,1)S(1)} %collective-permute-done.13.refs_7_), channel_id=1, source_target_pairs={{0,2},{1,3},{2,4},{3,5},{4,6},{5,7},{6,8},{7,9},{8,10},{9,11},{10,... | collective-permute-start | bytes 786440 | tf_op jit(solution)/shard_map/ppermute | solution.py:102
  42.9 35.8 %copy-start.7 = (bf16[256,512]{1,0:T(8,128)(2,1)}, bf16[256,512]{1,0:T(8,128)(2,1)S(1)}, u32[]{:S(2)}) copy-start(bf16[256,512]{1,0:T(8,128)(2,1)S(1)} %collective-permute-done.9.refs_2_) | copy-start | bytes 786436
  42.9 13.2 %collective-permute-start.10 = (bf16[256,512]{1,0:T(8,128)(2,1)S(1)}, bf16[256,512]{1,0:T(8,128)(2,1)S(1)}, u32[]{:S(2)}, u32[]{:S(2)}) collective-permute-start(bf16[256,512]{1,0:T(8,128)(2,1)S(1)} %collective-permute-done.9.refs_2_), channel_id=1, source_target_pairs={{0,2},{1,3},{2,4},{3,5},{4,6},{5,7},{6,8},{7,9},{8,10},{9,11},{10,... | collective-permute-start | bytes 786440 | tf_op jit(solution)/shard_map/ppermute | solution.py:102
  48.2 11.3 %collective-permute-start.3 = (bf16[256,512]{1,0:T(8,128)(2,1)S(1)}, bf16[256,512]{1,0:T(8,128)(2,1)S(1)}, u32[]{:S(2)}, u32[]{:S(2)}) collective-permute-start(bf16[256,512]{1,0:T(8,128)(2,1)S(1)} %get-tuple-element.44), channel_id=1, source_target_pairs={{0,1},{1,0},{2,3},{3,2},{4,5},{5,4},{6,7},{7,6},{8,9},{9,8},{10,11... | collective-permute-start | bytes 786440 | tf_op jit(solution)/shard_map/ppermute | solution.py:143
  55.6 4.8 %collective-permute-start.4 = (bf16[256,512]{1,0:T(8,128)(2,1)S(1)}, bf16[256,512]{1,0:T(8,128)(2,1)S(1)}, u32[]{:S(2)}, u32[]{:S(2)}) collective-permute-start(bf16[256,512]{1,0:T(8,128)(2,1)S(1)} %get-tuple-element.41), channel_id=1, source_target_pairs={{0,1},{1,0},{2,3},{3,2},{4,5},{5,4},{6,7},{7,6},{8,9},{9,8},{10,11... | collective-permute-start | bytes 786440 | tf_op jit(solution)/shard_map/ppermute | solution.py:143
  55.7 23.0 %copy-start.8 = (bf16[256,512]{1,0:T(8,128)(2,1)}, bf16[256,512]{1,0:T(8,128)(2,1)S(1)}, u32[]{:S(2)}) copy-start(bf16[256,512]{1,0:T(8,128)(2,1)S(1)} %collective-permute-done.14.refs_5_) | copy-start | bytes 786436
  55.7 5.8 %collective-permute-start.7 = (bf16[256,512]{1,0:T(8,128)(2,1)S(1)}, bf16[256,512]{1,0:T(8,128)(2,1)S(1)}, u32[]{:S(2)}, u32[]{:S(2)}) collective-permute-start(bf16[256,512]{1,0:T(8,128)(2,1)S(1)} %get-tuple-element.43), channel_id=1, source_target_pairs={{0,1},{1,0},{2,3},{3,2},{4,5},{5,4},{6,7},{7,6},{8,9},{9,8},{10,11... | collective-permute-start | bytes 786440 | tf_op jit(solution)/shard_map/ppermute | solution.py:143
  56.1 22.6 %copy-start.9 = (bf16[256,512]{1,0:T(8,128)(2,1)}, bf16[256,512]{1,0:T(8,128)(2,1)S(1)}, u32[]{:S(2)}) copy-start(bf16[256,512]{1,0:T(8,128)(2,1)S(1)} %collective-permute-done.10.refs_0_) | copy-start | bytes 786436
  56.1 5.5 %collective-permute-start.8 = (bf16[256,512]{1,0:T(8,128)(2,1)S(1)}, bf16[256,512]{1,0:T(8,128)(2,1)S(1)}, u32[]{:S(2)}, u32[]{:S(2)}) collective-permute-start(bf16[256,512]{1,0:T(8,128)(2,1)S(1)} %get-tuple-element.39), channel_id=1, source_target_pairs={{0,1},{1,0},{2,3},{3,2},{4,5},{5,4},{6,7},{7,6},{8,9},{9,8},{10,11... | collective-permute-start | bytes 786440 | tf_op jit(solution)/shard_map/ppermute | solution.py:143
  59.6 0.7 copy-start.22
  60.3 20.0 %collective-permute-start.15 = (bf16[256,512]{1,0:T(8,128)(2,1)}, bf16[256,512]{1,0:T(8,128)(2,1)S(1)}, u32[]{:S(2)}, u32[]{:S(2)}) collective-permute-start(bf16[256,512]{1,0:T(8,128)(2,1)} %get-tuple-element.46), channel_id=1, source_target_pairs={{0,1},{1,0},{2,3},{3,2},{4,5},{5,4},{6,7},{7,6},{8,9},{9,8},{10,11... | collective-permute-start | bytes 786440 | tf_op jit(solution)/shard_map/ppermute | solution.py:143
  60.3 0.7 copy-start.23
  61.0 19.9 %collective-permute-start.16 = (bf16[256,512]{1,0:T(8,128)(2,1)S(1)}, bf16[256,512]{1,0:T(8,128)(2,1)S(1)}, u32[]{:S(2)}, u32[]{:S(2)}) collective-permute-start(bf16[256,512]{1,0:T(8,128)(2,1)S(1)} %get-tuple-element.45), channel_id=1, source_target_pairs={{0,1},{1,0},{2,3},{3,2},{4,5},{5,4},{6,7},{7,6},{8,9},{9,8},{10,11... | collective-permute-start | bytes 786440 | tf_op jit(solution)/shard_map/ppermute | solution.py:143
  61.5 0.7 copy-start.24
  61.5 19.4 %collective-permute-start.11 = (bf16[256,512]{1,0:T(8,128)(2,1)S(1)}, bf16[256,512]{1,0:T(8,128)(2,1)}, u32[]{:S(2)}, u32[]{:S(2)}) collective-permute-start(bf16[256,512]{1,0:T(8,128)(2,1)S(1)} %get-tuple-element.48), channel_id=1, source_target_pairs={{0,1},{1,0},{2,3},{3,2},{4,5},{5,4},{6,7},{7,6},{8,9},{9,8},{10,11... | collective-permute-start | bytes 786440 | tf_op jit(solution)/shard_map/ppermute | solution.py:143
  61.6 0.7 copy-start.25
  61.6 19.3 %collective-permute-start.12 = (bf16[256,512]{1,0:T(8,128)(2,1)S(1)}, bf16[256,512]{1,0:T(8,128)(2,1)}, u32[]{:S(2)}, u32[]{:S(2)}) collective-permute-start(bf16[256,512]{1,0:T(8,128)(2,1)S(1)} %get-tuple-element.47), channel_id=1, source_target_pairs={{0,1},{1,0},{2,3},{3,2},{4,5},{5,4},{6,7},{7,6},{8,9},{9,8},{10,11... | collective-permute-start | bytes 786440 | tf_op jit(solution)/shard_map/ppermute | solution.py:143
  62.2 1.0 copy-start
  80.0 20.3 %collective-permute-start.17 = (bf16[2,256,512]{2,1,0:T(8,128)(2,1)S(1)}, bf16[2,256,512]{2,1,0:T(8,128)(2,1)S(1)}, u32[]{:S(2)}, u32[]{:S(2)}) collective-permute-start(bf16[2,256,512]{2,1,0:T(8,128)(2,1)S(1)} %pad_maximum_fusion), channel_id=1, source_target_pairs={{0,1},{1,0},{2,3},{3,2},{4,5},{5,4},{6,7},{7,6},{8,9},{9,8},{10,11... | collective-permute-start | bytes 1572872 | tf_op jit(solution)/shard_map/ppermute | solution.py:143
  80.3 0.7 copy-start.20
  80.3 20.2 %collective-permute-start.23 = (bf16[2,256,512]{2,1,0:T(8,128)(2,1)S(1)}, bf16[2,256,512]{2,1,0:T(8,128)(2,1)S(1)}, u32[]{:S(2)}, u32[]{:S(2)}) collective-permute-start(bf16[2,256,512]{2,1,0:T(8,128)(2,1)S(1)} %pad_maximum_fusion.2), channel_id=1, source_target_pairs={{0,1},{1,0},{2,3},{3,2},{4,5},{5,4},{6,7},{7,6},{8,9},{9,8},{10,11... | collective-permute-start | bytes 1572872 | tf_op jit(solution)/shard_map/ppermute | solution.py:143
  80.9 0.7 copy-start.21
  97.1 2.2 %copy-start.18 = (bf16[256,1024]{1,0:T(8,128)(2,1)S(1)}, bf16[256,1024]{1,0:T(8,128)(2,1)}, u32[]{:S(2)}) copy-start(bf16[256,1024]{1,0:T(8,128)(2,1)} %get-tuple-element.11) | copy-start | bytes 1572868
  97.1 2.2 %copy-start.19 = (bf16[256,1024]{1,0:T(8,128)(2,1)S(1)}, bf16[256,1024]{1,0:T(8,128)(2,1)}, u32[]{:S(2)}) copy-start(bf16[256,1024]{1,0:T(8,128)(2,1)} %get-tuple-element.14) | copy-start | bytes 1572868
  98.5 7.6 %collective-permute-start.20 = (bf16[2,256,512]{2,1,0:T(8,128)(2,1)S(1)}, bf16[2,256,512]{2,1,0:T(8,128)(2,1)S(1)}, u32[]{:S(2)}, u32[]{:S(2)}) collective-permute-start(bf16[2,256,512]{2,1,0:T(8,128)(2,1)S(1)} %pad_maximum_fusion.1), channel_id=1, source_target_pairs={{0,1},{1,0},{2,3},{3,2},{4,5},{5,4},{6,7},{7,6},{8,9},{9,8},{10,11... | collective-permute-start | bytes 1572872 | tf_op jit(solution)/shard_map/ppermute | solution.py:143
  98.8 7.5 %collective-permute-start.26 = (bf16[2,256,512]{2,1,0:T(8,128)(2,1)S(1)}, bf16[2,256,512]{2,1,0:T(8,128)(2,1)S(1)}, u32[]{:S(2)}, u32[]{:S(2)}) collective-permute-start(bf16[2,256,512]{2,1,0:T(8,128)(2,1)S(1)} %pad_maximum_fusion.3), channel_id=1, source_target_pairs={{0,1},{1,0},{2,3},{3,2},{4,5},{5,4},{6,7},{7,6},{8,9},{9,8},{10,11... | collective-permute-start | bytes 1572872 | tf_op jit(solution)/shard_map/ppermute | solution.py:143
  100.3 1.6 %copy-start.3 = (bf16[4,2,256,512]{3,2,1,0:T(8,128)(2,1)S(1)}, bf16[4,2,256,512]{3,2,1,0:T(8,128)(2,1)}, u32[]{:S(2)}) copy-start(bf16[4,2,256,512]{3,2,1,0:T(8,128)(2,1)} %get-tuple-element.16) | copy-start | bytes 6291460
  102.1 4.3 %copy-start.4 = (bf16[4,2,256,512]{3,2,1,0:T(8,128)(2,1)S(1)}, bf16[4,2,256,512]{3,2,1,0:T(8,128)(2,1)}, u32[]{:S(2)}) copy-start(bf16[4,2,256,512]{3,2,1,0:T(8,128)(2,1)} %get-tuple-element.18) | copy-start | bytes 6291460
  102.1 11.9 %collective-permute-start.18 = (bf16[256,512]{1,0:T(8,128)(2,1)S(1)}, bf16[256,512]{1,0:T(8,128)(2,1)S(1)}, u32[]{:S(2)}, u32[]{:S(2)}) collective-permute-start(bf16[256,512]{1,0:T(8,128)(2,1)S(1)} %get-tuple-element.22), channel_id=1, source_target_pairs={{2,0},{3,1},{4,2},{5,3},{6,4},{7,5},{8,6},{9,7},{10,8},{11,9},{12,... | collective-permute-start | bytes 786440 | tf_op jit(solution)/shard_map/ppermute | solution.py:102
  104.2 15.4 %collective-permute-start.24 = (bf16[256,512]{1,0:T(8,128)(2,1)S(1)}, bf16[256,512]{1,0:T(8,128)(2,1)S(1)}, u32[]{:S(2)}, u32[]{:S(2)}) collective-permute-start(bf16[256,512]{1,0:T(8,128)(2,1)S(1)} %get-tuple-element.21), channel_id=1, source_target_pairs={{2,0},{3,1},{4,2},{5,3},{6,4},{7,5},{8,6},{9,7},{10,8},{11,9},{12,... | collective-permute-start | bytes 786440 | tf_op jit(solution)/shard_map/ppermute | solution.py:102
  106.6 18.7 %collective-permute-start.21 = (bf16[256,512]{1,0:T(8,128)(2,1)S(1)}, bf16[256,512]{1,0:T(8,128)(2,1)S(1)}, u32[]{:S(2)}, u32[]{:S(2)}) collective-permute-start(bf16[256,512]{1,0:T(8,128)(2,1)S(1)} %get-tuple-element.30), channel_id=1, source_target_pairs={{2,0},{3,1},{4,2},{5,3},{6,4},{7,5},{8,6},{9,7},{10,8},{11,9},{12,... | collective-permute-start | bytes 786440 | tf_op jit(solution)/shard_map/ppermute | solution.py:102
  108.5 22.3 %collective-permute-start.27 = (bf16[256,512]{1,0:T(8,128)(2,1)S(1)}, bf16[256,512]{1,0:T(8,128)(2,1)S(1)}, u32[]{:S(2)}, u32[]{:S(2)}) collective-permute-start(bf16[256,512]{1,0:T(8,128)(2,1)S(1)} %get-tuple-element.29), channel_id=1, source_target_pairs={{2,0},{3,1},{4,2},{5,3},{6,4},{7,5},{8,6},{9,7},{10,8},{11,9},{12,... | collective-permute-start | bytes 786440 | tf_op jit(solution)/shard_map/ppermute | solution.py:102
  120.0 22.1 %copy-start.12 = (f32[2,256,512]{2,1,0:T(8,128)S(1)}, f32[2,256,512]{2,1,0:T(8,128)}, u32[]{:S(2)}) copy-start(f32[2,256,512]{2,1,0:T(8,128)} %get-tuple-element.15) | copy-start | bytes 3145732
  120.0 16.5 %collective-permute-start.19 = (bf16[256,512]{1,0:T(8,128)(2,1)S(1)}, bf16[256,512]{1,0:T(8,128)(2,1)S(1)}, u32[]{:S(2)}, u32[]{:S(2)}) collective-permute-start(bf16[256,512]{1,0:T(8,128)(2,1)S(1)} %get-tuple-element.20), channel_id=1, source_target_pairs={{2,0},{3,1},{4,2},{5,3},{6,4},{7,5},{8,6},{9,7},{10,8},{11,9},{12,... | collective-permute-start | bytes 786440 | tf_op jit(solution)/shard_map/ppermute | solution.py:102
  122.0 20.1 %collective-permute-start.25 = (bf16[256,512]{1,0:T(8,128)(2,1)S(1)}, bf16[256,512]{1,0:T(8,128)(2,1)S(1)}, u32[]{:S(2)}, u32[]{:S(2)}) collective-permute-start(bf16[256,512]{1,0:T(8,128)(2,1)S(1)} %get-tuple-element.19), channel_id=1, source_target_pairs={{2,0},{3,1},{4,2},{5,3},{6,4},{7,5},{8,6},{9,7},{10,8},{11,9},{12,... | collective-permute-start | bytes 786440 | tf_op jit(solution)/shard_map/ppermute | solution.py:102
  131.2 22.1 %copy-start.13 = (f32[2,256,512]{2,1,0:T(8,128)S(1)}, f32[2,256,512]{2,1,0:T(8,128)}, u32[]{:S(2)}) copy-start(f32[2,256,512]{2,1,0:T(8,128)} %get-tuple-element.17) | copy-start | bytes 3145732
  131.2 16.5 %collective-permute-start.22 = (bf16[256,512]{1,0:T(8,128)(2,1)S(1)}, bf16[256,512]{1,0:T(8,128)(2,1)S(1)}, u32[]{:S(2)}, u32[]{:S(2)}) collective-permute-start(bf16[256,512]{1,0:T(8,128)(2,1)S(1)} %get-tuple-element.28), channel_id=1, source_target_pairs={{2,0},{3,1},{4,2},{5,3},{6,4},{7,5},{8,6},{9,7},{10,8},{11,9},{12,... | collective-permute-start | bytes 786440 | tf_op jit(solution)/shard_map/ppermute | solution.py:102
  133.3 20.1 %collective-permute-start.28 = (bf16[256,512]{1,0:T(8,128)(2,1)S(1)}, bf16[256,512]{1,0:T(8,128)(2,1)S(1)}, u32[]{:S(2)}, u32[]{:S(2)}) collective-permute-start(bf16[256,512]{1,0:T(8,128)(2,1)S(1)} %get-tuple-element.27), channel_id=1, source_target_pairs={{2,0},{3,1},{4,2},{5,3},{6,4},{7,5},{8,6},{9,7},{10,8},{11,9},{12,... | collective-permute-start | bytes 786440 | tf_op jit(solution)/shard_map/ppermute | solution.py:102
